TPU v7x, 128 devices: a whole 4x4x4 slice. The times are simulated.
128 devices in a mesh: occ: 8 (over z_hi, x), vir: 16 (over z_lo, y, core).
Axes of the slice: x: 4, y: 4, z: 4 (z_hi: 2, z_lo: 2; z = z_hi * 2 + z_lo), core: 2. Of those that a mesh axis runs over, the one named last changes fastest.
Arguments:
- amplitudes: float32 [512, 10240], P('vir', 'occ'), may hold values from -12 to 12
- integrals: float32 [10240, 10240], P('occ', 'vir'), may hold values from -0.0625 to 0.0625
Outputs:
- ladder: float32 [512, 10240], P('occ', 'vir')
All inputs are finite; a program needn't handle non-finite values.
Results may differ from a plain program's by a relative error of at most 0.00007.
Values sent between devices are 32-bit elements; how exact they have to be, the bound alone decides.
No kernel may reach another device: no remote copies, remote signals or barrier semaphores. Data moves between devices by JAX's collectives and lax.ppermute only.
A program may use at most 64 MiB of HBM per device.

v0:
```python
import jax
import jax.numpy as jnp
from jax import lax
from jax.sharding import PartitionSpec as P


def body(amplitudes, integrals):
    gathered = lax.all_gather(amplitudes, "vir", axis=0, tiled=True)
    contracted = lax.psum_scatter(
        jnp.dot(
            gathered, integrals, preferred_element_type=jnp.float32, precision=lax.Precision.HIGHEST
        ),
        "occ",
        scatter_dimension=0,
        tiled=True,
    )
    return 0.5 * contracted


def solution(mesh):
    placed = (P("vir", "occ"), P("occ", "vir"))
    return jax.shard_map(
        body, mesh=mesh, in_specs=placed, out_specs=P("occ", "vir"), check_vma=False
    )
```

profile of v0, /device:TPU:24, one launch (start us, length us, event | category | flops | bytes accessed | tf_op | source)
XLA Modules:
  0.0 138.4 jit_solution(13106731399685882113)
XLA Ops:
  6.5 0.0 copy-start
  6.5 0.0 all-gather.2.cloned.1.call-start
  6.5 0.7 all-gather.2.cloned.1.call-update
  7.3 0.0 reduce-scatter.2.cloned.1.call-start
  7.3 37.6 %all-gather.2.cloned.1.call-done = f32[512,1280]{1,0:T(8,128)} async-done(((f32[32,1280]{1,0:T(8,128)}), f32[512,1280]{1,0:T(8,128)}) %all-gather.2.cloned.1.call-update) | async-done | bytes 2621456 | tf_op jit(solution)/shard_map/all_gather | solution.py:8
  44.9 0.0 copy-done
  44.9 9.3 %fusion = f32[512,640]{1,0:T(8,128)} fusion(f32[512,1280]{1,0:T(8,128)} %all-gather.2.cloned.1.call-done, f32[1280,640]{1,0:T(8,128)S(1)} %copy-done), kind=kOutput, calls=%fused_computation.1 | convolution fusion | flops 5033164800 | bytes 7208960 | tf_op jit(solution)/shard_map/dot_general | solution.py:10
  54.2 0.0 reduce-scatter.2.cloned.1.call-update
  54.2 75.7 %reduce-scatter.2.cloned.1.call-done = f32[64,640]{1,0:T(8,128)} async-done(((f32[512,640]{1,0:T(8,128)}), f32[64,640]{1,0:T(8,128)}) %reduce-scatter.2.cloned.1.call-update) | async-done | bytes 163856 | tf_op jit(solution)/shard_map/reduce_scatter | solution.py:9
  129.9 1.6 %broadcast_multiply_fusion = f32[64,640]{1,0:T(8,128)} fusion(f32[64,640]{1,0:T(8,128)} %reduce-scatter.2.cloned.1.call-done), kind=kLoop, calls=%fused_computation | loop fusion | flops 40960 | bytes 327680 | tf_op jit(solution)/shard_map/mul | solution.py:17
Async XLA Ops:
  6.5 38.4 %copy-start = (f32[1280,640]{1,0:T(8,128)S(1)}, f32[1280,640]{1,0:T(8,128)}, u32[]{:S(2)}) copy-start(f32[1280,640]{1,0:T(8,128)} %param.3) | copy-start | bytes 9830404
  6.5 38.4 %all-gather.2.cloned.1.call-start = ((), (), s32[]{:S(2)}) async-start(), calls=%async_computation.1 | async-start | bytes 2785280 | tf_op jit(solution)/shard_map/all_gather | solution.py:8
  7.3 122.7 %reduce-scatter.2.cloned.1.call-start = ((), (), s32[]{:S(2)}) async-start(), calls=%async_computation.2 | async-start | bytes 1474560 | tf_op jit(solution)/shard_map/reduce_scatter | solution.py:9
Sparse Core Ops, SparseCore 0:
  9.0 35.8 all-gather.1
  54.3 75.5 reduce-scatter.1
where the time goes:
time: 139 us; the launch traced here: 138 us
  waiting for transfers between devices  114 us (82%)
  between operations  13.4 us (10%)
  matrix products  9.28 us (7%)
  other arithmetic  1.59 us (1%)
    reduce_scatter x1, waiting for transfers between devices, body(): lax.psum_scatter(jnp.dot(gathered, integrals, preferred_element_type=jnp....  75.7 us
    all_gather x1, waiting for transfers between devices, body(): gathered = lax.all_gather(amplitudes, 'vir', axis=0, tiled=True)  37.6 us
    dot_general x1, matrix products, body(): jnp.dot(gathered, integrals, preferred_element_type=jnp.float32, precisio...  9.28 us
  transfers between devices with their start and end apart: 2, of which 2 were waited for; matrix products, arithmetic and copies ran while one was open for 0% of the time, Pallas kernels for 0%

commit v1 on v0

v1 whole, which is shorter than its diff:
```python
import jax
import jax.numpy as jnp
from jax import lax
from jax.sharding import PartitionSpec as P

HIGHEST = lax.Precision.HIGHEST


def _pairs(n, dest):
    return [(k, dest(k)) for k in range(n)]


def make_body(n_occ, n_vir):
    ny = n_vir // 4
    nx = n_occ // 2

    def vir_of(zl, y, c):
        return zl * (2 * ny) + y * 2 + c

    def vir_split(j):
        return j // (2 * ny), (j // 2) % ny, j % 2

    def y_shift(s):
        def dest(j):
            zl, y, c = vir_split(j)
            return vir_of(zl, (y + s) % ny, c)

        return _pairs(n_vir, dest)

    def x_shift(s):
        return _pairs(n_occ, lambda i: (i // nx) * nx + (i % nx + s) % nx)

    z_swap = _pairs(n_vir, lambda j: j ^ (2 * ny))
    core_swap = _pairs(n_vir, lambda j: j ^ 1)
    zhi_swap = _pairs(n_occ, lambda i: (i + nx) % n_occ)

    def body(amplitudes, integrals):
        rows, cd = amplitudes.shape
        me = lax.axis_index("vir")
        zl, y, c = me // (2 * ny), (me // 2) % ny, me % 2

        b_z = lax.ppermute(amplitudes, "vir", z_swap)
        pair = jnp.concatenate([amplitudes, b_z], axis=0)
        from_m = lax.ppermute(pair, "vir", y_shift(1))
        from_p = lax.ppermute(pair, "vir", y_shift(-1))
        far_m = lax.ppermute(from_m[:rows], "vir", y_shift(1))
        far_p = lax.ppermute(from_p[rows:], "vir", y_shift(-1))
        local = jnp.concatenate([amplitudes, b_z, from_m, from_p, far_m, far_p], axis=0)
        other = lax.ppermute(local, "vir", core_swap)
        offsets = [(0, 0), (0, 1), (-1, 0), (-1, 1), (1, 0), (1, 1), (2, 0), (2, 1)]
        full = jnp.zeros((n_vir, rows, cd), amplitudes.dtype)
        for k, (dy, dz) in enumerate(offsets):
            base = (zl ^ dz) * (2 * ny) + ((y + dy) % ny) * 2
            full = lax.dynamic_update_index_in_dim(full, local[k * rows:(k + 1) * rows], base + c, 0)
            full = lax.dynamic_update_index_in_dim(full, other[k * rows:(k + 1) * rows], base + (1 - c), 0)
        full = full.reshape(n_vir * rows, cd)

        partial = 0.5 * jnp.dot(
            full, integrals, preferred_element_type=jnp.float32, precision=HIGHEST
        )

        mo = lax.axis_index("occ")
        x, zh = mo % nx, mo // nx
        blocks = partial.reshape(n_occ, -1, partial.shape[1])

        def a_blk(t):
            return lax.dynamic_index_in_dim(blocks, t % nx, 0, keepdims=False)

        def b_blk(t):
            return lax.dynamic_index_in_dim(blocks, nx + t % nx, 0, keepdims=False)

        sa = a_blk(x - 1 + nx)
        sb = b_blk(x + 1)
        for s in range(1, nx):
            sa = lax.ppermute(sa, "occ", x_shift(1)) + a_blk(x - s - 1 + 2 * nx)
            sb = lax.ppermute(sb, "occ", x_shift(-1)) + b_blk(x + s + 1)
        keep = jnp.where(zh == 0, sa, sb)
        send = jnp.where(zh == 0, sb, sa)
        return keep + lax.ppermute(send, "occ", zhi_swap)

    return body


def solution(mesh):
    placed = (P("vir", "occ"), P("occ", "vir"))
    return jax.shard_map(
        make_body(mesh.shape["occ"], mesh.shape["vir"]),
        mesh=mesh,
        in_specs=placed,
        out_specs=P("occ", "vir"),
        check_vma=False,
    )
```

time: 139 us -> 83.6 us (0.60)
  waiting for transfers between devices: 114 us -> 35 us
  starting transfers between devices: 0.04 us -> 17.7 us
  local copies, waits for them, and re-layouts: 0.01 us -> 16.2 us
  between operations: 13.4 us -> 0.2 us
  other arithmetic: 1.59 us -> 6.64 us
  matrix products: 9.28 us -> 6.52 us
    reduce_scatter x1 -> x0, waiting for transfers between devices: 75.7 us -> none  [body(): lax.psum_scatter(jnp.dot(gathered, integrals, preferred_element_type=jnp....]
    all_gather x1 -> x0, waiting for transfers between devices: 37.6 us -> none  [body(): gathered = lax.all_gather(amplitudes, 'vir', axis=0, tiled=True)]
    ppermute x0 -> x13, waiting for transfers between devices: none -> 35 us  [the longest x3 8.2 us: body(): sa = lax.ppermute(sa, 'occ', x_shift(1)) + a_blk(x - s - 1 + 2 * nx)]
    ppermute x0 -> x13, starting transfers between devices: none -> 17.7 us  [the longest x3 6.12 us: body(): sb = lax.ppermute(sb, 'occ', x_shift(-1)) + b_blk(x + s + 1)]
    dynamic_update_slice x0 -> x16, local copies, waits for them, and re-layouts: none -> 7.61 us  [the longest x8 7.47 us: body(): lax.dynamic_update_index_in_dim(full, other[k * rows:(k + 1) * rows], bas...]
    unnamed x2 -> x26, local copies, waits for them, and re-layouts: 0.01 us -> 6.22 us
    add x0 -> x3, other arithmetic: none -> 5.53 us  [the longest x2 3.74 us: body(): sb = lax.ppermute(sb, 'occ', x_shift(-1)) + b_blk(x + s + 1)]
    dot_general x1, matrix products: 9.28 us -> 6.52 us  [body(): jnp.dot(full, integrals, preferred_element_type=jnp.float32, precision=HI...]
  transfers between devices with their start and end apart: 2 -> 13, of which waited for: 2 -> 11; matrix products, arithmetic and copies ran while one was open for 0% -> 5% of each run, Pallas kernels for 0% -> 0%
where the time goes in v1:
time: 83.6 us; the launch traced here: 82.2 us
  waiting for transfers between devices  35 us (42%)
  starting transfers between devices  17.7 us (21%)
  local copies, waits for them, and re-layouts  16.2 us (19%)
  other arithmetic  6.64 us (8%)
  matrix products  6.52 us (8%)
    ppermute x3, waiting for transfers between devices, body(): sa = lax.ppermute(sa, 'occ', x_shift(1)) + a_blk(x - s - 1 + 2 * nx)  8.2 us
    ppermute x3, waiting for transfers between devices, body(): sb = lax.ppermute(sb, 'occ', x_shift(-1)) + b_blk(x + s + 1)  7.68 us
    dynamic_update_slice x8, local copies, waits for them, and re-layouts, body(): lax.dynamic_update_index_in_dim(full, other[k * rows:(k + 1) * rows], bas...  7.47 us
    ppermute x1, waiting for transfers between devices, body(): from_m = lax.ppermute(pair, 'vir', y_shift(1))  6.74 us
    dot_general x1, matrix products, body(): jnp.dot(full, integrals, preferred_element_type=jnp.float32, precision=HI...  6.52 us
    unnamed x26, local copies, waits for them, and re-layouts  6.22 us
    ppermute x3, starting transfers between devices, body(): sb = lax.ppermute(sb, 'occ', x_shift(-1)) + b_blk(x + s + 1)  6.12 us
    add x2, other arithmetic, body(): sb = lax.ppermute(sb, 'occ', x_shift(-1)) + b_blk(x + s + 1)  3.74 us
  transfers between devices with their start and end apart: 13, of which 11 were waited for; matrix products, arithmetic and copies ran while one was open for 5% of the time, Pallas kernels for 0%

profile of v1, /device:TPU:24, one launch (start us, length us, event | category | flops | bytes accessed | tf_op | source)
XLA Modules:
  0.0 82.2 jit_solution(6571148925889691019)
XLA Ops:
  0.0 1.9 %collective-permute-start = (f32[32,1280]{1,0:T(8,128)}, f32[32,1280]{1,0:T(8,128)S(1)}, u32[]{:S(2)}, u32[]{:S(2)}) collective-permute-start(f32[32,1280]{1,0:T(8,128)} %param.2), channel_id=1, source_target_pairs={{0,8},{1,9},{2,10},{3,11},{4,12},{5,13},{6,14},{7,15},{8,0},{9,1},... | collective-permute-start | bytes 491528 | tf_op jit(solution)/shard_map/ppermute | solution.py:42
  1.9 1.6 %constant_dynamic-update-slice_fusion.1 = (f32[64,1280]{1,0:T(8,128)S(1)}, f32[256,1280]{1,0:T(8,128)}) fusion(f32[32,1280]{1,0:T(8,128)} %param.2), kind=kLoop, calls=%fused_computation.38 | loop fusion | bytes 491520
  3.5 2.8 %collective-permute-done = f32[32,1280]{1,0:T(8,128)S(1)} collective-permute-done((f32[32,1280]{1,0:T(8,128)}, f32[32,1280]{1,0:T(8,128)S(1)}, u32[]{:S(2)}, u32[]{:S(2)}) %collective-permute-start) | collective-permute-done | bytes 163872 | tf_op jit(solution)/shard_map/ppermute | solution.py:42
  7.3 1.8 %collective-permute-start.2 = (f32[64,1280]{1,0:T(8,128)S(1)}, f32[64,1280]{1,0:T(8,128)S(1)}, u32[]{:S(2)}, u32[]{:S(2)}) collective-permute-start(f32[64,1280]{1,0:T(8,128)S(1)} %get-tuple-element.11), channel_id=1, source_target_pairs={{0,6},{1,7},{2,0},{3,1},{4,2},{5,3},{6,4},{7,5},{8,14},{9,15},{10,... | collective-permute-start | bytes 983048 | tf_op jit(solution)/shard_map/ppermute | solution.py:45
  9.1 6.7 %collective-permute-done.1 = f32[64,1280]{1,0:T(8,128)S(1)} collective-permute-done((f32[64,1280]{1,0:T(8,128)S(1)}, f32[64,1280]{1,0:T(8,128)S(1)}, u32[]{:S(2)}, u32[]{:S(2)}) %collective-permute-start.1) | collective-permute-done | bytes 327712 | tf_op jit(solution)/shard_map/ppermute | solution.py:44
  15.8 1.6 %collective-permute-start.3 = (f32[32,1280]{1,0:T(8,128)S(1)}, f32[32,1280]{1,0:T(8,128)S(1)}, u32[]{:S(2)}, u32[]{:S(2)}) collective-permute-start(f32[32,1280]{1,0:T(8,128)S(1)} %slice.50), channel_id=1, source_target_pairs={{0,2},{1,3},{2,4},{3,5},{4,6},{5,7},{6,0},{7,1},{8,10},{9,11},{10,... | collective-permute-start | bytes 491528 | tf_op jit(solution)/shard_map/ppermute | solution.py:46
  19.6 1.7 %collective-permute-done.3 = f32[32,1280]{1,0:T(8,128)S(1)} collective-permute-done((f32[32,1280]{1,0:T(8,128)S(1)}, f32[32,1280]{1,0:T(8,128)S(1)}, u32[]{:S(2)}, u32[]{:S(2)}) %collective-permute-start.3) | collective-permute-done | bytes 163872 | tf_op jit(solution)/shard_map/ppermute | solution.py:46
  21.9 2.2 %collective-permute-done.4 = f32[32,1280]{1,0:T(8,128)S(1)} collective-permute-done((f32[32,1280]{1,0:T(8,128)S(1)}, f32[32,1280]{1,0:T(8,128)S(1)}, u32[]{:S(2)}, u32[]{:S(2)}) %collective-permute-start.4) | collective-permute-done | bytes 163872 | tf_op jit(solution)/shard_map/ppermute | solution.py:47
  26.3 2.4 %collective-permute-done.5 = f32[256,1280]{1,0:T(8,128)} collective-permute-done((f32[256,1280]{1,0:T(8,128)}, f32[256,1280]{1,0:T(8,128)}, u32[]{:S(2)}, u32[]{:S(2)}) %collective-permute-start.5) | collective-permute-done | bytes 1310752 | tf_op jit(solution)/shard_map/ppermute | solution.py:49
  36.5 6.5 %convolution_multiply_fusion = f32[512,640]{1,0:T(8,128)S(1)} fusion(f32[512,1280]{1,0:T(8,128)S(1)} %bitcast.80, f32[1280,640]{1,0:T(8,128)S(1)} %copy-done), kind=kOutput, calls=%fused_computation | convolution fusion | flops 5033492480 | bytes 7208960 | tf_op jit(solution)/shard_map/dot_general | solution.py:58
  44.8 2.7 %collective-permute-start.9 = (f32[64,640]{1,0:T(8,128)}, f32[64,640]{1,0:T(8,128)}, u32[]{:S(2)}, u32[]{:S(2)}) collective-permute-start(f32[64,640]{1,0:T(8,128)} %get-tuple-element.9), channel_id=1, source_target_pairs={{0,48},{16,0},{32,16},{48,32},{64,112},{80,64},{96,80},{112,96},{1... | collective-permute-start | bytes 491528 | tf_op jit(solution)/shard_map/ppermute | solution.py:76
  47.5 4.1 %collective-permute-done.9 = f32[64,640]{1,0:T(8,128)} collective-permute-done((f32[64,640]{1,0:T(8,128)}, f32[64,640]{1,0:T(8,128)}, u32[]{:S(2)}, u32[]{:S(2)}) %collective-permute-start.9) | collective-permute-done | bytes 163872 | tf_op jit(solution)/shard_map/ppermute | solution.py:76
  51.6 3.2 %collective-permute-done.6 = f32[64,640]{1,0:T(8,128)} collective-permute-done((f32[64,640]{1,0:T(8,128)S(1)}, f32[64,640]{1,0:T(8,128)}, u32[]{:S(2)}, u32[]{:S(2)}) %collective-permute-start.6) | collective-permute-done | bytes 163872 | tf_op jit(solution)/shard_map/ppermute | solution.py:75
  54.8 1.9 %bitcast_add_fusion.2 = (f32[64,640]{1,0:T(8,128)}, f32[64,640]{1,0:T(8,128)S(1)}) fusion(f32[64,640]{1,0:T(8,128)} %collective-permute-done.9, f32[8,64,640]{2,1,0:T(8,128)} %bitcast.82, s32[]{:T(128)S(6)} %select_n.201, f32[64,640]{1,0:T(8,128)} %collective-permute-done.6, s32[]{:T(128)S(6)} %select_n.193), kind=kLoop, calls=%fused_computation.23 | loop fusion | flops 81920 | bytes 983048 | tf_op jit(solution)/shard_map/add | solution.py:76
  57.1 1.5 %collective-permute-start.7 = (f32[64,640]{1,0:T(8,128)S(1)}, f32[64,640]{1,0:T(8,128)}, u32[]{:S(2)}, u32[]{:S(2)}) collective-permute-start(f32[64,640]{1,0:T(8,128)S(1)} %get-tuple-element.8), channel_id=1, source_target_pairs={{0,16},{16,32},{32,48},{48,0},{64,80},{80,96},{96,112},{112,64},{1... | collective-permute-start | bytes 491528 | tf_op jit(solution)/shard_map/ppermute | solution.py:75
  58.7 3.6 %collective-permute-done.10 = f32[64,640]{1,0:T(8,128)} collective-permute-done((f32[64,640]{1,0:T(8,128)}, f32[64,640]{1,0:T(8,128)}, u32[]{:S(2)}, u32[]{:S(2)}) %collective-permute-start.10) | collective-permute-done | bytes 163872 | tf_op jit(solution)/shard_map/ppermute | solution.py:76
  62.3 1.5 %collective-permute-done.7 = f32[64,640]{1,0:T(8,128)} collective-permute-done((f32[64,640]{1,0:T(8,128)S(1)}, f32[64,640]{1,0:T(8,128)}, u32[]{:S(2)}, u32[]{:S(2)}) %collective-permute-start.7) | collective-permute-done | bytes 163872 | tf_op jit(solution)/shard_map/ppermute | solution.py:75
  63.8 1.9 %bitcast_add_fusion.1 = (f32[64,640]{1,0:T(8,128)}, f32[64,640]{1,0:T(8,128)}) fusion(f32[64,640]{1,0:T(8,128)} %collective-permute-done.10, f32[8,64,640]{2,1,0:T(8,128)} %bitcast.83, s32[]{:T(128)S(6)} %select_n.202, f32[64,640]{1,0:T(8,128)} %collective-permute-done.7, s32[]{:T(128)S(6)} %select_n.195), kind=kLoop, calls=%fused_computation.22 | loop fusion | flops 81920 | bytes 983048 | tf_op jit(solution)/shard_map/add | solution.py:76
  66.0 2.9 %collective-permute-start.11 = (f32[64,640]{1,0:T(8,128)}, f32[64,640]{1,0:T(8,128)}, u32[]{:S(2)}, u32[]{:S(2)}) collective-permute-start(f32[64,640]{1,0:T(8,128)} %get-tuple-element.5), channel_id=1, source_target_pairs={{0,48},{16,0},{32,16},{48,32},{64,112},{80,64},{96,80},{112,96},{1... | collective-permute-start | bytes 491528 | tf_op jit(solution)/shard_map/ppermute | solution.py:76
  68.9 3.5 %collective-permute-done.8 = f32[64,640]{1,0:T(8,128)S(1)} collective-permute-done((f32[64,640]{1,0:T(8,128)}, f32[64,640]{1,0:T(8,128)S(1)}, u32[]{:S(2)}, u32[]{:S(2)}) %collective-permute-start.8) | collective-permute-done | bytes 163872 | tf_op jit(solution)/shard_map/ppermute | solution.py:75
  72.4 1.1 %broadcast_select_fusion = f32[64,640]{1,0:T(8,128)S(1)} fusion(pred[]{:T(512)S(6)} %eq.24, f32[64,640]{1,0:T(8,128)S(1)} %collective-permute-done.8, f32[8,64,640]{2,1,0:T(8,128)} %bitcast.84, s32[]{:T(128)S(6)} %select_n.197, f32[64,640]{1,0:T(8,128)} %collective-permute-done.11, s32[]{:T(128)S(6)} %select_n.203), kind=kLoop, calls=%fused_computation.36 | loop fusion | flops 122880 | bytes 819209 | tf_op jit(solution)/shard_map/jit(_where)/select_n | solution.py:78
  73.5 3.6 %collective-permute-start.12 = (f32[64,640]{1,0:T(8,128)S(1)}, f32[64,640]{1,0:T(8,128)S(1)}, u32[]{:S(2)}, u32[]{:S(2)}) collective-permute-start(f32[64,640]{1,0:T(8,128)S(1)} %broadcast_select_fusion), channel_id=1, source_target_pairs={{0,64},{16,80},{32,96},{48,112},{64,0},{80,16},{96,32},{112,48},{1... | collective-permute-start | bytes 491528 | tf_op jit(solution)/shard_map/ppermute | solution.py:79
  77.1 3.3 %collective-permute-done.12 = f32[64,640]{1,0:T(8,128)S(1)} collective-permute-done((f32[64,640]{1,0:T(8,128)S(1)}, f32[64,640]{1,0:T(8,128)S(1)}, u32[]{:S(2)}, u32[]{:S(2)}) %collective-permute-start.12) | collective-permute-done | bytes 163872 | tf_op jit(solution)/shard_map/ppermute | solution.py:79
  80.4 1.8 %select_add_fusion = f32[64,640]{1,0:T(8,128)} fusion(f32[64,640]{1,0:T(8,128)S(1)} %collective-permute-done.12, pred[]{:T(512)S(6)} %eq.24, f32[64,640]{1,0:T(8,128)S(1)} %collective-permute-done.8, f32[8,64,640]{2,1,0:T(8,128)} %bitcast.85, s32[]{:T(128)S(6)} %select_n.197, f32[64,640]{1,0:T(8,128)} %collective-permute-done.11, s32[]{:T(128)S(6)} %select_n.203), kind=kLoop, calls=%fused_computation.33 | loop fusion | flops 163840 | bytes 983049 | tf_op jit(solution)/shard_map/add | solution.py:79
  (55 shorter events, 16.2 us)
Async XLA Ops:
  0.0 36.5 %copy-start = (f32[1280,640]{1,0:T(8,128)S(1)}, f32[1280,640]{1,0:T(8,128)}, u32[]{:S(2)}) copy-start(f32[1280,640]{1,0:T(8,128)} %param.3) | copy-start | bytes 9830404
  0.0 6.3 %collective-permute-start = (f32[32,1280]{1,0:T(8,128)}, f32[32,1280]{1,0:T(8,128)S(1)}, u32[]{:S(2)}, u32[]{:S(2)}) collective-permute-start(f32[32,1280]{1,0:T(8,128)} %param.2), channel_id=1, source_target_pairs={{0,8},{1,9},{2,10},{3,11},{4,12},{5,13},{6,14},{7,15},{8,0},{9,1},... | collective-permute-start | bytes 491528 | tf_op jit(solution)/shard_map/ppermute | solution.py:42
  6.3 0.7 copy-start.9
  7.1 8.8 %collective-permute-start.1 = (f32[64,1280]{1,0:T(8,128)S(1)}, f32[64,1280]{1,0:T(8,128)S(1)}, u32[]{:S(2)}, u32[]{:S(2)}) collective-permute-start(f32[64,1280]{1,0:T(8,128)S(1)} %get-tuple-element.11), channel_id=1, source_target_pairs={{0,2},{1,3},{2,4},{3,5},{4,6},{5,7},{6,0},{7,1},{8,10},{9,11},{10,... | collective-permute-start | bytes 983048 | tf_op jit(solution)/shard_map/ppermute | solution.py:44
  7.3 10.2 %collective-permute-start.2 = (f32[64,1280]{1,0:T(8,128)S(1)}, f32[64,1280]{1,0:T(8,128)S(1)}, u32[]{:S(2)}, u32[]{:S(2)}) collective-permute-start(f32[64,1280]{1,0:T(8,128)S(1)} %get-tuple-element.11), channel_id=1, source_target_pairs={{0,6},{1,7},{2,0},{3,1},{4,2},{5,3},{6,4},{7,5},{8,14},{9,15},{10,... | collective-permute-start | bytes 983048 | tf_op jit(solution)/shard_map/ppermute | solution.py:45
  15.8 3.7 %copy-start.4 = (f32[64,1280]{1,0:T(8,128)}, f32[64,1280]{1,0:T(8,128)S(1)}, u32[]{:S(2)}) copy-start(f32[64,1280]{1,0:T(8,128)S(1)} %collective-permute-done.1) | copy-start | bytes 983044
  15.8 5.4 %collective-permute-start.3 = (f32[32,1280]{1,0:T(8,128)S(1)}, f32[32,1280]{1,0:T(8,128)S(1)}, u32[]{:S(2)}, u32[]{:S(2)}) collective-permute-start(f32[32,1280]{1,0:T(8,128)S(1)} %slice.50), channel_id=1, source_target_pairs={{0,2},{1,3},{2,4},{3,5},{4,6},{5,7},{6,0},{7,1},{8,10},{9,11},{10,... | collective-permute-start | bytes 491528 | tf_op jit(solution)/shard_map/ppermute | solution.py:46
  17.5 1.4 %copy-start.2 = (f32[64,1280]{1,0:T(8,128)}, f32[64,1280]{1,0:T(8,128)S(1)}, u32[]{:S(2)}) copy-start(f32[64,1280]{1,0:T(8,128)S(1)} %collective-permute-done.2) | copy-start | bytes 983044
  17.5 6.6 %collective-permute-start.4 = (f32[32,1280]{1,0:T(8,128)S(1)}, f32[32,1280]{1,0:T(8,128)S(1)}, u32[]{:S(2)}, u32[]{:S(2)}) collective-permute-start(f32[32,1280]{1,0:T(8,128)S(1)} %slice.51), channel_id=1, source_target_pairs={{0,6},{1,7},{2,0},{3,1},{4,2},{5,3},{6,4},{7,5},{8,14},{9,15},{10,... | collective-permute-start | bytes 491528 | tf_op jit(solution)/shard_map/ppermute | solution.py:47
  24.1 0.7 copy-start.6
  25.4 3.4 %collective-permute-start.5 = (f32[256,1280]{1,0:T(8,128)}, f32[256,1280]{1,0:T(8,128)}, u32[]{:S(2)}, u32[]{:S(2)}) collective-permute-start(f32[256,1280]{1,0:T(8,128)} %constant_dynamic-update-slice_fusion.2), channel_id=1, source_target_pairs={{0,1},{1,0},{2,3},{3,2},{4,5},{5,4},{6,7},{7,6},{8,9},{9,8},{10,11... | collective-permute-start | bytes 3932168 | tf_op jit(solution)/shard_map/ppermute | solution.py:49
  25.4 0.9 %copy-start.8 = (f32[32,1280]{1,0:T(8,128)S(1)}, f32[32,1280]{1,0:T(8,128)}, u32[]{:S(2)}) copy-start(f32[32,1280]{1,0:T(8,128)} %param.2) | copy-start | bytes 491524
  25.4 4.3 %copy-start.10 = (f32[32,1280]{1,0:T(8,128)S(1)}, f32[32,1280]{1,0:T(8,128)}, u32[]{:S(2)}) copy-start(f32[32,1280]{1,0:T(8,128)} %copy-done.9) | copy-start | bytes 491524
  25.4 5.3 %copy-start.5 = (f32[64,1280]{1,0:T(8,128)S(1)}, f32[64,1280]{1,0:T(8,128)}, u32[]{:S(2)}) copy-start(f32[64,1280]{1,0:T(8,128)} %copy-done.4) | copy-start | bytes 983044
  25.4 7.2 %copy-start.3 = (f32[64,1280]{1,0:T(8,128)S(1)}, f32[64,1280]{1,0:T(8,128)}, u32[]{:S(2)}) copy-start(f32[64,1280]{1,0:T(8,128)} %copy-done.2) | copy-start | bytes 983044
  26.3 9.2 %copy-start.7 = (f32[32,1280]{1,0:T(8,128)S(1)}, f32[32,1280]{1,0:T(8,128)}, u32[]{:S(2)}) copy-start(f32[32,1280]{1,0:T(8,128)} %copy-done.6) | copy-start | bytes 491524
  43.0 1.1 %copy-start.1 = (f32[512,640]{1,0:T(8,128)}, f32[512,640]{1,0:T(8,128)S(1)}, u32[]{:S(2)}) copy-start(f32[512,640]{1,0:T(8,128)S(1)} %convolution_multiply_fusion) | copy-start | bytes 3932164
  44.8 6.8 %collective-permute-start.9 = (f32[64,640]{1,0:T(8,128)}, f32[64,640]{1,0:T(8,128)}, u32[]{:S(2)}, u32[]{:S(2)}) collective-permute-start(f32[64,640]{1,0:T(8,128)} %get-tuple-element.9), channel_id=1, source_target_pairs={{0,48},{16,0},{32,16},{48,32},{64,112},{80,64},{96,80},{112,96},{1... | collective-permute-start | bytes 491528 | tf_op jit(solution)/shard_map/ppermute | solution.py:76
  47.5 7.3 %collective-permute-start.6 = (f32[64,640]{1,0:T(8,128)S(1)}, f32[64,640]{1,0:T(8,128)}, u32[]{:S(2)}, u32[]{:S(2)}) collective-permute-start(f32[64,640]{1,0:T(8,128)S(1)} %get-tuple-element.10), channel_id=1, source_target_pairs={{0,16},{16,32},{32,48},{48,0},{64,80},{80,96},{96,112},{112,64},{1... | collective-permute-start | bytes 491528 | tf_op jit(solution)/shard_map/ppermute | solution.py:75
  56.6 5.6 %collective-permute-start.10 = (f32[64,640]{1,0:T(8,128)}, f32[64,640]{1,0:T(8,128)}, u32[]{:S(2)}, u32[]{:S(2)}) collective-permute-start(f32[64,640]{1,0:T(8,128)} %get-tuple-element.7), channel_id=1, source_target_pairs={{0,48},{16,0},{32,16},{48,32},{64,112},{80,64},{96,80},{112,96},{1... | collective-permute-start | bytes 491528 | tf_op jit(solution)/shard_map/ppermute | solution.py:76
  57.1 6.6 %collective-permute-start.7 = (f32[64,640]{1,0:T(8,128)S(1)}, f32[64,640]{1,0:T(8,128)}, u32[]{:S(2)}, u32[]{:S(2)}) collective-permute-start(f32[64,640]{1,0:T(8,128)S(1)} %get-tuple-element.8), channel_id=1, source_target_pairs={{0,16},{16,32},{32,48},{48,0},{64,80},{80,96},{96,112},{112,64},{1... | collective-permute-start | bytes 491528 | tf_op jit(solution)/shard_map/ppermute | solution.py:75
  65.7 6.7 %collective-permute-start.8 = (f32[64,640]{1,0:T(8,128)}, f32[64,640]{1,0:T(8,128)S(1)}, u32[]{:S(2)}, u32[]{:S(2)}) collective-permute-start(f32[64,640]{1,0:T(8,128)} %get-tuple-element.6), channel_id=1, source_target_pairs={{0,16},{16,32},{32,48},{48,0},{64,80},{80,96},{96,112},{112,64},{1... | collective-permute-start | bytes 491528 | tf_op jit(solution)/shard_map/ppermute | solution.py:75
  66.0 6.4 %collective-permute-start.11 = (f32[64,640]{1,0:T(8,128)}, f32[64,640]{1,0:T(8,128)}, u32[]{:S(2)}, u32[]{:S(2)}) collective-permute-start(f32[64,640]{1,0:T(8,128)} %get-tuple-element.5), channel_id=1, source_target_pairs={{0,48},{16,0},{32,16},{48,32},{64,112},{80,64},{96,80},{112,96},{1... | collective-permute-start | bytes 491528 | tf_op jit(solution)/shard_map/ppermute | solution.py:76
  73.5 6.9 %collective-permute-start.12 = (f32[64,640]{1,0:T(8,128)S(1)}, f32[64,640]{1,0:T(8,128)S(1)}, u32[]{:S(2)}, u32[]{:S(2)}) collective-permute-start(f32[64,640]{1,0:T(8,128)S(1)} %broadcast_select_fusion), channel_id=1, source_target_pairs={{0,64},{16,80},{32,96},{48,112},{64,0},{80,16},{96,32},{112,48},{1... | collective-permute-start | bytes 491528 | tf_op jit(solution)/shard_map/ppermute | solution.py:79

commit v2 on v1

v2 whole, which is shorter than its diff:
```python
import jax
import jax.numpy as jnp
from jax import lax
from jax.sharding import PartitionSpec as P

HIGHEST = lax.Precision.HIGHEST


def _pairs(n, dest):
    return [(k, dest(k)) for k in range(n)]


def make_body(n_occ, n_vir):
    ny = n_vir // 4
    nx = n_occ // 2

    def y_shift(s):
        def dest(j):
            zl, y, c = j // (2 * ny), (j // 2) % ny, j % 2
            return zl * (2 * ny) + ((y + s) % ny) * 2 + c

        return _pairs(n_vir, dest)

    def x_shift(s):
        return _pairs(n_occ, lambda i: (i // nx) * nx + (i % nx + s) % nx)

    z_swap = _pairs(n_vir, lambda j: j ^ (2 * ny))
    core_swap = _pairs(n_vir, lambda j: j ^ 1)
    zhi_swap = _pairs(n_occ, lambda i: (i + nx) % n_occ)
    slot_of = [0, 1, 3, 4, 5, 7, 2, 6]

    def matmul(a, b):
        return jnp.dot(a, b, preferred_element_type=jnp.float32, precision=HIGHEST)

    def body(amplitudes, integrals):
        rows, cd = amplitudes.shape
        me = lax.axis_index("vir")
        zl, y, c = me // (2 * ny), (me // 2) % ny, me % 2

        own = amplitudes
        z1 = lax.ppermute(own, "vir", z_swap)
        ym1 = lax.ppermute(own, "vir", y_shift(1))
        yp1 = lax.ppermute(own, "vir", y_shift(-1))
        z2 = lax.ppermute(yp1, "vir", z_swap)
        yp2 = lax.ppermute(yp1, "vir", y_shift(-1))
        ym1z = lax.ppermute(z1, "vir", y_shift(1))
        z3 = lax.ppermute(yp2, "vir", z_swap)
        local = jnp.concatenate([own, z1, ym1, yp1, z2, yp2, ym1z, z3], axis=0)
        other = lax.ppermute(local, "vir", core_swap)
        res_l = (0.5 * matmul(local, integrals)).reshape(8, rows, -1)
        res_o = (0.5 * matmul(other, integrals)).reshape(8, rows, -1)
        table = jnp.array(slot_of, jnp.int32)

        def out_block(r):
            dy = (r % nx - y) % ny
            dz = (r // nx) ^ zl
            k = table[dy * 2 + dz]
            lk = lax.dynamic_index_in_dim(res_l, k, 0, keepdims=False)
            ok = lax.dynamic_index_in_dim(res_o, k, 0, keepdims=False)
            first = jnp.where(c == 0, lk, ok)
            second = jnp.where(c == 0, ok, lk)
            return jnp.concatenate([first, second], axis=0)

        mo = lax.axis_index("occ")
        x, zh = mo % nx, mo // nx
        sa = out_block((x - 1) % nx)
        sb = out_block(nx + (x + 1) % nx)
        for s in range(1, nx):
            sa = lax.ppermute(sa, "occ", x_shift(1)) + out_block((x - s - 1) % nx)
            sb = lax.ppermute(sb, "occ", x_shift(-1)) + out_block(nx + (x + s + 1) % nx)
        keep = jnp.where(zh == 0, sa, sb)
        send = jnp.where(zh == 0, sb, sa)
        return keep + lax.ppermute(send, "occ", zhi_swap)

    return body


def solution(mesh):
    placed = (P("vir", "occ"), P("occ", "vir"))
    return jax.shard_map(
        make_body(mesh.shape["occ"], mesh.shape["vir"]),
        mesh=mesh,
        in_specs=placed,
        out_specs=P("occ", "vir"),
        check_vma=False,
    )
```

time: 83.6 us -> 83.8 us (level); the launches traced: 82.2 us -> 83.4 us
  between operations: 0.2 us -> 14.8 us
  waiting for transfers between devices: 35 us -> 23.7 us
  local copies, waits for them, and re-layouts: 16.2 us -> 7.04 us
  starting transfers between devices: 17.7 us -> 23.3 us
  matrix products: 6.52 us -> 9.51 us
  other arithmetic: 6.64 us -> 5.04 us
    ppermute x11 -> x13, waiting for transfers between devices: 29.2 us -> 20.4 us  [the longest x3 9.65 us: body(): sb = lax.ppermute(sb, 'occ', x_shift(-1)) + out_block(nx + (x + s + 1) % nx)]
    dynamic_update_slice x16 -> x0, local copies, waits for them, and re-layouts: 7.61 us -> none  [the longest x8 7.47 us: body(): lax.dynamic_update_index_in_dim(full, other[k * rows:(k + 1) * rows], bas...]
    ppermute x11 -> x13, starting transfers between devices: 14.1 us -> 19.6 us  [the longest x3 10.3 us: body(): sb = lax.ppermute(sb, 'occ', x_shift(-1)) + out_block(nx + (x + s + 1) % nx)]
    dot_general x1 -> x2, matrix products: 6.52 us -> 9.51 us  [matmul(): return jnp.dot(a, b, preferred_element_type=jnp.float32, precision=HIGHEST)]
    ppermute x1, waiting for transfers between devices: 2.44 us -> 0.01 us  [body(): other = lax.ppermute(local, 'vir', core_swap)]
    add x2 -> x4, other arithmetic: 3.74 us -> 1.43 us  [the longest x2 0.71 us: body(): sb = lax.ppermute(sb, 'occ', x_shift(-1)) + out_block(nx + (x + s + 1) % nx)]
    unnamed x26 -> x11, local copies, waits for them, and re-layouts: 6.22 us -> 5.7 us
  transfers between devices with their start and end apart: 13 -> 15, of which waited for: 11 -> 8; matrix products, arithmetic and copies ran while one was open for 5% -> 15% of each run, Pallas kernels for 0% -> 0%
where the time goes in v2:
time: 83.8 us; the launch traced here: 83.4 us
  waiting for transfers between devices  23.7 us (28%)
  starting transfers between devices  23.3 us (28%)
  between operations  14.8 us (18%)
  matrix products  9.51 us (11%)
  local copies, waits for them, and re-layouts  7.04 us (8%)
  other arithmetic  5.04 us (6%)
    ppermute x3, starting transfers between devices, body(): sb = lax.ppermute(sb, 'occ', x_shift(-1)) + out_block(nx + (x + s + 1) % nx)  10.3 us
    ppermute x3, waiting for transfers between devices, body(): sb = lax.ppermute(sb, 'occ', x_shift(-1)) + out_block(nx + (x + s + 1) % nx)  9.65 us
    dot_general x2, matrix products, matmul(): return jnp.dot(a, b, preferred_element_type=jnp.float32, precision=HIGHEST)  9.51 us
    unnamed x11, local copies, waits for them, and re-layouts  5.7 us
    ppermute x3, waiting for transfers between devices, body(): sa = lax.ppermute(sa, 'occ', x_shift(1)) + out_block((x - s - 1) % nx)  4.39 us
    ppermute x1, starting transfers between devices, body(): return keep + lax.ppermute(send, 'occ', zhi_swap)  3.66 us
    ppermute x1, waiting for transfers between devices, body(): yp1 = lax.ppermute(own, 'vir', y_shift(-1))  3.42 us
    ppermute x1, waiting for transfers between devices, body(): return keep + lax.ppermute(send, 'occ', zhi_swap)  3.3 us
  transfers between devices with their start and end apart: 15, of which 8 were waited for; matrix products, arithmetic and copies ran while one was open for 15% of the time, Pallas kernels for 0%

profile of v2, /device:TPU:24, one launch (start us, length us, event | category | flops | bytes accessed | tf_op | source)
XLA Modules:
  0.0 83.4 jit_solution(2761788333275300061)
XLA Ops:
  0.0 1.9 %collective-permute-start = (f32[32,1280]{1,0:T(8,128)}, f32[32,1280]{1,0:T(8,128)S(1)}, u32[]{:S(2)}, u32[]{:S(2)}) collective-permute-start(f32[32,1280]{1,0:T(8,128)} %param.3), channel_id=1, source_target_pairs={{0,8},{1,9},{2,10},{3,11},{4,12},{5,13},{6,14},{7,15},{8,0},{9,1},... | collective-permute-start | bytes 491528 | tf_op jit(solution)/shard_map/ppermute | solution.py:41
  2.1 1.8 %collective-permute-start.2 = (f32[32,1280]{1,0:T(8,128)}, f32[32,1280]{1,0:T(8,128)S(1)}, u32[]{:S(2)}, u32[]{:S(2)}) collective-permute-start(f32[32,1280]{1,0:T(8,128)} %param.3), channel_id=1, source_target_pairs={{0,6},{1,7},{2,0},{3,1},{4,2},{5,3},{6,4},{7,5},{8,14},{9,15},{10,... | collective-permute-start | bytes 491528 | tf_op jit(solution)/shard_map/ppermute | solution.py:43
  3.9 1.6 %constant_dynamic-update-slice_fusion.7 = f32[256,1280]{1,0:T(8,128)} fusion(f32[32,1280]{1,0:T(8,128)} %param.3), kind=kLoop, calls=%fused_computation.35 | loop fusion | bytes 327680
  5.6 3.4 %collective-permute-done.2 = f32[32,1280]{1,0:T(8,128)S(1)} collective-permute-done((f32[32,1280]{1,0:T(8,128)}, f32[32,1280]{1,0:T(8,128)S(1)}, u32[]{:S(2)}, u32[]{:S(2)}) %collective-permute-start.2) | collective-permute-done | bytes 163872 | tf_op jit(solution)/shard_map/ppermute | solution.py:43
  9.9 2.8 %collective-permute-start.5 = (f32[32,1280]{1,0:T(8,128)S(1)}, f32[32,1280]{1,0:T(8,128)S(1)}, u32[]{:S(2)}, u32[]{:S(2)}) collective-permute-start(f32[32,1280]{1,0:T(8,128)S(1)} %collective-permute-done), channel_id=1, source_target_pairs={{0,2},{1,3},{2,4},{3,5},{4,6},{5,7},{6,0},{7,1},{8,10},{9,11},{10,... | collective-permute-start | bytes 491528 | tf_op jit(solution)/shard_map/ppermute | solution.py:46
  14.0 0.7 constant_dynamic-update-slice_fusion.4
  14.7 1.2 %collective-permute-done.4 = f32[32,1280]{1,0:T(8,128)S(1)} collective-permute-done((f32[32,1280]{1,0:T(8,128)S(1)}, f32[32,1280]{1,0:T(8,128)S(1)}, u32[]{:S(2)}, u32[]{:S(2)}) %collective-permute-start.4) | collective-permute-done | bytes 163872 | tf_op jit(solution)/shard_map/ppermute | solution.py:45
  16.0 1.6 %collective-permute-start.6 = (f32[32,1280]{1,0:T(8,128)S(1)}, f32[32,1280]{1,0:T(8,128)S(1)}, u32[]{:S(2)}, u32[]{:S(2)}) collective-permute-start(f32[32,1280]{1,0:T(8,128)S(1)} %collective-permute-done.4), channel_id=1, source_target_pairs={{0,8},{1,9},{2,10},{3,11},{4,12},{5,13},{6,14},{7,15},{8,0},{9,1},... | collective-permute-start | bytes 491528 | tf_op jit(solution)/shard_map/ppermute | solution.py:47
  19.6 1.7 %collective-permute-done.6 = f32[32,1280]{1,0:T(8,128)S(1)} collective-permute-done((f32[32,1280]{1,0:T(8,128)S(1)}, f32[32,1280]{1,0:T(8,128)S(1)}, u32[]{:S(2)}, u32[]{:S(2)}) %collective-permute-start.6) | collective-permute-done | bytes 163872 | tf_op jit(solution)/shard_map/ppermute | solution.py:47
  37.3 4.8 %convolution_multiply_fusion.1 = f32[256,640]{1,0:T(8,128)S(1)} fusion(f32[256,1280]{1,0:T(8,128)} %constant_dynamic-update-slice_fusion, f32[1280,640]{1,0:T(8,128)S(1)} %copy-done), kind=kOutput, calls=%fused_computation.1 | convolution fusion | flops 2516746240 | bytes 5242880 | tf_op jit(solution)/shard_map/dot_general | solution.py:33
  42.1 4.8 %convolution_multiply_fusion = f32[256,640]{1,0:T(8,128)S(1)} fusion(f32[256,1280]{1,0:T(8,128)} %collective-permute-done.7, f32[1280,640]{1,0:T(8,128)S(1)} %copy-done), kind=kOutput, calls=%fused_computation | convolution fusion | flops 2516746240 | bytes 5242880 | tf_op jit(solution)/shard_map/dot_general | solution.py:33
  46.9 0.8 select_bitcast_fusion.9
  47.6 2.8 %collective-permute-start.11 = (f32[64,640]{1,0:T(8,128)S(1)}, f32[64,640]{1,0:T(8,128)S(1)}, u32[]{:S(2)}, u32[]{:S(2)}) collective-permute-start(f32[64,640]{1,0:T(8,128)S(1)} %pad_maximum_fusion.1), channel_id=1, source_target_pairs={{0,48},{16,0},{32,16},{48,32},{64,112},{80,64},{96,80},{112,96},{1... | collective-permute-start | bytes 491528 | tf_op jit(solution)/shard_map/ppermute | solution.py:70
  50.6 4.0 %collective-permute-done.11 = f32[64,640]{1,0:T(8,128)S(1)} collective-permute-done((f32[64,640]{1,0:T(8,128)S(1)}, f32[64,640]{1,0:T(8,128)S(1)}, u32[]{:S(2)}, u32[]{:S(2)}) %collective-permute-start.11) | collective-permute-done | bytes 163872 | tf_op jit(solution)/shard_map/ppermute | solution.py:70
  54.6 3.8 %collective-permute-start.12 = (f32[64,640]{1,0:T(8,128)S(1)}, f32[64,640]{1,0:T(8,128)S(1)}, u32[]{:S(2)}, u32[]{:S(2)}) collective-permute-start(f32[64,640]{1,0:T(8,128)S(1)} %maximum_add_fusion.3), channel_id=1, source_target_pairs={{0,48},{16,0},{32,16},{48,32},{64,112},{80,64},{96,80},{112,96},{1... | collective-permute-start | bytes 491528 | tf_op jit(solution)/shard_map/ppermute | solution.py:70
  58.5 3.2 %collective-permute-done.12 = f32[64,640]{1,0:T(8,128)S(1)} collective-permute-done((f32[64,640]{1,0:T(8,128)S(1)}, f32[64,640]{1,0:T(8,128)S(1)}, u32[]{:S(2)}, u32[]{:S(2)}) %collective-permute-start.12) | collective-permute-done | bytes 163872 | tf_op jit(solution)/shard_map/ppermute | solution.py:70
  61.7 0.7 maximum_add_fusion.4
  62.4 3.7 %collective-permute-start.13 = (f32[64,640]{1,0:T(8,128)}, f32[64,640]{1,0:T(8,128)}, u32[]{:S(2)}, u32[]{:S(2)}) collective-permute-start(f32[64,640]{1,0:T(8,128)} %maximum_add_fusion.4), channel_id=1, source_target_pairs={{0,48},{16,0},{32,16},{48,32},{64,112},{80,64},{96,80},{112,96},{1... | collective-permute-start | bytes 491528 | tf_op jit(solution)/shard_map/ppermute | solution.py:70
  66.7 2.5 %collective-permute-done.13 = f32[64,640]{1,0:T(8,128)} collective-permute-done((f32[64,640]{1,0:T(8,128)}, f32[64,640]{1,0:T(8,128)}, u32[]{:S(2)}, u32[]{:S(2)}) %collective-permute-start.13) | collective-permute-done | bytes 163872 | tf_op jit(solution)/shard_map/ppermute | solution.py:70
  69.2 4.4 %collective-permute-done.10 = f32[64,640]{1,0:T(8,128)} collective-permute-done((f32[64,640]{1,0:T(8,128)}, f32[64,640]{1,0:T(8,128)}, u32[]{:S(2)}, u32[]{:S(2)}) %collective-permute-start.10) | collective-permute-done | bytes 163872 | tf_op jit(solution)/shard_map/ppermute | solution.py:69
  73.6 1.1 %broadcast_select_fusion = f32[64,640]{1,0:T(8,128)S(1)} fusion(pred[]{:T(512)S(6)} %eq.50, f32[64,640]{1,0:T(8,128)} %collective-permute-done.13, f32[32,640]{1,0:T(8,128)S(1)} %get-tuple-element.13, f32[32,640]{1,0:T(8,128)} %get-tuple-element.14, f32[64,640]{1,0:T(8,128)} %collective-permute-done.10, f32[32,640]{1,0:T(8,128)S(1)} %get-tuple-element.9, ...), kind=kLoop, calls=%fused_computation.27 | loop fusion | flops 204800 | bytes 819201 | tf_op jit(solution)/shard_map/jit(_where)/select_n | solution.py:72
  74.7 3.7 %collective-permute-start.14 = (f32[64,640]{1,0:T(8,128)S(1)}, f32[64,640]{1,0:T(8,128)S(1)}, u32[]{:S(2)}, u32[]{:S(2)}) collective-permute-start(f32[64,640]{1,0:T(8,128)S(1)} %broadcast_select_fusion), channel_id=1, source_target_pairs={{0,64},{16,80},{32,96},{48,112},{64,0},{80,16},{96,32},{112,48},{1... | collective-permute-start | bytes 491528 | tf_op jit(solution)/shard_map/ppermute | solution.py:73
  78.3 3.3 %collective-permute-done.14 = f32[64,640]{1,0:T(8,128)S(1)} collective-permute-done((f32[64,640]{1,0:T(8,128)S(1)}, f32[64,640]{1,0:T(8,128)S(1)}, u32[]{:S(2)}, u32[]{:S(2)}) %collective-permute-start.14) | collective-permute-done | bytes 163872 | tf_op jit(solution)/shard_map/ppermute | solution.py:73
  81.6 1.7 %select_add_fusion = f32[64,640]{1,0:T(8,128)} fusion(f32[64,640]{1,0:T(8,128)S(1)} %collective-permute-done.14, pred[]{:T(512)S(6)} %eq.50, f32[64,640]{1,0:T(8,128)} %collective-permute-done.13, f32[32,640]{1,0:T(8,128)S(1)} %get-tuple-element.13, f32[32,640]{1,0:T(8,128)} %get-tuple-element.14, f32[64,640]{1,0:T(8,128)} %collective-permute-done.10, ...), kind=kLoop, calls=%fused_computation.10 | loop fusion | flops 245760 | bytes 983041 | tf_op jit(solution)/shard_map/add | solution.py:73
  (30 shorter events, 6.8 us)
Async XLA Ops:
  0.0 37.3 %copy-start = (f32[1280,640]{1,0:T(8,128)S(1)}, f32[1280,640]{1,0:T(8,128)}, u32[]{:S(2)}) copy-start(f32[1280,640]{1,0:T(8,128)} %param.4) | copy-start | bytes 9830404
  0.0 9.9 %collective-permute-start = (f32[32,1280]{1,0:T(8,128)}, f32[32,1280]{1,0:T(8,128)S(1)}, u32[]{:S(2)}, u32[]{:S(2)}) collective-permute-start(f32[32,1280]{1,0:T(8,128)} %param.3), channel_id=1, source_target_pairs={{0,8},{1,9},{2,10},{3,11},{4,12},{5,13},{6,14},{7,15},{8,0},{9,1},... | collective-permute-start | bytes 491528 | tf_op jit(solution)/shard_map/ppermute | solution.py:41
  1.9 11.4 %collective-permute-start.1 = (f32[32,1280]{1,0:T(8,128)}, f32[32,1280]{1,0:T(8,128)S(1)}, u32[]{:S(2)}, u32[]{:S(2)}) collective-permute-start(f32[32,1280]{1,0:T(8,128)} %param.3), channel_id=1, source_target_pairs={{0,2},{1,3},{2,4},{3,5},{4,6},{5,7},{6,0},{7,1},{8,10},{9,11},{10,... | collective-permute-start | bytes 491528 | tf_op jit(solution)/shard_map/ppermute | solution.py:42
  2.1 6.9 %collective-permute-start.2 = (f32[32,1280]{1,0:T(8,128)}, f32[32,1280]{1,0:T(8,128)S(1)}, u32[]{:S(2)}, u32[]{:S(2)}) collective-permute-start(f32[32,1280]{1,0:T(8,128)} %param.3), channel_id=1, source_target_pairs={{0,6},{1,7},{2,0},{3,1},{4,2},{5,3},{6,4},{7,5},{8,14},{9,15},{10,... | collective-permute-start | bytes 491528 | tf_op jit(solution)/shard_map/ppermute | solution.py:43
  9.0 8.6 %collective-permute-start.3 = (f32[32,1280]{1,0:T(8,128)S(1)}, f32[32,1280]{1,0:T(8,128)S(1)}, u32[]{:S(2)}, u32[]{:S(2)}) collective-permute-start(f32[32,1280]{1,0:T(8,128)S(1)} %collective-permute-done.2), channel_id=1, source_target_pairs={{0,8},{1,9},{2,10},{3,11},{4,12},{5,13},{6,14},{7,15},{8,0},{9,1},... | collective-permute-start | bytes 491528 | tf_op jit(solution)/shard_map/ppermute | solution.py:44
  9.4 6.5 %collective-permute-start.4 = (f32[32,1280]{1,0:T(8,128)S(1)}, f32[32,1280]{1,0:T(8,128)S(1)}, u32[]{:S(2)}, u32[]{:S(2)}) collective-permute-start(f32[32,1280]{1,0:T(8,128)S(1)} %collective-permute-done.2), channel_id=1, source_target_pairs={{0,6},{1,7},{2,0},{3,1},{4,2},{5,3},{6,4},{7,5},{8,14},{9,15},{10,... | collective-permute-start | bytes 491528 | tf_op jit(solution)/shard_map/ppermute | solution.py:45
  9.9 9.0 %collective-permute-start.5 = (f32[32,1280]{1,0:T(8,128)S(1)}, f32[32,1280]{1,0:T(8,128)S(1)}, u32[]{:S(2)}, u32[]{:S(2)}) collective-permute-start(f32[32,1280]{1,0:T(8,128)S(1)} %collective-permute-done), channel_id=1, source_target_pairs={{0,2},{1,3},{2,4},{3,5},{4,6},{5,7},{6,0},{7,1},{8,10},{9,11},{10,... | collective-permute-start | bytes 491528 | tf_op jit(solution)/shard_map/ppermute | solution.py:46
  14.0 7.9 %copy-start.1 = (s32[8]{0:T(128)S(1)}, s32[8]{0:T(128)}, u32[]{:S(2)}) copy-start(s32[8]{0:T(128)} %constant.274.clone) | copy-start | bytes 100
  16.0 5.3 %collective-permute-start.6 = (f32[32,1280]{1,0:T(8,128)S(1)}, f32[32,1280]{1,0:T(8,128)S(1)}, u32[]{:S(2)}, u32[]{:S(2)}) collective-permute-start(f32[32,1280]{1,0:T(8,128)S(1)} %collective-permute-done.4), channel_id=1, source_target_pairs={{0,8},{1,9},{2,10},{3,11},{4,12},{5,13},{6,14},{7,15},{8,0},{9,1},... | collective-permute-start | bytes 491528 | tf_op jit(solution)/shard_map/ppermute | solution.py:47
  22.0 20.1 %collective-permute-start.7 = (f32[256,1280]{1,0:T(8,128)}, f32[256,1280]{1,0:T(8,128)}, u32[]{:S(2)}, u32[]{:S(2)}) collective-permute-start(f32[256,1280]{1,0:T(8,128)} %constant_dynamic-update-slice_fusion), channel_id=1, source_target_pairs={{0,1},{1,0},{2,3},{3,2},{4,5},{5,4},{6,7},{7,6},{8,9},{9,8},{10,11... | collective-permute-start | bytes 3932168 | tf_op jit(solution)/shard_map/ppermute | solution.py:49
  47.6 7.0 %collective-permute-start.11 = (f32[64,640]{1,0:T(8,128)S(1)}, f32[64,640]{1,0:T(8,128)S(1)}, u32[]{:S(2)}, u32[]{:S(2)}) collective-permute-start(f32[64,640]{1,0:T(8,128)S(1)} %pad_maximum_fusion.1), channel_id=1, source_target_pairs={{0,48},{16,0},{32,16},{48,32},{64,112},{80,64},{96,80},{112,96},{1... | collective-permute-start | bytes 491528 | tf_op jit(solution)/shard_map/ppermute | solution.py:70
  50.5 7.9 %collective-permute-start.8 = (f32[64,640]{1,0:T(8,128)S(1)}, f32[64,640]{1,0:T(8,128)S(1)}, u32[]{:S(2)}, u32[]{:S(2)}) collective-permute-start(f32[64,640]{1,0:T(8,128)S(1)} %pad_maximum_fusion), channel_id=1, source_target_pairs={{0,16},{16,32},{32,48},{48,0},{64,80},{80,96},{96,112},{112,64},{1... | collective-permute-start | bytes 491528 | tf_op jit(solution)/shard_map/ppermute | solution.py:69
  54.6 7.0 %collective-permute-start.12 = (f32[64,640]{1,0:T(8,128)S(1)}, f32[64,640]{1,0:T(8,128)S(1)}, u32[]{:S(2)}, u32[]{:S(2)}) collective-permute-start(f32[64,640]{1,0:T(8,128)S(1)} %maximum_add_fusion.3), channel_id=1, source_target_pairs={{0,48},{16,0},{32,16},{48,32},{64,112},{80,64},{96,80},{112,96},{1... | collective-permute-start | bytes 491528 | tf_op jit(solution)/shard_map/ppermute | solution.py:70
  58.4 7.6 %collective-permute-start.9 = (f32[64,640]{1,0:T(8,128)S(1)}, f32[64,640]{1,0:T(8,128)S(1)}, u32[]{:S(2)}, u32[]{:S(2)}) collective-permute-start(f32[64,640]{1,0:T(8,128)S(1)} %maximum_add_fusion), channel_id=1, source_target_pairs={{0,16},{16,32},{32,48},{48,0},{64,80},{80,96},{96,112},{112,64},{1... | collective-permute-start | bytes 491528 | tf_op jit(solution)/shard_map/ppermute | solution.py:69
  62.4 6.8 %collective-permute-start.13 = (f32[64,640]{1,0:T(8,128)}, f32[64,640]{1,0:T(8,128)}, u32[]{:S(2)}, u32[]{:S(2)}) collective-permute-start(f32[64,640]{1,0:T(8,128)} %maximum_add_fusion.4), channel_id=1, source_target_pairs={{0,48},{16,0},{32,16},{48,32},{64,112},{80,64},{96,80},{112,96},{1... | collective-permute-start | bytes 491528 | tf_op jit(solution)/shard_map/ppermute | solution.py:70
  66.7 6.8 %collective-permute-start.10 = (f32[64,640]{1,0:T(8,128)}, f32[64,640]{1,0:T(8,128)}, u32[]{:S(2)}, u32[]{:S(2)}) collective-permute-start(f32[64,640]{1,0:T(8,128)} %maximum_add_fusion.1), channel_id=1, source_target_pairs={{0,16},{16,32},{32,48},{48,0},{64,80},{80,96},{96,112},{112,64},{1... | collective-permute-start | bytes 491528 | tf_op jit(solution)/shard_map/ppermute | solution.py:69
  74.7 7.0 %collective-permute-start.14 = (f32[64,640]{1,0:T(8,128)S(1)}, f32[64,640]{1,0:T(8,128)S(1)}, u32[]{:S(2)}, u32[]{:S(2)}) collective-permute-start(f32[64,640]{1,0:T(8,128)S(1)} %broadcast_select_fusion), channel_id=1, source_target_pairs={{0,64},{16,80},{32,96},{48,112},{64,0},{80,16},{96,32},{112,48},{1... | collective-permute-start | bytes 491528 | tf_op jit(solution)/shard_map/ppermute | solution.py:73

commit v3 on v2

--- a/solution.py
+++ b/solution.py
@@ -1,6 +1,8 @@
 import jax
 import jax.numpy as jnp
 from jax import lax
+from jax.experimental import pallas as pl
+from jax.experimental.pallas import tpu as pltpu
 from jax.sharding import PartitionSpec as P
 
 HIGHEST = lax.Precision.HIGHEST
@@ -8,6 +10,34 @@
 
 def _pairs(n, dest):
     return [(k, dest(k)) for k in range(n)]
+
+
+def _matmul_kernel(a_ref, b_ref, o_ref):
+    @pl.when(pl.program_id(0) == 0)
+    def _():
+        o_ref[...] = jnp.zeros_like(o_ref)
+
+    o_ref[...] += jnp.dot(
+        a_ref[...], b_ref[...], preferred_element_type=jnp.float32, precision=HIGHEST
+    )
+
+
+def _stream_matmul(a, b, tk=256):
+    m, k = a.shape
+    n = b.shape[1]
+    return pl.pallas_call(
+        _matmul_kernel,
+        out_shape=jax.ShapeDtypeStruct((m, n), jnp.float32),
+        grid=(k // tk,),
+        in_specs=[
+            pl.BlockSpec((m, tk), lambda i: (0, i)),
+            pl.BlockSpec((tk, n), lambda i: (i, 0)),
+        ],
+        out_specs=pl.BlockSpec((m, n), lambda i: (0, 0)),
+        cost_estimate=pl.CostEstimate(
+            flops=2 * m * n * k, transcendentals=0, bytes_accessed=4 * (m * k + k * n + m * n)
+        ),
+    )(a, b)
 
 
 def make_body(n_occ, n_vir):
@@ -30,7 +60,7 @@
     slot_of = [0, 1, 3, 4, 5, 7, 2, 6]
 
     def matmul(a, b):
-        return jnp.dot(a, b, preferred_element_type=jnp.float32, precision=HIGHEST)
+        return _stream_matmul(a, b)
 
     def body(amplitudes, integrals):
         rows, cd = amplitudes.shape

time: 83.8 us -> 87.1 us (1.039)
  Pallas kernels: 0 us -> 13.8 us
  matrix products: 9.51 us -> 0 us
  local copies, waits for them, and re-layouts: 7.04 us -> 2.85 us
  waiting for transfers between devices: 23.7 us -> 27 us
  other arithmetic: 5.04 us -> 3.25 us
  between operations: 14.8 us -> 16 us
    pallas_call x0 -> x2, Pallas kernels: none -> 13.8 us  [_stream_matmul(): pl.pallas_call(_matmul_kernel, out_shape=jax.ShapeDtypeStruct((m, n), jnp...]
    dot_general x2 -> x0, matrix products: 9.51 us -> none  [matmul(): return jnp.dot(a, b, preferred_element_type=jnp.float32, precision=HIGHEST)]
    unnamed x11 -> x13, local copies, waits for them, and re-layouts: 5.7 us -> 2.13 us
    mul x0 -> x2, other arithmetic: none -> 2.26 us  [the longest x1 1.13 us: body(): res_l = (0.5 * matmul(local, integrals)).reshape(8, rows, -1)]
    ppermute x1, waiting for transfers between devices: 1.24 us -> 3.21 us  [body(): yp2 = lax.ppermute(yp1, 'vir', y_shift(-1))]
    ppermute x1, waiting for transfers between devices: 1.7 us -> 3.57 us  [body(): z3 = lax.ppermute(yp2, 'vir', z_swap)]
    add x1, other arithmetic: 1.75 us -> 0.71 us  [body(): return keep + lax.ppermute(send, 'occ', zhi_swap)]
    select_n x1, other arithmetic: 1.07 us -> 0.03 us  [body(): send = jnp.where(zh == 0, sb, sa)]
  transfers between devices with their start and end apart: 15 -> 15, of which waited for: 8 -> 8; matrix products, arithmetic and copies ran while one was open for 15% -> 3% of each run, Pallas kernels for 0% -> 8%
where the time goes in v3:
time: 87.1 us; the launch traced here: 86.5 us
  waiting for transfers between devices  27 us (31%)
  starting transfers between devices  23.6 us (27%)
  between operations  16 us (18%)
  Pallas kernels  13.8 us (16%)
  other arithmetic  3.25 us (4%)
  local copies, waits for them, and re-layouts  2.85 us (3%)
    pallas_call x2, Pallas kernels, _stream_matmul(): pl.pallas_call(_matmul_kernel, out_shape=jax.ShapeDtypeStruct((m, n), jnp...  13.8 us
    ppermute x3, starting transfers between devices, body(): sb = lax.ppermute(sb, 'occ', x_shift(-1)) + out_block(nx + (x + s + 1) % nx)  10.3 us
    ppermute x3, waiting for transfers between devices, body(): sb = lax.ppermute(sb, 'occ', x_shift(-1)) + out_block(nx + (x + s + 1) % nx)  8.97 us
    ppermute x1, waiting for transfers between devices, body(): yp1 = lax.ppermute(own, 'vir', y_shift(-1))  4.09 us
    ppermute x3, waiting for transfers between devices, body(): sa = lax.ppermute(sa, 'occ', x_shift(1)) + out_block((x - s - 1) % nx)  3.8 us
    ppermute x1, starting transfers between devices, body(): return keep + lax.ppermute(send, 'occ', zhi_swap)  3.71 us
    ppermute x1, waiting for transfers between devices, body(): z3 = lax.ppermute(yp2, 'vir', z_swap)  3.57 us
    ppermute x1, waiting for transfers between devices, body(): return keep + lax.ppermute(send, 'occ', zhi_swap)  3.3 us
  transfers between devices with their start and end apart: 15, of which 8 were waited for; matrix products, arithmetic and copies ran while one was open for 3% of the time, Pallas kernels for 8%

profile of v3, /device:TPU:24, one launch (start us, length us, event | category | flops | bytes accessed | tf_op | source)
XLA Modules:
  0.0 86.5 jit_solution(9974627184460004568)
XLA Ops:
  0.0 1.9 %collective-permute-start = (f32[32,1280]{1,0:T(8,128)}, f32[32,1280]{1,0:T(8,128)S(1)}, u32[]{:S(2)}, u32[]{:S(2)}) collective-permute-start(f32[32,1280]{1,0:T(8,128)} %param.3), channel_id=1, source_target_pairs={{0,8},{1,9},{2,10},{3,11},{4,12},{5,13},{6,14},{7,15},{8,0},{9,1},... | collective-permute-start | bytes 491528 | tf_op jit(solution)/shard_map/ppermute | solution.py:71
  2.1 1.8 %collective-permute-start.2 = (f32[32,1280]{1,0:T(8,128)}, f32[32,1280]{1,0:T(8,128)S(1)}, u32[]{:S(2)}, u32[]{:S(2)}) collective-permute-start(f32[32,1280]{1,0:T(8,128)} %param.3), channel_id=1, source_target_pairs={{0,6},{1,7},{2,0},{3,1},{4,2},{5,3},{6,4},{7,5},{8,14},{9,15},{10,... | collective-permute-start | bytes 491528 | tf_op jit(solution)/shard_map/ppermute | solution.py:73
  3.9 1.0 %constant_dynamic-update-slice_fusion.7 = f32[256,1280]{1,0:T(8,128)S(1)} fusion(f32[32,1280]{1,0:T(8,128)} %param.3), kind=kLoop, calls=%fused_computation.35 | loop fusion | bytes 327680
  4.9 4.1 %collective-permute-done.2 = f32[32,1280]{1,0:T(8,128)S(1)} collective-permute-done((f32[32,1280]{1,0:T(8,128)}, f32[32,1280]{1,0:T(8,128)S(1)}, u32[]{:S(2)}, u32[]{:S(2)}) %collective-permute-start.2) | collective-permute-done | bytes 163872 | tf_op jit(solution)/shard_map/ppermute | solution.py:73
  9.8 2.8 %collective-permute-start.5 = (f32[32,1280]{1,0:T(8,128)S(1)}, f32[32,1280]{1,0:T(8,128)S(1)}, u32[]{:S(2)}, u32[]{:S(2)}) collective-permute-start(f32[32,1280]{1,0:T(8,128)S(1)} %collective-permute-done), channel_id=1, source_target_pairs={{0,2},{1,3},{2,4},{3,5},{4,6},{5,7},{6,0},{7,1},{8,10},{9,11},{10,... | collective-permute-start | bytes 491528 | tf_op jit(solution)/shard_map/ppermute | solution.py:76
  12.7 3.2 %collective-permute-done.4 = f32[32,1280]{1,0:T(8,128)S(1)} collective-permute-done((f32[32,1280]{1,0:T(8,128)S(1)}, f32[32,1280]{1,0:T(8,128)S(1)}, u32[]{:S(2)}, u32[]{:S(2)}) %collective-permute-start.4) | collective-permute-done | bytes 163872 | tf_op jit(solution)/shard_map/ppermute | solution.py:75
  15.9 1.7 %collective-permute-start.6 = (f32[32,1280]{1,0:T(8,128)S(1)}, f32[32,1280]{1,0:T(8,128)S(1)}, u32[]{:S(2)}, u32[]{:S(2)}) collective-permute-start(f32[32,1280]{1,0:T(8,128)S(1)} %collective-permute-done.4), channel_id=1, source_target_pairs={{0,8},{1,9},{2,10},{3,11},{4,12},{5,13},{6,14},{7,15},{8,0},{9,1},... | collective-permute-start | bytes 491528 | tf_op jit(solution)/shard_map/ppermute | solution.py:77
  17.6 3.6 %collective-permute-done.6 = f32[32,1280]{1,0:T(8,128)S(1)} collective-permute-done((f32[32,1280]{1,0:T(8,128)S(1)}, f32[32,1280]{1,0:T(8,128)S(1)}, u32[]{:S(2)}, u32[]{:S(2)}) %collective-permute-start.6) | collective-permute-done | bytes 163872 | tf_op jit(solution)/shard_map/ppermute | solution.py:77
  21.8 0.7 fusion
  37.9 6.9 %shard_map.37 = f32[256,640]{1,0:T(8,128)} custom-call(f32[256,1280]{1,0:T(8,128)} %copy-done, f32[1280,640]{1,0:T(8,128)} %b_ref.3), custom_call_target="tpu_custom_call" | custom-call | flops 419430400 | bytes 5242880 | tf_op jit(solution)/shard_map/pallas_call | solution.py:28
  44.8 1.1 %broadcast_multiply_fusion.1 = f32[256,640]{1,0:T(8,128)S(1)} fusion(f32[256,640]{1,0:T(8,128)} %shard_map.37), kind=kLoop, calls=%fused_computation.1 | loop fusion | flops 163840 | bytes 1310720 | tf_op jit(solution)/shard_map/mul | solution.py:80
  45.9 1.1 %copy-done.1 = f32[256,1280]{1,0:T(8,128)} copy-done((f32[256,1280]{1,0:T(8,128)}, f32[256,1280]{1,0:T(8,128)S(1)}, u32[]{:S(2)}) %copy-start.1) | copy-done | bytes 1310744
  47.0 6.9 %shard_map.38 = f32[256,640]{1,0:T(8,128)} custom-call(f32[256,1280]{1,0:T(8,128)} %copy-done.1, f32[1280,640]{1,0:T(8,128)} %b_ref.3), custom_call_target="tpu_custom_call" | custom-call | flops 419430400 | bytes 5242880 | tf_op jit(solution)/shard_map/pallas_call | solution.py:28
  53.9 1.1 %broadcast_multiply_fusion = f32[256,640]{1,0:T(8,128)S(1)} fusion(f32[256,640]{1,0:T(8,128)} %shard_map.38), kind=kLoop, calls=%fused_computation | loop fusion | flops 163840 | bytes 1310720 | tf_op jit(solution)/shard_map/mul | solution.py:81
  55.2 2.8 %collective-permute-start.11 = (f32[64,640]{1,0:T(8,128)S(1)}, f32[64,640]{1,0:T(8,128)S(1)}, u32[]{:S(2)}, u32[]{:S(2)}) collective-permute-start(f32[64,640]{1,0:T(8,128)S(1)} %pad_maximum_fusion.1), channel_id=1, source_target_pairs={{0,48},{16,0},{32,16},{48,32},{64,112},{80,64},{96,80},{112,96},{1... | collective-permute-start | bytes 491528 | tf_op jit(solution)/shard_map/ppermute | solution.py:100
  58.1 3.5 %collective-permute-done.11 = f32[64,640]{1,0:T(8,128)S(1)} collective-permute-done((f32[64,640]{1,0:T(8,128)S(1)}, f32[64,640]{1,0:T(8,128)S(1)}, u32[]{:S(2)}, u32[]{:S(2)}) %collective-permute-start.11) | collective-permute-done | bytes 163872 | tf_op jit(solution)/shard_map/ppermute | solution.py:100
  61.7 3.8 %collective-permute-start.12 = (f32[64,640]{1,0:T(8,128)S(1)}, f32[64,640]{1,0:T(8,128)S(1)}, u32[]{:S(2)}, u32[]{:S(2)}) collective-permute-start(f32[64,640]{1,0:T(8,128)S(1)} %maximum_add_fusion.3), channel_id=1, source_target_pairs={{0,48},{16,0},{32,16},{48,32},{64,112},{80,64},{96,80},{112,96},{1... | collective-permute-start | bytes 491528 | tf_op jit(solution)/shard_map/ppermute | solution.py:100
  65.6 2.7 %collective-permute-done.12 = f32[64,640]{1,0:T(8,128)S(1)} collective-permute-done((f32[64,640]{1,0:T(8,128)S(1)}, f32[64,640]{1,0:T(8,128)S(1)}, u32[]{:S(2)}, u32[]{:S(2)}) %collective-permute-start.12) | collective-permute-done | bytes 163872 | tf_op jit(solution)/shard_map/ppermute | solution.py:100
  68.3 3.8 %collective-permute-start.13 = (f32[64,640]{1,0:T(8,128)S(1)}, f32[64,640]{1,0:T(8,128)S(1)}, u32[]{:S(2)}, u32[]{:S(2)}) collective-permute-start(f32[64,640]{1,0:T(8,128)S(1)} %maximum_add_fusion.4), channel_id=1, source_target_pairs={{0,48},{16,0},{32,16},{48,32},{64,112},{80,64},{96,80},{112,96},{1... | collective-permute-start | bytes 491528 | tf_op jit(solution)/shard_map/ppermute | solution.py:100
  72.2 2.7 %collective-permute-done.13 = f32[64,640]{1,0:T(8,128)S(1)} collective-permute-done((f32[64,640]{1,0:T(8,128)S(1)}, f32[64,640]{1,0:T(8,128)S(1)}, u32[]{:S(2)}, u32[]{:S(2)}) %collective-permute-start.13) | collective-permute-done | bytes 163872 | tf_op jit(solution)/shard_map/ppermute | solution.py:100
  74.9 3.8 %collective-permute-done.10 = f32[64,640]{1,0:T(8,128)S(1)} collective-permute-done((f32[64,640]{1,0:T(8,128)S(1)}, f32[64,640]{1,0:T(8,128)S(1)}, u32[]{:S(2)}, u32[]{:S(2)}) %collective-permute-start.10) | collective-permute-done | bytes 163872 | tf_op jit(solution)/shard_map/ppermute | solution.py:99
  78.7 3.7 %collective-permute-start.14 = (f32[64,640]{1,0:T(8,128)S(1)}, f32[64,640]{1,0:T(8,128)S(1)}, u32[]{:S(2)}, u32[]{:S(2)}) collective-permute-start(f32[64,640]{1,0:T(8,128)S(1)} %broadcast_select_fusion), channel_id=1, source_target_pairs={{0,64},{16,80},{32,96},{48,112},{64,0},{80,16},{96,32},{112,48},{1... | collective-permute-start | bytes 491528 | tf_op jit(solution)/shard_map/ppermute | solution.py:103
  82.5 3.3 %collective-permute-done.14 = f32[64,640]{1,0:T(8,128)S(1)} collective-permute-done((f32[64,640]{1,0:T(8,128)S(1)}, f32[64,640]{1,0:T(8,128)S(1)}, u32[]{:S(2)}, u32[]{:S(2)}) %collective-permute-start.14) | collective-permute-done | bytes 163872 | tf_op jit(solution)/shard_map/ppermute | solution.py:103
  85.8 0.7 select_add_fusion
  (34 shorter events, 1.8 us)
Async XLA Ops:
  0.0 9.8 %collective-permute-start = (f32[32,1280]{1,0:T(8,128)}, f32[32,1280]{1,0:T(8,128)S(1)}, u32[]{:S(2)}, u32[]{:S(2)}) collective-permute-start(f32[32,1280]{1,0:T(8,128)} %param.3), channel_id=1, source_target_pairs={{0,8},{1,9},{2,10},{3,11},{4,12},{5,13},{6,14},{7,15},{8,0},{9,1},... | collective-permute-start | bytes 491528 | tf_op jit(solution)/shard_map/ppermute | solution.py:71
  1.9 10.7 %collective-permute-start.1 = (f32[32,1280]{1,0:T(8,128)}, f32[32,1280]{1,0:T(8,128)S(1)}, u32[]{:S(2)}, u32[]{:S(2)}) collective-permute-start(f32[32,1280]{1,0:T(8,128)} %param.3), channel_id=1, source_target_pairs={{0,2},{1,3},{2,4},{3,5},{4,6},{5,7},{6,0},{7,1},{8,10},{9,11},{10,... | collective-permute-start | bytes 491528 | tf_op jit(solution)/shard_map/ppermute | solution.py:72
  2.1 6.9 %collective-permute-start.2 = (f32[32,1280]{1,0:T(8,128)}, f32[32,1280]{1,0:T(8,128)S(1)}, u32[]{:S(2)}, u32[]{:S(2)}) collective-permute-start(f32[32,1280]{1,0:T(8,128)} %param.3), channel_id=1, source_target_pairs={{0,6},{1,7},{2,0},{3,1},{4,2},{5,3},{6,4},{7,5},{8,14},{9,15},{10,... | collective-permute-start | bytes 491528 | tf_op jit(solution)/shard_map/ppermute | solution.py:73
  9.0 8.6 %collective-permute-start.3 = (f32[32,1280]{1,0:T(8,128)S(1)}, f32[32,1280]{1,0:T(8,128)S(1)}, u32[]{:S(2)}, u32[]{:S(2)}) collective-permute-start(f32[32,1280]{1,0:T(8,128)S(1)} %collective-permute-done.2), channel_id=1, source_target_pairs={{0,8},{1,9},{2,10},{3,11},{4,12},{5,13},{6,14},{7,15},{8,0},{9,1},... | collective-permute-start | bytes 491528 | tf_op jit(solution)/shard_map/ppermute | solution.py:74
  9.4 6.5 %collective-permute-start.4 = (f32[32,1280]{1,0:T(8,128)S(1)}, f32[32,1280]{1,0:T(8,128)S(1)}, u32[]{:S(2)}, u32[]{:S(2)}) collective-permute-start(f32[32,1280]{1,0:T(8,128)S(1)} %collective-permute-done.2), channel_id=1, source_target_pairs={{0,6},{1,7},{2,0},{3,1},{4,2},{5,3},{6,4},{7,5},{8,14},{9,15},{10,... | collective-permute-start | bytes 491528 | tf_op jit(solution)/shard_map/ppermute | solution.py:75
  9.8 7.8 %collective-permute-start.5 = (f32[32,1280]{1,0:T(8,128)S(1)}, f32[32,1280]{1,0:T(8,128)S(1)}, u32[]{:S(2)}, u32[]{:S(2)}) collective-permute-start(f32[32,1280]{1,0:T(8,128)S(1)} %collective-permute-done), channel_id=1, source_target_pairs={{0,2},{1,3},{2,4},{3,5},{4,6},{5,7},{6,0},{7,1},{8,10},{9,11},{10,... | collective-permute-start | bytes 491528 | tf_op jit(solution)/shard_map/ppermute | solution.py:76
  12.6 9.1 %copy-start.2 = (s32[8]{0:T(128)S(1)}, s32[8]{0:T(128)}, u32[]{:S(2)}) copy-start(s32[8]{0:T(128)} %constant.274.clone) | copy-start | bytes 100
  15.9 5.3 %collective-permute-start.6 = (f32[32,1280]{1,0:T(8,128)S(1)}, f32[32,1280]{1,0:T(8,128)S(1)}, u32[]{:S(2)}, u32[]{:S(2)}) collective-permute-start(f32[32,1280]{1,0:T(8,128)S(1)} %collective-permute-done.4), channel_id=1, source_target_pairs={{0,8},{1,9},{2,10},{3,11},{4,12},{5,13},{6,14},{7,15},{8,0},{9,1},... | collective-permute-start | bytes 491528 | tf_op jit(solution)/shard_map/ppermute | solution.py:77
  21.2 16.6 %copy-start = (f32[256,1280]{1,0:T(8,128)}, f32[256,1280]{1,0:T(8,128)S(1)}, u32[]{:S(2)}) copy-start(f32[256,1280]{1,0:T(8,128)S(1)} %constant_dynamic-update-slice_fusion.a_ref) | copy-start | bytes 3932164
  21.2 24.7 %collective-permute-start.7 = (f32[256,1280]{1,0:T(8,128)S(1)}, f32[256,1280]{1,0:T(8,128)S(1)}, u32[]{:S(2)}, u32[]{:S(2)}) collective-permute-start(f32[256,1280]{1,0:T(8,128)S(1)} %constant_dynamic-update-slice_fusion.a_ref), channel_id=1, source_target_pairs={{0,1},{1,0},{2,3},{3,2},{4,5},{5,4},{6,7},{7,6},{8,9},{9,8},{10,11... | collective-permute-start | bytes 3932168 | tf_op jit(solution)/shard_map/ppermute | solution.py:79
  45.9 1.1 %copy-start.1 = (f32[256,1280]{1,0:T(8,128)}, f32[256,1280]{1,0:T(8,128)S(1)}, u32[]{:S(2)}) copy-start(f32[256,1280]{1,0:T(8,128)S(1)} %collective-permute-done.7.a_ref) | copy-start | bytes 3932164
  55.2 6.5 %collective-permute-start.11 = (f32[64,640]{1,0:T(8,128)S(1)}, f32[64,640]{1,0:T(8,128)S(1)}, u32[]{:S(2)}, u32[]{:S(2)}) collective-permute-start(f32[64,640]{1,0:T(8,128)S(1)} %pad_maximum_fusion.1), channel_id=1, source_target_pairs={{0,48},{16,0},{32,16},{48,32},{64,112},{80,64},{96,80},{112,96},{1... | collective-permute-start | bytes 491528 | tf_op jit(solution)/shard_map/ppermute | solution.py:100
  58.0 7.4 %collective-permute-start.8 = (f32[64,640]{1,0:T(8,128)S(1)}, f32[64,640]{1,0:T(8,128)S(1)}, u32[]{:S(2)}, u32[]{:S(2)}) collective-permute-start(f32[64,640]{1,0:T(8,128)S(1)} %pad_maximum_fusion), channel_id=1, source_target_pairs={{0,16},{16,32},{32,48},{48,0},{64,80},{80,96},{96,112},{112,64},{1... | collective-permute-start | bytes 491528 | tf_op jit(solution)/shard_map/ppermute | solution.py:99
  61.7 6.6 %collective-permute-start.12 = (f32[64,640]{1,0:T(8,128)S(1)}, f32[64,640]{1,0:T(8,128)S(1)}, u32[]{:S(2)}, u32[]{:S(2)}) collective-permute-start(f32[64,640]{1,0:T(8,128)S(1)} %maximum_add_fusion.3), channel_id=1, source_target_pairs={{0,48},{16,0},{32,16},{48,32},{64,112},{80,64},{96,80},{112,96},{1... | collective-permute-start | bytes 491528 | tf_op jit(solution)/shard_map/ppermute | solution.py:100
  65.5 6.6 %collective-permute-start.9 = (f32[64,640]{1,0:T(8,128)S(1)}, f32[64,640]{1,0:T(8,128)S(1)}, u32[]{:S(2)}, u32[]{:S(2)}) collective-permute-start(f32[64,640]{1,0:T(8,128)S(1)} %maximum_add_fusion), channel_id=1, source_target_pairs={{0,16},{16,32},{32,48},{48,0},{64,80},{80,96},{96,112},{112,64},{1... | collective-permute-start | bytes 491528 | tf_op jit(solution)/shard_map/ppermute | solution.py:99
  68.3 6.6 %collective-permute-start.13 = (f32[64,640]{1,0:T(8,128)S(1)}, f32[64,640]{1,0:T(8,128)S(1)}, u32[]{:S(2)}, u32[]{:S(2)}) collective-permute-start(f32[64,640]{1,0:T(8,128)S(1)} %maximum_add_fusion.4), channel_id=1, source_target_pairs={{0,48},{16,0},{32,16},{48,32},{64,112},{80,64},{96,80},{112,96},{1... | collective-permute-start | bytes 491528 | tf_op jit(solution)/shard_map/ppermute | solution.py:100
  72.1 6.6 %collective-permute-start.10 = (f32[64,640]{1,0:T(8,128)S(1)}, f32[64,640]{1,0:T(8,128)S(1)}, u32[]{:S(2)}, u32[]{:S(2)}) collective-permute-start(f32[64,640]{1,0:T(8,128)S(1)} %maximum_add_fusion.1), channel_id=1, source_target_pairs={{0,16},{16,32},{32,48},{48,0},{64,80},{80,96},{96,112},{112,64},{1... | collective-permute-start | bytes 491528 | tf_op jit(solution)/shard_map/ppermute | solution.py:99
  78.7 7.0 %collective-permute-start.14 = (f32[64,640]{1,0:T(8,128)S(1)}, f32[64,640]{1,0:T(8,128)S(1)}, u32[]{:S(2)}, u32[]{:S(2)}) collective-permute-start(f32[64,640]{1,0:T(8,128)S(1)} %broadcast_select_fusion), channel_id=1, source_target_pairs={{0,64},{16,80},{32,96},{48,112},{64,0},{80,16},{96,32},{112,48},{1... | collective-permute-start | bytes 491528 | tf_op jit(solution)/shard_map/ppermute | solution.py:103

commit v4 on v2

--- a/solution.py
+++ b/solution.py
@@ -3,7 +3,7 @@
 from jax import lax
 from jax.sharding import PartitionSpec as P
 
-HIGHEST = lax.Precision.HIGHEST
+HIGH = lax.Precision.HIGH
 
 
 def _pairs(n, dest):
@@ -30,14 +30,16 @@
     slot_of = [0, 1, 3, 4, 5, 7, 2, 6]
 
     def matmul(a, b):
-        return jnp.dot(a, b, preferred_element_type=jnp.float32, precision=HIGHEST)
+        return jnp.dot(a, b, preferred_element_type=jnp.float32, precision=HIGH)
 
     def body(amplitudes, integrals):
         rows, cd = amplitudes.shape
         me = lax.axis_index("vir")
         zl, y, c = me // (2 * ny), (me // 2) % ny, me % 2
 
-        own = amplitudes
+        half = 0.5 * integrals
+        res_own = matmul(amplitudes, half)
+        own, res_own = lax.optimization_barrier((amplitudes, res_own))
         z1 = lax.ppermute(own, "vir", z_swap)
         ym1 = lax.ppermute(own, "vir", y_shift(1))
         yp1 = lax.ppermute(own, "vir", y_shift(-1))
@@ -47,8 +49,8 @@
         z3 = lax.ppermute(yp2, "vir", z_swap)
         local = jnp.concatenate([own, z1, ym1, yp1, z2, yp2, ym1z, z3], axis=0)
         other = lax.ppermute(local, "vir", core_swap)
-        res_l = (0.5 * matmul(local, integrals)).reshape(8, rows, -1)
-        res_o = (0.5 * matmul(other, integrals)).reshape(8, rows, -1)
+        res_l = jnp.concatenate([res_own, matmul(local[rows:], half)], axis=0).reshape(8, rows, -1)
+        res_o = matmul(other, half).reshape(8, rows, -1)
         table = jnp.array(slot_of, jnp.int32)
 
         def out_block(r):

time: 83.8 us -> 79.7 us (0.951)
  other arithmetic: 5.04 us -> 1.05 us
    select_n x1, other arithmetic: 1.07 us -> 0.03 us  [body(): send = jnp.where(zh == 0, sb, sa)]
    add x1, other arithmetic: 1.75 us -> 0.72 us  [body(): return keep + lax.ppermute(send, 'occ', zhi_swap)]
    unnamed x11 -> x13, local copies, waits for them, and re-layouts: 5.7 us -> 5.23 us
    dot_general x2 -> x3, matrix products: 9.51 us -> 9.41 us  [matmul(): return jnp.dot(a, b, preferred_element_type=jnp.float32, precision=HIGH)]
  transfers between devices with their start and end apart: 15 -> 15, of which waited for: 8 -> 8; matrix products, arithmetic and copies ran while one was open for 15% -> 12% of each run, Pallas kernels for 0% -> 0%
where the time goes in v4:
time: 79.7 us; the launch traced here: 79.3 us
  waiting for transfers between devices  23.6 us (30%)
  starting transfers between devices  23.5 us (29%)
  between operations  15 us (19%)
  matrix products  9.41 us (12%)
  local copies, waits for them, and re-layouts  6.66 us (8%)
  other arithmetic  1.05 us (1%)
    ppermute x3, starting transfers between devices, body(): sb = lax.ppermute(sb, 'occ', x_shift(-1)) + out_block(nx + (x + s + 1) % nx)  10.3 us
    ppermute x3, waiting for transfers between devices, body(): sb = lax.ppermute(sb, 'occ', x_shift(-1)) + out_block(nx + (x + s + 1) % nx)  9.91 us
    dot_general x3, matrix products, matmul(): return jnp.dot(a, b, preferred_element_type=jnp.float32, precision=HIGH)  9.41 us
    unnamed x13, local copies, waits for them, and re-layouts  5.23 us
    ppermute x1, waiting for transfers between devices, body(): yp1 = lax.ppermute(own, 'vir', y_shift(-1))  4.17 us
    ppermute x3, waiting for transfers between devices, body(): sa = lax.ppermute(sa, 'occ', x_shift(1)) + out_block((x - s - 1) % nx)  3.79 us
    ppermute x1, starting transfers between devices, body(): return keep + lax.ppermute(send, 'occ', zhi_swap)  3.66 us
    ppermute x1, waiting for transfers between devices, body(): return keep + lax.ppermute(send, 'occ', zhi_swap)  3.3 us
  transfers between devices with their start and end apart: 15, of which 8 were waited for; matrix products, arithmetic and copies ran while one was open for 12% of the time, Pallas kernels for 0%

profile of v4, /device:TPU:24, one launch (start us, length us, event | category | flops | bytes accessed | tf_op | source)
XLA Modules:
  0.0 79.3 jit_solution(2863068176850102331)
XLA Ops:
  0.0 2.9 %fusion.9 = f32[32,640]{1,0:T(8,128)S(1)} fusion(f32[32,1280]{1,0:T(8,128)} %param.3, f32[1280,640]{1,0:T(8,128)} %param.4), kind=kOutput, calls=%fused_computation.9 | convolution fusion | flops 158105600 | bytes 3522560 | tf_op jit(solution)/shard_map/dot_general | solution.py:33
  2.9 2.0 %collective-permute-start = (f32[32,1280]{1,0:T(8,128)S(1)}, f32[32,1280]{1,0:T(8,128)S(1)}, u32[]{:S(2)}, u32[]{:S(2)}) collective-permute-start(f32[32,1280]{1,0:T(8,128)S(1)} %copy-done.1), channel_id=1, source_target_pairs={{0,8},{1,9},{2,10},{3,11},{4,12},{5,13},{6,14},{7,15},{8,0},{9,1},... | collective-permute-start | bytes 491528 | tf_op jit(solution)/shard_map/ppermute | solution.py:43
  5.2 1.8 %collective-permute-start.2 = (f32[32,1280]{1,0:T(8,128)S(1)}, f32[32,1280]{1,0:T(8,128)S(1)}, u32[]{:S(2)}, u32[]{:S(2)}) collective-permute-start(f32[32,1280]{1,0:T(8,128)S(1)} %copy-done.1), channel_id=1, source_target_pairs={{0,6},{1,7},{2,0},{3,1},{4,2},{5,3},{6,4},{7,5},{8,14},{9,15},{10,... | collective-permute-start | bytes 491528 | tf_op jit(solution)/shard_map/ppermute | solution.py:45
  7.6 4.2 %collective-permute-done.2 = f32[32,1280]{1,0:T(8,128)S(1)} collective-permute-done((f32[32,1280]{1,0:T(8,128)S(1)}, f32[32,1280]{1,0:T(8,128)S(1)}, u32[]{:S(2)}, u32[]{:S(2)}) %collective-permute-start.2) | collective-permute-done | bytes 163872 | tf_op jit(solution)/shard_map/ppermute | solution.py:45
  12.7 2.8 %collective-permute-start.5 = (f32[32,1280]{1,0:T(8,128)S(1)}, f32[32,1280]{1,0:T(8,128)S(1)}, u32[]{:S(2)}, u32[]{:S(2)}) collective-permute-start(f32[32,1280]{1,0:T(8,128)S(1)} %collective-permute-done), channel_id=1, source_target_pairs={{0,2},{1,3},{2,4},{3,5},{4,6},{5,7},{6,0},{7,1},{8,10},{9,11},{10,... | collective-permute-start | bytes 491528 | tf_op jit(solution)/shard_map/ppermute | solution.py:48
  15.5 0.8 constant_dynamic-update-slice_fusion.6
  16.3 0.8 constant_dynamic-update-slice_fusion.5
  17.8 1.0 %collective-permute-done.4 = f32[32,1280]{1,0:T(8,128)S(1)} collective-permute-done((f32[32,1280]{1,0:T(8,128)S(1)}, f32[32,1280]{1,0:T(8,128)S(1)}, u32[]{:S(2)}, u32[]{:S(2)}) %collective-permute-start.4) | collective-permute-done | bytes 163872 | tf_op jit(solution)/shard_map/ppermute | solution.py:47
  18.8 1.6 %collective-permute-start.6 = (f32[32,1280]{1,0:T(8,128)S(1)}, f32[32,1280]{1,0:T(8,128)S(1)}, u32[]{:S(2)}, u32[]{:S(2)}) collective-permute-start(f32[32,1280]{1,0:T(8,128)S(1)} %collective-permute-done.4), channel_id=1, source_target_pairs={{0,8},{1,9},{2,10},{3,11},{4,12},{5,13},{6,14},{7,15},{8,0},{9,1},... | collective-permute-start | bytes 491528 | tf_op jit(solution)/shard_map/ppermute | solution.py:49
  21.1 0.8 constant_dynamic-update-slice_fusion.2
  21.9 0.8 constant_dynamic-update-slice_fusion.1
  22.6 1.5 %collective-permute-done.6 = f32[32,1280]{1,0:T(8,128)S(1)} collective-permute-done((f32[32,1280]{1,0:T(8,128)S(1)}, f32[32,1280]{1,0:T(8,128)S(1)}, u32[]{:S(2)}, u32[]{:S(2)}) %collective-permute-start.6) | collective-permute-done | bytes 163872 | tf_op jit(solution)/shard_map/ppermute | solution.py:49
  24.1 0.7 constant_dynamic-update-slice_fusion
  40.5 3.1 %fusion.2 = f32[224,640]{1,0:T(8,128)S(1)} fusion(f32[224,1280]{1,0:T(8,128)} %get-tuple-element.25, f32[1280,640]{1,0:T(8,128)S(1)} %copy-done), kind=kOutput, calls=%fused_computation.2 | convolution fusion | flops 1101824000 | bytes 4997120 | tf_op jit(solution)/shard_map/dot_general | solution.py:33
  43.7 3.4 %fusion = f32[256,640]{1,0:T(8,128)S(1)} fusion(f32[256,1280]{1,0:T(8,128)} %collective-permute-done.7, f32[1280,640]{1,0:T(8,128)S(1)} %copy-done), kind=kOutput, calls=%fused_computation | convolution fusion | flops 1259110400 | bytes 5242880 | tf_op jit(solution)/shard_map/dot_general | solution.py:33
  47.2 2.8 %collective-permute-start.11 = (f32[64,640]{1,0:T(8,128)S(1)}, f32[64,640]{1,0:T(8,128)S(1)}, u32[]{:S(2)}, u32[]{:S(2)}) collective-permute-start(f32[64,640]{1,0:T(8,128)S(1)} %pad_maximum_fusion.2), channel_id=1, source_target_pairs={{0,48},{16,0},{32,16},{48,32},{64,112},{80,64},{96,80},{112,96},{1... | collective-permute-start | bytes 491528 | tf_op jit(solution)/shard_map/ppermute | solution.py:72
  50.1 4.0 %collective-permute-done.11 = f32[64,640]{1,0:T(8,128)S(1)} collective-permute-done((f32[64,640]{1,0:T(8,128)S(1)}, f32[64,640]{1,0:T(8,128)S(1)}, u32[]{:S(2)}, u32[]{:S(2)}) %collective-permute-start.11) | collective-permute-done | bytes 163872 | tf_op jit(solution)/shard_map/ppermute | solution.py:72
  54.2 3.8 %collective-permute-start.12 = (f32[64,640]{1,0:T(8,128)S(1)}, f32[64,640]{1,0:T(8,128)S(1)}, u32[]{:S(2)}, u32[]{:S(2)}) collective-permute-start(f32[64,640]{1,0:T(8,128)S(1)} %maximum_add_fusion.3), channel_id=1, source_target_pairs={{0,48},{16,0},{32,16},{48,32},{64,112},{80,64},{96,80},{112,96},{1... | collective-permute-start | bytes 491528 | tf_op jit(solution)/shard_map/ppermute | solution.py:72
  58.0 3.2 %collective-permute-done.12 = f32[64,640]{1,0:T(8,128)S(1)} collective-permute-done((f32[64,640]{1,0:T(8,128)S(1)}, f32[64,640]{1,0:T(8,128)S(1)}, u32[]{:S(2)}, u32[]{:S(2)}) %collective-permute-start.12) | collective-permute-done | bytes 163872 | tf_op jit(solution)/shard_map/ppermute | solution.py:72
  61.2 3.8 %collective-permute-start.13 = (f32[64,640]{1,0:T(8,128)S(1)}, f32[64,640]{1,0:T(8,128)S(1)}, u32[]{:S(2)}, u32[]{:S(2)}) collective-permute-start(f32[64,640]{1,0:T(8,128)S(1)} %maximum_add_fusion.4), channel_id=1, source_target_pairs={{0,48},{16,0},{32,16},{48,32},{64,112},{80,64},{96,80},{112,96},{1... | collective-permute-start | bytes 491528 | tf_op jit(solution)/shard_map/ppermute | solution.py:72
  65.1 2.7 %collective-permute-done.13 = f32[64,640]{1,0:T(8,128)S(1)} collective-permute-done((f32[64,640]{1,0:T(8,128)S(1)}, f32[64,640]{1,0:T(8,128)S(1)}, u32[]{:S(2)}, u32[]{:S(2)}) %collective-permute-start.13) | collective-permute-done | bytes 163872 | tf_op jit(solution)/shard_map/ppermute | solution.py:72
  67.8 3.8 %collective-permute-done.10 = f32[64,640]{1,0:T(8,128)S(1)} collective-permute-done((f32[64,640]{1,0:T(8,128)S(1)}, f32[64,640]{1,0:T(8,128)S(1)}, u32[]{:S(2)}, u32[]{:S(2)}) %collective-permute-start.10) | collective-permute-done | bytes 163872 | tf_op jit(solution)/shard_map/ppermute | solution.py:71
  71.6 3.7 %collective-permute-start.14 = (f32[64,640]{1,0:T(8,128)S(1)}, f32[64,640]{1,0:T(8,128)S(1)}, u32[]{:S(2)}, u32[]{:S(2)}) collective-permute-start(f32[64,640]{1,0:T(8,128)S(1)} %broadcast_select_fusion), channel_id=1, source_target_pairs={{0,64},{16,80},{32,96},{48,112},{64,0},{80,16},{96,32},{112,48},{1... | collective-permute-start | bytes 491528 | tf_op jit(solution)/shard_map/ppermute | solution.py:75
  75.3 3.3 %collective-permute-done.14 = f32[64,640]{1,0:T(8,128)S(1)} collective-permute-done((f32[64,640]{1,0:T(8,128)S(1)}, f32[64,640]{1,0:T(8,128)S(1)}, u32[]{:S(2)}, u32[]{:S(2)}) %collective-permute-start.14) | collective-permute-done | bytes 163872 | tf_op jit(solution)/shard_map/ppermute | solution.py:75
  (34 shorter events, 5.3 us)
Async XLA Ops:
  0.0 2.9 %copy-start.1 = (f32[32,1280]{1,0:T(8,128)S(1)}, f32[32,1280]{1,0:T(8,128)}, u32[]{:S(2)}) copy-start(f32[32,1280]{1,0:T(8,128)} %param.3) | copy-start | bytes 491524
  2.9 9.8 %collective-permute-start = (f32[32,1280]{1,0:T(8,128)S(1)}, f32[32,1280]{1,0:T(8,128)S(1)}, u32[]{:S(2)}, u32[]{:S(2)}) collective-permute-start(f32[32,1280]{1,0:T(8,128)S(1)} %copy-done.1), channel_id=1, source_target_pairs={{0,8},{1,9},{2,10},{3,11},{4,12},{5,13},{6,14},{7,15},{8,0},{9,1},... | collective-permute-start | bytes 491528 | tf_op jit(solution)/shard_map/ppermute | solution.py:43
  4.9 11.3 %collective-permute-start.1 = (f32[32,1280]{1,0:T(8,128)S(1)}, f32[32,1280]{1,0:T(8,128)S(1)}, u32[]{:S(2)}, u32[]{:S(2)}) collective-permute-start(f32[32,1280]{1,0:T(8,128)S(1)} %copy-done.1), channel_id=1, source_target_pairs={{0,2},{1,3},{2,4},{3,5},{4,6},{5,7},{6,0},{7,1},{8,10},{9,11},{10,... | collective-permute-start | bytes 491528 | tf_op jit(solution)/shard_map/ppermute | solution.py:44
  5.2 6.7 %collective-permute-start.2 = (f32[32,1280]{1,0:T(8,128)S(1)}, f32[32,1280]{1,0:T(8,128)S(1)}, u32[]{:S(2)}, u32[]{:S(2)}) collective-permute-start(f32[32,1280]{1,0:T(8,128)S(1)} %copy-done.1), channel_id=1, source_target_pairs={{0,6},{1,7},{2,0},{3,1},{4,2},{5,3},{6,4},{7,5},{8,14},{9,15},{10,... | collective-permute-start | bytes 491528 | tf_op jit(solution)/shard_map/ppermute | solution.py:45
  11.8 8.6 %collective-permute-start.3 = (f32[32,1280]{1,0:T(8,128)S(1)}, f32[32,1280]{1,0:T(8,128)S(1)}, u32[]{:S(2)}, u32[]{:S(2)}) collective-permute-start(f32[32,1280]{1,0:T(8,128)S(1)} %collective-permute-done.2), channel_id=1, source_target_pairs={{0,8},{1,9},{2,10},{3,11},{4,12},{5,13},{6,14},{7,15},{8,0},{9,1},... | collective-permute-start | bytes 491528 | tf_op jit(solution)/shard_map/ppermute | solution.py:46
  12.2 6.5 %collective-permute-start.4 = (f32[32,1280]{1,0:T(8,128)S(1)}, f32[32,1280]{1,0:T(8,128)S(1)}, u32[]{:S(2)}, u32[]{:S(2)}) collective-permute-start(f32[32,1280]{1,0:T(8,128)S(1)} %collective-permute-done.2), channel_id=1, source_target_pairs={{0,6},{1,7},{2,0},{3,1},{4,2},{5,3},{6,4},{7,5},{8,14},{9,15},{10,... | collective-permute-start | bytes 491528 | tf_op jit(solution)/shard_map/ppermute | solution.py:47
  12.7 9.2 %collective-permute-start.5 = (f32[32,1280]{1,0:T(8,128)S(1)}, f32[32,1280]{1,0:T(8,128)S(1)}, u32[]{:S(2)}, u32[]{:S(2)}) collective-permute-start(f32[32,1280]{1,0:T(8,128)S(1)} %collective-permute-done), channel_id=1, source_target_pairs={{0,2},{1,3},{2,4},{3,5},{4,6},{5,7},{6,0},{7,1},{8,10},{9,11},{10,... | collective-permute-start | bytes 491528 | tf_op jit(solution)/shard_map/ppermute | solution.py:48
  17.0 23.4 %copy-start = (f32[1280,640]{1,0:T(8,128)S(1)}, f32[1280,640]{1,0:T(8,128)}, u32[]{:S(2)}) copy-start(f32[1280,640]{1,0:T(8,128)} %param.4) | copy-start | bytes 9830404
  18.8 5.3 %collective-permute-start.6 = (f32[32,1280]{1,0:T(8,128)S(1)}, f32[32,1280]{1,0:T(8,128)S(1)}, u32[]{:S(2)}, u32[]{:S(2)}) collective-permute-start(f32[32,1280]{1,0:T(8,128)S(1)} %collective-permute-done.4), channel_id=1, source_target_pairs={{0,8},{1,9},{2,10},{3,11},{4,12},{5,13},{6,14},{7,15},{8,0},{9,1},... | collective-permute-start | bytes 491528 | tf_op jit(solution)/shard_map/ppermute | solution.py:49
  20.4 4.5 %copy-start.2 = (s32[8]{0:T(128)S(1)}, s32[8]{0:T(128)}, u32[]{:S(2)}) copy-start(s32[8]{0:T(128)} %constant.274.clone) | copy-start | bytes 100
  24.8 18.8 %collective-permute-start.7 = (f32[256,1280]{1,0:T(8,128)}, f32[256,1280]{1,0:T(8,128)}, u32[]{:S(2)}, u32[]{:S(2)}) collective-permute-start(f32[256,1280]{1,0:T(8,128)} %get-tuple-element.26), channel_id=1, source_target_pairs={{0,1},{1,0},{2,3},{3,2},{4,5},{5,4},{6,7},{7,6},{8,9},{9,8},{10,11... | collective-permute-start | bytes 3932168 | tf_op jit(solution)/shard_map/ppermute | solution.py:51
  47.2 7.0 %collective-permute-start.11 = (f32[64,640]{1,0:T(8,128)S(1)}, f32[64,640]{1,0:T(8,128)S(1)}, u32[]{:S(2)}, u32[]{:S(2)}) collective-permute-start(f32[64,640]{1,0:T(8,128)S(1)} %pad_maximum_fusion.2), channel_id=1, source_target_pairs={{0,48},{16,0},{32,16},{48,32},{64,112},{80,64},{96,80},{112,96},{1... | collective-permute-start | bytes 491528 | tf_op jit(solution)/shard_map/ppermute | solution.py:72
  50.0 7.9 %collective-permute-start.8 = (f32[64,640]{1,0:T(8,128)S(1)}, f32[64,640]{1,0:T(8,128)S(1)}, u32[]{:S(2)}, u32[]{:S(2)}) collective-permute-start(f32[64,640]{1,0:T(8,128)S(1)} %pad_maximum_fusion.1), channel_id=1, source_target_pairs={{0,16},{16,32},{32,48},{48,0},{64,80},{80,96},{96,112},{112,64},{1... | collective-permute-start | bytes 491528 | tf_op jit(solution)/shard_map/ppermute | solution.py:71
  54.2 7.0 %collective-permute-start.12 = (f32[64,640]{1,0:T(8,128)S(1)}, f32[64,640]{1,0:T(8,128)S(1)}, u32[]{:S(2)}, u32[]{:S(2)}) collective-permute-start(f32[64,640]{1,0:T(8,128)S(1)} %maximum_add_fusion.3), channel_id=1, source_target_pairs={{0,48},{16,0},{32,16},{48,32},{64,112},{80,64},{96,80},{112,96},{1... | collective-permute-start | bytes 491528 | tf_op jit(solution)/shard_map/ppermute | solution.py:72
  58.0 7.0 %collective-permute-start.9 = (f32[64,640]{1,0:T(8,128)S(1)}, f32[64,640]{1,0:T(8,128)S(1)}, u32[]{:S(2)}, u32[]{:S(2)}) collective-permute-start(f32[64,640]{1,0:T(8,128)S(1)} %maximum_add_fusion), channel_id=1, source_target_pairs={{0,16},{16,32},{32,48},{48,0},{64,80},{80,96},{96,112},{112,64},{1... | collective-permute-start | bytes 491528 | tf_op jit(solution)/shard_map/ppermute | solution.py:71
  61.2 6.6 %collective-permute-start.13 = (f32[64,640]{1,0:T(8,128)S(1)}, f32[64,640]{1,0:T(8,128)S(1)}, u32[]{:S(2)}, u32[]{:S(2)}) collective-permute-start(f32[64,640]{1,0:T(8,128)S(1)} %maximum_add_fusion.4), channel_id=1, source_target_pairs={{0,48},{16,0},{32,16},{48,32},{64,112},{80,64},{96,80},{112,96},{1... | collective-permute-start | bytes 491528 | tf_op jit(solution)/shard_map/ppermute | solution.py:72
  65.0 6.6 %collective-permute-start.10 = (f32[64,640]{1,0:T(8,128)S(1)}, f32[64,640]{1,0:T(8,128)S(1)}, u32[]{:S(2)}, u32[]{:S(2)}) collective-permute-start(f32[64,640]{1,0:T(8,128)S(1)} %maximum_add_fusion.1), channel_id=1, source_target_pairs={{0,16},{16,32},{32,48},{48,0},{64,80},{80,96},{96,112},{112,64},{1... | collective-permute-start | bytes 491528 | tf_op jit(solution)/shard_map/ppermute | solution.py:71
  71.6 7.0 %collective-permute-start.14 = (f32[64,640]{1,0:T(8,128)S(1)}, f32[64,640]{1,0:T(8,128)S(1)}, u32[]{:S(2)}, u32[]{:S(2)}) collective-permute-start(f32[64,640]{1,0:T(8,128)S(1)} %broadcast_select_fusion), channel_id=1, source_target_pairs={{0,64},{16,80},{32,96},{48,112},{64,0},{80,16},{96,32},{112,48},{1... | collective-permute-start | bytes 491528 | tf_op jit(solution)/shard_map/ppermute | solution.py:75

commit v5 on v4

--- a/solution.py
+++ b/solution.py
@@ -48,8 +48,10 @@
         ym1z = lax.ppermute(z1, "vir", y_shift(1))
         z3 = lax.ppermute(yp2, "vir", z_swap)
         local = jnp.concatenate([own, z1, ym1, yp1, z2, yp2, ym1z, z3], axis=0)
+        res_l = jnp.concatenate([res_own, matmul(local[rows:], half)], axis=0)
+        local, res_l = lax.optimization_barrier((local, res_l))
+        res_l = res_l.reshape(8, rows, -1)
         other = lax.ppermute(local, "vir", core_swap)
-        res_l = jnp.concatenate([res_own, matmul(local[rows:], half)], axis=0).reshape(8, rows, -1)
         res_o = matmul(other, half).reshape(8, rows, -1)
         table = jnp.array(slot_of, jnp.int32)
 

time: 79.7 us -> 79.4 us (level)
  matrix products: 9.41 us -> 8.22 us
  other arithmetic: 1.05 us -> 1.89 us
    dot_general x3, matrix products: 9.41 us -> 8.22 us  [matmul(): return jnp.dot(a, b, preferred_element_type=jnp.float32, precision=HIGH)]
    concatenate x1, other arithmetic: 0.05 us -> 0.89 us  [body(): res_l = jnp.concatenate([res_own, matmul(local[rows:], half)], axis=0)]
    unnamed x13 -> x15, local copies, waits for them, and re-layouts: 5.23 us -> 4.81 us
  transfers between devices with their start and end apart: 15 -> 15, of which waited for: 8 -> 8; matrix products, arithmetic and copies ran while one was open for 12% -> 7% of each run, Pallas kernels for 0% -> 0%
where the time goes in v5:
time: 79.4 us; the launch traced here: 79 us
  waiting for transfers between devices  24.1 us (30%)
  starting transfers between devices  23.5 us (30%)
  between operations  15.1 us (19%)
  matrix products  8.22 us (10%)
  local copies, waits for them, and re-layouts  6.2 us (8%)
  other arithmetic  1.89 us (2%)
    ppermute x3, starting transfers between devices, body(): sb = lax.ppermute(sb, 'occ', x_shift(-1)) + out_block(nx + (x + s + 1) % nx)  10.3 us
    ppermute x3, waiting for transfers between devices, body(): sb = lax.ppermute(sb, 'occ', x_shift(-1)) + out_block(nx + (x + s + 1) % nx)  9.9 us
    dot_general x3, matrix products, matmul(): return jnp.dot(a, b, preferred_element_type=jnp.float32, precision=HIGH)  8.22 us
    unnamed x15, local copies, waits for them, and re-layouts  4.81 us
    ppermute x1, waiting for transfers between devices, body(): yp1 = lax.ppermute(own, 'vir', y_shift(-1))  4.18 us
    ppermute x3, waiting for transfers between devices, body(): sa = lax.ppermute(sa, 'occ', x_shift(1)) + out_block((x - s - 1) % nx)  3.79 us
    ppermute x1, starting transfers between devices, body(): return keep + lax.ppermute(send, 'occ', zhi_swap)  3.66 us
    ppermute x1, waiting for transfers between devices, body(): return keep + lax.ppermute(send, 'occ', zhi_swap)  3.3 us
  transfers between devices with their start and end apart: 15, of which 8 were waited for; matrix products, arithmetic and copies ran while one was open for 7% of the time, Pallas kernels for 0%

profile of v5, /device:TPU:24, one launch (start us, length us, event | category | flops | bytes accessed | tf_op | source)
XLA Modules:
  0.0 79.0 jit_solution(4991105257325825873)
XLA Ops:
  0.0 2.9 %fusion.9 = f32[32,640]{1,0:T(8,128)S(1)} fusion(f32[32,1280]{1,0:T(8,128)} %param.3, f32[1280,640]{1,0:T(8,128)} %param.4), kind=kOutput, calls=%fused_computation.9 | convolution fusion | flops 158105600 | bytes 3522560 | tf_op jit(solution)/shard_map/dot_general | solution.py:33
  2.9 2.0 %collective-permute-start = (f32[32,1280]{1,0:T(8,128)S(1)}, f32[32,1280]{1,0:T(8,128)S(1)}, u32[]{:S(2)}, u32[]{:S(2)}) collective-permute-start(f32[32,1280]{1,0:T(8,128)S(1)} %copy-done.2), channel_id=1, source_target_pairs={{0,8},{1,9},{2,10},{3,11},{4,12},{5,13},{6,14},{7,15},{8,0},{9,1},... | collective-permute-start | bytes 491528 | tf_op jit(solution)/shard_map/ppermute | solution.py:43
  5.2 1.8 %collective-permute-start.2 = (f32[32,1280]{1,0:T(8,128)S(1)}, f32[32,1280]{1,0:T(8,128)S(1)}, u32[]{:S(2)}, u32[]{:S(2)}) collective-permute-start(f32[32,1280]{1,0:T(8,128)S(1)} %copy-done.2), channel_id=1, source_target_pairs={{0,6},{1,7},{2,0},{3,1},{4,2},{5,3},{6,4},{7,5},{8,14},{9,15},{10,... | collective-permute-start | bytes 491528 | tf_op jit(solution)/shard_map/ppermute | solution.py:45
  7.6 4.2 %collective-permute-done.2 = f32[32,1280]{1,0:T(8,128)S(1)} collective-permute-done((f32[32,1280]{1,0:T(8,128)S(1)}, f32[32,1280]{1,0:T(8,128)S(1)}, u32[]{:S(2)}, u32[]{:S(2)}) %collective-permute-start.2) | collective-permute-done | bytes 163872 | tf_op jit(solution)/shard_map/ppermute | solution.py:45
  12.7 2.8 %collective-permute-start.5 = (f32[32,1280]{1,0:T(8,128)S(1)}, f32[32,1280]{1,0:T(8,128)S(1)}, u32[]{:S(2)}, u32[]{:S(2)}) collective-permute-start(f32[32,1280]{1,0:T(8,128)S(1)} %collective-permute-done), channel_id=1, source_target_pairs={{0,2},{1,3},{2,4},{3,5},{4,6},{5,7},{6,0},{7,1},{8,10},{9,11},{10,... | collective-permute-start | bytes 491528 | tf_op jit(solution)/shard_map/ppermute | solution.py:48
  16.2 0.7 constant_dynamic-update-slice_fusion.13
  17.6 1.2 %collective-permute-done.4 = f32[32,1280]{1,0:T(8,128)S(1)} collective-permute-done((f32[32,1280]{1,0:T(8,128)S(1)}, f32[32,1280]{1,0:T(8,128)S(1)}, u32[]{:S(2)}, u32[]{:S(2)}) %collective-permute-start.4) | collective-permute-done | bytes 163872 | tf_op jit(solution)/shard_map/ppermute | solution.py:47
  18.8 1.6 %collective-permute-start.6 = (f32[32,1280]{1,0:T(8,128)S(1)}, f32[32,1280]{1,0:T(8,128)S(1)}, u32[]{:S(2)}, u32[]{:S(2)}) collective-permute-start(f32[32,1280]{1,0:T(8,128)S(1)} %collective-permute-done.4), channel_id=1, source_target_pairs={{0,8},{1,9},{2,10},{3,11},{4,12},{5,13},{6,14},{7,15},{8,0},{9,1},... | collective-permute-start | bytes 491528 | tf_op jit(solution)/shard_map/ppermute | solution.py:49
  21.7 0.7 constant_dynamic-update-slice_fusion.9
  22.4 1.7 %collective-permute-done.6 = f32[32,1280]{1,0:T(8,128)S(1)} collective-permute-done((f32[32,1280]{1,0:T(8,128)S(1)}, f32[32,1280]{1,0:T(8,128)S(1)}, u32[]{:S(2)}, u32[]{:S(2)}) %collective-permute-start.6) | collective-permute-done | bytes 163872 | tf_op jit(solution)/shard_map/ppermute | solution.py:49
  24.8 1.9 %fusion.2 = f32[224,640]{1,0:T(8,128)S(1)} fusion(f32[224,1280]{1,0:T(8,128)S(1)} %get-tuple-element.29, f32[1280,640]{1,0:T(8,128)S(1)} %copy-done), kind=kOutput, calls=%fused_computation.2 | convolution fusion | flops 1101824000 | bytes 4997120 | tf_op jit(solution)/shard_map/dot_general | solution.py:33
  26.7 0.9 %pad_maximum_fusion = f32[256,640]{1,0:T(8,128)} fusion(f32[224,640]{1,0:T(8,128)S(1)} %fusion.2, f32[32,640]{1,0:T(8,128)S(1)} %fusion.9), kind=kLoop, calls=%fused_computation.10 | loop fusion | flops 163840 | bytes 1310720 | tf_op jit(solution)/shard_map/concatenate | solution.py:51
  27.6 0.7 fusion.15
  43.3 3.4 %fusion = f32[256,640]{1,0:T(8,128)S(1)} fusion(f32[256,1280]{1,0:T(8,128)} %collective-permute-done.7, f32[1280,640]{1,0:T(8,128)S(1)} %copy-done), kind=kOutput, calls=%fused_computation | convolution fusion | flops 1259110400 | bytes 5242880 | tf_op jit(solution)/shard_map/dot_general | solution.py:33
  46.9 2.8 %collective-permute-start.11 = (f32[64,640]{1,0:T(8,128)S(1)}, f32[64,640]{1,0:T(8,128)S(1)}, u32[]{:S(2)}, u32[]{:S(2)}) collective-permute-start(f32[64,640]{1,0:T(8,128)S(1)} %pad_maximum_fusion.2), channel_id=1, source_target_pairs={{0,48},{16,0},{32,16},{48,32},{64,112},{80,64},{96,80},{112,96},{1... | collective-permute-start | bytes 491528 | tf_op jit(solution)/shard_map/ppermute | solution.py:74
  49.8 4.0 %collective-permute-done.11 = f32[64,640]{1,0:T(8,128)S(1)} collective-permute-done((f32[64,640]{1,0:T(8,128)S(1)}, f32[64,640]{1,0:T(8,128)S(1)}, u32[]{:S(2)}, u32[]{:S(2)}) %collective-permute-start.11) | collective-permute-done | bytes 163872 | tf_op jit(solution)/shard_map/ppermute | solution.py:74
  53.9 3.8 %collective-permute-start.12 = (f32[64,640]{1,0:T(8,128)S(1)}, f32[64,640]{1,0:T(8,128)S(1)}, u32[]{:S(2)}, u32[]{:S(2)}) collective-permute-start(f32[64,640]{1,0:T(8,128)S(1)} %maximum_add_fusion.3), channel_id=1, source_target_pairs={{0,48},{16,0},{32,16},{48,32},{64,112},{80,64},{96,80},{112,96},{1... | collective-permute-start | bytes 491528 | tf_op jit(solution)/shard_map/ppermute | solution.py:74
  57.7 3.2 %collective-permute-done.12 = f32[64,640]{1,0:T(8,128)S(1)} collective-permute-done((f32[64,640]{1,0:T(8,128)S(1)}, f32[64,640]{1,0:T(8,128)S(1)}, u32[]{:S(2)}, u32[]{:S(2)}) %collective-permute-start.12) | collective-permute-done | bytes 163872 | tf_op jit(solution)/shard_map/ppermute | solution.py:74
  60.9 3.8 %collective-permute-start.13 = (f32[64,640]{1,0:T(8,128)S(1)}, f32[64,640]{1,0:T(8,128)S(1)}, u32[]{:S(2)}, u32[]{:S(2)}) collective-permute-start(f32[64,640]{1,0:T(8,128)S(1)} %maximum_add_fusion.4), channel_id=1, source_target_pairs={{0,48},{16,0},{32,16},{48,32},{64,112},{80,64},{96,80},{112,96},{1... | collective-permute-start | bytes 491528 | tf_op jit(solution)/shard_map/ppermute | solution.py:74
  64.8 2.7 %collective-permute-done.13 = f32[64,640]{1,0:T(8,128)S(1)} collective-permute-done((f32[64,640]{1,0:T(8,128)S(1)}, f32[64,640]{1,0:T(8,128)S(1)}, u32[]{:S(2)}, u32[]{:S(2)}) %collective-permute-start.13) | collective-permute-done | bytes 163872 | tf_op jit(solution)/shard_map/ppermute | solution.py:74
  67.5 3.8 %collective-permute-done.10 = f32[64,640]{1,0:T(8,128)S(1)} collective-permute-done((f32[64,640]{1,0:T(8,128)S(1)}, f32[64,640]{1,0:T(8,128)S(1)}, u32[]{:S(2)}, u32[]{:S(2)}) %collective-permute-start.10) | collective-permute-done | bytes 163872 | tf_op jit(solution)/shard_map/ppermute | solution.py:73
  71.4 3.7 %collective-permute-start.14 = (f32[64,640]{1,0:T(8,128)S(1)}, f32[64,640]{1,0:T(8,128)S(1)}, u32[]{:S(2)}, u32[]{:S(2)}) collective-permute-start(f32[64,640]{1,0:T(8,128)S(1)} %broadcast_select_fusion), channel_id=1, source_target_pairs={{0,64},{16,80},{32,96},{48,112},{64,0},{80,16},{96,32},{112,48},{1... | collective-permute-start | bytes 491528 | tf_op jit(solution)/shard_map/ppermute | solution.py:77
  75.0 3.3 %collective-permute-done.14 = f32[64,640]{1,0:T(8,128)S(1)} collective-permute-done((f32[64,640]{1,0:T(8,128)S(1)}, f32[64,640]{1,0:T(8,128)S(1)}, u32[]{:S(2)}, u32[]{:S(2)}) %collective-permute-start.14) | collective-permute-done | bytes 163872 | tf_op jit(solution)/shard_map/ppermute | solution.py:77
  78.3 0.7 select_add_fusion
  (36 shorter events, 5.8 us)
Async XLA Ops:
  0.0 2.9 %copy-start.2 = (f32[32,1280]{1,0:T(8,128)S(1)}, f32[32,1280]{1,0:T(8,128)}, u32[]{:S(2)}) copy-start(f32[32,1280]{1,0:T(8,128)} %param.3) | copy-start | bytes 491524
  2.9 9.8 %collective-permute-start = (f32[32,1280]{1,0:T(8,128)S(1)}, f32[32,1280]{1,0:T(8,128)S(1)}, u32[]{:S(2)}, u32[]{:S(2)}) collective-permute-start(f32[32,1280]{1,0:T(8,128)S(1)} %copy-done.2), channel_id=1, source_target_pairs={{0,8},{1,9},{2,10},{3,11},{4,12},{5,13},{6,14},{7,15},{8,0},{9,1},... | collective-permute-start | bytes 491528 | tf_op jit(solution)/shard_map/ppermute | solution.py:43
  4.9 11.3 %collective-permute-start.1 = (f32[32,1280]{1,0:T(8,128)S(1)}, f32[32,1280]{1,0:T(8,128)S(1)}, u32[]{:S(2)}, u32[]{:S(2)}) collective-permute-start(f32[32,1280]{1,0:T(8,128)S(1)} %copy-done.2), channel_id=1, source_target_pairs={{0,2},{1,3},{2,4},{3,5},{4,6},{5,7},{6,0},{7,1},{8,10},{9,11},{10,... | collective-permute-start | bytes 491528 | tf_op jit(solution)/shard_map/ppermute | solution.py:44
  5.2 6.7 %collective-permute-start.2 = (f32[32,1280]{1,0:T(8,128)S(1)}, f32[32,1280]{1,0:T(8,128)S(1)}, u32[]{:S(2)}, u32[]{:S(2)}) collective-permute-start(f32[32,1280]{1,0:T(8,128)S(1)} %copy-done.2), channel_id=1, source_target_pairs={{0,6},{1,7},{2,0},{3,1},{4,2},{5,3},{6,4},{7,5},{8,14},{9,15},{10,... | collective-permute-start | bytes 491528 | tf_op jit(solution)/shard_map/ppermute | solution.py:45
  11.8 8.6 %collective-permute-start.3 = (f32[32,1280]{1,0:T(8,128)S(1)}, f32[32,1280]{1,0:T(8,128)S(1)}, u32[]{:S(2)}, u32[]{:S(2)}) collective-permute-start(f32[32,1280]{1,0:T(8,128)S(1)} %collective-permute-done.2), channel_id=1, source_target_pairs={{0,8},{1,9},{2,10},{3,11},{4,12},{5,13},{6,14},{7,15},{8,0},{9,1},... | collective-permute-start | bytes 491528 | tf_op jit(solution)/shard_map/ppermute | solution.py:46
  12.3 6.5 %collective-permute-start.4 = (f32[32,1280]{1,0:T(8,128)S(1)}, f32[32,1280]{1,0:T(8,128)S(1)}, u32[]{:S(2)}, u32[]{:S(2)}) collective-permute-start(f32[32,1280]{1,0:T(8,128)S(1)} %collective-permute-done.2), channel_id=1, source_target_pairs={{0,6},{1,7},{2,0},{3,1},{4,2},{5,3},{6,4},{7,5},{8,14},{9,15},{10,... | collective-permute-start | bytes 491528 | tf_op jit(solution)/shard_map/ppermute | solution.py:47
  12.7 9.0 %collective-permute-start.5 = (f32[32,1280]{1,0:T(8,128)S(1)}, f32[32,1280]{1,0:T(8,128)S(1)}, u32[]{:S(2)}, u32[]{:S(2)}) collective-permute-start(f32[32,1280]{1,0:T(8,128)S(1)} %collective-permute-done), channel_id=1, source_target_pairs={{0,2},{1,3},{2,4},{3,5},{4,6},{5,7},{6,0},{7,1},{8,10},{9,11},{10,... | collective-permute-start | bytes 491528 | tf_op jit(solution)/shard_map/ppermute | solution.py:48
  15.5 9.3 %copy-start = (f32[1280,640]{1,0:T(8,128)S(1)}, f32[1280,640]{1,0:T(8,128)}, u32[]{:S(2)}) copy-start(f32[1280,640]{1,0:T(8,128)} %param.4) | copy-start | bytes 9830404
  18.8 5.3 %collective-permute-start.6 = (f32[32,1280]{1,0:T(8,128)S(1)}, f32[32,1280]{1,0:T(8,128)S(1)}, u32[]{:S(2)}, u32[]{:S(2)}) collective-permute-start(f32[32,1280]{1,0:T(8,128)S(1)} %collective-permute-done.4), channel_id=1, source_target_pairs={{0,8},{1,9},{2,10},{3,11},{4,12},{5,13},{6,14},{7,15},{8,0},{9,1},... | collective-permute-start | bytes 491528 | tf_op jit(solution)/shard_map/ppermute | solution.py:49
  26.7 0.9 %copy-start.3 = (s32[8]{0:T(128)S(1)}, s32[8]{0:T(128)}, u32[]{:S(2)}) copy-start(s32[8]{0:T(128)} %constant.274.clone) | copy-start | bytes 100
  27.6 15.7 %collective-permute-start.7 = (f32[256,1280]{1,0:T(8,128)}, f32[256,1280]{1,0:T(8,128)}, u32[]{:S(2)}, u32[]{:S(2)}) collective-permute-start(f32[256,1280]{1,0:T(8,128)} %get-tuple-element.12), channel_id=1, source_target_pairs={{0,1},{1,0},{2,3},{3,2},{4,5},{5,4},{6,7},{7,6},{8,9},{9,8},{10,11... | collective-permute-start | bytes 3932168 | tf_op jit(solution)/shard_map/ppermute | solution.py:54
  43.3 3.4 %copy-start.1 = (f32[256,640]{1,0:T(8,128)S(1)}, f32[256,640]{1,0:T(8,128)}, u32[]{:S(2)}) copy-start(f32[256,640]{1,0:T(8,128)} %pad_maximum_fusion) | copy-start | bytes 1966084
  46.9 7.0 %collective-permute-start.11 = (f32[64,640]{1,0:T(8,128)S(1)}, f32[64,640]{1,0:T(8,128)S(1)}, u32[]{:S(2)}, u32[]{:S(2)}) collective-permute-start(f32[64,640]{1,0:T(8,128)S(1)} %pad_maximum_fusion.2), channel_id=1, source_target_pairs={{0,48},{16,0},{32,16},{48,32},{64,112},{80,64},{96,80},{112,96},{1... | collective-permute-start | bytes 491528 | tf_op jit(solution)/shard_map/ppermute | solution.py:74
  49.7 7.9 %collective-permute-start.8 = (f32[64,640]{1,0:T(8,128)S(1)}, f32[64,640]{1,0:T(8,128)S(1)}, u32[]{:S(2)}, u32[]{:S(2)}) collective-permute-start(f32[64,640]{1,0:T(8,128)S(1)} %pad_maximum_fusion.1), channel_id=1, source_target_pairs={{0,16},{16,32},{32,48},{48,0},{64,80},{80,96},{96,112},{112,64},{1... | collective-permute-start | bytes 491528 | tf_op jit(solution)/shard_map/ppermute | solution.py:73
  53.9 7.0 %collective-permute-start.12 = (f32[64,640]{1,0:T(8,128)S(1)}, f32[64,640]{1,0:T(8,128)S(1)}, u32[]{:S(2)}, u32[]{:S(2)}) collective-permute-start(f32[64,640]{1,0:T(8,128)S(1)} %maximum_add_fusion.3), channel_id=1, source_target_pairs={{0,48},{16,0},{32,16},{48,32},{64,112},{80,64},{96,80},{112,96},{1... | collective-permute-start | bytes 491528 | tf_op jit(solution)/shard_map/ppermute | solution.py:74
  57.7 7.0 %collective-permute-start.9 = (f32[64,640]{1,0:T(8,128)S(1)}, f32[64,640]{1,0:T(8,128)S(1)}, u32[]{:S(2)}, u32[]{:S(2)}) collective-permute-start(f32[64,640]{1,0:T(8,128)S(1)} %maximum_add_fusion), channel_id=1, source_target_pairs={{0,16},{16,32},{32,48},{48,0},{64,80},{80,96},{96,112},{112,64},{1... | collective-permute-start | bytes 491528 | tf_op jit(solution)/shard_map/ppermute | solution.py:73
  60.9 6.6 %collective-permute-start.13 = (f32[64,640]{1,0:T(8,128)S(1)}, f32[64,640]{1,0:T(8,128)S(1)}, u32[]{:S(2)}, u32[]{:S(2)}) collective-permute-start(f32[64,640]{1,0:T(8,128)S(1)} %maximum_add_fusion.4), channel_id=1, source_target_pairs={{0,48},{16,0},{32,16},{48,32},{64,112},{80,64},{96,80},{112,96},{1... | collective-permute-start | bytes 491528 | tf_op jit(solution)/shard_map/ppermute | solution.py:74
  64.7 6.6 %collective-permute-start.10 = (f32[64,640]{1,0:T(8,128)S(1)}, f32[64,640]{1,0:T(8,128)S(1)}, u32[]{:S(2)}, u32[]{:S(2)}) collective-permute-start(f32[64,640]{1,0:T(8,128)S(1)} %maximum_add_fusion.1), channel_id=1, source_target_pairs={{0,16},{16,32},{32,48},{48,0},{64,80},{80,96},{96,112},{112,64},{1... | collective-permute-start | bytes 491528 | tf_op jit(solution)/shard_map/ppermute | solution.py:73
  71.4 7.0 %collective-permute-start.14 = (f32[64,640]{1,0:T(8,128)S(1)}, f32[64,640]{1,0:T(8,128)S(1)}, u32[]{:S(2)}, u32[]{:S(2)}) collective-permute-start(f32[64,640]{1,0:T(8,128)S(1)} %broadcast_select_fusion), channel_id=1, source_target_pairs={{0,64},{16,80},{32,96},{48,112},{64,0},{80,16},{96,32},{112,48},{1... | collective-permute-start | bytes 491528 | tf_op jit(solution)/shard_map/ppermute | solution.py:77

commit v6 on v5

--- a/solution.py
+++ b/solution.py
@@ -43,15 +43,20 @@
         z1 = lax.ppermute(own, "vir", z_swap)
         ym1 = lax.ppermute(own, "vir", y_shift(1))
         yp1 = lax.ppermute(own, "vir", y_shift(-1))
+        first = jnp.concatenate([own, z1, ym1, yp1], axis=0)
+        other_first = lax.ppermute(first, "vir", core_swap)
         z2 = lax.ppermute(yp1, "vir", z_swap)
         yp2 = lax.ppermute(yp1, "vir", y_shift(-1))
         ym1z = lax.ppermute(z1, "vir", y_shift(1))
+        second = jnp.concatenate([z2, yp2, ym1z], axis=0)
+        other_second = lax.ppermute(second, "vir", core_swap)
         z3 = lax.ppermute(yp2, "vir", z_swap)
-        local = jnp.concatenate([own, z1, ym1, yp1, z2, yp2, ym1z, z3], axis=0)
+        local = jnp.concatenate([first, second, z3], axis=0)
         res_l = jnp.concatenate([res_own, matmul(local[rows:], half)], axis=0)
-        local, res_l = lax.optimization_barrier((local, res_l))
+        z3, res_l = lax.optimization_barrier((z3, res_l))
         res_l = res_l.reshape(8, rows, -1)
-        other = lax.ppermute(local, "vir", core_swap)
+        other_last = lax.ppermute(z3, "vir", core_swap)
+        other = jnp.concatenate([other_first, other_second, other_last], axis=0)
         res_o = matmul(other, half).reshape(8, rows, -1)
         table = jnp.array(slot_of, jnp.int32)
 

time: 79.4 us -> 86.3 us (1.087)
  the two profiles are of different devices: /device:TPU:24 before, /device:TPU:0 now
where the time goes in v6:
time: 86.3 us; the launch traced here: 85.9 us
  waiting for transfers between devices  34.2 us (40%)
  starting transfers between devices  23.4 us (27%)
  between operations  14.9 us (17%)
  matrix products  8.14 us (9%)
  other arithmetic  3.59 us (4%)
  local copies, waits for them, and re-layouts  1.69 us (2%)
    ppermute x3, starting transfers between devices, body(): sb = lax.ppermute(sb, 'occ', x_shift(-1)) + out_block(nx + (x + s + 1) % nx)  10.3 us
    ppermute x3, waiting for transfers between devices, body(): sb = lax.ppermute(sb, 'occ', x_shift(-1)) + out_block(nx + (x + s + 1) % nx)  9.91 us
    dot_general x3, matrix products, matmul(): return jnp.dot(a, b, preferred_element_type=jnp.float32, precision=HIGH)  8.14 us
    ppermute x1, waiting for transfers between devices, body(): z3 = lax.ppermute(yp2, 'vir', z_swap)  4.99 us
    ppermute x1, waiting for transfers between devices, body(): yp2 = lax.ppermute(yp1, 'vir', y_shift(-1))  4.17 us
    ppermute x3, waiting for transfers between devices, body(): sa = lax.ppermute(sa, 'occ', x_shift(1)) + out_block((x - s - 1) % nx)  3.79 us
    ppermute x1, starting transfers between devices, body(): return keep + lax.ppermute(send, 'occ', zhi_swap)  3.7 us
    ppermute x1, waiting for transfers between devices, body(): return keep + lax.ppermute(send, 'occ', zhi_swap)  3.3 us
  transfers between devices with their start and end apart: 17, of which 12 were waited for; matrix products, arithmetic and copies ran while one was open for 6% of the time, Pallas kernels for 0%

profile of v6, /device:TPU:0, one launch (start us, length us, event | category | flops | bytes accessed | tf_op | source)
XLA Modules:
  0.0 85.9 jit_solution(6350278264127535203)
XLA Ops:
  0.0 2.9 %fusion.14 = f32[32,640]{1,0:T(8,128)S(1)} fusion(f32[32,1280]{1,0:T(8,128)} %param.3, f32[1280,640]{1,0:T(8,128)} %param.4), kind=kOutput, calls=%fused_computation.14 | convolution fusion | flops 158105600 | bytes 3522560 | tf_op jit(solution)/shard_map/dot_general | solution.py:33
  2.9 3.2 %collective-permute-start = (f32[32,1280]{1,0:T(8,128)S(1)}, f32[32,1280]{1,0:T(8,128)S(1)}, u32[]{:S(2)}, u32[]{:S(2)}) collective-permute-start(f32[32,1280]{1,0:T(8,128)S(1)} %copy-done.2), channel_id=1, source_target_pairs={{0,6},{1,7},{2,0},{3,1},{4,2},{5,3},{6,4},{7,5},{8,14},{9,15},{10,... | collective-permute-start | bytes 491528 | tf_op jit(solution)/shard_map/ppermute | solution.py:45
  6.1 1.9 %collective-permute-start.3 = (f32[32,1280]{1,0:T(8,128)S(1)}, f32[32,1280]{1,0:T(8,128)S(1)}, u32[]{:S(2)}, u32[]{:S(2)}) collective-permute-start(f32[32,1280]{1,0:T(8,128)S(1)} %copy-done.2), channel_id=1, source_target_pairs={{0,8},{1,9},{2,10},{3,11},{4,12},{5,13},{6,14},{7,15},{8,0},{9,1},... | collective-permute-start | bytes 491528 | tf_op jit(solution)/shard_map/ppermute | solution.py:43
  8.1 1.5 %collective-permute-done = f32[32,1280]{1,0:T(8,128)S(1)} collective-permute-done((f32[32,1280]{1,0:T(8,128)S(1)}, f32[32,1280]{1,0:T(8,128)S(1)}, u32[]{:S(2)}, u32[]{:S(2)}) %collective-permute-start) | collective-permute-done | bytes 163872 | tf_op jit(solution)/shard_map/ppermute | solution.py:45
  9.6 2.4 %collective-permute-done.3 = f32[32,1280]{1,0:T(8,128)S(1)} collective-permute-done((f32[32,1280]{1,0:T(8,128)S(1)}, f32[32,1280]{1,0:T(8,128)S(1)}, u32[]{:S(2)}, u32[]{:S(2)}) %collective-permute-start.3) | collective-permute-done | bytes 163872 | tf_op jit(solution)/shard_map/ppermute | solution.py:43
  12.0 2.7 %collective-permute-done.4 = f32[32,1280]{1,0:T(8,128)S(1)} collective-permute-done((f32[32,1280]{1,0:T(8,128)S(1)}, f32[32,1280]{1,0:T(8,128)S(1)}, u32[]{:S(2)}, u32[]{:S(2)}) %collective-permute-start.4) | collective-permute-done | bytes 163872 | tf_op jit(solution)/shard_map/ppermute | solution.py:44
  14.6 0.9 %pad_maximum_fusion.1 = f32[128,1280]{1,0:T(8,128)} fusion(f32[32,1280]{1,0:T(8,128)S(1)} %collective-permute-done, f32[32,1280]{1,0:T(8,128)S(1)} %collective-permute-done.4, f32[32,1280]{1,0:T(8,128)S(1)} %collective-permute-done.3, f32[32,1280]{1,0:T(8,128)S(1)} %copy-done.2), kind=kLoop, calls=%fused_computation.16 | loop fusion | flops 491520 | bytes 1310720 | tf_op jit(solution)/shard_map/concatenate | solution.py:46
  16.2 1.7 %collective-permute-start.6 = (f32[32,1280]{1,0:T(8,128)S(1)}, f32[32,1280]{1,0:T(8,128)S(1)}, u32[]{:S(2)}, u32[]{:S(2)}) collective-permute-start(f32[32,1280]{1,0:T(8,128)S(1)} %collective-permute-done.3), channel_id=1, source_target_pairs={{0,2},{1,3},{2,4},{3,5},{4,6},{5,7},{6,0},{7,1},{8,10},{9,11},{10,... | collective-permute-start | bytes 491528 | tf_op jit(solution)/shard_map/ppermute | solution.py:50
  18.0 4.2 %collective-permute-done.1 = f32[32,1280]{1,0:T(8,128)S(1)} collective-permute-done((f32[32,1280]{1,0:T(8,128)S(1)}, f32[32,1280]{1,0:T(8,128)S(1)}, u32[]{:S(2)}, u32[]{:S(2)}) %collective-permute-start.1) | collective-permute-done | bytes 163872 | tf_op jit(solution)/shard_map/ppermute | solution.py:49
  22.3 1.3 %collective-permute-done.6 = f32[32,1280]{1,0:T(8,128)S(1)} collective-permute-done((f32[32,1280]{1,0:T(8,128)S(1)}, f32[32,1280]{1,0:T(8,128)S(1)}, u32[]{:S(2)}, u32[]{:S(2)}) %collective-permute-start.6) | collective-permute-done | bytes 163872 | tf_op jit(solution)/shard_map/ppermute | solution.py:50
  24.4 1.7 %collective-permute-start.2 = (f32[32,1280]{1,0:T(8,128)S(1)}, f32[32,1280]{1,0:T(8,128)}, u32[]{:S(2)}, u32[]{:S(2)}) collective-permute-start(f32[32,1280]{1,0:T(8,128)S(1)} %collective-permute-done.1), channel_id=1, source_target_pairs={{0,8},{1,9},{2,10},{3,11},{4,12},{5,13},{6,14},{7,15},{8,0},{9,1},... | collective-permute-start | bytes 491528 | tf_op jit(solution)/shard_map/ppermute | solution.py:53
  26.1 5.0 %collective-permute-done.2 = f32[32,1280]{1,0:T(8,128)} collective-permute-done((f32[32,1280]{1,0:T(8,128)S(1)}, f32[32,1280]{1,0:T(8,128)}, u32[]{:S(2)}, u32[]{:S(2)}) %collective-permute-start.2) | collective-permute-done | bytes 163872 | tf_op jit(solution)/shard_map/ppermute | solution.py:53
  31.1 0.9 %constant_dynamic-update-slice_fusion = f32[224,1280]{1,0:T(8,128)S(1)} fusion(f32[224,1280]{1,0:T(8,128)S(1)} %constant_dynamic-update-slice_fusion.1, f32[32,1280]{1,0:T(8,128)} %collective-permute-done.2), kind=kLoop, calls=%fused_computation.44 | loop fusion | bytes 327680 | tf_op jit(solution)/shard_map/concatenate | solution.py:54
  32.0 1.9 %fusion.2 = f32[224,640]{1,0:T(8,128)S(1)} fusion(f32[224,1280]{1,0:T(8,128)S(1)} %constant_dynamic-update-slice_fusion, f32[1280,640]{1,0:T(8,128)S(1)} %copy-done), kind=kOutput, calls=%fused_computation.2 | convolution fusion | flops 1101824000 | bytes 4997120 | tf_op jit(solution)/shard_map/dot_general | solution.py:33
  50.2 3.3 %fusion = f32[256,640]{1,0:T(8,128)S(1)} fusion(f32[1280,640]{1,0:T(8,128)S(1)} %copy-done, f32[32,1280]{1,0:T(8,128)S(1)} %collective-permute-done.9, f32[96,1280]{1,0:T(8,128)} %collective-permute-done.8, f32[128,1280]{1,0:T(8,128)} %collective-permute-done.7), kind=kOutput, calls=%fused_computation | convolution fusion | flops 1259765760 | bytes 5242880 | tf_op jit(solution)/shard_map/dot_general | solution.py:33
  53.7 2.8 %collective-permute-start.13 = (f32[64,640]{1,0:T(8,128)S(1)}, f32[64,640]{1,0:T(8,128)S(1)}, u32[]{:S(2)}, u32[]{:S(2)}) collective-permute-start(f32[64,640]{1,0:T(8,128)S(1)} %pad_maximum_fusion.4), channel_id=1, source_target_pairs={{0,48},{16,0},{32,16},{48,32},{64,112},{80,64},{96,80},{112,96},{1... | collective-permute-start | bytes 491528 | tf_op jit(solution)/shard_map/ppermute | solution.py:79
  56.7 4.0 %collective-permute-done.13 = f32[64,640]{1,0:T(8,128)S(1)} collective-permute-done((f32[64,640]{1,0:T(8,128)S(1)}, f32[64,640]{1,0:T(8,128)S(1)}, u32[]{:S(2)}, u32[]{:S(2)}) %collective-permute-start.13) | collective-permute-done | bytes 163872 | tf_op jit(solution)/shard_map/ppermute | solution.py:79
  60.7 3.8 %collective-permute-start.14 = (f32[64,640]{1,0:T(8,128)S(1)}, f32[64,640]{1,0:T(8,128)S(1)}, u32[]{:S(2)}, u32[]{:S(2)}) collective-permute-start(f32[64,640]{1,0:T(8,128)S(1)} %maximum_add_fusion.3), channel_id=1, source_target_pairs={{0,48},{16,0},{32,16},{48,32},{64,112},{80,64},{96,80},{112,96},{1... | collective-permute-start | bytes 491528 | tf_op jit(solution)/shard_map/ppermute | solution.py:79
  64.6 3.2 %collective-permute-done.14 = f32[64,640]{1,0:T(8,128)S(1)} collective-permute-done((f32[64,640]{1,0:T(8,128)S(1)}, f32[64,640]{1,0:T(8,128)S(1)}, u32[]{:S(2)}, u32[]{:S(2)}) %collective-permute-start.14) | collective-permute-done | bytes 163872 | tf_op jit(solution)/shard_map/ppermute | solution.py:79
  67.8 3.8 %collective-permute-start.15 = (f32[64,640]{1,0:T(8,128)S(1)}, f32[64,640]{1,0:T(8,128)S(1)}, u32[]{:S(2)}, u32[]{:S(2)}) collective-permute-start(f32[64,640]{1,0:T(8,128)S(1)} %maximum_add_fusion.4), channel_id=1, source_target_pairs={{0,48},{16,0},{32,16},{48,32},{64,112},{80,64},{96,80},{112,96},{1... | collective-permute-start | bytes 491528 | tf_op jit(solution)/shard_map/ppermute | solution.py:79
  71.7 2.7 %collective-permute-done.15 = f32[64,640]{1,0:T(8,128)S(1)} collective-permute-done((f32[64,640]{1,0:T(8,128)S(1)}, f32[64,640]{1,0:T(8,128)S(1)}, u32[]{:S(2)}, u32[]{:S(2)}) %collective-permute-start.15) | collective-permute-done | bytes 163872 | tf_op jit(solution)/shard_map/ppermute | solution.py:79
  74.4 3.8 %collective-permute-done.12 = f32[64,640]{1,0:T(8,128)S(1)} collective-permute-done((f32[64,640]{1,0:T(8,128)S(1)}, f32[64,640]{1,0:T(8,128)S(1)}, u32[]{:S(2)}, u32[]{:S(2)}) %collective-permute-start.12) | collective-permute-done | bytes 163872 | tf_op jit(solution)/shard_map/ppermute | solution.py:78
  78.2 3.7 %collective-permute-start.16 = (f32[64,640]{1,0:T(8,128)S(1)}, f32[64,640]{1,0:T(8,128)S(1)}, u32[]{:S(2)}, u32[]{:S(2)}) collective-permute-start(f32[64,640]{1,0:T(8,128)S(1)} %broadcast_select_fusion), channel_id=1, source_target_pairs={{0,64},{16,80},{32,96},{48,112},{64,0},{80,16},{96,32},{112,48},{1... | collective-permute-start | bytes 491528 | tf_op jit(solution)/shard_map/ppermute | solution.py:82
  81.9 3.3 %collective-permute-done.16 = f32[64,640]{1,0:T(8,128)S(1)} collective-permute-done((f32[64,640]{1,0:T(8,128)S(1)}, f32[64,640]{1,0:T(8,128)S(1)}, u32[]{:S(2)}, u32[]{:S(2)}) %collective-permute-start.16) | collective-permute-done | bytes 163872 | tf_op jit(solution)/shard_map/ppermute | solution.py:82
  (41 shorter events, 4.4 us)
Async XLA Ops:
  0.0 2.9 %copy-start.2 = (f32[32,1280]{1,0:T(8,128)S(1)}, f32[32,1280]{1,0:T(8,128)}, u32[]{:S(2)}) copy-start(f32[32,1280]{1,0:T(8,128)} %param.3) | copy-start | bytes 491524
  2.9 6.7 %collective-permute-start = (f32[32,1280]{1,0:T(8,128)S(1)}, f32[32,1280]{1,0:T(8,128)S(1)}, u32[]{:S(2)}, u32[]{:S(2)}) collective-permute-start(f32[32,1280]{1,0:T(8,128)S(1)} %copy-done.2), channel_id=1, source_target_pairs={{0,6},{1,7},{2,0},{3,1},{4,2},{5,3},{6,4},{7,5},{8,14},{9,15},{10,... | collective-permute-start | bytes 491528 | tf_op jit(solution)/shard_map/ppermute | solution.py:45
  6.1 5.8 %collective-permute-start.3 = (f32[32,1280]{1,0:T(8,128)S(1)}, f32[32,1280]{1,0:T(8,128)S(1)}, u32[]{:S(2)}, u32[]{:S(2)}) collective-permute-start(f32[32,1280]{1,0:T(8,128)S(1)} %copy-done.2), channel_id=1, source_target_pairs={{0,8},{1,9},{2,10},{3,11},{4,12},{5,13},{6,14},{7,15},{8,0},{9,1},... | collective-permute-start | bytes 491528 | tf_op jit(solution)/shard_map/ppermute | solution.py:43
  8.1 6.6 %collective-permute-start.4 = (f32[32,1280]{1,0:T(8,128)S(1)}, f32[32,1280]{1,0:T(8,128)S(1)}, u32[]{:S(2)}, u32[]{:S(2)}) collective-permute-start(f32[32,1280]{1,0:T(8,128)S(1)} %copy-done.2), channel_id=1, source_target_pairs={{0,2},{1,3},{2,4},{3,5},{4,6},{5,7},{6,0},{7,1},{8,10},{9,11},{10,... | collective-permute-start | bytes 491528 | tf_op jit(solution)/shard_map/ppermute | solution.py:44
  14.6 17.4 %copy-start = (f32[1280,640]{1,0:T(8,128)S(1)}, f32[1280,640]{1,0:T(8,128)}, u32[]{:S(2)}) copy-start(f32[1280,640]{1,0:T(8,128)} %param.4) | copy-start | bytes 9830404
  15.6 34.7 %collective-permute-start.7 = (f32[128,1280]{1,0:T(8,128)}, f32[128,1280]{1,0:T(8,128)}, u32[]{:S(2)}, u32[]{:S(2)}) collective-permute-start(f32[128,1280]{1,0:T(8,128)} %pad_maximum_fusion.1), channel_id=1, source_target_pairs={{0,1},{1,0},{2,3},{3,2},{4,5},{5,4},{6,7},{7,6},{8,9},{9,8},{10,11... | collective-permute-start | bytes 1966088 | tf_op jit(solution)/shard_map/ppermute | solution.py:47
  15.6 6.6 %collective-permute-start.1 = (f32[32,1280]{1,0:T(8,128)S(1)}, f32[32,1280]{1,0:T(8,128)S(1)}, u32[]{:S(2)}, u32[]{:S(2)}) collective-permute-start(f32[32,1280]{1,0:T(8,128)S(1)} %collective-permute-done), channel_id=1, source_target_pairs={{0,6},{1,7},{2,0},{3,1},{4,2},{5,3},{6,4},{7,5},{8,14},{9,15},{10,... | collective-permute-start | bytes 491528 | tf_op jit(solution)/shard_map/ppermute | solution.py:49
  15.6 6.7 %collective-permute-start.5 = (f32[32,1280]{1,0:T(8,128)S(1)}, f32[32,1280]{1,0:T(8,128)S(1)}, u32[]{:S(2)}, u32[]{:S(2)}) collective-permute-start(f32[32,1280]{1,0:T(8,128)S(1)} %collective-permute-done), channel_id=1, source_target_pairs={{0,8},{1,9},{2,10},{3,11},{4,12},{5,13},{6,14},{7,15},{8,0},{9,1},... | collective-permute-start | bytes 491528 | tf_op jit(solution)/shard_map/ppermute | solution.py:48
  16.2 7.3 %collective-permute-start.6 = (f32[32,1280]{1,0:T(8,128)S(1)}, f32[32,1280]{1,0:T(8,128)S(1)}, u32[]{:S(2)}, u32[]{:S(2)}) collective-permute-start(f32[32,1280]{1,0:T(8,128)S(1)} %collective-permute-done.3), channel_id=1, source_target_pairs={{0,2},{1,3},{2,4},{3,5},{4,6},{5,7},{6,0},{7,1},{8,10},{9,11},{10,... | collective-permute-start | bytes 491528 | tf_op jit(solution)/shard_map/ppermute | solution.py:50
  24.4 25.8 %collective-permute-start.8 = (f32[96,1280]{1,0:T(8,128)}, f32[96,1280]{1,0:T(8,128)}, u32[]{:S(2)}, u32[]{:S(2)}) collective-permute-start(f32[96,1280]{1,0:T(8,128)} %pad_maximum_fusion.2), channel_id=1, source_target_pairs={{0,1},{1,0},{2,3},{3,2},{4,5},{5,4},{6,7},{7,6},{8,9},{9,8},{10,11... | collective-permute-start | bytes 1474568 | tf_op jit(solution)/shard_map/ppermute | solution.py:52
  24.4 6.7 %collective-permute-start.2 = (f32[32,1280]{1,0:T(8,128)S(1)}, f32[32,1280]{1,0:T(8,128)}, u32[]{:S(2)}, u32[]{:S(2)}) collective-permute-start(f32[32,1280]{1,0:T(8,128)S(1)} %collective-permute-done.1), channel_id=1, source_target_pairs={{0,8},{1,9},{2,10},{3,11},{4,12},{5,13},{6,14},{7,15},{8,0},{9,1},... | collective-permute-start | bytes 491528 | tf_op jit(solution)/shard_map/ppermute | solution.py:53
  33.9 0.9 %copy-start.3 = (s32[8]{0:T(128)S(1)}, s32[8]{0:T(128)}, u32[]{:S(2)}) copy-start(s32[8]{0:T(128)} %constant.274.clone) | copy-start | bytes 100
  34.8 15.4 %collective-permute-start.9 = (f32[32,1280]{1,0:T(8,128)}, f32[32,1280]{1,0:T(8,128)S(1)}, u32[]{:S(2)}, u32[]{:S(2)}) collective-permute-start(f32[32,1280]{1,0:T(8,128)} %collective-permute-done.2), channel_id=1, source_target_pairs={{0,1},{1,0},{2,3},{3,2},{4,5},{5,4},{6,7},{7,6},{8,9},{9,8},{10,11... | collective-permute-start | bytes 491528 | tf_op jit(solution)/shard_map/ppermute | solution.py:58
  50.2 3.4 %copy-start.1 = (f32[256,640]{1,0:T(8,128)S(1)}, f32[256,640]{1,0:T(8,128)}, u32[]{:S(2)}) copy-start(f32[256,640]{1,0:T(8,128)} %pad_maximum_fusion) | copy-start | bytes 1966084
  53.7 7.0 %collective-permute-start.13 = (f32[64,640]{1,0:T(8,128)S(1)}, f32[64,640]{1,0:T(8,128)S(1)}, u32[]{:S(2)}, u32[]{:S(2)}) collective-permute-start(f32[64,640]{1,0:T(8,128)S(1)} %pad_maximum_fusion.4), channel_id=1, source_target_pairs={{0,48},{16,0},{32,16},{48,32},{64,112},{80,64},{96,80},{112,96},{1... | collective-permute-start | bytes 491528 | tf_op jit(solution)/shard_map/ppermute | solution.py:79
  56.6 7.9 %collective-permute-start.10 = (f32[64,640]{1,0:T(8,128)S(1)}, f32[64,640]{1,0:T(8,128)S(1)}, u32[]{:S(2)}, u32[]{:S(2)}) collective-permute-start(f32[64,640]{1,0:T(8,128)S(1)} %pad_maximum_fusion.3), channel_id=1, source_target_pairs={{0,16},{16,32},{32,48},{48,0},{64,80},{80,96},{96,112},{112,64},{1... | collective-permute-start | bytes 491528 | tf_op jit(solution)/shard_map/ppermute | solution.py:78
  60.7 7.0 %collective-permute-start.14 = (f32[64,640]{1,0:T(8,128)S(1)}, f32[64,640]{1,0:T(8,128)S(1)}, u32[]{:S(2)}, u32[]{:S(2)}) collective-permute-start(f32[64,640]{1,0:T(8,128)S(1)} %maximum_add_fusion.3), channel_id=1, source_target_pairs={{0,48},{16,0},{32,16},{48,32},{64,112},{80,64},{96,80},{112,96},{1... | collective-permute-start | bytes 491528 | tf_op jit(solution)/shard_map/ppermute | solution.py:79
  64.5 7.0 %collective-permute-start.11 = (f32[64,640]{1,0:T(8,128)S(1)}, f32[64,640]{1,0:T(8,128)S(1)}, u32[]{:S(2)}, u32[]{:S(2)}) collective-permute-start(f32[64,640]{1,0:T(8,128)S(1)} %maximum_add_fusion), channel_id=1, source_target_pairs={{0,16},{16,32},{32,48},{48,0},{64,80},{80,96},{96,112},{112,64},{1... | collective-permute-start | bytes 491528 | tf_op jit(solution)/shard_map/ppermute | solution.py:78
  67.8 6.6 %collective-permute-start.15 = (f32[64,640]{1,0:T(8,128)S(1)}, f32[64,640]{1,0:T(8,128)S(1)}, u32[]{:S(2)}, u32[]{:S(2)}) collective-permute-start(f32[64,640]{1,0:T(8,128)S(1)} %maximum_add_fusion.4), channel_id=1, source_target_pairs={{0,48},{16,0},{32,16},{48,32},{64,112},{80,64},{96,80},{112,96},{1... | collective-permute-start | bytes 491528 | tf_op jit(solution)/shard_map/ppermute | solution.py:79
  71.6 6.6 %collective-permute-start.12 = (f32[64,640]{1,0:T(8,128)S(1)}, f32[64,640]{1,0:T(8,128)S(1)}, u32[]{:S(2)}, u32[]{:S(2)}) collective-permute-start(f32[64,640]{1,0:T(8,128)S(1)} %maximum_add_fusion.1), channel_id=1, source_target_pairs={{0,16},{16,32},{32,48},{48,0},{64,80},{80,96},{96,112},{112,64},{1... | collective-permute-start | bytes 491528 | tf_op jit(solution)/shard_map/ppermute | solution.py:78
  78.2 7.0 %collective-permute-start.16 = (f32[64,640]{1,0:T(8,128)S(1)}, f32[64,640]{1,0:T(8,128)S(1)}, u32[]{:S(2)}, u32[]{:S(2)}) collective-permute-start(f32[64,640]{1,0:T(8,128)S(1)} %broadcast_select_fusion), channel_id=1, source_target_pairs={{0,64},{16,80},{32,96},{48,112},{64,0},{80,16},{96,32},{112,48},{1... | collective-permute-start | bytes 491528 | tf_op jit(solution)/shard_map/ppermute | solution.py:82

commit v7 on v5

--- a/solution.py
+++ b/solution.py
@@ -27,7 +27,7 @@
     z_swap = _pairs(n_vir, lambda j: j ^ (2 * ny))
     core_swap = _pairs(n_vir, lambda j: j ^ 1)
     zhi_swap = _pairs(n_occ, lambda i: (i + nx) % n_occ)
-    slot_of = [0, 1, 3, 4, 5, 7, 2, 6]
+    slot_of = [0, 1, 4, 5, 6, 7, 2, 3]
 
     def matmul(a, b):
         return jnp.dot(a, b, preferred_element_type=jnp.float32, precision=HIGH)
@@ -41,13 +41,12 @@
         res_own = matmul(amplitudes, half)
         own, res_own = lax.optimization_barrier((amplitudes, res_own))
         z1 = lax.ppermute(own, "vir", z_swap)
-        ym1 = lax.ppermute(own, "vir", y_shift(1))
-        yp1 = lax.ppermute(own, "vir", y_shift(-1))
-        z2 = lax.ppermute(yp1, "vir", z_swap)
-        yp2 = lax.ppermute(yp1, "vir", y_shift(-1))
-        ym1z = lax.ppermute(z1, "vir", y_shift(1))
-        z3 = lax.ppermute(yp2, "vir", z_swap)
-        local = jnp.concatenate([own, z1, ym1, yp1, z2, yp2, ym1z, z3], axis=0)
+        pair = jnp.concatenate([own, z1], axis=0)
+        from_m = lax.ppermute(pair, "vir", y_shift(1))
+        from_p = lax.ppermute(pair, "vir", y_shift(-1))
+        far_m = lax.ppermute(from_m[:rows], "vir", y_shift(1))
+        far_p = lax.ppermute(from_p[rows:], "vir", y_shift(-1))
+        local = jnp.concatenate([own, z1, from_m, from_p, far_m, far_p], axis=0)
         res_l = jnp.concatenate([res_own, matmul(local[rows:], half)], axis=0)
         local, res_l = lax.optimization_barrier((local, res_l))
         res_l = res_l.reshape(8, rows, -1)

time: 79.4 us -> 82.6 us (1.040)
  waiting for transfers between devices: 24.1 us -> 31 us
  starting transfers between devices: 23.5 us -> 20.3 us
  local copies, waits for them, and re-layouts: 6.2 us -> 5.06 us
    ppermute x1, waiting for transfers between devices: 0.01 us -> 3.51 us  [body(): z1 = lax.ppermute(own, 'vir', z_swap)]
    ppermute x6 -> x4, waiting for transfers between devices: 7.07 us -> 10.5 us  [the longest x1 6.74 us: body(): from_m = lax.ppermute(pair, 'vir', y_shift(1))]
    ppermute x6 -> x4, starting transfers between devices: 7.29 us -> 4.19 us  [the longest x1 1.8 us: body(): from_p = lax.ppermute(pair, 'vir', y_shift(-1))]
    unnamed x15 -> x13, local copies, waits for them, and re-layouts: 4.81 us -> 3.68 us
  transfers between devices with their start and end apart: 15 -> 13, of which waited for: 8 -> 9; matrix products, arithmetic and copies ran while one was open for 7% -> 5% of each run, Pallas kernels for 0% -> 0%
where the time goes in v7:
time: 82.6 us; the launch traced here: 81.7 us
  waiting for transfers between devices  31 us (38%)
  starting transfers between devices  20.3 us (25%)
  between operations  15.2 us (18%)
  matrix products  8.22 us (10%)
  local copies, waits for them, and re-layouts  5.06 us (6%)
  other arithmetic  1.89 us (2%)
    ppermute x3, starting transfers between devices, body(): sb = lax.ppermute(sb, 'occ', x_shift(-1)) + out_block(nx + (x + s + 1) % nx)  10.3 us
    ppermute x3, waiting for transfers between devices, body(): sb = lax.ppermute(sb, 'occ', x_shift(-1)) + out_block(nx + (x + s + 1) % nx)  9.9 us
    dot_general x3, matrix products, matmul(): return jnp.dot(a, b, preferred_element_type=jnp.float32, precision=HIGH)  8.22 us
    ppermute x1, waiting for transfers between devices, body(): from_m = lax.ppermute(pair, 'vir', y_shift(1))  6.74 us
    ppermute x3, waiting for transfers between devices, body(): sa = lax.ppermute(sa, 'occ', x_shift(1)) + out_block((x - s - 1) % nx)  3.79 us
    unnamed x13, local copies, waits for them, and re-layouts  3.68 us
    ppermute x1, starting transfers between devices, body(): return keep + lax.ppermute(send, 'occ', zhi_swap)  3.6 us
    ppermute x1, waiting for transfers between devices, body(): z1 = lax.ppermute(own, 'vir', z_swap)  3.51 us
  transfers between devices with their start and end apart: 13, of which 9 were waited for; matrix products, arithmetic and copies ran while one was open for 5% of the time, Pallas kernels for 0%

profile of v7, /device:TPU:24, one launch (start us, length us, event | category | flops | bytes accessed | tf_op | source)
XLA Modules:
  0.0 81.7 jit_solution(12877872282692124607)
XLA Ops:
  0.0 2.9 %fusion.9 = f32[32,640]{1,0:T(8,128)S(1)} fusion(f32[32,1280]{1,0:T(8,128)} %param.3, f32[1280,640]{1,0:T(8,128)} %param.4), kind=kOutput, calls=%fused_computation.9 | convolution fusion | flops 158105600 | bytes 3522560 | tf_op jit(solution)/shard_map/dot_general | solution.py:33
  2.9 2.0 %collective-permute-start = (f32[32,1280]{1,0:T(8,128)S(1)}, f32[32,1280]{1,0:T(8,128)S(1)}, u32[]{:S(2)}, u32[]{:S(2)}) collective-permute-start(f32[32,1280]{1,0:T(8,128)S(1)} %copy-done.2), channel_id=1, source_target_pairs={{0,8},{1,9},{2,10},{3,11},{4,12},{5,13},{6,14},{7,15},{8,0},{9,1},... | collective-permute-start | bytes 491528 | tf_op jit(solution)/shard_map/ppermute | solution.py:43
  5.6 3.5 %collective-permute-done = f32[32,1280]{1,0:T(8,128)S(1)} collective-permute-done((f32[32,1280]{1,0:T(8,128)S(1)}, f32[32,1280]{1,0:T(8,128)S(1)}, u32[]{:S(2)}, u32[]{:S(2)}) %collective-permute-start) | collective-permute-done | bytes 163872 | tf_op jit(solution)/shard_map/ppermute | solution.py:43
  9.1 0.7 constant_dynamic-update-slice_fusion.12
  10.1 1.8 %collective-permute-start.2 = (f32[64,1280]{1,0:T(8,128)S(1)}, f32[64,1280]{1,0:T(8,128)S(1)}, u32[]{:S(2)}, u32[]{:S(2)}) collective-permute-start(f32[64,1280]{1,0:T(8,128)S(1)} %get-tuple-element.39), channel_id=1, source_target_pairs={{0,6},{1,7},{2,0},{3,1},{4,2},{5,3},{6,4},{7,5},{8,14},{9,15},{10,... | collective-permute-start | bytes 983048 | tf_op jit(solution)/shard_map/ppermute | solution.py:46
  11.9 6.7 %collective-permute-done.1 = f32[64,1280]{1,0:T(8,128)S(1)} collective-permute-done((f32[64,1280]{1,0:T(8,128)S(1)}, f32[64,1280]{1,0:T(8,128)S(1)}, u32[]{:S(2)}, u32[]{:S(2)}) %collective-permute-start.1) | collective-permute-done | bytes 327712 | tf_op jit(solution)/shard_map/ppermute | solution.py:45
  18.6 1.6 %collective-permute-start.3 = (f32[32,1280]{1,0:T(8,128)S(1)}, f32[32,1280]{1,0:T(8,128)S(1)}, u32[]{:S(2)}, u32[]{:S(2)}) collective-permute-start(f32[32,1280]{1,0:T(8,128)S(1)} %slice.10), channel_id=1, source_target_pairs={{0,2},{1,3},{2,4},{3,5},{4,6},{5,7},{6,0},{7,1},{8,10},{9,11},{10,... | collective-permute-start | bytes 491528 | tf_op jit(solution)/shard_map/ppermute | solution.py:47
  20.8 0.8 constant_dynamic-update-slice_fusion.11
  21.6 0.8 constant_dynamic-update-slice_fusion.10
  22.4 1.6 %collective-permute-done.3 = f32[32,1280]{1,0:T(8,128)S(1)} collective-permute-done((f32[32,1280]{1,0:T(8,128)S(1)}, f32[32,1280]{1,0:T(8,128)S(1)}, u32[]{:S(2)}, u32[]{:S(2)}) %collective-permute-start.3) | collective-permute-done | bytes 163872 | tf_op jit(solution)/shard_map/ppermute | solution.py:47
  24.7 2.1 %collective-permute-done.4 = f32[32,1280]{1,0:T(8,128)S(1)} collective-permute-done((f32[32,1280]{1,0:T(8,128)S(1)}, f32[32,1280]{1,0:T(8,128)S(1)}, u32[]{:S(2)}, u32[]{:S(2)}) %collective-permute-start.4) | collective-permute-done | bytes 163872 | tf_op jit(solution)/shard_map/ppermute | solution.py:48
  27.5 1.9 %fusion.2 = f32[224,640]{1,0:T(8,128)S(1)} fusion(f32[224,1280]{1,0:T(8,128)S(1)} %get-tuple-element.33, f32[1280,640]{1,0:T(8,128)S(1)} %copy-done), kind=kOutput, calls=%fused_computation.2 | convolution fusion | flops 1101824000 | bytes 4997120 | tf_op jit(solution)/shard_map/dot_general | solution.py:33
  29.4 0.9 %pad_maximum_fusion = f32[256,640]{1,0:T(8,128)} fusion(f32[224,640]{1,0:T(8,128)S(1)} %fusion.2, f32[32,640]{1,0:T(8,128)S(1)} %fusion.9), kind=kLoop, calls=%fused_computation.10 | loop fusion | flops 163840 | bytes 1310720 | tf_op jit(solution)/shard_map/concatenate | solution.py:50
  46.1 3.4 %fusion = f32[256,640]{1,0:T(8,128)S(1)} fusion(f32[256,1280]{1,0:T(8,128)} %collective-permute-done.5, f32[1280,640]{1,0:T(8,128)S(1)} %copy-done), kind=kOutput, calls=%fused_computation | convolution fusion | flops 1259110400 | bytes 5242880 | tf_op jit(solution)/shard_map/dot_general | solution.py:33
  49.7 2.8 %collective-permute-start.9 = (f32[64,640]{1,0:T(8,128)S(1)}, f32[64,640]{1,0:T(8,128)S(1)}, u32[]{:S(2)}, u32[]{:S(2)}) collective-permute-start(f32[64,640]{1,0:T(8,128)S(1)} %pad_maximum_fusion.2), channel_id=1, source_target_pairs={{0,48},{16,0},{32,16},{48,32},{64,112},{80,64},{96,80},{112,96},{1... | collective-permute-start | bytes 491528 | tf_op jit(solution)/shard_map/ppermute | solution.py:73
  52.5 4.0 %collective-permute-done.9 = f32[64,640]{1,0:T(8,128)S(1)} collective-permute-done((f32[64,640]{1,0:T(8,128)S(1)}, f32[64,640]{1,0:T(8,128)S(1)}, u32[]{:S(2)}, u32[]{:S(2)}) %collective-permute-start.9) | collective-permute-done | bytes 163872 | tf_op jit(solution)/shard_map/ppermute | solution.py:73
  56.6 3.8 %collective-permute-start.10 = (f32[64,640]{1,0:T(8,128)S(1)}, f32[64,640]{1,0:T(8,128)S(1)}, u32[]{:S(2)}, u32[]{:S(2)}) collective-permute-start(f32[64,640]{1,0:T(8,128)S(1)} %maximum_add_fusion.3), channel_id=1, source_target_pairs={{0,48},{16,0},{32,16},{48,32},{64,112},{80,64},{96,80},{112,96},{1... | collective-permute-start | bytes 491528 | tf_op jit(solution)/shard_map/ppermute | solution.py:73
  60.5 3.2 %collective-permute-done.10 = f32[64,640]{1,0:T(8,128)S(1)} collective-permute-done((f32[64,640]{1,0:T(8,128)S(1)}, f32[64,640]{1,0:T(8,128)S(1)}, u32[]{:S(2)}, u32[]{:S(2)}) %collective-permute-start.10) | collective-permute-done | bytes 163872 | tf_op jit(solution)/shard_map/ppermute | solution.py:73
  63.7 3.8 %collective-permute-start.11 = (f32[64,640]{1,0:T(8,128)S(1)}, f32[64,640]{1,0:T(8,128)S(1)}, u32[]{:S(2)}, u32[]{:S(2)}) collective-permute-start(f32[64,640]{1,0:T(8,128)S(1)} %maximum_add_fusion.4), channel_id=1, source_target_pairs={{0,48},{16,0},{32,16},{48,32},{64,112},{80,64},{96,80},{112,96},{1... | collective-permute-start | bytes 491528 | tf_op jit(solution)/shard_map/ppermute | solution.py:73
  67.6 2.7 %collective-permute-done.11 = f32[64,640]{1,0:T(8,128)S(1)} collective-permute-done((f32[64,640]{1,0:T(8,128)S(1)}, f32[64,640]{1,0:T(8,128)S(1)}, u32[]{:S(2)}, u32[]{:S(2)}) %collective-permute-start.11) | collective-permute-done | bytes 163872 | tf_op jit(solution)/shard_map/ppermute | solution.py:73
  70.3 3.8 %collective-permute-done.8 = f32[64,640]{1,0:T(8,128)S(1)} collective-permute-done((f32[64,640]{1,0:T(8,128)S(1)}, f32[64,640]{1,0:T(8,128)S(1)}, u32[]{:S(2)}, u32[]{:S(2)}) %collective-permute-start.8) | collective-permute-done | bytes 163872 | tf_op jit(solution)/shard_map/ppermute | solution.py:72
  74.1 3.6 %collective-permute-start.12 = (f32[64,640]{1,0:T(8,128)S(1)}, f32[64,640]{1,0:T(8,128)S(1)}, u32[]{:S(2)}, u32[]{:S(2)}) collective-permute-start(f32[64,640]{1,0:T(8,128)S(1)} %broadcast_select_fusion), channel_id=1, source_target_pairs={{0,64},{16,80},{32,96},{48,112},{64,0},{80,16},{96,32},{112,48},{1... | collective-permute-start | bytes 491528 | tf_op jit(solution)/shard_map/ppermute | solution.py:76
  77.7 3.3 %collective-permute-done.12 = f32[64,640]{1,0:T(8,128)S(1)} collective-permute-done((f32[64,640]{1,0:T(8,128)S(1)}, f32[64,640]{1,0:T(8,128)S(1)}, u32[]{:S(2)}, u32[]{:S(2)}) %collective-permute-start.12) | collective-permute-done | bytes 163872 | tf_op jit(solution)/shard_map/ppermute | solution.py:76
  81.0 0.7 select_add_fusion
  (32 shorter events, 4.1 us)
Async XLA Ops:
  0.0 2.9 %copy-start.2 = (f32[32,1280]{1,0:T(8,128)S(1)}, f32[32,1280]{1,0:T(8,128)}, u32[]{:S(2)}) copy-start(f32[32,1280]{1,0:T(8,128)} %param.3) | copy-start | bytes 491524
  2.9 6.2 %collective-permute-start = (f32[32,1280]{1,0:T(8,128)S(1)}, f32[32,1280]{1,0:T(8,128)S(1)}, u32[]{:S(2)}, u32[]{:S(2)}) collective-permute-start(f32[32,1280]{1,0:T(8,128)S(1)} %copy-done.2), channel_id=1, source_target_pairs={{0,8},{1,9},{2,10},{3,11},{4,12},{5,13},{6,14},{7,15},{8,0},{9,1},... | collective-permute-start | bytes 491528 | tf_op jit(solution)/shard_map/ppermute | solution.py:43
  9.8 8.8 %collective-permute-start.1 = (f32[64,1280]{1,0:T(8,128)S(1)}, f32[64,1280]{1,0:T(8,128)S(1)}, u32[]{:S(2)}, u32[]{:S(2)}) collective-permute-start(f32[64,1280]{1,0:T(8,128)S(1)} %get-tuple-element.39), channel_id=1, source_target_pairs={{0,2},{1,3},{2,4},{3,5},{4,6},{5,7},{6,0},{7,1},{8,10},{9,11},{10,... | collective-permute-start | bytes 983048 | tf_op jit(solution)/shard_map/ppermute | solution.py:45
  10.1 10.2 %collective-permute-start.2 = (f32[64,1280]{1,0:T(8,128)S(1)}, f32[64,1280]{1,0:T(8,128)S(1)}, u32[]{:S(2)}, u32[]{:S(2)}) collective-permute-start(f32[64,1280]{1,0:T(8,128)S(1)} %get-tuple-element.39), channel_id=1, source_target_pairs={{0,6},{1,7},{2,0},{3,1},{4,2},{5,3},{6,4},{7,5},{8,14},{9,15},{10,... | collective-permute-start | bytes 983048 | tf_op jit(solution)/shard_map/ppermute | solution.py:46
  18.6 5.4 %collective-permute-start.3 = (f32[32,1280]{1,0:T(8,128)S(1)}, f32[32,1280]{1,0:T(8,128)S(1)}, u32[]{:S(2)}, u32[]{:S(2)}) collective-permute-start(f32[32,1280]{1,0:T(8,128)S(1)} %slice.10), channel_id=1, source_target_pairs={{0,2},{1,3},{2,4},{3,5},{4,6},{5,7},{6,0},{7,1},{8,10},{9,11},{10,... | collective-permute-start | bytes 491528 | tf_op jit(solution)/shard_map/ppermute | solution.py:47
  20.2 7.3 %copy-start = (f32[1280,640]{1,0:T(8,128)S(1)}, f32[1280,640]{1,0:T(8,128)}, u32[]{:S(2)}) copy-start(f32[1280,640]{1,0:T(8,128)} %param.4) | copy-start | bytes 9830404
  20.3 6.6 %collective-permute-start.4 = (f32[32,1280]{1,0:T(8,128)S(1)}, f32[32,1280]{1,0:T(8,128)S(1)}, u32[]{:S(2)}, u32[]{:S(2)}) collective-permute-start(f32[32,1280]{1,0:T(8,128)S(1)} %slice.11), channel_id=1, source_target_pairs={{0,6},{1,7},{2,0},{3,1},{4,2},{5,3},{6,4},{7,5},{8,14},{9,15},{10,... | collective-permute-start | bytes 491528 | tf_op jit(solution)/shard_map/ppermute | solution.py:48
  29.4 0.9 %copy-start.3 = (s32[8]{0:T(128)S(1)}, s32[8]{0:T(128)}, u32[]{:S(2)}) copy-start(s32[8]{0:T(128)} %constant.274.clone) | copy-start | bytes 100
  30.3 15.7 %collective-permute-start.5 = (f32[256,1280]{1,0:T(8,128)}, f32[256,1280]{1,0:T(8,128)}, u32[]{:S(2)}, u32[]{:S(2)}) collective-permute-start(f32[256,1280]{1,0:T(8,128)} %get-tuple-element.12), channel_id=1, source_target_pairs={{0,1},{1,0},{2,3},{3,2},{4,5},{5,4},{6,7},{7,6},{8,9},{9,8},{10,11... | collective-permute-start | bytes 3932168 | tf_op jit(solution)/shard_map/ppermute | solution.py:53
  46.1 3.4 %copy-start.1 = (f32[256,640]{1,0:T(8,128)S(1)}, f32[256,640]{1,0:T(8,128)}, u32[]{:S(2)}) copy-start(f32[256,640]{1,0:T(8,128)} %pad_maximum_fusion) | copy-start | bytes 1966084
  49.7 6.9 %collective-permute-start.9 = (f32[64,640]{1,0:T(8,128)S(1)}, f32[64,640]{1,0:T(8,128)S(1)}, u32[]{:S(2)}, u32[]{:S(2)}) collective-permute-start(f32[64,640]{1,0:T(8,128)S(1)} %pad_maximum_fusion.2), channel_id=1, source_target_pairs={{0,48},{16,0},{32,16},{48,32},{64,112},{80,64},{96,80},{112,96},{1... | collective-permute-start | bytes 491528 | tf_op jit(solution)/shard_map/ppermute | solution.py:73
  52.5 7.9 %collective-permute-start.6 = (f32[64,640]{1,0:T(8,128)S(1)}, f32[64,640]{1,0:T(8,128)S(1)}, u32[]{:S(2)}, u32[]{:S(2)}) collective-permute-start(f32[64,640]{1,0:T(8,128)S(1)} %pad_maximum_fusion.1), channel_id=1, source_target_pairs={{0,16},{16,32},{32,48},{48,0},{64,80},{80,96},{96,112},{112,64},{1... | collective-permute-start | bytes 491528 | tf_op jit(solution)/shard_map/ppermute | solution.py:72
  56.6 7.0 %collective-permute-start.10 = (f32[64,640]{1,0:T(8,128)S(1)}, f32[64,640]{1,0:T(8,128)S(1)}, u32[]{:S(2)}, u32[]{:S(2)}) collective-permute-start(f32[64,640]{1,0:T(8,128)S(1)} %maximum_add_fusion.3), channel_id=1, source_target_pairs={{0,48},{16,0},{32,16},{48,32},{64,112},{80,64},{96,80},{112,96},{1... | collective-permute-start | bytes 491528 | tf_op jit(solution)/shard_map/ppermute | solution.py:73
  60.4 7.0 %collective-permute-start.7 = (f32[64,640]{1,0:T(8,128)S(1)}, f32[64,640]{1,0:T(8,128)S(1)}, u32[]{:S(2)}, u32[]{:S(2)}) collective-permute-start(f32[64,640]{1,0:T(8,128)S(1)} %maximum_add_fusion), channel_id=1, source_target_pairs={{0,16},{16,32},{32,48},{48,0},{64,80},{80,96},{96,112},{112,64},{1... | collective-permute-start | bytes 491528 | tf_op jit(solution)/shard_map/ppermute | solution.py:72
  63.7 6.6 %collective-permute-start.11 = (f32[64,640]{1,0:T(8,128)S(1)}, f32[64,640]{1,0:T(8,128)S(1)}, u32[]{:S(2)}, u32[]{:S(2)}) collective-permute-start(f32[64,640]{1,0:T(8,128)S(1)} %maximum_add_fusion.4), channel_id=1, source_target_pairs={{0,48},{16,0},{32,16},{48,32},{64,112},{80,64},{96,80},{112,96},{1... | collective-permute-start | bytes 491528 | tf_op jit(solution)/shard_map/ppermute | solution.py:73
  67.5 6.6 %collective-permute-start.8 = (f32[64,640]{1,0:T(8,128)S(1)}, f32[64,640]{1,0:T(8,128)S(1)}, u32[]{:S(2)}, u32[]{:S(2)}) collective-permute-start(f32[64,640]{1,0:T(8,128)S(1)} %maximum_add_fusion.1), channel_id=1, source_target_pairs={{0,16},{16,32},{32,48},{48,0},{64,80},{80,96},{96,112},{112,64},{1... | collective-permute-start | bytes 491528 | tf_op jit(solution)/shard_map/ppermute | solution.py:72
  74.1 6.9 %collective-permute-start.12 = (f32[64,640]{1,0:T(8,128)S(1)}, f32[64,640]{1,0:T(8,128)S(1)}, u32[]{:S(2)}, u32[]{:S(2)}) collective-permute-start(f32[64,640]{1,0:T(8,128)S(1)} %broadcast_select_fusion), channel_id=1, source_target_pairs={{0,64},{16,80},{32,96},{48,112},{64,0},{80,16},{96,32},{112,48},{1... | collective-permute-start | bytes 491528 | tf_op jit(solution)/shard_map/ppermute | solution.py:76

commit v8 on v5

--- a/solution.py
+++ b/solution.py
@@ -52,29 +52,22 @@
         local, res_l = lax.optimization_barrier((local, res_l))
         res_l = res_l.reshape(8, rows, -1)
         other = lax.ppermute(local, "vir", core_swap)
-        res_o = matmul(other, half).reshape(8, rows, -1)
         table = jnp.array(slot_of, jnp.int32)
 
-        def out_block(r):
-            dy = (r % nx - y) % ny
-            dz = (r // nx) ^ zl
-            k = table[dy * 2 + dz]
-            lk = lax.dynamic_index_in_dim(res_l, k, 0, keepdims=False)
-            ok = lax.dynamic_index_in_dim(res_o, k, 0, keepdims=False)
-            first = jnp.where(c == 0, lk, ok)
-            second = jnp.where(c == 0, ok, lk)
-            return jnp.concatenate([first, second], axis=0)
+        dest = jnp.arange(n_occ, dtype=jnp.int32)
+        slots = table[((dest % nx - y) % ny) * 2 + ((dest // nx) ^ zl)]
 
-        mo = lax.axis_index("occ")
-        x, zh = mo % nx, mo // nx
-        sa = out_block((x - 1) % nx)
-        sb = out_block(nx + (x + 1) % nx)
-        for s in range(1, nx):
-            sa = lax.ppermute(sa, "occ", x_shift(1)) + out_block((x - s - 1) % nx)
-            sb = lax.ppermute(sb, "occ", x_shift(-1)) + out_block(nx + (x + s + 1) % nx)
-        keep = jnp.where(zh == 0, sa, sb)
-        send = jnp.where(zh == 0, sb, sa)
-        return keep + lax.ppermute(send, "occ", zhi_swap)
+        def scatter_sum(res):
+            parts = jnp.take(res, slots, axis=0)
+            return lax.all_to_all(parts, "occ", 0, 0, tiled=False).sum(axis=0)
+
+        sum_l = scatter_sum(res_l)
+        other, sum_l = lax.optimization_barrier((other, sum_l))
+        res_o = matmul(other, half).reshape(8, rows, -1)
+        sum_o = scatter_sum(res_o)
+        first = jnp.where(c == 0, sum_l, sum_o)
+        second = jnp.where(c == 0, sum_o, sum_l)
+        return jnp.concatenate([first, second], axis=0)
 
     return body
 

time: 79.4 us -> 80 us (level)
  blocking collectives: 0 us -> 20.9 us
  between operations: 15.1 us -> 0.1 us
  starting transfers between devices: 23.5 us -> 12.8 us
  local copies, waits for them, and re-layouts: 6.2 us -> 13.2 us
  waiting for transfers between devices: 24.1 us -> 18 us
  other arithmetic: 1.89 us -> 4.95 us
    all_to_all x0 -> x1, blocking collectives: none -> 20.9 us  [scatter_sum(): return lax.all_to_all(parts, 'occ', 0, 0, tiled=False).sum(axis=0)]
    ppermute x7 -> x0, waiting for transfers between devices: 17 us -> none  [the longest x3 9.9 us: body(): sb = lax.ppermute(sb, 'occ', x_shift(-1)) + out_block(nx + (x + s + 1) % nx)]
    ppermute x7 -> x0, starting transfers between devices: 14.2 us -> none  [the longest x3 10.3 us: body(): sb = lax.ppermute(sb, 'occ', x_shift(-1)) + out_block(nx + (x + s + 1) % nx)]
    all_to_all x0 -> x1, waiting for transfers between devices: none -> 12.7 us  [scatter_sum(): return lax.all_to_all(parts, 'occ', 0, 0, tiled=False).sum(axis=0)]
    gather x0 -> x3, local copies, waits for them, and re-layouts: none -> 4.84 us  [the longest x2 4.2 us: scatter_sum(): parts = jnp.take(res, slots, axis=0)]
    all_to_all x0 -> x1, starting transfers between devices: none -> 3.54 us  [scatter_sum(): return lax.all_to_all(parts, 'occ', 0, 0, tiled=False).sum(axis=0)]
    unnamed x15 -> x13, local copies, waits for them, and re-layouts: 4.81 us -> 7.7 us
    select_n x2 -> x5, other arithmetic: 0.17 us -> 2.19 us  [the longest x3 2.16 us: scatter_sum(): parts = jnp.take(res, slots, axis=0)]
  transfers between devices with their start and end apart: 15 -> 9, of which waited for: 8 -> 3; matrix products, arithmetic and copies ran while one was open for 7% -> 17% of each run, Pallas kernels for 0% -> 0%
where the time goes in v8:
time: 80 us; the launch traced here: 79 us
  blocking collectives  20.9 us (26%)
  waiting for transfers between devices  18 us (22%)
  local copies, waits for them, and re-layouts  13.2 us (16%)
  starting transfers between devices  12.8 us (16%)
  matrix products  9 us (11%)
  other arithmetic  4.95 us (6%)
    all_to_all x1, blocking collectives, scatter_sum(): return lax.all_to_all(parts, 'occ', 0, 0, tiled=False).sum(axis=0)  20.9 us
    all_to_all x1, waiting for transfers between devices, scatter_sum(): return lax.all_to_all(parts, 'occ', 0, 0, tiled=False).sum(axis=0)  12.7 us
    dot_general x3, matrix products, matmul(): return jnp.dot(a, b, preferred_element_type=jnp.float32, precision=HIGH)  9 us
    unnamed x13, local copies, waits for them, and re-layouts  7.7 us
    gather x2, local copies, waits for them, and re-layouts, scatter_sum(): parts = jnp.take(res, slots, axis=0)  4.2 us
    ppermute x1, waiting for transfers between devices, body(): yp1 = lax.ppermute(own, 'vir', y_shift(-1))  3.59 us
    all_to_all x1, starting transfers between devices, scatter_sum(): return lax.all_to_all(parts, 'occ', 0, 0, tiled=False).sum(axis=0)  3.54 us
    ppermute x1, starting transfers between devices, body(): ym1z = lax.ppermute(z1, 'vir', y_shift(1))  2.78 us
  transfers between devices with their start and end apart: 9, of which 3 were waited for; matrix products, arithmetic and copies ran while one was open for 17% of the time, Pallas kernels for 0%

profile of v8, /device:TPU:24, one launch (start us, length us, event | category | flops | bytes accessed | tf_op | source)
XLA Modules:
  0.0 79.0 jit_solution(3919950105929418705)
XLA Ops:
  0.0 2.9 %fusion.9 = f32[32,640]{1,0:T(8,128)S(1)} fusion(f32[32,1280]{1,0:T(8,128)} %param.5, f32[1280,640]{1,0:T(8,128)} %param.6), kind=kOutput, calls=%fused_computation.12 | convolution fusion | flops 158105600 | bytes 3522560 | tf_op jit(solution)/shard_map/dot_general | solution.py:33
  2.9 2.0 %collective-permute-start = (f32[32,1280]{1,0:T(8,128)S(1)}, f32[32,1280]{1,0:T(8,128)}, u32[]{:S(2)}, u32[]{:S(2)}) collective-permute-start(f32[32,1280]{1,0:T(8,128)S(1)} %copy-done.2), channel_id=1, source_target_pairs={{0,8},{1,9},{2,10},{3,11},{4,12},{5,13},{6,14},{7,15},{8,0},{9,1},... | collective-permute-start | bytes 491528 | tf_op jit(solution)/shard_map/ppermute | solution.py:43
  5.2 1.8 %collective-permute-start.2 = (f32[32,1280]{1,0:T(8,128)S(1)}, f32[32,1280]{1,0:T(8,128)}, u32[]{:S(2)}, u32[]{:S(2)}) collective-permute-start(f32[32,1280]{1,0:T(8,128)S(1)} %copy-done.2), channel_id=1, source_target_pairs={{0,6},{1,7},{2,0},{3,1},{4,2},{5,3},{6,4},{7,5},{8,14},{9,15},{10,... | collective-permute-start | bytes 491528 | tf_op jit(solution)/shard_map/ppermute | solution.py:45
  7.6 0.7 constant_dynamic-update-slice_fusion.7
  8.3 3.6 %collective-permute-done.2 = f32[32,1280]{1,0:T(8,128)} collective-permute-done((f32[32,1280]{1,0:T(8,128)S(1)}, f32[32,1280]{1,0:T(8,128)}, u32[]{:S(2)}, u32[]{:S(2)}) %collective-permute-start.2) | collective-permute-done | bytes 163872 | tf_op jit(solution)/shard_map/ppermute | solution.py:45
  12.8 2.8 %collective-permute-start.5 = (f32[32,1280]{1,0:T(8,128)}, f32[32,1280]{1,0:T(8,128)S(1)}, u32[]{:S(2)}, u32[]{:S(2)}) collective-permute-start(f32[32,1280]{1,0:T(8,128)} %collective-permute-done), channel_id=1, source_target_pairs={{0,2},{1,3},{2,4},{3,5},{4,6},{5,7},{6,0},{7,1},{8,10},{9,11},{10,... | collective-permute-start | bytes 491528 | tf_op jit(solution)/shard_map/ppermute | solution.py:48
  15.6 1.8 %constant_dynamic-update-slice_fusion.14 = (f32[224,1280]{1,0:T(8,128)S(1)}, f32[256,1280]{1,0:T(8,128)}) fusion(f32[32,1280]{1,0:T(8,128)} %collective-permute-done, f32[256,1280]{1,0:T(8,128)} %constant_dynamic-update-slice_fusion.7), kind=kLoop, calls=%fused_computation.33 | loop fusion | bytes 491520
  17.4 1.6 %constant_dynamic-update-slice_fusion.13 = (f32[224,1280]{1,0:T(8,128)S(1)}, f32[256,1280]{1,0:T(8,128)}) fusion(f32[224,1280]{1,0:T(8,128)S(1)} %get-tuple-element.32, f32[32,1280]{1,0:T(8,128)} %collective-permute-done.1, f32[256,1280]{1,0:T(8,128)} %get-tuple-element.33), kind=kLoop, calls=%fused_computation.32 | loop fusion | bytes 491520
  19.0 1.6 %constant_dynamic-update-slice_fusion.12 = (f32[224,1280]{1,0:T(8,128)S(1)}, f32[256,1280]{1,0:T(8,128)}) fusion(f32[224,1280]{1,0:T(8,128)S(1)} %get-tuple-element.30, f32[32,1280]{1,0:T(8,128)} %collective-permute-done.2, f32[256,1280]{1,0:T(8,128)} %get-tuple-element.31), kind=kLoop, calls=%fused_computation.31 | loop fusion | bytes 491520
  20.6 1.6 %collective-permute-start.6 = (f32[32,1280]{1,0:T(8,128)S(1)}, f32[32,1280]{1,0:T(8,128)S(1)}, u32[]{:S(2)}, u32[]{:S(2)}) collective-permute-start(f32[32,1280]{1,0:T(8,128)S(1)} %collective-permute-done.4), channel_id=1, source_target_pairs={{0,8},{1,9},{2,10},{3,11},{4,12},{5,13},{6,14},{7,15},{8,0},{9,1},... | collective-permute-start | bytes 491528 | tf_op jit(solution)/shard_map/ppermute | solution.py:49
  22.2 0.7 constant_dynamic-update-slice_fusion.11
  24.2 1.7 %collective-permute-done.6 = f32[32,1280]{1,0:T(8,128)S(1)} collective-permute-done((f32[32,1280]{1,0:T(8,128)S(1)}, f32[32,1280]{1,0:T(8,128)S(1)}, u32[]{:S(2)}, u32[]{:S(2)}) %collective-permute-start.6) | collective-permute-done | bytes 163872 | tf_op jit(solution)/shard_map/ppermute | solution.py:49
  25.9 0.7 constant_dynamic-update-slice_fusion.8
  26.6 1.9 %fusion.2 = f32[224,640]{1,0:T(8,128)S(1)} fusion(f32[224,1280]{1,0:T(8,128)S(1)} %get-tuple-element.20, f32[1280,640]{1,0:T(8,128)S(1)} %copy-done.1), kind=kOutput, calls=%fused_computation.5 | convolution fusion | flops 1101824000 | bytes 4997120 | tf_op jit(solution)/shard_map/dot_general | solution.py:33
  28.5 0.9 %pad_maximum_fusion = f32[256,640]{1,0:T(8,128)} fusion(f32[224,640]{1,0:T(8,128)S(1)} %fusion.2, f32[32,640]{1,0:T(8,128)S(1)} %fusion.9), kind=kLoop, calls=%fused_computation.13 | loop fusion | flops 163840 | bytes 1310720 | tf_op jit(solution)/shard_map/concatenate | solution.py:51
  29.4 2.5 %gather_fusion.1 = f32[8,32,640]{2,1,0:T(8,128)} fusion(f32[8,32,640]{2,1,0:T(8,128)} %bitcast.10, s32[1024]{0:T(1024)S(1)} %pad_clamp_fusion), kind=kCustom, calls=%fused_computation.clone | custom fusion | bytes 1310752 | tf_op jit(solution)/shard_map/jit(_take)/gather | solution.py:61
  31.9 1.2 %broadcast_select_fusion.1 = f32[8,32,640]{2,1,0:T(8,128)S(1)} fusion(f32[8,32,640]{2,1,0:T(8,128)} %gather_fusion.1, pred[8]{0:T(512)(128)(4,1)S(1)} %compare_and_fusion), kind=kLoop, calls=%fused_computation.15 | loop fusion | flops 163840 | bytes 1310728 | tf_op jit(solution)/shard_map/jit(_take)/select_n | solution.py:61
  33.1 20.9 %all_to_all.10 = f32[8,32,640]{2,1,0:T(8,128)} all-to-all(f32[8,32,640]{2,1,0:T(8,128)S(1)} %broadcast_select_fusion.1), channel_id=1, replica_groups=mesh['occ'=8,'vir'=16] {'occ'}, dimensions={0} | all-to-all | bytes 1310720 | tf_op jit(solution)/shard_map/all_to_all | solution.py:62
  54.0 1.1 %reduce_sum.18 = f32[32,640]{1,0:T(8,128)S(1)} reduce(f32[8,32,640]{2,1,0:T(8,128)} %all_to_all.10, f32[]{:T(128)} %constant.94.clone.1), dimensions={0}, to_apply=%region_0.2 | reduce | flops 143360 | bytes 737284 | tf_op jit(solution)/shard_map/reduce_sum | solution.py:62
  55.2 4.2 %fusion = f32[256,640]{1,0:T(8,128)} fusion(f32[256,1280]{1,0:T(8,128)} %collective-permute-done.7, f32[1280,640]{1,0:T(8,128)S(1)} %copy-done.1), kind=kOutput, calls=%fused_computation.3 | convolution fusion | flops 1259110400 | bytes 5242880 | tf_op jit(solution)/shard_map/dot_general | solution.py:33
  59.3 1.7 %gather_fusion.2 = f32[8,32,640]{2,1,0:T(8,128)S(1)} fusion(f32[8,32,640]{2,1,0:T(8,128)} %bitcast.9, s32[1024]{0:T(1024)S(1)} %pad_clamp_fusion), kind=kCustom, calls=%fused_computation.1.clone | custom fusion | bytes 1310752 | tf_op jit(solution)/shard_map/jit(_take)/gather | solution.py:61
  61.0 1.0 %broadcast_select_fusion = f32[8,32,640]{2,1,0:T(8,128)} fusion(f32[8,32,640]{2,1,0:T(8,128)S(1)} %gather_fusion.2, pred[8]{0:T(512)(128)(4,1)S(1)} %compare_and_fusion), kind=kLoop, calls=%fused_computation.14 | loop fusion | flops 163840 | bytes 1310728 | tf_op jit(solution)/shard_map/jit(_take)/select_n | solution.py:61
  62.0 3.5 %all-to-all-start.1 = ((f32[8,32,640]{2,1,0:T(8,128)}), f32[8,32,640]{2,1,0:T(8,128)S(1)}, u32[]{:S(2)}, u32[]{:S(2)}) async-start(f32[8,32,640]{2,1,0:T(8,128)} %broadcast_select_fusion), calls=%async_computation.1 | async-start | bytes 1310720 | tf_op jit(solution)/shard_map/all_to_all | solution.py:62
  65.5 12.7 %all-to-all-done.1 = f32[8,32,640]{2,1,0:T(8,128)S(1)} async-done(((f32[8,32,640]{2,1,0:T(8,128)}), f32[8,32,640]{2,1,0:T(8,128)S(1)}, u32[]{:S(2)}, u32[]{:S(2)}) %all-to-all-start.1) | async-done | bytes 655392 | tf_op jit(solution)/shard_map/all_to_all | solution.py:62
  (27 shorter events, 3.9 us)
Async XLA Ops:
  0.0 7.0 %copy-start = (s32[8]{0:T(128)S(1)}, s32[8]{0:T(128)}, u32[]{:S(2)}) copy-start(s32[8]{0:T(128)} %constant.95.clone) | copy-start | bytes 100
  0.0 2.9 %copy-start.2 = (f32[32,1280]{1,0:T(8,128)S(1)}, f32[32,1280]{1,0:T(8,128)}, u32[]{:S(2)}) copy-start(f32[32,1280]{1,0:T(8,128)} %param.5) | copy-start | bytes 491524
  2.9 9.9 %collective-permute-start = (f32[32,1280]{1,0:T(8,128)S(1)}, f32[32,1280]{1,0:T(8,128)}, u32[]{:S(2)}, u32[]{:S(2)}) collective-permute-start(f32[32,1280]{1,0:T(8,128)S(1)} %copy-done.2), channel_id=1, source_target_pairs={{0,8},{1,9},{2,10},{3,11},{4,12},{5,13},{6,14},{7,15},{8,0},{9,1},... | collective-permute-start | bytes 491528 | tf_op jit(solution)/shard_map/ppermute | solution.py:43
  4.9 12.4 %collective-permute-start.1 = (f32[32,1280]{1,0:T(8,128)S(1)}, f32[32,1280]{1,0:T(8,128)}, u32[]{:S(2)}, u32[]{:S(2)}) collective-permute-start(f32[32,1280]{1,0:T(8,128)S(1)} %copy-done.2), channel_id=1, source_target_pairs={{0,2},{1,3},{2,4},{3,5},{4,6},{5,7},{6,0},{7,1},{8,10},{9,11},{10,... | collective-permute-start | bytes 491528 | tf_op jit(solution)/shard_map/ppermute | solution.py:44
  5.2 6.8 %collective-permute-start.2 = (f32[32,1280]{1,0:T(8,128)S(1)}, f32[32,1280]{1,0:T(8,128)}, u32[]{:S(2)}, u32[]{:S(2)}) collective-permute-start(f32[32,1280]{1,0:T(8,128)S(1)} %copy-done.2), channel_id=1, source_target_pairs={{0,6},{1,7},{2,0},{3,1},{4,2},{5,3},{6,4},{7,5},{8,14},{9,15},{10,... | collective-permute-start | bytes 491528 | tf_op jit(solution)/shard_map/ppermute | solution.py:45
  11.9 10.3 %collective-permute-start.3 = (f32[32,1280]{1,0:T(8,128)}, f32[32,1280]{1,0:T(8,128)S(1)}, u32[]{:S(2)}, u32[]{:S(2)}) collective-permute-start(f32[32,1280]{1,0:T(8,128)} %collective-permute-done.2), channel_id=1, source_target_pairs={{0,8},{1,9},{2,10},{3,11},{4,12},{5,13},{6,14},{7,15},{8,0},{9,1},... | collective-permute-start | bytes 491528 | tf_op jit(solution)/shard_map/ppermute | solution.py:46
  12.4 8.2 %collective-permute-start.4 = (f32[32,1280]{1,0:T(8,128)}, f32[32,1280]{1,0:T(8,128)S(1)}, u32[]{:S(2)}, u32[]{:S(2)}) collective-permute-start(f32[32,1280]{1,0:T(8,128)} %collective-permute-done.2), channel_id=1, source_target_pairs={{0,6},{1,7},{2,0},{3,1},{4,2},{5,3},{6,4},{7,5},{8,14},{9,15},{10,... | collective-permute-start | bytes 491528 | tf_op jit(solution)/shard_map/ppermute | solution.py:47
  12.8 10.7 %collective-permute-start.5 = (f32[32,1280]{1,0:T(8,128)}, f32[32,1280]{1,0:T(8,128)S(1)}, u32[]{:S(2)}, u32[]{:S(2)}) collective-permute-start(f32[32,1280]{1,0:T(8,128)} %collective-permute-done), channel_id=1, source_target_pairs={{0,2},{1,3},{2,4},{3,5},{4,6},{5,7},{6,0},{7,1},{8,10},{9,11},{10,... | collective-permute-start | bytes 491528 | tf_op jit(solution)/shard_map/ppermute | solution.py:48
  15.6 11.0 %copy-start.1 = (f32[1280,640]{1,0:T(8,128)S(1)}, f32[1280,640]{1,0:T(8,128)}, u32[]{:S(2)}) copy-start(f32[1280,640]{1,0:T(8,128)} %param.6) | copy-start | bytes 9830404
  20.6 5.3 %collective-permute-start.6 = (f32[32,1280]{1,0:T(8,128)S(1)}, f32[32,1280]{1,0:T(8,128)S(1)}, u32[]{:S(2)}, u32[]{:S(2)}) collective-permute-start(f32[32,1280]{1,0:T(8,128)S(1)} %collective-permute-done.4), channel_id=1, source_target_pairs={{0,8},{1,9},{2,10},{3,11},{4,12},{5,13},{6,14},{7,15},{8,0},{9,1},... | collective-permute-start | bytes 491528 | tf_op jit(solution)/shard_map/ppermute | solution.py:49
  29.4 25.8 %collective-permute-start.7 = (f32[256,1280]{1,0:T(8,128)}, f32[256,1280]{1,0:T(8,128)}, u32[]{:S(2)}, u32[]{:S(2)}) collective-permute-start(f32[256,1280]{1,0:T(8,128)} %get-tuple-element.14), channel_id=1, source_target_pairs={{0,1},{1,0},{2,3},{3,2},{4,5},{5,4},{6,7},{7,6},{8,9},{9,8},{10,11... | collective-permute-start | bytes 3932168 | tf_op jit(solution)/shard_map/ppermute | solution.py:54
  62.0 16.3 %all-to-all-start.1 = ((f32[8,32,640]{2,1,0:T(8,128)}), f32[8,32,640]{2,1,0:T(8,128)S(1)}, u32[]{:S(2)}, u32[]{:S(2)}) async-start(f32[8,32,640]{2,1,0:T(8,128)} %broadcast_select_fusion), calls=%async_computation.1 | async-start | bytes 1310720 | tf_op jit(solution)/shard_map/all_to_all | solution.py:62

commit v9 on v8

--- a/solution.py
+++ b/solution.py
@@ -53,18 +53,26 @@
         res_l = res_l.reshape(8, rows, -1)
         other = lax.ppermute(local, "vir", core_swap)
         table = jnp.array(slot_of, jnp.int32)
+        mo = lax.axis_index("occ")
+        x, zh = mo % nx, mo // nx
 
-        dest = jnp.arange(n_occ, dtype=jnp.int32)
-        slots = table[((dest % nx - y) % ny) * 2 + ((dest // nx) ^ zl)]
+        def ring(res):
+            def half_block(r):
+                k = table[((r % nx - y) % ny) * 2 + ((r // nx) ^ zl)]
+                return lax.dynamic_index_in_dim(res, k, 0, keepdims=False)
 
-        def scatter_sum(res):
-            parts = jnp.take(res, slots, axis=0)
-            return lax.all_to_all(parts, "occ", 0, 0, tiled=False).sum(axis=0)
+            sa = half_block((x - 1) % nx)
+            sb = half_block(nx + (x + 1) % nx)
+            for s in range(1, nx):
+                sa = lax.ppermute(sa, "occ", x_shift(1)) + half_block((x - s - 1) % nx)
+                sb = lax.ppermute(sb, "occ", x_shift(-1)) + half_block(nx + (x + s + 1) % nx)
+            keep = jnp.where(zh == 0, sa, sb)
+            send = jnp.where(zh == 0, sb, sa)
+            return keep + lax.ppermute(send, "occ", zhi_swap)
 
-        sum_l = scatter_sum(res_l)
-        other, sum_l = lax.optimization_barrier((other, sum_l))
+        sum_l = ring(res_l)
         res_o = matmul(other, half).reshape(8, rows, -1)
-        sum_o = scatter_sum(res_o)
+        sum_o = ring(res_o)
         first = jnp.where(c == 0, sum_l, sum_o)
         second = jnp.where(c == 0, sum_o, sum_l)
         return jnp.concatenate([first, second], axis=0)

time: 80 us -> 79.7 us (level)
  blocking collectives: 20.9 us -> 0 us
  starting transfers between devices: 12.8 us -> 31.9 us
  between operations: 0.1 us -> 15.1 us
  local copies, waits for them, and re-layouts: 13.2 us -> 7.14 us
  waiting for transfers between devices: 18 us -> 14.1 us
  other arithmetic: 4.95 us -> 2.75 us
    ppermute x0 -> x14, starting transfers between devices: none -> 22.6 us  [the longest x6 11.9 us: ring(): lax.ppermute(sb, 'occ', x_shift(-1)) + half_block(nx + (x + s + 1) % nx)]
    all_to_all x1 -> x0, blocking collectives: 20.9 us -> none  [scatter_sum(): return lax.all_to_all(parts, 'occ', 0, 0, tiled=False).sum(axis=0)]
    all_to_all x1 -> x0, waiting for transfers between devices: 12.7 us -> none  [scatter_sum(): return lax.all_to_all(parts, 'occ', 0, 0, tiled=False).sum(axis=0)]
    ppermute x0 -> x14, waiting for transfers between devices: none -> 7.06 us  [the longest x2 4.4 us: ring(): return keep + lax.ppermute(send, 'occ', zhi_swap)]
    gather x3 -> x0, local copies, waits for them, and re-layouts: 4.84 us -> none  [the longest x2 4.2 us: scatter_sum(): parts = jnp.take(res, slots, axis=0)]
    all_to_all x1 -> x0, starting transfers between devices: 3.54 us -> none  [scatter_sum(): return lax.all_to_all(parts, 'occ', 0, 0, tiled=False).sum(axis=0)]
    unnamed x13 -> x17, local copies, waits for them, and re-layouts: 7.7 us -> 4.81 us
    select_n x4 -> x3, other arithmetic: 2.18 us -> 0.06 us  [the longest x2 0.05 us: ring(): send = jnp.where(zh == 0, sb, sa)]
  transfers between devices with their start and end apart: 9 -> 22, of which waited for: 3 -> 8; matrix products, arithmetic and copies ran while one was open for 17% -> 13% of each run, Pallas kernels for 0% -> 0%
where the time goes in v9:
time: 79.7 us; the launch traced here: 79.2 us
  starting transfers between devices  31.9 us (40%)
  between operations  15.1 us (19%)
  waiting for transfers between devices  14.1 us (18%)
  matrix products  8.22 us (10%)
  local copies, waits for them, and re-layouts  7.14 us (9%)
  other arithmetic  2.75 us (3%)
    ppermute x6, starting transfers between devices, ring(): lax.ppermute(sb, 'occ', x_shift(-1)) + half_block(nx + (x + s + 1) % nx)  11.9 us
    dot_general x3, matrix products, matmul(): return jnp.dot(a, b, preferred_element_type=jnp.float32, precision=HIGH)  8.22 us
    ppermute x6, starting transfers between devices, ring(): sa = lax.ppermute(sa, 'occ', x_shift(1)) + half_block((x - s - 1) % nx)  5.41 us
    ppermute x2, starting transfers between devices, ring(): return keep + lax.ppermute(send, 'occ', zhi_swap)  5.28 us
    unnamed x17, local copies, waits for them, and re-layouts  4.81 us
    ppermute x2, waiting for transfers between devices, ring(): return keep + lax.ppermute(send, 'occ', zhi_swap)  4.4 us
    ppermute x1, waiting for transfers between devices, body(): yp1 = lax.ppermute(own, 'vir', y_shift(-1))  4.18 us
    ppermute x1, starting transfers between devices, body(): ym1z = lax.ppermute(z1, 'vir', y_shift(1))  2.78 us
  transfers between devices with their start and end apart: 22, of which 8 were waited for; matrix products, arithmetic and copies ran while one was open for 13% of the time, Pallas kernels for 0%

profile of v9, /device:TPU:24, one launch (start us, length us, event | category | flops | bytes accessed | tf_op | source)
XLA Modules:
  0.0 79.2 jit_solution(2389316061660190343)
XLA Ops:
  0.0 2.9 %fusion.9 = f32[32,640]{1,0:T(8,128)S(1)} fusion(f32[32,1280]{1,0:T(8,128)} %param.3, f32[1280,640]{1,0:T(8,128)} %param.4), kind=kOutput, calls=%fused_computation.9 | convolution fusion | flops 158105600 | bytes 3522560 | tf_op jit(solution)/shard_map/dot_general | solution.py:33
  2.9 2.0 %collective-permute-start = (f32[32,1280]{1,0:T(8,128)S(1)}, f32[32,1280]{1,0:T(8,128)S(1)}, u32[]{:S(2)}, u32[]{:S(2)}) collective-permute-start(f32[32,1280]{1,0:T(8,128)S(1)} %copy-done.3), channel_id=1, source_target_pairs={{0,8},{1,9},{2,10},{3,11},{4,12},{5,13},{6,14},{7,15},{8,0},{9,1},... | collective-permute-start | bytes 491528 | tf_op jit(solution)/shard_map/ppermute | solution.py:43
  5.2 1.8 %collective-permute-start.2 = (f32[32,1280]{1,0:T(8,128)S(1)}, f32[32,1280]{1,0:T(8,128)S(1)}, u32[]{:S(2)}, u32[]{:S(2)}) collective-permute-start(f32[32,1280]{1,0:T(8,128)S(1)} %copy-done.3), channel_id=1, source_target_pairs={{0,6},{1,7},{2,0},{3,1},{4,2},{5,3},{6,4},{7,5},{8,14},{9,15},{10,... | collective-permute-start | bytes 491528 | tf_op jit(solution)/shard_map/ppermute | solution.py:45
  7.6 4.2 %collective-permute-done.2 = f32[32,1280]{1,0:T(8,128)S(1)} collective-permute-done((f32[32,1280]{1,0:T(8,128)S(1)}, f32[32,1280]{1,0:T(8,128)S(1)}, u32[]{:S(2)}, u32[]{:S(2)}) %collective-permute-start.2) | collective-permute-done | bytes 163872 | tf_op jit(solution)/shard_map/ppermute | solution.py:45
  12.7 2.8 %collective-permute-start.5 = (f32[32,1280]{1,0:T(8,128)S(1)}, f32[32,1280]{1,0:T(8,128)S(1)}, u32[]{:S(2)}, u32[]{:S(2)}) collective-permute-start(f32[32,1280]{1,0:T(8,128)S(1)} %collective-permute-done), channel_id=1, source_target_pairs={{0,2},{1,3},{2,4},{3,5},{4,6},{5,7},{6,0},{7,1},{8,10},{9,11},{10,... | collective-permute-start | bytes 491528 | tf_op jit(solution)/shard_map/ppermute | solution.py:48
  17.6 1.2 %collective-permute-done.4 = f32[32,1280]{1,0:T(8,128)S(1)} collective-permute-done((f32[32,1280]{1,0:T(8,128)S(1)}, f32[32,1280]{1,0:T(8,128)S(1)}, u32[]{:S(2)}, u32[]{:S(2)}) %collective-permute-start.4) | collective-permute-done | bytes 163872 | tf_op jit(solution)/shard_map/ppermute | solution.py:47
  18.8 1.6 %collective-permute-start.6 = (f32[32,1280]{1,0:T(8,128)S(1)}, f32[32,1280]{1,0:T(8,128)S(1)}, u32[]{:S(2)}, u32[]{:S(2)}) collective-permute-start(f32[32,1280]{1,0:T(8,128)S(1)} %collective-permute-done.4), channel_id=1, source_target_pairs={{0,8},{1,9},{2,10},{3,11},{4,12},{5,13},{6,14},{7,15},{8,0},{9,1},... | collective-permute-start | bytes 491528 | tf_op jit(solution)/shard_map/ppermute | solution.py:49
  22.4 1.7 %collective-permute-done.6 = f32[32,1280]{1,0:T(8,128)S(1)} collective-permute-done((f32[32,1280]{1,0:T(8,128)S(1)}, f32[32,1280]{1,0:T(8,128)S(1)}, u32[]{:S(2)}, u32[]{:S(2)}) %collective-permute-start.6) | collective-permute-done | bytes 163872 | tf_op jit(solution)/shard_map/ppermute | solution.py:49
  24.8 1.9 %fusion.2 = f32[224,640]{1,0:T(8,128)S(1)} fusion(f32[224,1280]{1,0:T(8,128)S(1)} %get-tuple-element.28, f32[1280,640]{1,0:T(8,128)S(1)} %copy-done), kind=kOutput, calls=%fused_computation.2 | convolution fusion | flops 1101824000 | bytes 4997120 | tf_op jit(solution)/shard_map/dot_general | solution.py:33
  43.2 0.9 %dynamic-slice_bitcast_fusion.2 = (f32[32,640]{1,0:T(8,128)S(1)}, f32[32,640]{1,0:T(8,128)S(1)}) fusion(f32[8,32,640]{2,1,0:T(8,128)} %bitcast.72, s32[]{:T(128)S(6)} %select_n.333, s32[]{:T(128)S(6)} %select_n.309), kind=kLoop, calls=%fused_computation.28 | loop fusion | bytes 327688 | tf_op jit(solution)/shard_map/jit(dynamic_index_in_dim)/squeeze | solution.py:62
  44.2 2.8 %collective-permute-start.10 = (f32[32,640]{1,0:T(8,128)S(1)}, f32[32,640]{1,0:T(8,128)S(1)}, u32[]{:S(2)}, u32[]{:S(2)}) collective-permute-start(f32[32,640]{1,0:T(8,128)S(1)} %get-tuple-element.26), channel_id=1, source_target_pairs={{0,48},{16,0},{32,16},{48,32},{64,112},{80,64},{96,80},{112,96},{1... | collective-permute-start | bytes 245768 | tf_op jit(solution)/shard_map/ppermute | solution.py:68
  47.0 3.4 %fusion = f32[256,640]{1,0:T(8,128)S(1)} fusion(f32[256,1280]{1,0:T(8,128)} %collective-permute-done.14, f32[1280,640]{1,0:T(8,128)S(1)} %copy-done), kind=kOutput, calls=%fused_computation | convolution fusion | flops 1259110400 | bytes 5242880 | tf_op jit(solution)/shard_map/dot_general | solution.py:33
  51.3 2.6 %collective-permute-start.18 = (f32[32,640]{1,0:T(8,128)S(1)}, f32[32,640]{1,0:T(8,128)S(1)}, u32[]{:S(2)}, u32[]{:S(2)}) collective-permute-start(f32[32,640]{1,0:T(8,128)S(1)} %get-tuple-element.20), channel_id=1, source_target_pairs={{0,48},{16,0},{32,16},{48,32},{64,112},{80,64},{96,80},{112,96},{1... | collective-permute-start | bytes 245768 | tf_op jit(solution)/shard_map/ppermute | solution.py:68
  53.9 2.0 %collective-permute-start.11 = (f32[32,640]{1,0:T(8,128)S(1)}, f32[32,640]{1,0:T(8,128)S(1)}, u32[]{:S(2)}, u32[]{:S(2)}) collective-permute-start(f32[32,640]{1,0:T(8,128)S(1)} %get-tuple-element.24), channel_id=1, source_target_pairs={{0,48},{16,0},{32,16},{48,32},{64,112},{80,64},{96,80},{112,96},{1... | collective-permute-start | bytes 245768 | tf_op jit(solution)/shard_map/ppermute | solution.py:68
  56.4 2.0 %collective-permute-start.16 = (f32[32,640]{1,0:T(8,128)S(1)}, f32[32,640]{1,0:T(8,128)S(1)}, u32[]{:S(2)}, u32[]{:S(2)}) collective-permute-start(f32[32,640]{1,0:T(8,128)S(1)} %get-tuple-element.19), channel_id=1, source_target_pairs={{0,16},{16,32},{32,48},{48,0},{64,80},{80,96},{96,112},{112,64},{1... | collective-permute-start | bytes 245768 | tf_op jit(solution)/shard_map/ppermute | solution.py:67
  58.4 1.6 %collective-permute-start.19 = (f32[32,640]{1,0:T(8,128)S(1)}, f32[32,640]{1,0:T(8,128)S(1)}, u32[]{:S(2)}, u32[]{:S(2)}) collective-permute-start(f32[32,640]{1,0:T(8,128)S(1)} %get-tuple-element.18), channel_id=1, source_target_pairs={{0,48},{16,0},{32,16},{48,32},{64,112},{80,64},{96,80},{112,96},{1... | collective-permute-start | bytes 245768 | tf_op jit(solution)/shard_map/ppermute | solution.py:68
  60.0 1.5 %collective-permute-done.8 = f32[32,640]{1,0:T(8,128)S(1)} collective-permute-done((f32[32,640]{1,0:T(8,128)S(1)}, f32[32,640]{1,0:T(8,128)S(1)}, u32[]{:S(2)}, u32[]{:S(2)}) %collective-permute-start.8) | collective-permute-done | bytes 81952 | tf_op jit(solution)/shard_map/ppermute | solution.py:67
  62.1 1.6 %collective-permute-start.9 = (f32[32,640]{1,0:T(8,128)S(1)}, f32[32,640]{1,0:T(8,128)S(1)}, u32[]{:S(2)}, u32[]{:S(2)}) collective-permute-start(f32[32,640]{1,0:T(8,128)S(1)} %get-tuple-element.23), channel_id=1, source_target_pairs={{0,16},{16,32},{32,48},{48,0},{64,80},{80,96},{96,112},{112,64},{1... | collective-permute-start | bytes 245768 | tf_op jit(solution)/shard_map/ppermute | solution.py:67
  63.7 1.0 %collective-permute-start.17 = (f32[32,640]{1,0:T(8,128)S(1)}, f32[32,640]{1,0:T(8,128)S(1)}, u32[]{:S(2)}, u32[]{:S(2)}) collective-permute-start(f32[32,640]{1,0:T(8,128)S(1)} %get-tuple-element.17), channel_id=1, source_target_pairs={{0,16},{16,32},{32,48},{48,0},{64,80},{80,96},{96,112},{112,64},{1... | collective-permute-start | bytes 245768 | tf_op jit(solution)/shard_map/ppermute | solution.py:67
  64.7 2.3 %collective-permute-start.20 = (f32[32,640]{1,0:T(8,128)S(1)}, f32[32,640]{1,0:T(8,128)S(1)}, u32[]{:S(2)}, u32[]{:S(2)}) collective-permute-start(f32[32,640]{1,0:T(8,128)S(1)} %get-tuple-element.16), channel_id=1, source_target_pairs={{0,48},{16,0},{32,16},{48,32},{64,112},{80,64},{96,80},{112,96},{1... | collective-permute-start | bytes 245768 | tf_op jit(solution)/shard_map/ppermute | solution.py:68
  67.8 3.7 %collective-permute-start.13 = (f32[32,640]{1,0:T(8,128)S(1)}, f32[32,640]{1,0:T(8,128)S(1)}, u32[]{:S(2)}, u32[]{:S(2)}) collective-permute-start(f32[32,640]{1,0:T(8,128)S(1)} %broadcast_select_fusion.1), channel_id=1, source_target_pairs={{0,64},{16,80},{32,96},{48,112},{64,0},{80,16},{96,32},{112,48},{1... | collective-permute-start | bytes 245768 | tf_op jit(solution)/shard_map/ppermute | solution.py:71
  71.5 1.6 %collective-permute-start.21 = (f32[32,640]{1,0:T(8,128)S(1)}, f32[32,640]{1,0:T(8,128)S(1)}, u32[]{:S(2)}, u32[]{:S(2)}) collective-permute-start(f32[32,640]{1,0:T(8,128)S(1)} %broadcast_select_fusion), channel_id=1, source_target_pairs={{0,64},{16,80},{32,96},{48,112},{64,0},{80,16},{96,32},{112,48},{1... | collective-permute-start | bytes 245768 | tf_op jit(solution)/shard_map/ppermute | solution.py:71
  73.9 3.6 %collective-permute-done.21 = f32[32,640]{1,0:T(8,128)S(1)} collective-permute-done((f32[32,640]{1,0:T(8,128)S(1)}, f32[32,640]{1,0:T(8,128)S(1)}, u32[]{:S(2)}, u32[]{:S(2)}) %collective-permute-start.21) | collective-permute-done | bytes 81952 | tf_op jit(solution)/shard_map/ppermute | solution.py:71
  77.5 1.0 %broadcast_select_fusion.3 = (f32[32,640]{1,0:T(8,128)S(1)}, f32[32,640]{1,0:T(8,128)S(1)}, f32[32,640]{1,0:T(8,128)S(1)}) fusion(pred[]{:T(512)S(6)} %eq.62, f32[32,640]{1,0:T(8,128)S(1)} %collective-permute-done.13, f32[32,640]{1,0:T(8,128)S(1)} %collective-permute-done.12, f32[8,32,640]{2,1,0:T(8,128)} %bitcast.73, s32[]{:T(128)S(6)} %select_n.351, ...), kind=kLoop, calls=%fused_computation.33 | loop fusion | flops 184320 | bytes 1064970 | tf_op jit(solution)/shard_map/jit(_where)/select_n | solution.py:76
  (54 shorter events, 12.4 us)
Async XLA Ops:
  2.9 9.8 %collective-permute-start = (f32[32,1280]{1,0:T(8,128)S(1)}, f32[32,1280]{1,0:T(8,128)S(1)}, u32[]{:S(2)}, u32[]{:S(2)}) collective-permute-start(f32[32,1280]{1,0:T(8,128)S(1)} %copy-done.3), channel_id=1, source_target_pairs={{0,8},{1,9},{2,10},{3,11},{4,12},{5,13},{6,14},{7,15},{8,0},{9,1},... | collective-permute-start | bytes 491528 | tf_op jit(solution)/shard_map/ppermute | solution.py:43
  4.9 11.2 %collective-permute-start.1 = (f32[32,1280]{1,0:T(8,128)S(1)}, f32[32,1280]{1,0:T(8,128)S(1)}, u32[]{:S(2)}, u32[]{:S(2)}) collective-permute-start(f32[32,1280]{1,0:T(8,128)S(1)} %copy-done.3), channel_id=1, source_target_pairs={{0,2},{1,3},{2,4},{3,5},{4,6},{5,7},{6,0},{7,1},{8,10},{9,11},{10,... | collective-permute-start | bytes 491528 | tf_op jit(solution)/shard_map/ppermute | solution.py:44
  5.2 6.7 %collective-permute-start.2 = (f32[32,1280]{1,0:T(8,128)S(1)}, f32[32,1280]{1,0:T(8,128)S(1)}, u32[]{:S(2)}, u32[]{:S(2)}) collective-permute-start(f32[32,1280]{1,0:T(8,128)S(1)} %copy-done.3), channel_id=1, source_target_pairs={{0,6},{1,7},{2,0},{3,1},{4,2},{5,3},{6,4},{7,5},{8,14},{9,15},{10,... | collective-permute-start | bytes 491528 | tf_op jit(solution)/shard_map/ppermute | solution.py:45
  11.8 8.6 %collective-permute-start.3 = (f32[32,1280]{1,0:T(8,128)S(1)}, f32[32,1280]{1,0:T(8,128)S(1)}, u32[]{:S(2)}, u32[]{:S(2)}) collective-permute-start(f32[32,1280]{1,0:T(8,128)S(1)} %collective-permute-done.2), channel_id=1, source_target_pairs={{0,8},{1,9},{2,10},{3,11},{4,12},{5,13},{6,14},{7,15},{8,0},{9,1},... | collective-permute-start | bytes 491528 | tf_op jit(solution)/shard_map/ppermute | solution.py:46
  12.3 6.5 %collective-permute-start.4 = (f32[32,1280]{1,0:T(8,128)S(1)}, f32[32,1280]{1,0:T(8,128)S(1)}, u32[]{:S(2)}, u32[]{:S(2)}) collective-permute-start(f32[32,1280]{1,0:T(8,128)S(1)} %collective-permute-done.2), channel_id=1, source_target_pairs={{0,6},{1,7},{2,0},{3,1},{4,2},{5,3},{6,4},{7,5},{8,14},{9,15},{10,... | collective-permute-start | bytes 491528 | tf_op jit(solution)/shard_map/ppermute | solution.py:47
  12.7 9.0 %collective-permute-start.5 = (f32[32,1280]{1,0:T(8,128)S(1)}, f32[32,1280]{1,0:T(8,128)S(1)}, u32[]{:S(2)}, u32[]{:S(2)}) collective-permute-start(f32[32,1280]{1,0:T(8,128)S(1)} %collective-permute-done), channel_id=1, source_target_pairs={{0,2},{1,3},{2,4},{3,5},{4,6},{5,7},{6,0},{7,1},{8,10},{9,11},{10,... | collective-permute-start | bytes 491528 | tf_op jit(solution)/shard_map/ppermute | solution.py:48
  15.5 9.3 %copy-start = (f32[1280,640]{1,0:T(8,128)S(1)}, f32[1280,640]{1,0:T(8,128)}, u32[]{:S(2)}) copy-start(f32[1280,640]{1,0:T(8,128)} %param.4) | copy-start | bytes 9830404
  18.8 5.3 %collective-permute-start.6 = (f32[32,1280]{1,0:T(8,128)S(1)}, f32[32,1280]{1,0:T(8,128)S(1)}, u32[]{:S(2)}, u32[]{:S(2)}) collective-permute-start(f32[32,1280]{1,0:T(8,128)S(1)} %collective-permute-done.4), channel_id=1, source_target_pairs={{0,8},{1,9},{2,10},{3,11},{4,12},{5,13},{6,14},{7,15},{8,0},{9,1},... | collective-permute-start | bytes 491528 | tf_op jit(solution)/shard_map/ppermute | solution.py:49
  27.6 19.5 %collective-permute-start.14 = (f32[256,1280]{1,0:T(8,128)}, f32[256,1280]{1,0:T(8,128)}, u32[]{:S(2)}, u32[]{:S(2)}) collective-permute-start(f32[256,1280]{1,0:T(8,128)} %get-tuple-element.12), channel_id=1, source_target_pairs={{0,1},{1,0},{2,3},{3,2},{4,5},{5,4},{6,7},{7,6},{8,9},{9,8},{10,11... | collective-permute-start | bytes 3932168 | tf_op jit(solution)/shard_map/ppermute | solution.py:54
  44.2 9.6 %collective-permute-start.10 = (f32[32,640]{1,0:T(8,128)S(1)}, f32[32,640]{1,0:T(8,128)S(1)}, u32[]{:S(2)}, u32[]{:S(2)}) collective-permute-start(f32[32,640]{1,0:T(8,128)S(1)} %get-tuple-element.26), channel_id=1, source_target_pairs={{0,48},{16,0},{32,16},{48,32},{64,112},{80,64},{96,80},{112,96},{1... | collective-permute-start | bytes 245768 | tf_op jit(solution)/shard_map/ppermute | solution.py:68
  47.0 6.8 %collective-permute-start.7 = (f32[32,640]{1,0:T(8,128)S(1)}, f32[32,640]{1,0:T(8,128)S(1)}, u32[]{:S(2)}, u32[]{:S(2)}) collective-permute-start(f32[32,640]{1,0:T(8,128)S(1)} %get-tuple-element.27), channel_id=1, source_target_pairs={{0,16},{16,32},{32,48},{48,0},{64,80},{80,96},{96,112},{112,64},{1... | collective-permute-start | bytes 245768 | tf_op jit(solution)/shard_map/ppermute | solution.py:67
  50.5 21.0 %copy-start.1 = (f32[256,640]{1,0:T(8,128)}, f32[256,640]{1,0:T(8,128)S(1)}, u32[]{:S(2)}) copy-start(f32[256,640]{1,0:T(8,128)S(1)} %fusion) | copy-start | bytes 1966084
  50.5 5.9 %collective-permute-start.15 = (f32[32,640]{1,0:T(8,128)S(1)}, f32[32,640]{1,0:T(8,128)S(1)}, u32[]{:S(2)}, u32[]{:S(2)}) collective-permute-start(f32[32,640]{1,0:T(8,128)S(1)} %get-tuple-element.21), channel_id=1, source_target_pairs={{0,16},{16,32},{32,48},{48,0},{64,80},{80,96},{96,112},{112,64},{1... | collective-permute-start | bytes 245768 | tf_op jit(solution)/shard_map/ppermute | solution.py:67
  51.3 5.1 %collective-permute-start.18 = (f32[32,640]{1,0:T(8,128)S(1)}, f32[32,640]{1,0:T(8,128)S(1)}, u32[]{:S(2)}, u32[]{:S(2)}) collective-permute-start(f32[32,640]{1,0:T(8,128)S(1)} %get-tuple-element.20), channel_id=1, source_target_pairs={{0,48},{16,0},{32,16},{48,32},{64,112},{80,64},{96,80},{112,96},{1... | collective-permute-start | bytes 245768 | tf_op jit(solution)/shard_map/ppermute | solution.py:68
  53.9 6.2 %collective-permute-start.11 = (f32[32,640]{1,0:T(8,128)S(1)}, f32[32,640]{1,0:T(8,128)S(1)}, u32[]{:S(2)}, u32[]{:S(2)}) collective-permute-start(f32[32,640]{1,0:T(8,128)S(1)} %get-tuple-element.24), channel_id=1, source_target_pairs={{0,48},{16,0},{32,16},{48,32},{64,112},{80,64},{96,80},{112,96},{1... | collective-permute-start | bytes 245768 | tf_op jit(solution)/shard_map/ppermute | solution.py:68
  55.9 5.7 %collective-permute-start.8 = (f32[32,640]{1,0:T(8,128)S(1)}, f32[32,640]{1,0:T(8,128)S(1)}, u32[]{:S(2)}, u32[]{:S(2)}) collective-permute-start(f32[32,640]{1,0:T(8,128)S(1)} %get-tuple-element.25), channel_id=1, source_target_pairs={{0,16},{16,32},{32,48},{48,0},{64,80},{80,96},{96,112},{112,64},{1... | collective-permute-start | bytes 245768 | tf_op jit(solution)/shard_map/ppermute | solution.py:67
  56.4 7.3 %collective-permute-start.16 = (f32[32,640]{1,0:T(8,128)S(1)}, f32[32,640]{1,0:T(8,128)S(1)}, u32[]{:S(2)}, u32[]{:S(2)}) collective-permute-start(f32[32,640]{1,0:T(8,128)S(1)} %get-tuple-element.19), channel_id=1, source_target_pairs={{0,16},{16,32},{32,48},{48,0},{64,80},{80,96},{96,112},{112,64},{1... | collective-permute-start | bytes 245768 | tf_op jit(solution)/shard_map/ppermute | solution.py:67
  58.4 5.3 %collective-permute-start.19 = (f32[32,640]{1,0:T(8,128)S(1)}, f32[32,640]{1,0:T(8,128)S(1)}, u32[]{:S(2)}, u32[]{:S(2)}) collective-permute-start(f32[32,640]{1,0:T(8,128)S(1)} %get-tuple-element.18), channel_id=1, source_target_pairs={{0,48},{16,0},{32,16},{48,32},{64,112},{80,64},{96,80},{112,96},{1... | collective-permute-start | bytes 245768 | tf_op jit(solution)/shard_map/ppermute | solution.py:68
  61.5 5.4 %collective-permute-start.12 = (f32[32,640]{1,0:T(8,128)S(1)}, f32[32,640]{1,0:T(8,128)S(1)}, u32[]{:S(2)}, u32[]{:S(2)}) collective-permute-start(f32[32,640]{1,0:T(8,128)S(1)} %get-tuple-element.22), channel_id=1, source_target_pairs={{0,48},{16,0},{32,16},{48,32},{64,112},{80,64},{96,80},{112,96},{1... | collective-permute-start | bytes 245768 | tf_op jit(solution)/shard_map/ppermute | solution.py:68
  62.1 5.7 %collective-permute-start.9 = (f32[32,640]{1,0:T(8,128)S(1)}, f32[32,640]{1,0:T(8,128)S(1)}, u32[]{:S(2)}, u32[]{:S(2)}) collective-permute-start(f32[32,640]{1,0:T(8,128)S(1)} %get-tuple-element.23), channel_id=1, source_target_pairs={{0,16},{16,32},{32,48},{48,0},{64,80},{80,96},{96,112},{112,64},{1... | collective-permute-start | bytes 245768 | tf_op jit(solution)/shard_map/ppermute | solution.py:67
  63.7 7.8 %collective-permute-start.17 = (f32[32,640]{1,0:T(8,128)S(1)}, f32[32,640]{1,0:T(8,128)S(1)}, u32[]{:S(2)}, u32[]{:S(2)}) collective-permute-start(f32[32,640]{1,0:T(8,128)S(1)} %get-tuple-element.17), channel_id=1, source_target_pairs={{0,16},{16,32},{32,48},{48,0},{64,80},{80,96},{96,112},{112,64},{1... | collective-permute-start | bytes 245768 | tf_op jit(solution)/shard_map/ppermute | solution.py:67
  64.7 6.8 %collective-permute-start.20 = (f32[32,640]{1,0:T(8,128)S(1)}, f32[32,640]{1,0:T(8,128)S(1)}, u32[]{:S(2)}, u32[]{:S(2)}) collective-permute-start(f32[32,640]{1,0:T(8,128)S(1)} %get-tuple-element.16), channel_id=1, source_target_pairs={{0,48},{16,0},{32,16},{48,32},{64,112},{80,64},{96,80},{112,96},{1... | collective-permute-start | bytes 245768 | tf_op jit(solution)/shard_map/ppermute | solution.py:68
  67.8 6.1 %collective-permute-start.13 = (f32[32,640]{1,0:T(8,128)S(1)}, f32[32,640]{1,0:T(8,128)S(1)}, u32[]{:S(2)}, u32[]{:S(2)}) collective-permute-start(f32[32,640]{1,0:T(8,128)S(1)} %broadcast_select_fusion.1), channel_id=1, source_target_pairs={{0,64},{16,80},{32,96},{48,112},{64,0},{80,16},{96,32},{112,48},{1... | collective-permute-start | bytes 245768 | tf_op jit(solution)/shard_map/ppermute | solution.py:71
  71.5 6.0 %collective-permute-start.21 = (f32[32,640]{1,0:T(8,128)S(1)}, f32[32,640]{1,0:T(8,128)S(1)}, u32[]{:S(2)}, u32[]{:S(2)}) collective-permute-start(f32[32,640]{1,0:T(8,128)S(1)} %broadcast_select_fusion), channel_id=1, source_target_pairs={{0,64},{16,80},{32,96},{48,112},{64,0},{80,16},{96,32},{112,48},{1... | collective-permute-start | bytes 245768 | tf_op jit(solution)/shard_map/ppermute | solution.py:71
  (3 other events, 10.6 us)

commit v10 on v5

--- a/solution.py
+++ b/solution.py
@@ -25,7 +25,8 @@
         return _pairs(n_occ, lambda i: (i // nx) * nx + (i % nx + s) % nx)
 
     z_swap = _pairs(n_vir, lambda j: j ^ (2 * ny))
-    core_swap = _pairs(n_vir, lambda j: j ^ 1)
+    to_odd = [(j, j + 1) for j in range(0, n_vir, 2)]
+    to_even = [(j + 1, j) for j in range(0, n_vir, 2)]
     zhi_swap = _pairs(n_occ, lambda i: (i + nx) % n_occ)
     slot_of = [0, 1, 3, 4, 5, 7, 2, 6]
 
@@ -51,7 +52,7 @@
         res_l = jnp.concatenate([res_own, matmul(local[rows:], half)], axis=0)
         local, res_l = lax.optimization_barrier((local, res_l))
         res_l = res_l.reshape(8, rows, -1)
-        other = lax.ppermute(local, "vir", core_swap)
+        other = lax.ppermute(local, "vir", to_odd) + lax.ppermute(local, "vir", to_even)
         res_o = matmul(other, half).reshape(8, rows, -1)
         table = jnp.array(slot_of, jnp.int32)
 

time: 79.4 us -> 84.7 us (1.067)
  starting transfers between devices: 23.5 us -> 27.2 us
    ppermute x1 -> x2, starting transfers between devices: 0.01 us -> 3.65 us  [the longest x1 2.37 us: body(): lax.ppermute(local, 'vir', to_odd) + lax.ppermute(local, 'vir', to_even)]
  transfers between devices with their start and end apart: 15 -> 16, of which waited for: 8 -> 9; matrix products, arithmetic and copies ran while one was open for 7% -> 7% of each run, Pallas kernels for 0% -> 0%
where the time goes in v10:
time: 84.7 us; the launch traced here: 84.4 us
  starting transfers between devices  27.2 us (32%)
  waiting for transfers between devices  24.9 us (29%)
  between operations  15.6 us (18%)
  matrix products  8.64 us (10%)
  local copies, waits for them, and re-layouts  6.19 us (7%)
  other arithmetic  1.86 us (2%)
    ppermute x3, waiting for transfers between devices, body(): sb = lax.ppermute(sb, 'occ', x_shift(-1)) + out_block(nx + (x + s + 1) % nx)  10.7 us
    ppermute x3, starting transfers between devices, body(): sb = lax.ppermute(sb, 'occ', x_shift(-1)) + out_block(nx + (x + s + 1) % nx)  10.3 us
    dot_general x3, matrix products, matmul(): return jnp.dot(a, b, preferred_element_type=jnp.float32, precision=HIGH)  8.64 us
    unnamed x15, local copies, waits for them, and re-layouts  4.82 us
    ppermute x1, waiting for transfers between devices, body(): yp1 = lax.ppermute(own, 'vir', y_shift(-1))  4.16 us
    ppermute x3, waiting for transfers between devices, body(): sa = lax.ppermute(sa, 'occ', x_shift(1)) + out_block((x - s - 1) % nx)  3.78 us
    ppermute x1, starting transfers between devices, body(): return keep + lax.ppermute(send, 'occ', zhi_swap)  3.66 us
    ppermute x1, waiting for transfers between devices, body(): return keep + lax.ppermute(send, 'occ', zhi_swap)  3.3 us
  transfers between devices with their start and end apart: 16, of which 9 were waited for; matrix products, arithmetic and copies ran while one was open for 7% of the time, Pallas kernels for 0%

profile of v10, /device:TPU:24, one launch (start us, length us, event | category | flops | bytes accessed | tf_op | source)
XLA Modules:
  0.0 84.4 jit_solution(18342919748322853426)
XLA Ops:
  0.0 2.9 %fusion.10 = f32[32,640]{1,0:T(8,128)S(1)} fusion(f32[32,1280]{1,0:T(8,128)} %param.3, f32[1280,640]{1,0:T(8,128)} %param.4), kind=kOutput, calls=%fused_computation.10 | convolution fusion | flops 158105600 | bytes 3522560 | tf_op jit(solution)/shard_map/dot_general | solution.py:34
  2.9 2.0 %collective-permute-start = (f32[32,1280]{1,0:T(8,128)S(1)}, f32[32,1280]{1,0:T(8,128)S(1)}, u32[]{:S(2)}, u32[]{:S(2)}) collective-permute-start(f32[32,1280]{1,0:T(8,128)S(1)} %copy-done.2), channel_id=1, source_target_pairs={{0,8},{1,9},{2,10},{3,11},{4,12},{5,13},{6,14},{7,15},{8,0},{9,1},... | collective-permute-start | bytes 491528 | tf_op jit(solution)/shard_map/ppermute | solution.py:44
  5.2 1.8 %collective-permute-start.2 = (f32[32,1280]{1,0:T(8,128)S(1)}, f32[32,1280]{1,0:T(8,128)S(1)}, u32[]{:S(2)}, u32[]{:S(2)}) collective-permute-start(f32[32,1280]{1,0:T(8,128)S(1)} %copy-done.2), channel_id=1, source_target_pairs={{0,6},{1,7},{2,0},{3,1},{4,2},{5,3},{6,4},{7,5},{8,14},{9,15},{10,... | collective-permute-start | bytes 491528 | tf_op jit(solution)/shard_map/ppermute | solution.py:46
  7.0 0.7 constant_dynamic-update-slice_fusion.7
  7.7 4.2 %collective-permute-done.2 = f32[32,1280]{1,0:T(8,128)S(1)} collective-permute-done((f32[32,1280]{1,0:T(8,128)S(1)}, f32[32,1280]{1,0:T(8,128)S(1)}, u32[]{:S(2)}, u32[]{:S(2)}) %collective-permute-start.2) | collective-permute-done | bytes 163872 | tf_op jit(solution)/shard_map/ppermute | solution.py:46
  12.7 2.8 %collective-permute-start.5 = (f32[32,1280]{1,0:T(8,128)S(1)}, f32[32,1280]{1,0:T(8,128)S(1)}, u32[]{:S(2)}, u32[]{:S(2)}) collective-permute-start(f32[32,1280]{1,0:T(8,128)S(1)} %collective-permute-done), channel_id=1, source_target_pairs={{0,2},{1,3},{2,4},{3,5},{4,6},{5,7},{6,0},{7,1},{8,10},{9,11},{10,... | collective-permute-start | bytes 491528 | tf_op jit(solution)/shard_map/ppermute | solution.py:49
  17.6 1.2 %collective-permute-done.4 = f32[32,1280]{1,0:T(8,128)S(1)} collective-permute-done((f32[32,1280]{1,0:T(8,128)S(1)}, f32[32,1280]{1,0:T(8,128)S(1)}, u32[]{:S(2)}, u32[]{:S(2)}) %collective-permute-start.4) | collective-permute-done | bytes 163872 | tf_op jit(solution)/shard_map/ppermute | solution.py:48
  18.8 1.6 %collective-permute-start.6 = (f32[32,1280]{1,0:T(8,128)S(1)}, f32[32,1280]{1,0:T(8,128)S(1)}, u32[]{:S(2)}, u32[]{:S(2)}) collective-permute-start(f32[32,1280]{1,0:T(8,128)S(1)} %collective-permute-done.4), channel_id=1, source_target_pairs={{0,8},{1,9},{2,10},{3,11},{4,12},{5,13},{6,14},{7,15},{8,0},{9,1},... | collective-permute-start | bytes 491528 | tf_op jit(solution)/shard_map/ppermute | solution.py:50
  22.4 1.7 %collective-permute-done.6 = f32[32,1280]{1,0:T(8,128)S(1)} collective-permute-done((f32[32,1280]{1,0:T(8,128)S(1)}, f32[32,1280]{1,0:T(8,128)S(1)}, u32[]{:S(2)}, u32[]{:S(2)}) %collective-permute-start.6) | collective-permute-done | bytes 163872 | tf_op jit(solution)/shard_map/ppermute | solution.py:50
  24.8 1.9 %fusion.2 = f32[224,640]{1,0:T(8,128)S(1)} fusion(f32[224,1280]{1,0:T(8,128)S(1)} %get-tuple-element.29, f32[1280,640]{1,0:T(8,128)S(1)} %copy-done), kind=kOutput, calls=%fused_computation.2 | convolution fusion | flops 1101824000 | bytes 4997120 | tf_op jit(solution)/shard_map/dot_general | solution.py:34
  26.7 0.9 %pad_maximum_fusion = f32[256,640]{1,0:T(8,128)} fusion(f32[224,640]{1,0:T(8,128)S(1)} %fusion.2, f32[32,640]{1,0:T(8,128)S(1)} %fusion.10), kind=kLoop, calls=%fused_computation.11 | loop fusion | flops 163840 | bytes 1310720 | tf_op jit(solution)/shard_map/concatenate | solution.py:52
  27.6 2.4 %collective-permute-start.7 = (f32[256,1280]{1,0:T(8,128)}, f32[256,1280]{1,0:T(8,128)}, u32[]{:S(2)}, u32[]{:S(2)}) collective-permute-start(f32[256,1280]{1,0:T(8,128)} %get-tuple-element.12), channel_id=1, source_target_pairs={{0,1},{2,3},{4,5},{6,7},{8,9},{10,11},{12,13},{14,15},{16,17},{18,... | collective-permute-start | bytes 3932168 | tf_op jit(solution)/shard_map/ppermute | solution.py:55
  29.9 1.3 %collective-permute-start.8 = (f32[256,1280]{1,0:T(8,128)}, f32[256,1280]{1,0:T(8,128)}, u32[]{:S(2)}, u32[]{:S(2)}) collective-permute-start(f32[256,1280]{1,0:T(8,128)} %get-tuple-element.12), channel_id=1, source_target_pairs={{1,0},{3,2},{5,4},{7,6},{9,8},{11,10},{13,12},{15,14},{17,16},{19,... | collective-permute-start | bytes 3932168 | tf_op jit(solution)/shard_map/ppermute | solution.py:55
  47.4 3.8 %fusion = f32[256,640]{1,0:T(8,128)S(1)} fusion(f32[1280,640]{1,0:T(8,128)S(1)} %copy-done, f32[256,1280]{1,0:T(8,128)} %collective-permute-done.7, f32[256,1280]{1,0:T(8,128)} %collective-permute-done.8), kind=kOutput, calls=%fused_computation | convolution fusion | flops 1259438080 | bytes 6553600 | tf_op jit(solution)/shard_map/dot_general | solution.py:34
  51.4 2.8 %collective-permute-start.12 = (f32[64,640]{1,0:T(8,128)S(1)}, f32[64,640]{1,0:T(8,128)S(1)}, u32[]{:S(2)}, u32[]{:S(2)}) collective-permute-start(f32[64,640]{1,0:T(8,128)S(1)} %pad_maximum_fusion.2), channel_id=1, source_target_pairs={{0,48},{16,0},{32,16},{48,32},{64,112},{80,64},{96,80},{112,96},{1... | collective-permute-start | bytes 491528 | tf_op jit(solution)/shard_map/ppermute | solution.py:75
  54.4 3.8 %collective-permute-done.12 = f32[64,640]{1,0:T(8,128)S(1)} collective-permute-done((f32[64,640]{1,0:T(8,128)S(1)}, f32[64,640]{1,0:T(8,128)S(1)}, u32[]{:S(2)}, u32[]{:S(2)}) %collective-permute-start.12) | collective-permute-done | bytes 163872 | tf_op jit(solution)/shard_map/ppermute | solution.py:75
  58.2 3.8 %collective-permute-start.13 = (f32[64,640]{1,0:T(8,128)S(1)}, f32[64,640]{1,0:T(8,128)S(1)}, u32[]{:S(2)}, u32[]{:S(2)}) collective-permute-start(f32[64,640]{1,0:T(8,128)S(1)} %maximum_add_fusion.3), channel_id=1, source_target_pairs={{0,48},{16,0},{32,16},{48,32},{64,112},{80,64},{96,80},{112,96},{1... | collective-permute-start | bytes 491528 | tf_op jit(solution)/shard_map/ppermute | solution.py:75
  62.3 3.8 %collective-permute-done.13 = f32[64,640]{1,0:T(8,128)S(1)} collective-permute-done((f32[64,640]{1,0:T(8,128)S(1)}, f32[64,640]{1,0:T(8,128)S(1)}, u32[]{:S(2)}, u32[]{:S(2)}) %collective-permute-start.13) | collective-permute-done | bytes 163872 | tf_op jit(solution)/shard_map/ppermute | solution.py:75
  66.1 3.8 %collective-permute-start.14 = (f32[64,640]{1,0:T(8,128)S(1)}, f32[64,640]{1,0:T(8,128)S(1)}, u32[]{:S(2)}, u32[]{:S(2)}) collective-permute-start(f32[64,640]{1,0:T(8,128)S(1)} %maximum_add_fusion.4), channel_id=1, source_target_pairs={{0,48},{16,0},{32,16},{48,32},{64,112},{80,64},{96,80},{112,96},{1... | collective-permute-start | bytes 491528 | tf_op jit(solution)/shard_map/ppermute | solution.py:75
  70.0 3.2 %collective-permute-done.14 = f32[64,640]{1,0:T(8,128)S(1)} collective-permute-done((f32[64,640]{1,0:T(8,128)S(1)}, f32[64,640]{1,0:T(8,128)S(1)}, u32[]{:S(2)}, u32[]{:S(2)}) %collective-permute-start.14) | collective-permute-done | bytes 163872 | tf_op jit(solution)/shard_map/ppermute | solution.py:75
  73.2 3.5 %collective-permute-done.11 = f32[64,640]{1,0:T(8,128)S(1)} collective-permute-done((f32[64,640]{1,0:T(8,128)S(1)}, f32[64,640]{1,0:T(8,128)S(1)}, u32[]{:S(2)}, u32[]{:S(2)}) %collective-permute-start.11) | collective-permute-done | bytes 163872 | tf_op jit(solution)/shard_map/ppermute | solution.py:74
  76.7 3.7 %collective-permute-start.15 = (f32[64,640]{1,0:T(8,128)S(1)}, f32[64,640]{1,0:T(8,128)S(1)}, u32[]{:S(2)}, u32[]{:S(2)}) collective-permute-start(f32[64,640]{1,0:T(8,128)S(1)} %broadcast_select_fusion), channel_id=1, source_target_pairs={{0,64},{16,80},{32,96},{48,112},{64,0},{80,16},{96,32},{112,48},{1... | collective-permute-start | bytes 491528 | tf_op jit(solution)/shard_map/ppermute | solution.py:78
  80.4 3.3 %collective-permute-done.15 = f32[64,640]{1,0:T(8,128)S(1)} collective-permute-done((f32[64,640]{1,0:T(8,128)S(1)}, f32[64,640]{1,0:T(8,128)S(1)}, u32[]{:S(2)}, u32[]{:S(2)}) %collective-permute-start.15) | collective-permute-done | bytes 163872 | tf_op jit(solution)/shard_map/ppermute | solution.py:78
  83.7 0.7 select_add_fusion
  (38 shorter events, 7.4 us)
Async XLA Ops:
  0.0 2.9 %copy-start.2 = (f32[32,1280]{1,0:T(8,128)S(1)}, f32[32,1280]{1,0:T(8,128)}, u32[]{:S(2)}) copy-start(f32[32,1280]{1,0:T(8,128)} %param.3) | copy-start | bytes 491524
  2.9 9.8 %collective-permute-start = (f32[32,1280]{1,0:T(8,128)S(1)}, f32[32,1280]{1,0:T(8,128)S(1)}, u32[]{:S(2)}, u32[]{:S(2)}) collective-permute-start(f32[32,1280]{1,0:T(8,128)S(1)} %copy-done.2), channel_id=1, source_target_pairs={{0,8},{1,9},{2,10},{3,11},{4,12},{5,13},{6,14},{7,15},{8,0},{9,1},... | collective-permute-start | bytes 491528 | tf_op jit(solution)/shard_map/ppermute | solution.py:44
  4.9 11.2 %collective-permute-start.1 = (f32[32,1280]{1,0:T(8,128)S(1)}, f32[32,1280]{1,0:T(8,128)S(1)}, u32[]{:S(2)}, u32[]{:S(2)}) collective-permute-start(f32[32,1280]{1,0:T(8,128)S(1)} %copy-done.2), channel_id=1, source_target_pairs={{0,2},{1,3},{2,4},{3,5},{4,6},{5,7},{6,0},{7,1},{8,10},{9,11},{10,... | collective-permute-start | bytes 491528 | tf_op jit(solution)/shard_map/ppermute | solution.py:45
  5.2 6.7 %collective-permute-start.2 = (f32[32,1280]{1,0:T(8,128)S(1)}, f32[32,1280]{1,0:T(8,128)S(1)}, u32[]{:S(2)}, u32[]{:S(2)}) collective-permute-start(f32[32,1280]{1,0:T(8,128)S(1)} %copy-done.2), channel_id=1, source_target_pairs={{0,6},{1,7},{2,0},{3,1},{4,2},{5,3},{6,4},{7,5},{8,14},{9,15},{10,... | collective-permute-start | bytes 491528 | tf_op jit(solution)/shard_map/ppermute | solution.py:46
  11.8 8.6 %collective-permute-start.3 = (f32[32,1280]{1,0:T(8,128)S(1)}, f32[32,1280]{1,0:T(8,128)S(1)}, u32[]{:S(2)}, u32[]{:S(2)}) collective-permute-start(f32[32,1280]{1,0:T(8,128)S(1)} %collective-permute-done.2), channel_id=1, source_target_pairs={{0,8},{1,9},{2,10},{3,11},{4,12},{5,13},{6,14},{7,15},{8,0},{9,1},... | collective-permute-start | bytes 491528 | tf_op jit(solution)/shard_map/ppermute | solution.py:47
  12.3 6.5 %collective-permute-start.4 = (f32[32,1280]{1,0:T(8,128)S(1)}, f32[32,1280]{1,0:T(8,128)S(1)}, u32[]{:S(2)}, u32[]{:S(2)}) collective-permute-start(f32[32,1280]{1,0:T(8,128)S(1)} %collective-permute-done.2), channel_id=1, source_target_pairs={{0,6},{1,7},{2,0},{3,1},{4,2},{5,3},{6,4},{7,5},{8,14},{9,15},{10,... | collective-permute-start | bytes 491528 | tf_op jit(solution)/shard_map/ppermute | solution.py:48
  12.7 9.0 %collective-permute-start.5 = (f32[32,1280]{1,0:T(8,128)S(1)}, f32[32,1280]{1,0:T(8,128)S(1)}, u32[]{:S(2)}, u32[]{:S(2)}) collective-permute-start(f32[32,1280]{1,0:T(8,128)S(1)} %collective-permute-done), channel_id=1, source_target_pairs={{0,2},{1,3},{2,4},{3,5},{4,6},{5,7},{6,0},{7,1},{8,10},{9,11},{10,... | collective-permute-start | bytes 491528 | tf_op jit(solution)/shard_map/ppermute | solution.py:49
  15.5 9.3 %copy-start = (f32[1280,640]{1,0:T(8,128)S(1)}, f32[1280,640]{1,0:T(8,128)}, u32[]{:S(2)}) copy-start(f32[1280,640]{1,0:T(8,128)} %param.4) | copy-start | bytes 9830404
  18.8 5.3 %collective-permute-start.6 = (f32[32,1280]{1,0:T(8,128)S(1)}, f32[32,1280]{1,0:T(8,128)S(1)}, u32[]{:S(2)}, u32[]{:S(2)}) collective-permute-start(f32[32,1280]{1,0:T(8,128)S(1)} %collective-permute-done.4), channel_id=1, source_target_pairs={{0,8},{1,9},{2,10},{3,11},{4,12},{5,13},{6,14},{7,15},{8,0},{9,1},... | collective-permute-start | bytes 491528 | tf_op jit(solution)/shard_map/ppermute | solution.py:50
  26.7 5.0 %copy-start.3 = (s32[8]{0:T(128)S(1)}, s32[8]{0:T(128)}, u32[]{:S(2)}) copy-start(s32[8]{0:T(128)} %constant.274.clone) | copy-start | bytes 100
  27.6 19.8 %collective-permute-start.7 = (f32[256,1280]{1,0:T(8,128)}, f32[256,1280]{1,0:T(8,128)}, u32[]{:S(2)}, u32[]{:S(2)}) collective-permute-start(f32[256,1280]{1,0:T(8,128)} %get-tuple-element.12), channel_id=1, source_target_pairs={{0,1},{2,3},{4,5},{6,7},{8,9},{10,11},{12,13},{14,15},{16,17},{18,... | collective-permute-start | bytes 3932168 | tf_op jit(solution)/shard_map/ppermute | solution.py:55
  29.9 17.5 %collective-permute-start.8 = (f32[256,1280]{1,0:T(8,128)}, f32[256,1280]{1,0:T(8,128)}, u32[]{:S(2)}, u32[]{:S(2)}) collective-permute-start(f32[256,1280]{1,0:T(8,128)} %get-tuple-element.12), channel_id=1, source_target_pairs={{1,0},{3,2},{5,4},{7,6},{9,8},{11,10},{13,12},{15,14},{17,16},{19,... | collective-permute-start | bytes 3932168 | tf_op jit(solution)/shard_map/ppermute | solution.py:55
  47.4 3.9 %copy-start.1 = (f32[256,640]{1,0:T(8,128)S(1)}, f32[256,640]{1,0:T(8,128)}, u32[]{:S(2)}) copy-start(f32[256,640]{1,0:T(8,128)} %pad_maximum_fusion) | copy-start | bytes 1966084
  51.4 6.7 %collective-permute-start.12 = (f32[64,640]{1,0:T(8,128)S(1)}, f32[64,640]{1,0:T(8,128)S(1)}, u32[]{:S(2)}, u32[]{:S(2)}) collective-permute-start(f32[64,640]{1,0:T(8,128)S(1)} %pad_maximum_fusion.2), channel_id=1, source_target_pairs={{0,48},{16,0},{32,16},{48,32},{64,112},{80,64},{96,80},{112,96},{1... | collective-permute-start | bytes 491528 | tf_op jit(solution)/shard_map/ppermute | solution.py:75
  54.3 7.9 %collective-permute-start.9 = (f32[64,640]{1,0:T(8,128)S(1)}, f32[64,640]{1,0:T(8,128)S(1)}, u32[]{:S(2)}, u32[]{:S(2)}) collective-permute-start(f32[64,640]{1,0:T(8,128)S(1)} %pad_maximum_fusion.1), channel_id=1, source_target_pairs={{0,16},{16,32},{32,48},{48,0},{64,80},{80,96},{96,112},{112,64},{1... | collective-permute-start | bytes 491528 | tf_op jit(solution)/shard_map/ppermute | solution.py:74
  58.2 7.9 %collective-permute-start.13 = (f32[64,640]{1,0:T(8,128)S(1)}, f32[64,640]{1,0:T(8,128)S(1)}, u32[]{:S(2)}, u32[]{:S(2)}) collective-permute-start(f32[64,640]{1,0:T(8,128)S(1)} %maximum_add_fusion.3), channel_id=1, source_target_pairs={{0,48},{16,0},{32,16},{48,32},{64,112},{80,64},{96,80},{112,96},{1... | collective-permute-start | bytes 491528 | tf_op jit(solution)/shard_map/ppermute | solution.py:75
  62.2 7.7 %collective-permute-start.10 = (f32[64,640]{1,0:T(8,128)S(1)}, f32[64,640]{1,0:T(8,128)S(1)}, u32[]{:S(2)}, u32[]{:S(2)}) collective-permute-start(f32[64,640]{1,0:T(8,128)S(1)} %maximum_add_fusion), channel_id=1, source_target_pairs={{0,16},{16,32},{32,48},{48,0},{64,80},{80,96},{96,112},{112,64},{1... | collective-permute-start | bytes 491528 | tf_op jit(solution)/shard_map/ppermute | solution.py:74
  66.1 7.1 %collective-permute-start.14 = (f32[64,640]{1,0:T(8,128)S(1)}, f32[64,640]{1,0:T(8,128)S(1)}, u32[]{:S(2)}, u32[]{:S(2)}) collective-permute-start(f32[64,640]{1,0:T(8,128)S(1)} %maximum_add_fusion.4), channel_id=1, source_target_pairs={{0,48},{16,0},{32,16},{48,32},{64,112},{80,64},{96,80},{112,96},{1... | collective-permute-start | bytes 491528 | tf_op jit(solution)/shard_map/ppermute | solution.py:75
  69.9 6.8 %collective-permute-start.11 = (f32[64,640]{1,0:T(8,128)S(1)}, f32[64,640]{1,0:T(8,128)S(1)}, u32[]{:S(2)}, u32[]{:S(2)}) collective-permute-start(f32[64,640]{1,0:T(8,128)S(1)} %maximum_add_fusion.1), channel_id=1, source_target_pairs={{0,16},{16,32},{32,48},{48,0},{64,80},{80,96},{96,112},{112,64},{1... | collective-permute-start | bytes 491528 | tf_op jit(solution)/shard_map/ppermute | solution.py:74
  76.7 7.0 %collective-permute-start.15 = (f32[64,640]{1,0:T(8,128)S(1)}, f32[64,640]{1,0:T(8,128)S(1)}, u32[]{:S(2)}, u32[]{:S(2)}) collective-permute-start(f32[64,640]{1,0:T(8,128)S(1)} %broadcast_select_fusion), channel_id=1, source_target_pairs={{0,64},{16,80},{32,96},{48,112},{64,0},{80,16},{96,32},{112,48},{1... | collective-permute-start | bytes 491528 | tf_op jit(solution)/shard_map/ppermute | solution.py:78

commit v11 on v5

--- a/solution.py
+++ b/solution.py
@@ -27,7 +27,6 @@
     z_swap = _pairs(n_vir, lambda j: j ^ (2 * ny))
     core_swap = _pairs(n_vir, lambda j: j ^ 1)
     zhi_swap = _pairs(n_occ, lambda i: (i + nx) % n_occ)
-    slot_of = [0, 1, 3, 4, 5, 7, 2, 6]
 
     def matmul(a, b):
         return jnp.dot(a, b, preferred_element_type=jnp.float32, precision=HIGH)
@@ -47,18 +46,17 @@
         yp2 = lax.ppermute(yp1, "vir", y_shift(-1))
         ym1z = lax.ppermute(z1, "vir", y_shift(1))
         z3 = lax.ppermute(yp2, "vir", z_swap)
-        local = jnp.concatenate([own, z1, ym1, yp1, z2, yp2, ym1z, z3], axis=0)
+        local = jnp.concatenate([own, z1, yp1, z2, yp2, z3, ym1, ym1z], axis=0)
         res_l = jnp.concatenate([res_own, matmul(local[rows:], half)], axis=0)
         local, res_l = lax.optimization_barrier((local, res_l))
         res_l = res_l.reshape(8, rows, -1)
         other = lax.ppermute(local, "vir", core_swap)
         res_o = matmul(other, half).reshape(8, rows, -1)
-        table = jnp.array(slot_of, jnp.int32)
 
         def out_block(r):
             dy = (r % nx - y) % ny
             dz = (r // nx) ^ zl
-            k = table[dy * 2 + dz]
+            k = dy * 2 + dz
             lk = lax.dynamic_index_in_dim(res_l, k, 0, keepdims=False)
             ok = lax.dynamic_index_in_dim(res_o, k, 0, keepdims=False)
             first = jnp.where(c == 0, lk, ok)

time: 79.4 us -> 67.3 us (0.85)
  between operations: 15.1 us -> 0.11 us
  waiting for transfers between devices: 24.1 us -> 26.8 us
  starting transfers between devices: 23.5 us -> 24.8 us
    ppermute x1, waiting for transfers between devices: 0.01 us -> 3.37 us  [body(): other = lax.ppermute(local, 'vir', core_swap)]
    ppermute x1, starting transfers between devices: 0.22 us -> 2.49 us  [body(): ym1 = lax.ppermute(own, 'vir', y_shift(1))]
    ppermute x1, waiting for transfers between devices: 4.18 us -> 2.96 us  [body(): yp1 = lax.ppermute(own, 'vir', y_shift(-1))]
    ppermute x1, starting transfers between devices: 1.8 us -> 0.74 us  [body(): yp1 = lax.ppermute(own, 'vir', y_shift(-1))]
    unnamed x15 -> x13, local copies, waits for them, and re-layouts: 4.81 us -> 4.77 us
  transfers between devices with their start and end apart: 15 -> 15, of which waited for: 8 -> 9; matrix products, arithmetic and copies ran while one was open for 7% -> 7% of each run, Pallas kernels for 0% -> 0%
where the time goes in v11:
time: 67.3 us; the launch traced here: 67.2 us
  waiting for transfers between devices  26.8 us (40%)
  starting transfers between devices  24.8 us (37%)
  matrix products  8.16 us (12%)
  local copies, waits for them, and re-layouts  5.46 us (8%)
  other arithmetic  1.89 us (3%)
    ppermute x3, starting transfers between devices, body(): sb = lax.ppermute(sb, 'occ', x_shift(-1)) + out_block(nx + (x + s + 1) % nx)  10.3 us
    ppermute x3, waiting for transfers between devices, body(): sb = lax.ppermute(sb, 'occ', x_shift(-1)) + out_block(nx + (x + s + 1) % nx)  9.17 us
    dot_general x3, matrix products, matmul(): return jnp.dot(a, b, preferred_element_type=jnp.float32, precision=HIGH)  8.16 us
    unnamed x13, local copies, waits for them, and re-layouts  4.77 us
    ppermute x3, waiting for transfers between devices, body(): sa = lax.ppermute(sa, 'occ', x_shift(1)) + out_block((x - s - 1) % nx)  3.79 us
    ppermute x1, starting transfers between devices, body(): return keep + lax.ppermute(send, 'occ', zhi_swap)  3.7 us
    ppermute x1, waiting for transfers between devices, body(): other = lax.ppermute(local, 'vir', core_swap)  3.37 us
    ppermute x1, waiting for transfers between devices, body(): return keep + lax.ppermute(send, 'occ', zhi_swap)  3.3 us
  transfers between devices with their start and end apart: 15, of which 9 were waited for; matrix products, arithmetic and copies ran while one was open for 7% of the time, Pallas kernels for 0%

profile of v11, /device:TPU:24, one launch (start us, length us, event | category | flops | bytes accessed | tf_op | source)
XLA Modules:
  0.0 67.2 jit_solution(9890375776070453790)
XLA Ops:
  0.0 2.9 %fusion.9 = f32[32,640]{1,0:T(8,128)S(1)} fusion(f32[32,1280]{1,0:T(8,128)} %param.2, f32[1280,640]{1,0:T(8,128)} %param.3), kind=kOutput, calls=%fused_computation.9 | convolution fusion | flops 158105600 | bytes 3522560 | tf_op jit(solution)/shard_map/dot_general | solution.py:32
  2.9 2.0 %collective-permute-start = (f32[32,1280]{1,0:T(8,128)S(1)}, f32[32,1280]{1,0:T(8,128)S(1)}, u32[]{:S(2)}, u32[]{:S(2)}) collective-permute-start(f32[32,1280]{1,0:T(8,128)S(1)} %copy-done.2), channel_id=1, source_target_pairs={{0,8},{1,9},{2,10},{3,11},{4,12},{5,13},{6,14},{7,15},{8,0},{9,1},... | collective-permute-start | bytes 491528 | tf_op jit(solution)/shard_map/ppermute | solution.py:42
  4.9 0.7 %collective-permute-start.1 = (f32[32,1280]{1,0:T(8,128)S(1)}, f32[32,1280]{1,0:T(8,128)S(1)}, u32[]{:S(2)}, u32[]{:S(2)}) collective-permute-start(f32[32,1280]{1,0:T(8,128)S(1)} %copy-done.2), channel_id=1, source_target_pairs={{0,6},{1,7},{2,0},{3,1},{4,2},{5,3},{6,4},{7,5},{8,14},{9,15},{10,... | collective-permute-start | bytes 491528 | tf_op jit(solution)/shard_map/ppermute | solution.py:44
  5.7 2.5 %collective-permute-start.5 = (f32[32,1280]{1,0:T(8,128)S(1)}, f32[32,1280]{1,0:T(8,128)S(1)}, u32[]{:S(2)}, u32[]{:S(2)}) collective-permute-start(f32[32,1280]{1,0:T(8,128)S(1)} %copy-done.2), channel_id=1, source_target_pairs={{0,2},{1,3},{2,4},{3,5},{4,6},{5,7},{6,0},{7,1},{8,10},{9,11},{10,... | collective-permute-start | bytes 491528 | tf_op jit(solution)/shard_map/ppermute | solution.py:43
  8.8 3.0 %collective-permute-done.1 = f32[32,1280]{1,0:T(8,128)S(1)} collective-permute-done((f32[32,1280]{1,0:T(8,128)S(1)}, f32[32,1280]{1,0:T(8,128)S(1)}, u32[]{:S(2)}, u32[]{:S(2)}) %collective-permute-start.1) | collective-permute-done | bytes 163872 | tf_op jit(solution)/shard_map/ppermute | solution.py:44
  12.2 3.2 %collective-permute-start.6 = (f32[32,1280]{1,0:T(8,128)S(1)}, f32[32,1280]{1,0:T(8,128)S(1)}, u32[]{:S(2)}, u32[]{:S(2)}) collective-permute-start(f32[32,1280]{1,0:T(8,128)S(1)} %collective-permute-done), channel_id=1, source_target_pairs={{0,2},{1,3},{2,4},{3,5},{4,6},{5,7},{6,0},{7,1},{8,10},{9,11},{10,... | collective-permute-start | bytes 491528 | tf_op jit(solution)/shard_map/ppermute | solution.py:47
  16.8 1.9 %collective-permute-done.3 = f32[32,1280]{1,0:T(8,128)S(1)} collective-permute-done((f32[32,1280]{1,0:T(8,128)S(1)}, f32[32,1280]{1,0:T(8,128)S(1)}, u32[]{:S(2)}, u32[]{:S(2)}) %collective-permute-start.3) | collective-permute-done | bytes 163872 | tf_op jit(solution)/shard_map/ppermute | solution.py:46
  18.7 1.7 %collective-permute-start.4 = (f32[32,1280]{1,0:T(8,128)S(1)}, f32[32,1280]{1,0:T(8,128)S(1)}, u32[]{:S(2)}, u32[]{:S(2)}) collective-permute-start(f32[32,1280]{1,0:T(8,128)S(1)} %collective-permute-done.3), channel_id=1, source_target_pairs={{0,8},{1,9},{2,10},{3,11},{4,12},{5,13},{6,14},{7,15},{8,0},{9,1},... | collective-permute-start | bytes 491528 | tf_op jit(solution)/shard_map/ppermute | solution.py:48
  21.7 2.3 %collective-permute-done.4 = f32[32,1280]{1,0:T(8,128)S(1)} collective-permute-done((f32[32,1280]{1,0:T(8,128)S(1)}, f32[32,1280]{1,0:T(8,128)S(1)}, u32[]{:S(2)}, u32[]{:S(2)}) %collective-permute-start.4) | collective-permute-done | bytes 163872 | tf_op jit(solution)/shard_map/ppermute | solution.py:48
  24.7 0.7 %constant_dynamic-update-slice_fusion.9 = (f32[224,1280]{1,0:T(8,128)S(1)}, f32[256,1280]{1,0:T(8,128)}) fusion(f32[224,1280]{1,0:T(8,128)S(1)} %get-tuple-element.33, f32[32,1280]{1,0:T(8,128)S(1)} %collective-permute-done.5, f32[256,1280]{1,0:T(8,128)} %get-tuple-element.34), kind=kLoop, calls=%fused_computation.46 | loop fusion | bytes 491520
  26.1 1.9 %fusion.2 = f32[224,640]{1,0:T(8,128)S(1)} fusion(f32[224,1280]{1,0:T(8,128)S(1)} %get-tuple-element.29, f32[1280,640]{1,0:T(8,128)S(1)} %copy-done), kind=kOutput, calls=%fused_computation.2 | convolution fusion | flops 1101824000 | bytes 4997120 | tf_op jit(solution)/shard_map/dot_general | solution.py:32
  28.0 0.9 %pad_maximum_fusion = f32[256,640]{1,0:T(8,128)} fusion(f32[224,640]{1,0:T(8,128)S(1)} %fusion.2, f32[32,640]{1,0:T(8,128)S(1)} %fusion.9), kind=kLoop, calls=%fused_computation.10 | loop fusion | flops 163840 | bytes 1310720 | tf_op jit(solution)/shard_map/concatenate | solution.py:50
  28.8 3.4 %collective-permute-done.7 = f32[256,1280]{1,0:T(8,128)} collective-permute-done((f32[256,1280]{1,0:T(8,128)}, f32[256,1280]{1,0:T(8,128)}, u32[]{:S(2)}, u32[]{:S(2)}) %collective-permute-start.7) | collective-permute-done | bytes 1310752 | tf_op jit(solution)/shard_map/ppermute | solution.py:53
  32.2 3.3 %fusion = f32[256,640]{1,0:T(8,128)S(1)} fusion(f32[256,1280]{1,0:T(8,128)} %collective-permute-done.7, f32[1280,640]{1,0:T(8,128)S(1)} %copy-done), kind=kOutput, calls=%fused_computation | convolution fusion | flops 1259110400 | bytes 5242880 | tf_op jit(solution)/shard_map/dot_general | solution.py:32
  35.8 2.8 %collective-permute-start.11 = (f32[64,640]{1,0:T(8,128)S(1)}, f32[64,640]{1,0:T(8,128)S(1)}, u32[]{:S(2)}, u32[]{:S(2)}) collective-permute-start(f32[64,640]{1,0:T(8,128)S(1)} %pad_maximum_fusion.2), channel_id=1, source_target_pairs={{0,48},{16,0},{32,16},{48,32},{64,112},{80,64},{96,80},{112,96},{1... | collective-permute-start | bytes 491528 | tf_op jit(solution)/shard_map/ppermute | solution.py:72
  38.7 3.7 %collective-permute-done.11 = f32[64,640]{1,0:T(8,128)S(1)} collective-permute-done((f32[64,640]{1,0:T(8,128)S(1)}, f32[64,640]{1,0:T(8,128)S(1)}, u32[]{:S(2)}, u32[]{:S(2)}) %collective-permute-start.11) | collective-permute-done | bytes 163872 | tf_op jit(solution)/shard_map/ppermute | solution.py:72
  42.4 3.8 %collective-permute-start.12 = (f32[64,640]{1,0:T(8,128)S(1)}, f32[64,640]{1,0:T(8,128)S(1)}, u32[]{:S(2)}, u32[]{:S(2)}) collective-permute-start(f32[64,640]{1,0:T(8,128)S(1)} %maximum_add_fusion.3), channel_id=1, source_target_pairs={{0,48},{16,0},{32,16},{48,32},{64,112},{80,64},{96,80},{112,96},{1... | collective-permute-start | bytes 491528 | tf_op jit(solution)/shard_map/ppermute | solution.py:72
  46.2 2.8 %collective-permute-done.12 = f32[64,640]{1,0:T(8,128)S(1)} collective-permute-done((f32[64,640]{1,0:T(8,128)S(1)}, f32[64,640]{1,0:T(8,128)S(1)}, u32[]{:S(2)}, u32[]{:S(2)}) %collective-permute-start.12) | collective-permute-done | bytes 163872 | tf_op jit(solution)/shard_map/ppermute | solution.py:72
  49.1 3.8 %collective-permute-start.13 = (f32[64,640]{1,0:T(8,128)S(1)}, f32[64,640]{1,0:T(8,128)S(1)}, u32[]{:S(2)}, u32[]{:S(2)}) collective-permute-start(f32[64,640]{1,0:T(8,128)S(1)} %maximum_add_fusion.4), channel_id=1, source_target_pairs={{0,48},{16,0},{32,16},{48,32},{64,112},{80,64},{96,80},{112,96},{1... | collective-permute-start | bytes 491528 | tf_op jit(solution)/shard_map/ppermute | solution.py:72
  52.9 2.7 %collective-permute-done.13 = f32[64,640]{1,0:T(8,128)S(1)} collective-permute-done((f32[64,640]{1,0:T(8,128)S(1)}, f32[64,640]{1,0:T(8,128)S(1)}, u32[]{:S(2)}, u32[]{:S(2)}) %collective-permute-start.13) | collective-permute-done | bytes 163872 | tf_op jit(solution)/shard_map/ppermute | solution.py:72
  55.7 3.8 %collective-permute-done.10 = f32[64,640]{1,0:T(8,128)S(1)} collective-permute-done((f32[64,640]{1,0:T(8,128)S(1)}, f32[64,640]{1,0:T(8,128)S(1)}, u32[]{:S(2)}, u32[]{:S(2)}) %collective-permute-start.10) | collective-permute-done | bytes 163872 | tf_op jit(solution)/shard_map/ppermute | solution.py:71
  59.5 3.7 %collective-permute-start.14 = (f32[64,640]{1,0:T(8,128)S(1)}, f32[64,640]{1,0:T(8,128)S(1)}, u32[]{:S(2)}, u32[]{:S(2)}) collective-permute-start(f32[64,640]{1,0:T(8,128)S(1)} %broadcast_select_fusion), channel_id=1, source_target_pairs={{0,64},{16,80},{32,96},{48,112},{64,0},{80,16},{96,32},{112,48},{1... | collective-permute-start | bytes 491528 | tf_op jit(solution)/shard_map/ppermute | solution.py:75
  63.2 3.3 %collective-permute-done.14 = f32[64,640]{1,0:T(8,128)S(1)} collective-permute-done((f32[64,640]{1,0:T(8,128)S(1)}, f32[64,640]{1,0:T(8,128)S(1)}, u32[]{:S(2)}, u32[]{:S(2)}) %collective-permute-start.14) | collective-permute-done | bytes 163872 | tf_op jit(solution)/shard_map/ppermute | solution.py:75
  66.5 0.7 %select_add_fusion = f32[64,640]{1,0:T(8,128)} fusion(f32[64,640]{1,0:T(8,128)S(1)} %collective-permute-done.14, pred[]{:T(512)S(6)} %eq.50, f32[64,640]{1,0:T(8,128)S(1)} %collective-permute-done.13, f32[32,640]{1,0:T(8,128)S(1)} %get-tuple-element.21, f32[32,640]{1,0:T(8,128)S(1)} %get-tuple-element.22, f32[64,640]{1,0:T(8,128)S(1)} %collective-permute-done.10, ...), kind=kLoop, calls=%fused_computation.19 | loop fusion | flops 245760 | bytes 983041 | tf_op jit(solution)/shard_map/add | solution.py:75
  (33 shorter events, 5.7 us)
Async XLA Ops:
  0.0 2.9 %copy-start.2 = (f32[32,1280]{1,0:T(8,128)S(1)}, f32[32,1280]{1,0:T(8,128)}, u32[]{:S(2)}) copy-start(f32[32,1280]{1,0:T(8,128)} %param.2) | copy-start | bytes 491524
  2.9 9.2 %collective-permute-start = (f32[32,1280]{1,0:T(8,128)S(1)}, f32[32,1280]{1,0:T(8,128)S(1)}, u32[]{:S(2)}, u32[]{:S(2)}) collective-permute-start(f32[32,1280]{1,0:T(8,128)S(1)} %copy-done.2), channel_id=1, source_target_pairs={{0,8},{1,9},{2,10},{3,11},{4,12},{5,13},{6,14},{7,15},{8,0},{9,1},... | collective-permute-start | bytes 491528 | tf_op jit(solution)/shard_map/ppermute | solution.py:42
  4.9 6.9 %collective-permute-start.1 = (f32[32,1280]{1,0:T(8,128)S(1)}, f32[32,1280]{1,0:T(8,128)S(1)}, u32[]{:S(2)}, u32[]{:S(2)}) collective-permute-start(f32[32,1280]{1,0:T(8,128)S(1)} %copy-done.2), channel_id=1, source_target_pairs={{0,6},{1,7},{2,0},{3,1},{4,2},{5,3},{6,4},{7,5},{8,14},{9,15},{10,... | collective-permute-start | bytes 491528 | tf_op jit(solution)/shard_map/ppermute | solution.py:44
  5.7 19.0 %collective-permute-start.5 = (f32[32,1280]{1,0:T(8,128)S(1)}, f32[32,1280]{1,0:T(8,128)S(1)}, u32[]{:S(2)}, u32[]{:S(2)}) collective-permute-start(f32[32,1280]{1,0:T(8,128)S(1)} %copy-done.2), channel_id=1, source_target_pairs={{0,2},{1,3},{2,4},{3,5},{4,6},{5,7},{6,0},{7,1},{8,10},{9,11},{10,... | collective-permute-start | bytes 491528 | tf_op jit(solution)/shard_map/ppermute | solution.py:43
  11.8 8.6 %collective-permute-start.2 = (f32[32,1280]{1,0:T(8,128)S(1)}, f32[32,1280]{1,0:T(8,128)S(1)}, u32[]{:S(2)}, u32[]{:S(2)}) collective-permute-start(f32[32,1280]{1,0:T(8,128)S(1)} %collective-permute-done.1), channel_id=1, source_target_pairs={{0,8},{1,9},{2,10},{3,11},{4,12},{5,13},{6,14},{7,15},{8,0},{9,1},... | collective-permute-start | bytes 491528 | tf_op jit(solution)/shard_map/ppermute | solution.py:45
  12.2 6.5 %collective-permute-start.3 = (f32[32,1280]{1,0:T(8,128)S(1)}, f32[32,1280]{1,0:T(8,128)S(1)}, u32[]{:S(2)}, u32[]{:S(2)}) collective-permute-start(f32[32,1280]{1,0:T(8,128)S(1)} %collective-permute-done.1), channel_id=1, source_target_pairs={{0,6},{1,7},{2,0},{3,1},{4,2},{5,3},{6,4},{7,5},{8,14},{9,15},{10,... | collective-permute-start | bytes 491528 | tf_op jit(solution)/shard_map/ppermute | solution.py:46
  12.2 13.2 %collective-permute-start.6 = (f32[32,1280]{1,0:T(8,128)S(1)}, f32[32,1280]{1,0:T(8,128)S(1)}, u32[]{:S(2)}, u32[]{:S(2)}) collective-permute-start(f32[32,1280]{1,0:T(8,128)S(1)} %collective-permute-done), channel_id=1, source_target_pairs={{0,2},{1,3},{2,4},{3,5},{4,6},{5,7},{6,0},{7,1},{8,10},{9,11},{10,... | collective-permute-start | bytes 491528 | tf_op jit(solution)/shard_map/ppermute | solution.py:47
  15.4 10.7 %copy-start = (f32[1280,640]{1,0:T(8,128)S(1)}, f32[1280,640]{1,0:T(8,128)}, u32[]{:S(2)}) copy-start(f32[1280,640]{1,0:T(8,128)} %param.3) | copy-start | bytes 9830404
  18.7 5.3 %collective-permute-start.4 = (f32[32,1280]{1,0:T(8,128)S(1)}, f32[32,1280]{1,0:T(8,128)S(1)}, u32[]{:S(2)}, u32[]{:S(2)}) collective-permute-start(f32[32,1280]{1,0:T(8,128)S(1)} %collective-permute-done.3), channel_id=1, source_target_pairs={{0,8},{1,9},{2,10},{3,11},{4,12},{5,13},{6,14},{7,15},{8,0},{9,1},... | collective-permute-start | bytes 491528 | tf_op jit(solution)/shard_map/ppermute | solution.py:48
  28.8 3.4 %collective-permute-start.7 = (f32[256,1280]{1,0:T(8,128)}, f32[256,1280]{1,0:T(8,128)}, u32[]{:S(2)}, u32[]{:S(2)}) collective-permute-start(f32[256,1280]{1,0:T(8,128)} %get-tuple-element.12), channel_id=1, source_target_pairs={{0,1},{1,0},{2,3},{3,2},{4,5},{5,4},{6,7},{7,6},{8,9},{9,8},{10,11... | collective-permute-start | bytes 3932168 | tf_op jit(solution)/shard_map/ppermute | solution.py:53
  28.8 6.7 %copy-start.1 = (f32[256,640]{1,0:T(8,128)S(1)}, f32[256,640]{1,0:T(8,128)}, u32[]{:S(2)}) copy-start(f32[256,640]{1,0:T(8,128)} %pad_maximum_fusion) | copy-start | bytes 1966084
  35.8 6.6 %collective-permute-start.11 = (f32[64,640]{1,0:T(8,128)S(1)}, f32[64,640]{1,0:T(8,128)S(1)}, u32[]{:S(2)}, u32[]{:S(2)}) collective-permute-start(f32[64,640]{1,0:T(8,128)S(1)} %pad_maximum_fusion.2), channel_id=1, source_target_pairs={{0,48},{16,0},{32,16},{48,32},{64,112},{80,64},{96,80},{112,96},{1... | collective-permute-start | bytes 491528 | tf_op jit(solution)/shard_map/ppermute | solution.py:72
  38.6 7.5 %collective-permute-start.8 = (f32[64,640]{1,0:T(8,128)S(1)}, f32[64,640]{1,0:T(8,128)S(1)}, u32[]{:S(2)}, u32[]{:S(2)}) collective-permute-start(f32[64,640]{1,0:T(8,128)S(1)} %pad_maximum_fusion.1), channel_id=1, source_target_pairs={{0,16},{16,32},{32,48},{48,0},{64,80},{80,96},{96,112},{112,64},{1... | collective-permute-start | bytes 491528 | tf_op jit(solution)/shard_map/ppermute | solution.py:71
  42.4 6.7 %collective-permute-start.12 = (f32[64,640]{1,0:T(8,128)S(1)}, f32[64,640]{1,0:T(8,128)S(1)}, u32[]{:S(2)}, u32[]{:S(2)}) collective-permute-start(f32[64,640]{1,0:T(8,128)S(1)} %maximum_add_fusion.3), channel_id=1, source_target_pairs={{0,48},{16,0},{32,16},{48,32},{64,112},{80,64},{96,80},{112,96},{1... | collective-permute-start | bytes 491528 | tf_op jit(solution)/shard_map/ppermute | solution.py:72
  46.2 6.7 %collective-permute-start.9 = (f32[64,640]{1,0:T(8,128)S(1)}, f32[64,640]{1,0:T(8,128)S(1)}, u32[]{:S(2)}, u32[]{:S(2)}) collective-permute-start(f32[64,640]{1,0:T(8,128)S(1)} %maximum_add_fusion), channel_id=1, source_target_pairs={{0,16},{16,32},{32,48},{48,0},{64,80},{80,96},{96,112},{112,64},{1... | collective-permute-start | bytes 491528 | tf_op jit(solution)/shard_map/ppermute | solution.py:71
  49.1 6.6 %collective-permute-start.13 = (f32[64,640]{1,0:T(8,128)S(1)}, f32[64,640]{1,0:T(8,128)S(1)}, u32[]{:S(2)}, u32[]{:S(2)}) collective-permute-start(f32[64,640]{1,0:T(8,128)S(1)} %maximum_add_fusion.4), channel_id=1, source_target_pairs={{0,48},{16,0},{32,16},{48,32},{64,112},{80,64},{96,80},{112,96},{1... | collective-permute-start | bytes 491528 | tf_op jit(solution)/shard_map/ppermute | solution.py:72
  52.8 6.6 %collective-permute-start.10 = (f32[64,640]{1,0:T(8,128)S(1)}, f32[64,640]{1,0:T(8,128)S(1)}, u32[]{:S(2)}, u32[]{:S(2)}) collective-permute-start(f32[64,640]{1,0:T(8,128)S(1)} %maximum_add_fusion.1), channel_id=1, source_target_pairs={{0,16},{16,32},{32,48},{48,0},{64,80},{80,96},{96,112},{112,64},{1... | collective-permute-start | bytes 491528 | tf_op jit(solution)/shard_map/ppermute | solution.py:71
  59.5 7.0 %collective-permute-start.14 = (f32[64,640]{1,0:T(8,128)S(1)}, f32[64,640]{1,0:T(8,128)S(1)}, u32[]{:S(2)}, u32[]{:S(2)}) collective-permute-start(f32[64,640]{1,0:T(8,128)S(1)} %broadcast_select_fusion), channel_id=1, source_target_pairs={{0,64},{16,80},{32,96},{48,112},{64,0},{80,16},{96,32},{112,48},{1... | collective-permute-start | bytes 491528 | tf_op jit(solution)/shard_map/ppermute | solution.py:75

commit v12 on v9

--- a/solution.py
+++ b/solution.py
@@ -27,7 +27,6 @@
     z_swap = _pairs(n_vir, lambda j: j ^ (2 * ny))
     core_swap = _pairs(n_vir, lambda j: j ^ 1)
     zhi_swap = _pairs(n_occ, lambda i: (i + nx) % n_occ)
-    slot_of = [0, 1, 3, 4, 5, 7, 2, 6]
 
     def matmul(a, b):
         return jnp.dot(a, b, preferred_element_type=jnp.float32, precision=HIGH)
@@ -47,18 +46,17 @@
         yp2 = lax.ppermute(yp1, "vir", y_shift(-1))
         ym1z = lax.ppermute(z1, "vir", y_shift(1))
         z3 = lax.ppermute(yp2, "vir", z_swap)
-        local = jnp.concatenate([own, z1, ym1, yp1, z2, yp2, ym1z, z3], axis=0)
+        local = jnp.concatenate([own, z1, yp1, z2, yp2, z3, ym1, ym1z], axis=0)
         res_l = jnp.concatenate([res_own, matmul(local[rows:], half)], axis=0)
         local, res_l = lax.optimization_barrier((local, res_l))
         res_l = res_l.reshape(8, rows, -1)
         other = lax.ppermute(local, "vir", core_swap)
-        table = jnp.array(slot_of, jnp.int32)
         mo = lax.axis_index("occ")
         x, zh = mo % nx, mo // nx
 
         def ring(res):
             def half_block(r):
-                k = table[((r % nx - y) % ny) * 2 + ((r // nx) ^ zl)]
+                k = ((r % nx - y) % ny) * 2 + ((r // nx) ^ zl)
                 return lax.dynamic_index_in_dim(res, k, 0, keepdims=False)
 
             sa = half_block((x - 1) % nx)

time: 79.7 us -> 65.1 us (0.82)
  between operations: 15.1 us -> 0.11 us
  starting transfers between devices: 31.9 us -> 33.1 us
    ppermute x1, starting transfers between devices: 0.22 us -> 2.49 us  [body(): ym1 = lax.ppermute(own, 'vir', y_shift(1))]
    ppermute x1, waiting for transfers between devices: 4.18 us -> 2.97 us  [body(): yp1 = lax.ppermute(own, 'vir', y_shift(-1))]
    ppermute x1, starting transfers between devices: 1.8 us -> 0.74 us  [body(): yp1 = lax.ppermute(own, 'vir', y_shift(-1))]
    unnamed x17 -> x15, local copies, waits for them, and re-layouts: 4.81 us -> 4.8 us
  transfers between devices with their start and end apart: 22 -> 22, of which waited for: 8 -> 8; matrix products, arithmetic and copies ran while one was open for 13% -> 14% of each run, Pallas kernels for 0% -> 0%
where the time goes in v12:
time: 65.1 us; the launch traced here: 64.9 us
  starting transfers between devices  33.1 us (51%)
  waiting for transfers between devices  14.2 us (22%)
  matrix products  8.22 us (13%)
  local copies, waits for them, and re-layouts  6.43 us (10%)
  other arithmetic  2.76 us (4%)
    ppermute x6, starting transfers between devices, ring(): lax.ppermute(sb, 'occ', x_shift(-1)) + half_block(nx + (x + s + 1) % nx)  11.6 us
    dot_general x3, matrix products, matmul(): return jnp.dot(a, b, preferred_element_type=jnp.float32, precision=HIGH)  8.22 us
    ppermute x6, starting transfers between devices, ring(): sa = lax.ppermute(sa, 'occ', x_shift(1)) + half_block((x - s - 1) % nx)  5.74 us
    ppermute x2, starting transfers between devices, ring(): return keep + lax.ppermute(send, 'occ', zhi_swap)  5.32 us
    unnamed x15, local copies, waits for them, and re-layouts  4.8 us
    ppermute x2, waiting for transfers between devices, ring(): return keep + lax.ppermute(send, 'occ', zhi_swap)  4.4 us
    ppermute x1, starting transfers between devices, body(): ym1z = lax.ppermute(z1, 'vir', y_shift(1))  3.23 us
    ppermute x1, waiting for transfers between devices, body(): yp1 = lax.ppermute(own, 'vir', y_shift(-1))  2.97 us
  transfers between devices with their start and end apart: 22, of which 8 were waited for; matrix products, arithmetic and copies ran while one was open for 14% of the time, Pallas kernels for 0%

profile of v12, /device:TPU:24, one launch (start us, length us, event | category | flops | bytes accessed | tf_op | source)
XLA Modules:
  0.0 64.9 jit_solution(1615779028300194649)
XLA Ops:
  0.0 2.9 %fusion.9 = f32[32,640]{1,0:T(8,128)S(1)} fusion(f32[32,1280]{1,0:T(8,128)} %param.2, f32[1280,640]{1,0:T(8,128)} %param.3), kind=kOutput, calls=%fused_computation.9 | convolution fusion | flops 158105600 | bytes 3522560 | tf_op jit(solution)/shard_map/dot_general | solution.py:32
  2.9 2.0 %collective-permute-start = (f32[32,1280]{1,0:T(8,128)S(1)}, f32[32,1280]{1,0:T(8,128)S(1)}, u32[]{:S(2)}, u32[]{:S(2)}) collective-permute-start(f32[32,1280]{1,0:T(8,128)S(1)} %copy-done.3), channel_id=1, source_target_pairs={{0,8},{1,9},{2,10},{3,11},{4,12},{5,13},{6,14},{7,15},{8,0},{9,1},... | collective-permute-start | bytes 491528 | tf_op jit(solution)/shard_map/ppermute | solution.py:42
  5.7 2.5 %collective-permute-start.5 = (f32[32,1280]{1,0:T(8,128)S(1)}, f32[32,1280]{1,0:T(8,128)S(1)}, u32[]{:S(2)}, u32[]{:S(2)}) collective-permute-start(f32[32,1280]{1,0:T(8,128)S(1)} %copy-done.3), channel_id=1, source_target_pairs={{0,2},{1,3},{2,4},{3,5},{4,6},{5,7},{6,0},{7,1},{8,10},{9,11},{10,... | collective-permute-start | bytes 491528 | tf_op jit(solution)/shard_map/ppermute | solution.py:43
  8.8 3.0 %collective-permute-done.1 = f32[32,1280]{1,0:T(8,128)S(1)} collective-permute-done((f32[32,1280]{1,0:T(8,128)S(1)}, f32[32,1280]{1,0:T(8,128)S(1)}, u32[]{:S(2)}, u32[]{:S(2)}) %collective-permute-start.1) | collective-permute-done | bytes 163872 | tf_op jit(solution)/shard_map/ppermute | solution.py:44
  12.2 3.2 %collective-permute-start.6 = (f32[32,1280]{1,0:T(8,128)S(1)}, f32[32,1280]{1,0:T(8,128)S(1)}, u32[]{:S(2)}, u32[]{:S(2)}) collective-permute-start(f32[32,1280]{1,0:T(8,128)S(1)} %collective-permute-done), channel_id=1, source_target_pairs={{0,2},{1,3},{2,4},{3,5},{4,6},{5,7},{6,0},{7,1},{8,10},{9,11},{10,... | collective-permute-start | bytes 491528 | tf_op jit(solution)/shard_map/ppermute | solution.py:47
  16.8 1.9 %collective-permute-done.3 = f32[32,1280]{1,0:T(8,128)S(1)} collective-permute-done((f32[32,1280]{1,0:T(8,128)S(1)}, f32[32,1280]{1,0:T(8,128)S(1)}, u32[]{:S(2)}, u32[]{:S(2)}) %collective-permute-start.3) | collective-permute-done | bytes 163872 | tf_op jit(solution)/shard_map/ppermute | solution.py:46
  18.7 1.7 %collective-permute-start.4 = (f32[32,1280]{1,0:T(8,128)S(1)}, f32[32,1280]{1,0:T(8,128)S(1)}, u32[]{:S(2)}, u32[]{:S(2)}) collective-permute-start(f32[32,1280]{1,0:T(8,128)S(1)} %collective-permute-done.3), channel_id=1, source_target_pairs={{0,8},{1,9},{2,10},{3,11},{4,12},{5,13},{6,14},{7,15},{8,0},{9,1},... | collective-permute-start | bytes 491528 | tf_op jit(solution)/shard_map/ppermute | solution.py:48
  21.7 2.3 %collective-permute-done.4 = f32[32,1280]{1,0:T(8,128)S(1)} collective-permute-done((f32[32,1280]{1,0:T(8,128)S(1)}, f32[32,1280]{1,0:T(8,128)S(1)}, u32[]{:S(2)}, u32[]{:S(2)}) %collective-permute-start.4) | collective-permute-done | bytes 163872 | tf_op jit(solution)/shard_map/ppermute | solution.py:48
  26.1 1.9 %fusion.2 = f32[224,640]{1,0:T(8,128)S(1)} fusion(f32[224,1280]{1,0:T(8,128)S(1)} %get-tuple-element.28, f32[1280,640]{1,0:T(8,128)S(1)} %copy-done), kind=kOutput, calls=%fused_computation.2 | convolution fusion | flops 1101824000 | bytes 4997120 | tf_op jit(solution)/shard_map/dot_general | solution.py:32
  29.8 2.8 %collective-permute-start.10 = (f32[32,640]{1,0:T(8,128)S(1)}, f32[32,640]{1,0:T(8,128)S(1)}, u32[]{:S(2)}, u32[]{:S(2)}) collective-permute-start(f32[32,640]{1,0:T(8,128)S(1)} %get-tuple-element.26), channel_id=1, source_target_pairs={{0,48},{16,0},{32,16},{48,32},{64,112},{80,64},{96,80},{112,96},{1... | collective-permute-start | bytes 245768 | tf_op jit(solution)/shard_map/ppermute | solution.py:66
  32.6 3.4 %fusion = f32[256,640]{1,0:T(8,128)S(1)} fusion(f32[256,1280]{1,0:T(8,128)} %collective-permute-done.14, f32[1280,640]{1,0:T(8,128)S(1)} %copy-done), kind=kOutput, calls=%fused_computation | convolution fusion | flops 1259110400 | bytes 5242880 | tf_op jit(solution)/shard_map/dot_general | solution.py:32
  36.1 1.1 %collective-permute-start.15 = (f32[32,640]{1,0:T(8,128)S(1)}, f32[32,640]{1,0:T(8,128)S(1)}, u32[]{:S(2)}, u32[]{:S(2)}) collective-permute-start(f32[32,640]{1,0:T(8,128)S(1)} %get-tuple-element.21), channel_id=1, source_target_pairs={{0,16},{16,32},{32,48},{48,0},{64,80},{80,96},{96,112},{112,64},{1... | collective-permute-start | bytes 245768 | tf_op jit(solution)/shard_map/ppermute | solution.py:65
  37.2 2.2 %collective-permute-start.18 = (f32[32,640]{1,0:T(8,128)S(1)}, f32[32,640]{1,0:T(8,128)S(1)}, u32[]{:S(2)}, u32[]{:S(2)}) collective-permute-start(f32[32,640]{1,0:T(8,128)S(1)} %get-tuple-element.20), channel_id=1, source_target_pairs={{0,48},{16,0},{32,16},{48,32},{64,112},{80,64},{96,80},{112,96},{1... | collective-permute-start | bytes 245768 | tf_op jit(solution)/shard_map/ppermute | solution.py:66
  39.5 2.0 %collective-permute-start.11 = (f32[32,640]{1,0:T(8,128)S(1)}, f32[32,640]{1,0:T(8,128)S(1)}, u32[]{:S(2)}, u32[]{:S(2)}) collective-permute-start(f32[32,640]{1,0:T(8,128)S(1)} %get-tuple-element.24), channel_id=1, source_target_pairs={{0,48},{16,0},{32,16},{48,32},{64,112},{80,64},{96,80},{112,96},{1... | collective-permute-start | bytes 245768 | tf_op jit(solution)/shard_map/ppermute | solution.py:66
  42.0 2.0 %collective-permute-start.16 = (f32[32,640]{1,0:T(8,128)S(1)}, f32[32,640]{1,0:T(8,128)S(1)}, u32[]{:S(2)}, u32[]{:S(2)}) collective-permute-start(f32[32,640]{1,0:T(8,128)S(1)} %get-tuple-element.19), channel_id=1, source_target_pairs={{0,16},{16,32},{32,48},{48,0},{64,80},{80,96},{96,112},{112,64},{1... | collective-permute-start | bytes 245768 | tf_op jit(solution)/shard_map/ppermute | solution.py:65
  44.0 1.6 %collective-permute-start.19 = (f32[32,640]{1,0:T(8,128)S(1)}, f32[32,640]{1,0:T(8,128)S(1)}, u32[]{:S(2)}, u32[]{:S(2)}) collective-permute-start(f32[32,640]{1,0:T(8,128)S(1)} %get-tuple-element.18), channel_id=1, source_target_pairs={{0,48},{16,0},{32,16},{48,32},{64,112},{80,64},{96,80},{112,96},{1... | collective-permute-start | bytes 245768 | tf_op jit(solution)/shard_map/ppermute | solution.py:66
  45.6 1.5 %collective-permute-done.8 = f32[32,640]{1,0:T(8,128)S(1)} collective-permute-done((f32[32,640]{1,0:T(8,128)S(1)}, f32[32,640]{1,0:T(8,128)S(1)}, u32[]{:S(2)}, u32[]{:S(2)}) %collective-permute-start.8) | collective-permute-done | bytes 81952 | tf_op jit(solution)/shard_map/ppermute | solution.py:65
  47.7 1.6 %collective-permute-start.9 = (f32[32,640]{1,0:T(8,128)S(1)}, f32[32,640]{1,0:T(8,128)S(1)}, u32[]{:S(2)}, u32[]{:S(2)}) collective-permute-start(f32[32,640]{1,0:T(8,128)S(1)} %get-tuple-element.23), channel_id=1, source_target_pairs={{0,16},{16,32},{32,48},{48,0},{64,80},{80,96},{96,112},{112,64},{1... | collective-permute-start | bytes 245768 | tf_op jit(solution)/shard_map/ppermute | solution.py:65
  49.3 1.0 %collective-permute-start.17 = (f32[32,640]{1,0:T(8,128)S(1)}, f32[32,640]{1,0:T(8,128)S(1)}, u32[]{:S(2)}, u32[]{:S(2)}) collective-permute-start(f32[32,640]{1,0:T(8,128)S(1)} %get-tuple-element.17), channel_id=1, source_target_pairs={{0,16},{16,32},{32,48},{48,0},{64,80},{80,96},{96,112},{112,64},{1... | collective-permute-start | bytes 245768 | tf_op jit(solution)/shard_map/ppermute | solution.py:65
  50.3 2.3 %collective-permute-start.20 = (f32[32,640]{1,0:T(8,128)S(1)}, f32[32,640]{1,0:T(8,128)S(1)}, u32[]{:S(2)}, u32[]{:S(2)}) collective-permute-start(f32[32,640]{1,0:T(8,128)S(1)} %get-tuple-element.16), channel_id=1, source_target_pairs={{0,48},{16,0},{32,16},{48,32},{64,112},{80,64},{96,80},{112,96},{1... | collective-permute-start | bytes 245768 | tf_op jit(solution)/shard_map/ppermute | solution.py:66
  53.4 3.7 %collective-permute-start.13 = (f32[32,640]{1,0:T(8,128)S(1)}, f32[32,640]{1,0:T(8,128)S(1)}, u32[]{:S(2)}, u32[]{:S(2)}) collective-permute-start(f32[32,640]{1,0:T(8,128)S(1)} %broadcast_select_fusion.1), channel_id=1, source_target_pairs={{0,64},{16,80},{32,96},{48,112},{64,0},{80,16},{96,32},{112,48},{1... | collective-permute-start | bytes 245768 | tf_op jit(solution)/shard_map/ppermute | solution.py:69
  57.1 1.6 %collective-permute-start.21 = (f32[32,640]{1,0:T(8,128)S(1)}, f32[32,640]{1,0:T(8,128)S(1)}, u32[]{:S(2)}, u32[]{:S(2)}) collective-permute-start(f32[32,640]{1,0:T(8,128)S(1)} %broadcast_select_fusion), channel_id=1, source_target_pairs={{0,64},{16,80},{32,96},{48,112},{64,0},{80,16},{96,32},{112,48},{1... | collective-permute-start | bytes 245768 | tf_op jit(solution)/shard_map/ppermute | solution.py:69
  59.5 3.6 %collective-permute-done.21 = f32[32,640]{1,0:T(8,128)S(1)} collective-permute-done((f32[32,640]{1,0:T(8,128)S(1)}, f32[32,640]{1,0:T(8,128)S(1)}, u32[]{:S(2)}, u32[]{:S(2)}) %collective-permute-start.21) | collective-permute-done | bytes 81952 | tf_op jit(solution)/shard_map/ppermute | solution.py:69
  63.1 1.0 %broadcast_select_fusion.3 = (f32[32,640]{1,0:T(8,128)S(1)}, f32[32,640]{1,0:T(8,128)S(1)}, f32[32,640]{1,0:T(8,128)S(1)}) fusion(pred[]{:T(512)S(6)} %eq.62, f32[32,640]{1,0:T(8,128)S(1)} %collective-permute-done.13, f32[32,640]{1,0:T(8,128)S(1)} %collective-permute-done.12, f32[8,32,640]{2,1,0:T(8,128)} %bitcast.65, s32[]{:T(128)S(6)} %select_n.311, ...), kind=kLoop, calls=%fused_computation.33 | loop fusion | flops 184320 | bytes 1064970 | tf_op jit(solution)/shard_map/jit(_where)/select_n | solution.py:74
  (51 shorter events, 11.8 us)
Async XLA Ops:
  2.9 9.2 %collective-permute-start = (f32[32,1280]{1,0:T(8,128)S(1)}, f32[32,1280]{1,0:T(8,128)S(1)}, u32[]{:S(2)}, u32[]{:S(2)}) collective-permute-start(f32[32,1280]{1,0:T(8,128)S(1)} %copy-done.3), channel_id=1, source_target_pairs={{0,8},{1,9},{2,10},{3,11},{4,12},{5,13},{6,14},{7,15},{8,0},{9,1},... | collective-permute-start | bytes 491528 | tf_op jit(solution)/shard_map/ppermute | solution.py:42
  4.9 6.9 %collective-permute-start.1 = (f32[32,1280]{1,0:T(8,128)S(1)}, f32[32,1280]{1,0:T(8,128)S(1)}, u32[]{:S(2)}, u32[]{:S(2)}) collective-permute-start(f32[32,1280]{1,0:T(8,128)S(1)} %copy-done.3), channel_id=1, source_target_pairs={{0,6},{1,7},{2,0},{3,1},{4,2},{5,3},{6,4},{7,5},{8,14},{9,15},{10,... | collective-permute-start | bytes 491528 | tf_op jit(solution)/shard_map/ppermute | solution.py:44
  5.7 19.0 %collective-permute-start.5 = (f32[32,1280]{1,0:T(8,128)S(1)}, f32[32,1280]{1,0:T(8,128)S(1)}, u32[]{:S(2)}, u32[]{:S(2)}) collective-permute-start(f32[32,1280]{1,0:T(8,128)S(1)} %copy-done.3), channel_id=1, source_target_pairs={{0,2},{1,3},{2,4},{3,5},{4,6},{5,7},{6,0},{7,1},{8,10},{9,11},{10,... | collective-permute-start | bytes 491528 | tf_op jit(solution)/shard_map/ppermute | solution.py:43
  11.8 8.6 %collective-permute-start.2 = (f32[32,1280]{1,0:T(8,128)S(1)}, f32[32,1280]{1,0:T(8,128)S(1)}, u32[]{:S(2)}, u32[]{:S(2)}) collective-permute-start(f32[32,1280]{1,0:T(8,128)S(1)} %collective-permute-done.1), channel_id=1, source_target_pairs={{0,8},{1,9},{2,10},{3,11},{4,12},{5,13},{6,14},{7,15},{8,0},{9,1},... | collective-permute-start | bytes 491528 | tf_op jit(solution)/shard_map/ppermute | solution.py:45
  12.2 6.5 %collective-permute-start.3 = (f32[32,1280]{1,0:T(8,128)S(1)}, f32[32,1280]{1,0:T(8,128)S(1)}, u32[]{:S(2)}, u32[]{:S(2)}) collective-permute-start(f32[32,1280]{1,0:T(8,128)S(1)} %collective-permute-done.1), channel_id=1, source_target_pairs={{0,6},{1,7},{2,0},{3,1},{4,2},{5,3},{6,4},{7,5},{8,14},{9,15},{10,... | collective-permute-start | bytes 491528 | tf_op jit(solution)/shard_map/ppermute | solution.py:46
  12.2 13.2 %collective-permute-start.6 = (f32[32,1280]{1,0:T(8,128)S(1)}, f32[32,1280]{1,0:T(8,128)S(1)}, u32[]{:S(2)}, u32[]{:S(2)}) collective-permute-start(f32[32,1280]{1,0:T(8,128)S(1)} %collective-permute-done), channel_id=1, source_target_pairs={{0,2},{1,3},{2,4},{3,5},{4,6},{5,7},{6,0},{7,1},{8,10},{9,11},{10,... | collective-permute-start | bytes 491528 | tf_op jit(solution)/shard_map/ppermute | solution.py:47
  15.4 10.7 %copy-start = (f32[1280,640]{1,0:T(8,128)S(1)}, f32[1280,640]{1,0:T(8,128)}, u32[]{:S(2)}) copy-start(f32[1280,640]{1,0:T(8,128)} %param.3) | copy-start | bytes 9830404
  18.7 5.3 %collective-permute-start.4 = (f32[32,1280]{1,0:T(8,128)S(1)}, f32[32,1280]{1,0:T(8,128)S(1)}, u32[]{:S(2)}, u32[]{:S(2)}) collective-permute-start(f32[32,1280]{1,0:T(8,128)S(1)} %collective-permute-done.3), channel_id=1, source_target_pairs={{0,8},{1,9},{2,10},{3,11},{4,12},{5,13},{6,14},{7,15},{8,0},{9,1},... | collective-permute-start | bytes 491528 | tf_op jit(solution)/shard_map/ppermute | solution.py:48
  28.8 3.8 %collective-permute-start.14 = (f32[256,1280]{1,0:T(8,128)}, f32[256,1280]{1,0:T(8,128)}, u32[]{:S(2)}, u32[]{:S(2)}) collective-permute-start(f32[256,1280]{1,0:T(8,128)} %get-tuple-element.12), channel_id=1, source_target_pairs={{0,1},{1,0},{2,3},{3,2},{4,5},{5,4},{6,7},{7,6},{8,9},{9,8},{10,11... | collective-permute-start | bytes 3932168 | tf_op jit(solution)/shard_map/ppermute | solution.py:53
  29.8 9.6 %collective-permute-start.10 = (f32[32,640]{1,0:T(8,128)S(1)}, f32[32,640]{1,0:T(8,128)S(1)}, u32[]{:S(2)}, u32[]{:S(2)}) collective-permute-start(f32[32,640]{1,0:T(8,128)S(1)} %get-tuple-element.26), channel_id=1, source_target_pairs={{0,48},{16,0},{32,16},{48,32},{64,112},{80,64},{96,80},{112,96},{1... | collective-permute-start | bytes 245768 | tf_op jit(solution)/shard_map/ppermute | solution.py:66
  32.6 6.8 %collective-permute-start.7 = (f32[32,640]{1,0:T(8,128)S(1)}, f32[32,640]{1,0:T(8,128)S(1)}, u32[]{:S(2)}, u32[]{:S(2)}) collective-permute-start(f32[32,640]{1,0:T(8,128)S(1)} %get-tuple-element.27), channel_id=1, source_target_pairs={{0,16},{16,32},{32,48},{48,0},{64,80},{80,96},{96,112},{112,64},{1... | collective-permute-start | bytes 245768 | tf_op jit(solution)/shard_map/ppermute | solution.py:65
  36.1 21.0 %copy-start.1 = (f32[256,640]{1,0:T(8,128)}, f32[256,640]{1,0:T(8,128)S(1)}, u32[]{:S(2)}) copy-start(f32[256,640]{1,0:T(8,128)S(1)} %fusion) | copy-start | bytes 1966084
  36.1 5.9 %collective-permute-start.15 = (f32[32,640]{1,0:T(8,128)S(1)}, f32[32,640]{1,0:T(8,128)S(1)}, u32[]{:S(2)}, u32[]{:S(2)}) collective-permute-start(f32[32,640]{1,0:T(8,128)S(1)} %get-tuple-element.21), channel_id=1, source_target_pairs={{0,16},{16,32},{32,48},{48,0},{64,80},{80,96},{96,112},{112,64},{1... | collective-permute-start | bytes 245768 | tf_op jit(solution)/shard_map/ppermute | solution.py:65
  37.2 4.8 %collective-permute-start.18 = (f32[32,640]{1,0:T(8,128)S(1)}, f32[32,640]{1,0:T(8,128)S(1)}, u32[]{:S(2)}, u32[]{:S(2)}) collective-permute-start(f32[32,640]{1,0:T(8,128)S(1)} %get-tuple-element.20), channel_id=1, source_target_pairs={{0,48},{16,0},{32,16},{48,32},{64,112},{80,64},{96,80},{112,96},{1... | collective-permute-start | bytes 245768 | tf_op jit(solution)/shard_map/ppermute | solution.py:66
  39.5 6.2 %collective-permute-start.11 = (f32[32,640]{1,0:T(8,128)S(1)}, f32[32,640]{1,0:T(8,128)S(1)}, u32[]{:S(2)}, u32[]{:S(2)}) collective-permute-start(f32[32,640]{1,0:T(8,128)S(1)} %get-tuple-element.24), channel_id=1, source_target_pairs={{0,48},{16,0},{32,16},{48,32},{64,112},{80,64},{96,80},{112,96},{1... | collective-permute-start | bytes 245768 | tf_op jit(solution)/shard_map/ppermute | solution.py:66
  41.5 5.7 %collective-permute-start.8 = (f32[32,640]{1,0:T(8,128)S(1)}, f32[32,640]{1,0:T(8,128)S(1)}, u32[]{:S(2)}, u32[]{:S(2)}) collective-permute-start(f32[32,640]{1,0:T(8,128)S(1)} %get-tuple-element.25), channel_id=1, source_target_pairs={{0,16},{16,32},{32,48},{48,0},{64,80},{80,96},{96,112},{112,64},{1... | collective-permute-start | bytes 245768 | tf_op jit(solution)/shard_map/ppermute | solution.py:65
  42.0 7.3 %collective-permute-start.16 = (f32[32,640]{1,0:T(8,128)S(1)}, f32[32,640]{1,0:T(8,128)S(1)}, u32[]{:S(2)}, u32[]{:S(2)}) collective-permute-start(f32[32,640]{1,0:T(8,128)S(1)} %get-tuple-element.19), channel_id=1, source_target_pairs={{0,16},{16,32},{32,48},{48,0},{64,80},{80,96},{96,112},{112,64},{1... | collective-permute-start | bytes 245768 | tf_op jit(solution)/shard_map/ppermute | solution.py:65
  44.0 5.3 %collective-permute-start.19 = (f32[32,640]{1,0:T(8,128)S(1)}, f32[32,640]{1,0:T(8,128)S(1)}, u32[]{:S(2)}, u32[]{:S(2)}) collective-permute-start(f32[32,640]{1,0:T(8,128)S(1)} %get-tuple-element.18), channel_id=1, source_target_pairs={{0,48},{16,0},{32,16},{48,32},{64,112},{80,64},{96,80},{112,96},{1... | collective-permute-start | bytes 245768 | tf_op jit(solution)/shard_map/ppermute | solution.py:66
  47.1 5.4 %collective-permute-start.12 = (f32[32,640]{1,0:T(8,128)S(1)}, f32[32,640]{1,0:T(8,128)S(1)}, u32[]{:S(2)}, u32[]{:S(2)}) collective-permute-start(f32[32,640]{1,0:T(8,128)S(1)} %get-tuple-element.22), channel_id=1, source_target_pairs={{0,48},{16,0},{32,16},{48,32},{64,112},{80,64},{96,80},{112,96},{1... | collective-permute-start | bytes 245768 | tf_op jit(solution)/shard_map/ppermute | solution.py:66
  47.7 5.7 %collective-permute-start.9 = (f32[32,640]{1,0:T(8,128)S(1)}, f32[32,640]{1,0:T(8,128)S(1)}, u32[]{:S(2)}, u32[]{:S(2)}) collective-permute-start(f32[32,640]{1,0:T(8,128)S(1)} %get-tuple-element.23), channel_id=1, source_target_pairs={{0,16},{16,32},{32,48},{48,0},{64,80},{80,96},{96,112},{112,64},{1... | collective-permute-start | bytes 245768 | tf_op jit(solution)/shard_map/ppermute | solution.py:65
  49.3 7.8 %collective-permute-start.17 = (f32[32,640]{1,0:T(8,128)S(1)}, f32[32,640]{1,0:T(8,128)S(1)}, u32[]{:S(2)}, u32[]{:S(2)}) collective-permute-start(f32[32,640]{1,0:T(8,128)S(1)} %get-tuple-element.17), channel_id=1, source_target_pairs={{0,16},{16,32},{32,48},{48,0},{64,80},{80,96},{96,112},{112,64},{1... | collective-permute-start | bytes 245768 | tf_op jit(solution)/shard_map/ppermute | solution.py:65
  50.3 6.8 %collective-permute-start.20 = (f32[32,640]{1,0:T(8,128)S(1)}, f32[32,640]{1,0:T(8,128)S(1)}, u32[]{:S(2)}, u32[]{:S(2)}) collective-permute-start(f32[32,640]{1,0:T(8,128)S(1)} %get-tuple-element.16), channel_id=1, source_target_pairs={{0,48},{16,0},{32,16},{48,32},{64,112},{80,64},{96,80},{112,96},{1... | collective-permute-start | bytes 245768 | tf_op jit(solution)/shard_map/ppermute | solution.py:66
  53.4 6.1 %collective-permute-start.13 = (f32[32,640]{1,0:T(8,128)S(1)}, f32[32,640]{1,0:T(8,128)S(1)}, u32[]{:S(2)}, u32[]{:S(2)}) collective-permute-start(f32[32,640]{1,0:T(8,128)S(1)} %broadcast_select_fusion.1), channel_id=1, source_target_pairs={{0,64},{16,80},{32,96},{48,112},{64,0},{80,16},{96,32},{112,48},{1... | collective-permute-start | bytes 245768 | tf_op jit(solution)/shard_map/ppermute | solution.py:69
  57.1 6.0 %collective-permute-start.21 = (f32[32,640]{1,0:T(8,128)S(1)}, f32[32,640]{1,0:T(8,128)S(1)}, u32[]{:S(2)}, u32[]{:S(2)}) collective-permute-start(f32[32,640]{1,0:T(8,128)S(1)} %broadcast_select_fusion), channel_id=1, source_target_pairs={{0,64},{16,80},{32,96},{48,112},{64,0},{80,16},{96,32},{112,48},{1... | collective-permute-start | bytes 245768 | tf_op jit(solution)/shard_map/ppermute | solution.py:69
  (2 other events, 9.7 us)

commit v13 on v12

--- a/solution.py
+++ b/solution.py
@@ -37,8 +37,7 @@
         zl, y, c = me // (2 * ny), (me // 2) % ny, me % 2
 
         half = 0.5 * integrals
-        res_own = matmul(amplitudes, half)
-        own, res_own = lax.optimization_barrier((amplitudes, res_own))
+        own = amplitudes
         z1 = lax.ppermute(own, "vir", z_swap)
         ym1 = lax.ppermute(own, "vir", y_shift(1))
         yp1 = lax.ppermute(own, "vir", y_shift(-1))
@@ -47,8 +46,7 @@
         ym1z = lax.ppermute(z1, "vir", y_shift(1))
         z3 = lax.ppermute(yp2, "vir", z_swap)
         local = jnp.concatenate([own, z1, yp1, z2, yp2, z3, ym1, ym1z], axis=0)
-        res_l = jnp.concatenate([res_own, matmul(local[rows:], half)], axis=0)
-        local, res_l = lax.optimization_barrier((local, res_l))
+        res_l = matmul(local, half)
         res_l = res_l.reshape(8, rows, -1)
         other = lax.ppermute(local, "vir", core_swap)
         mo = lax.axis_index("occ")

time: 65.1 us -> 61.8 us (0.949)
  matrix products: 8.22 us -> 6.7 us
  waiting for transfers between devices: 14.2 us -> 13.3 us
  other arithmetic: 2.76 us -> 1.87 us
    ppermute x1, waiting for transfers between devices: 2.97 us -> 0.47 us  [body(): yp1 = lax.ppermute(own, 'vir', y_shift(-1))]
    ppermute x1, waiting for transfers between devices: 2.28 us -> 3.86 us  [body(): z3 = lax.ppermute(yp2, 'vir', z_swap)]
    ppermute x1, starting transfers between devices: 0.36 us -> 1.92 us  [body(): z2 = lax.ppermute(yp1, 'vir', z_swap)]
    ppermute x1, starting transfers between devices: 1.66 us -> 0.11 us  [body(): z3 = lax.ppermute(yp2, 'vir', z_swap)]
    dot_general x3 -> x2, matrix products: 8.22 us -> 6.7 us  [matmul(): return jnp.dot(a, b, preferred_element_type=jnp.float32, precision=HIGH)]
    unnamed x15 -> x13, local copies, waits for them, and re-layouts: 4.8 us -> 5.79 us
    squeeze x2, local copies, waits for them, and re-layouts: 0.96 us -> 0.04 us  [half_block(): return lax.dynamic_index_in_dim(res, k, 0, keepdims=False)]
    concatenate x1 -> x0, other arithmetic: 0.88 us -> none  [body(): res_l = jnp.concatenate([res_own, matmul(local[rows:], half)], axis=0)]
  transfers between devices with their start and end apart: 22 -> 22, of which waited for: 8 -> 8; matrix products, arithmetic and copies ran while one was open for 14% -> 21% of each run, Pallas kernels for 0% -> 0%
where the time goes in v13:
time: 61.8 us; the launch traced here: 61.6 us
  starting transfers between devices  33.1 us (54%)
  waiting for transfers between devices  13.3 us (22%)
  matrix products  6.7 us (11%)
  local copies, waits for them, and re-layouts  6.51 us (11%)
  other arithmetic  1.87 us (3%)
    ppermute x6, starting transfers between devices, ring(): lax.ppermute(sb, 'occ', x_shift(-1)) + half_block(nx + (x + s + 1) % nx)  11.9 us
    dot_general x2, matrix products, matmul(): return jnp.dot(a, b, preferred_element_type=jnp.float32, precision=HIGH)  6.7 us
    unnamed x13, local copies, waits for them, and re-layouts  5.79 us
    ppermute x6, starting transfers between devices, ring(): sa = lax.ppermute(sa, 'occ', x_shift(1)) + half_block((x - s - 1) % nx)  5.54 us
    ppermute x2, starting transfers between devices, ring(): return keep + lax.ppermute(send, 'occ', zhi_swap)  5.26 us
    ppermute x2, waiting for transfers between devices, ring(): return keep + lax.ppermute(send, 'occ', zhi_swap)  4.43 us
    ppermute x1, waiting for transfers between devices, body(): z3 = lax.ppermute(yp2, 'vir', z_swap)  3.86 us
    ppermute x1, starting transfers between devices, body(): ym1z = lax.ppermute(z1, 'vir', y_shift(1))  3.23 us
  transfers between devices with their start and end apart: 22, of which 8 were waited for; matrix products, arithmetic and copies ran while one was open for 21% of the time, Pallas kernels for 0%

profile of v13, /device:TPU:24, one launch (start us, length us, event | category | flops | bytes accessed | tf_op | source)
XLA Modules:
  0.0 61.6 jit_solution(3313142151155380336)
XLA Ops:
  0.7 1.9 %collective-permute-start = (f32[32,1280]{1,0:T(8,128)}, f32[32,1280]{1,0:T(8,128)S(1)}, u32[]{:S(2)}, u32[]{:S(2)}) collective-permute-start(f32[32,1280]{1,0:T(8,128)} %param.2), channel_id=1, source_target_pairs={{0,8},{1,9},{2,10},{3,11},{4,12},{5,13},{6,14},{7,15},{8,0},{9,1},... | collective-permute-start | bytes 491528 | tf_op jit(solution)/shard_map/ppermute | solution.py:41
  2.7 2.5 %collective-permute-start.5 = (f32[32,1280]{1,0:T(8,128)}, f32[32,1280]{1,0:T(8,128)S(1)}, u32[]{:S(2)}, u32[]{:S(2)}) collective-permute-start(f32[32,1280]{1,0:T(8,128)} %param.2), channel_id=1, source_target_pairs={{0,2},{1,3},{2,4},{3,5},{4,6},{5,7},{6,0},{7,1},{8,10},{9,11},{10,... | collective-permute-start | bytes 491528 | tf_op jit(solution)/shard_map/ppermute | solution.py:42
  5.2 1.7 %constant_dynamic-update-slice_fusion.7 = f32[256,1280]{1,0:T(8,128)} fusion(f32[32,1280]{1,0:T(8,128)} %param.2), kind=kLoop, calls=%fused_computation.36 | loop fusion | bytes 327680
  7.4 1.9 %collective-permute-start.2 = (f32[32,1280]{1,0:T(8,128)S(1)}, f32[32,1280]{1,0:T(8,128)S(1)}, u32[]{:S(2)}, u32[]{:S(2)}) collective-permute-start(f32[32,1280]{1,0:T(8,128)S(1)} %collective-permute-done.1), channel_id=1, source_target_pairs={{0,8},{1,9},{2,10},{3,11},{4,12},{5,13},{6,14},{7,15},{8,0},{9,1},... | collective-permute-start | bytes 491528 | tf_op jit(solution)/shard_map/ppermute | solution.py:44
  9.3 3.2 %collective-permute-start.6 = (f32[32,1280]{1,0:T(8,128)S(1)}, f32[32,1280]{1,0:T(8,128)S(1)}, u32[]{:S(2)}, u32[]{:S(2)}) collective-permute-start(f32[32,1280]{1,0:T(8,128)S(1)} %collective-permute-done), channel_id=1, source_target_pairs={{0,2},{1,3},{2,4},{3,5},{4,6},{5,7},{6,0},{7,1},{8,10},{9,11},{10,... | collective-permute-start | bytes 491528 | tf_op jit(solution)/shard_map/ppermute | solution.py:46
  13.9 1.9 %collective-permute-done.3 = f32[32,1280]{1,0:T(8,128)S(1)} collective-permute-done((f32[32,1280]{1,0:T(8,128)S(1)}, f32[32,1280]{1,0:T(8,128)S(1)}, u32[]{:S(2)}, u32[]{:S(2)}) %collective-permute-start.3) | collective-permute-done | bytes 163872 | tf_op jit(solution)/shard_map/ppermute | solution.py:45
  17.3 3.9 %collective-permute-done.4 = f32[32,1280]{1,0:T(8,128)S(1)} collective-permute-done((f32[32,1280]{1,0:T(8,128)S(1)}, f32[32,1280]{1,0:T(8,128)S(1)}, u32[]{:S(2)}, u32[]{:S(2)}) %collective-permute-start.4) | collective-permute-done | bytes 163872 | tf_op jit(solution)/shard_map/ppermute | solution.py:47
  23.2 3.4 %fusion.2 = f32[256,640]{1,0:T(8,128)S(1)} fusion(f32[256,1280]{1,0:T(8,128)} %constant_dynamic-update-slice_fusion, f32[1280,640]{1,0:T(8,128)S(1)} %copy-done), kind=kOutput, calls=%fused_computation.2 | convolution fusion | flops 1259110400 | bytes 5242880 | tf_op jit(solution)/shard_map/dot_general | solution.py:32
  26.6 2.8 %collective-permute-start.10 = (f32[32,640]{1,0:T(8,128)S(1)}, f32[32,640]{1,0:T(8,128)S(1)}, u32[]{:S(2)}, u32[]{:S(2)}) collective-permute-start(f32[32,640]{1,0:T(8,128)S(1)} %get-tuple-element.18), channel_id=1, source_target_pairs={{0,48},{16,0},{32,16},{48,32},{64,112},{80,64},{96,80},{112,96},{1... | collective-permute-start | bytes 245768 | tf_op jit(solution)/shard_map/ppermute | solution.py:64
  29.4 3.4 %fusion = f32[256,640]{1,0:T(8,128)S(1)} fusion(f32[256,1280]{1,0:T(8,128)} %collective-permute-done.14, f32[1280,640]{1,0:T(8,128)S(1)} %copy-done), kind=kOutput, calls=%fused_computation | convolution fusion | flops 1259110400 | bytes 5242880 | tf_op jit(solution)/shard_map/dot_general | solution.py:32
  32.8 0.8 %collective-permute-start.15 = (f32[32,640]{1,0:T(8,128)S(1)}, f32[32,640]{1,0:T(8,128)S(1)}, u32[]{:S(2)}, u32[]{:S(2)}) collective-permute-start(f32[32,640]{1,0:T(8,128)S(1)} %get-tuple-element.13), channel_id=1, source_target_pairs={{0,16},{16,32},{32,48},{48,0},{64,80},{80,96},{96,112},{112,64},{1... | collective-permute-start | bytes 245768 | tf_op jit(solution)/shard_map/ppermute | solution.py:63
  33.6 2.6 %collective-permute-start.18 = (f32[32,640]{1,0:T(8,128)S(1)}, f32[32,640]{1,0:T(8,128)S(1)}, u32[]{:S(2)}, u32[]{:S(2)}) collective-permute-start(f32[32,640]{1,0:T(8,128)S(1)} %get-tuple-element.12), channel_id=1, source_target_pairs={{0,48},{16,0},{32,16},{48,32},{64,112},{80,64},{96,80},{112,96},{1... | collective-permute-start | bytes 245768 | tf_op jit(solution)/shard_map/ppermute | solution.py:64
  36.2 2.0 %collective-permute-start.11 = (f32[32,640]{1,0:T(8,128)S(1)}, f32[32,640]{1,0:T(8,128)S(1)}, u32[]{:S(2)}, u32[]{:S(2)}) collective-permute-start(f32[32,640]{1,0:T(8,128)S(1)} %get-tuple-element.16), channel_id=1, source_target_pairs={{0,48},{16,0},{32,16},{48,32},{64,112},{80,64},{96,80},{112,96},{1... | collective-permute-start | bytes 245768 | tf_op jit(solution)/shard_map/ppermute | solution.py:64
  38.7 2.1 %collective-permute-start.16 = (f32[32,640]{1,0:T(8,128)S(1)}, f32[32,640]{1,0:T(8,128)S(1)}, u32[]{:S(2)}, u32[]{:S(2)}) collective-permute-start(f32[32,640]{1,0:T(8,128)S(1)} %get-tuple-element.11), channel_id=1, source_target_pairs={{0,16},{16,32},{32,48},{48,0},{64,80},{80,96},{96,112},{112,64},{1... | collective-permute-start | bytes 245768 | tf_op jit(solution)/shard_map/ppermute | solution.py:63
  40.8 1.7 %collective-permute-start.19 = (f32[32,640]{1,0:T(8,128)S(1)}, f32[32,640]{1,0:T(8,128)S(1)}, u32[]{:S(2)}, u32[]{:S(2)}) collective-permute-start(f32[32,640]{1,0:T(8,128)S(1)} %get-tuple-element.10), channel_id=1, source_target_pairs={{0,48},{16,0},{32,16},{48,32},{64,112},{80,64},{96,80},{112,96},{1... | collective-permute-start | bytes 245768 | tf_op jit(solution)/shard_map/ppermute | solution.py:64
  42.4 1.5 %collective-permute-done.8 = f32[32,640]{1,0:T(8,128)S(1)} collective-permute-done((f32[32,640]{1,0:T(8,128)S(1)}, f32[32,640]{1,0:T(8,128)S(1)}, u32[]{:S(2)}, u32[]{:S(2)}) %collective-permute-start.8) | collective-permute-done | bytes 81952 | tf_op jit(solution)/shard_map/ppermute | solution.py:63
  44.5 1.5 %collective-permute-start.9 = (f32[32,640]{1,0:T(8,128)S(1)}, f32[32,640]{1,0:T(8,128)S(1)}, u32[]{:S(2)}, u32[]{:S(2)}) collective-permute-start(f32[32,640]{1,0:T(8,128)S(1)} %get-tuple-element.15), channel_id=1, source_target_pairs={{0,16},{16,32},{32,48},{48,0},{64,80},{80,96},{96,112},{112,64},{1... | collective-permute-start | bytes 245768 | tf_op jit(solution)/shard_map/ppermute | solution.py:63
  46.0 1.0 %collective-permute-start.17 = (f32[32,640]{1,0:T(8,128)S(1)}, f32[32,640]{1,0:T(8,128)S(1)}, u32[]{:S(2)}, u32[]{:S(2)}) collective-permute-start(f32[32,640]{1,0:T(8,128)S(1)} %get-tuple-element.9), channel_id=1, source_target_pairs={{0,16},{16,32},{32,48},{48,0},{64,80},{80,96},{96,112},{112,64},{1... | collective-permute-start | bytes 245768 | tf_op jit(solution)/shard_map/ppermute | solution.py:63
  47.1 2.3 %collective-permute-start.20 = (f32[32,640]{1,0:T(8,128)S(1)}, f32[32,640]{1,0:T(8,128)S(1)}, u32[]{:S(2)}, u32[]{:S(2)}) collective-permute-start(f32[32,640]{1,0:T(8,128)S(1)} %get-tuple-element.8), channel_id=1, source_target_pairs={{0,48},{16,0},{32,16},{48,32},{64,112},{80,64},{96,80},{112,96},{1... | collective-permute-start | bytes 245768 | tf_op jit(solution)/shard_map/ppermute | solution.py:64
  50.2 3.7 %collective-permute-start.13 = (f32[32,640]{1,0:T(8,128)S(1)}, f32[32,640]{1,0:T(8,128)S(1)}, u32[]{:S(2)}, u32[]{:S(2)}) collective-permute-start(f32[32,640]{1,0:T(8,128)S(1)} %broadcast_select_fusion.1), channel_id=1, source_target_pairs={{0,64},{16,80},{32,96},{48,112},{64,0},{80,16},{96,32},{112,48},{1... | collective-permute-start | bytes 245768 | tf_op jit(solution)/shard_map/ppermute | solution.py:67
  53.9 1.6 %collective-permute-start.21 = (f32[32,640]{1,0:T(8,128)S(1)}, f32[32,640]{1,0:T(8,128)S(1)}, u32[]{:S(2)}, u32[]{:S(2)}) collective-permute-start(f32[32,640]{1,0:T(8,128)S(1)} %broadcast_select_fusion), channel_id=1, source_target_pairs={{0,64},{16,80},{32,96},{48,112},{64,0},{80,16},{96,32},{112,48},{1... | collective-permute-start | bytes 245768 | tf_op jit(solution)/shard_map/ppermute | solution.py:67
  55.5 0.8 %collective-permute-done.13 = f32[32,640]{1,0:T(8,128)S(1)} collective-permute-done((f32[32,640]{1,0:T(8,128)S(1)}, f32[32,640]{1,0:T(8,128)S(1)}, u32[]{:S(2)}, u32[]{:S(2)}) %collective-permute-start.13) | collective-permute-done | bytes 81952 | tf_op jit(solution)/shard_map/ppermute | solution.py:67
  56.2 3.6 %collective-permute-done.21 = f32[32,640]{1,0:T(8,128)S(1)} collective-permute-done((f32[32,640]{1,0:T(8,128)S(1)}, f32[32,640]{1,0:T(8,128)S(1)}, u32[]{:S(2)}, u32[]{:S(2)}) %collective-permute-start.21) | collective-permute-done | bytes 81952 | tf_op jit(solution)/shard_map/ppermute | solution.py:67
  59.9 1.0 %broadcast_select_fusion.3 = (f32[32,640]{1,0:T(8,128)S(1)}, f32[32,640]{1,0:T(8,128)S(1)}, f32[32,640]{1,0:T(8,128)S(1)}) fusion(pred[]{:T(512)S(6)} %eq.62, f32[32,640]{1,0:T(8,128)S(1)} %collective-permute-done.13, f32[32,640]{1,0:T(8,128)S(1)} %collective-permute-done.12, f32[8,32,640]{2,1,0:T(8,128)} %bitcast.60, s32[]{:T(128)S(6)} %select_n.311, ...), kind=kLoop, calls=%fused_computation.28 | loop fusion | flops 184320 | bytes 1064970 | tf_op jit(solution)/shard_map/jit(_where)/select_n | solution.py:72
  (47 shorter events, 8.7 us)
Async XLA Ops:
  0.0 7.4 %collective-permute-start.1 = (f32[32,1280]{1,0:T(8,128)}, f32[32,1280]{1,0:T(8,128)S(1)}, u32[]{:S(2)}, u32[]{:S(2)}) collective-permute-start(f32[32,1280]{1,0:T(8,128)} %param.2), channel_id=1, source_target_pairs={{0,6},{1,7},{2,0},{3,1},{4,2},{5,3},{6,4},{7,5},{8,14},{9,15},{10,... | collective-permute-start | bytes 491528 | tf_op jit(solution)/shard_map/ppermute | solution.py:43
  0.7 8.5 %collective-permute-start = (f32[32,1280]{1,0:T(8,128)}, f32[32,1280]{1,0:T(8,128)S(1)}, u32[]{:S(2)}, u32[]{:S(2)}) collective-permute-start(f32[32,1280]{1,0:T(8,128)} %param.2), channel_id=1, source_target_pairs={{0,8},{1,9},{2,10},{3,11},{4,12},{5,13},{6,14},{7,15},{8,0},{9,1},... | collective-permute-start | bytes 491528 | tf_op jit(solution)/shard_map/ppermute | solution.py:41
  2.7 19.1 %collective-permute-start.5 = (f32[32,1280]{1,0:T(8,128)}, f32[32,1280]{1,0:T(8,128)S(1)}, u32[]{:S(2)}, u32[]{:S(2)}) collective-permute-start(f32[32,1280]{1,0:T(8,128)} %param.2), channel_id=1, source_target_pairs={{0,2},{1,3},{2,4},{3,5},{4,6},{5,7},{6,0},{7,1},{8,10},{9,11},{10,... | collective-permute-start | bytes 491528 | tf_op jit(solution)/shard_map/ppermute | solution.py:42
  7.4 8.6 %collective-permute-start.2 = (f32[32,1280]{1,0:T(8,128)S(1)}, f32[32,1280]{1,0:T(8,128)S(1)}, u32[]{:S(2)}, u32[]{:S(2)}) collective-permute-start(f32[32,1280]{1,0:T(8,128)S(1)} %collective-permute-done.1), channel_id=1, source_target_pairs={{0,8},{1,9},{2,10},{3,11},{4,12},{5,13},{6,14},{7,15},{8,0},{9,1},... | collective-permute-start | bytes 491528 | tf_op jit(solution)/shard_map/ppermute | solution.py:44
  9.3 6.5 %collective-permute-start.3 = (f32[32,1280]{1,0:T(8,128)S(1)}, f32[32,1280]{1,0:T(8,128)S(1)}, u32[]{:S(2)}, u32[]{:S(2)}) collective-permute-start(f32[32,1280]{1,0:T(8,128)S(1)} %collective-permute-done.1), channel_id=1, source_target_pairs={{0,6},{1,7},{2,0},{3,1},{4,2},{5,3},{6,4},{7,5},{8,14},{9,15},{10,... | collective-permute-start | bytes 491528 | tf_op jit(solution)/shard_map/ppermute | solution.py:45
  9.3 13.2 %collective-permute-start.6 = (f32[32,1280]{1,0:T(8,128)S(1)}, f32[32,1280]{1,0:T(8,128)S(1)}, u32[]{:S(2)}, u32[]{:S(2)}) collective-permute-start(f32[32,1280]{1,0:T(8,128)S(1)} %collective-permute-done), channel_id=1, source_target_pairs={{0,2},{1,3},{2,4},{3,5},{4,6},{5,7},{6,0},{7,1},{8,10},{9,11},{10,... | collective-permute-start | bytes 491528 | tf_op jit(solution)/shard_map/ppermute | solution.py:46
  15.8 5.3 %collective-permute-start.4 = (f32[32,1280]{1,0:T(8,128)S(1)}, f32[32,1280]{1,0:T(8,128)S(1)}, u32[]{:S(2)}, u32[]{:S(2)}) collective-permute-start(f32[32,1280]{1,0:T(8,128)S(1)} %collective-permute-done.3), channel_id=1, source_target_pairs={{0,8},{1,9},{2,10},{3,11},{4,12},{5,13},{6,14},{7,15},{8,0},{9,1},... | collective-permute-start | bytes 491528 | tf_op jit(solution)/shard_map/ppermute | solution.py:47
  23.2 6.2 %collective-permute-start.14 = (f32[256,1280]{1,0:T(8,128)}, f32[256,1280]{1,0:T(8,128)}, u32[]{:S(2)}, u32[]{:S(2)}) collective-permute-start(f32[256,1280]{1,0:T(8,128)} %constant_dynamic-update-slice_fusion), channel_id=1, source_target_pairs={{0,1},{1,0},{2,3},{3,2},{4,5},{5,4},{6,7},{7,6},{8,9},{9,8},{10,11... | collective-permute-start | bytes 3932168 | tf_op jit(solution)/shard_map/ppermute | solution.py:51
  26.5 23.6 %copy-start.1 = (f32[256,640]{1,0:T(8,128)}, f32[256,640]{1,0:T(8,128)S(1)}, u32[]{:S(2)}) copy-start(f32[256,640]{1,0:T(8,128)S(1)} %fusion.2) | copy-start | bytes 1966084
  26.6 9.6 %collective-permute-start.10 = (f32[32,640]{1,0:T(8,128)S(1)}, f32[32,640]{1,0:T(8,128)S(1)}, u32[]{:S(2)}, u32[]{:S(2)}) collective-permute-start(f32[32,640]{1,0:T(8,128)S(1)} %get-tuple-element.18), channel_id=1, source_target_pairs={{0,48},{16,0},{32,16},{48,32},{64,112},{80,64},{96,80},{112,96},{1... | collective-permute-start | bytes 245768 | tf_op jit(solution)/shard_map/ppermute | solution.py:64
  29.4 6.8 %collective-permute-start.7 = (f32[32,640]{1,0:T(8,128)S(1)}, f32[32,640]{1,0:T(8,128)S(1)}, u32[]{:S(2)}, u32[]{:S(2)}) collective-permute-start(f32[32,640]{1,0:T(8,128)S(1)} %get-tuple-element.19), channel_id=1, source_target_pairs={{0,16},{16,32},{32,48},{48,0},{64,80},{80,96},{96,112},{112,64},{1... | collective-permute-start | bytes 245768 | tf_op jit(solution)/shard_map/ppermute | solution.py:63
  32.8 21.1 %copy-start.2 = (f32[256,640]{1,0:T(8,128)}, f32[256,640]{1,0:T(8,128)S(1)}, u32[]{:S(2)}) copy-start(f32[256,640]{1,0:T(8,128)S(1)} %fusion) | copy-start | bytes 1966084
  32.8 5.9 %collective-permute-start.15 = (f32[32,640]{1,0:T(8,128)S(1)}, f32[32,640]{1,0:T(8,128)S(1)}, u32[]{:S(2)}, u32[]{:S(2)}) collective-permute-start(f32[32,640]{1,0:T(8,128)S(1)} %get-tuple-element.13), channel_id=1, source_target_pairs={{0,16},{16,32},{32,48},{48,0},{64,80},{80,96},{96,112},{112,64},{1... | collective-permute-start | bytes 245768 | tf_op jit(solution)/shard_map/ppermute | solution.py:63
  33.6 5.0 %collective-permute-start.18 = (f32[32,640]{1,0:T(8,128)S(1)}, f32[32,640]{1,0:T(8,128)S(1)}, u32[]{:S(2)}, u32[]{:S(2)}) collective-permute-start(f32[32,640]{1,0:T(8,128)S(1)} %get-tuple-element.12), channel_id=1, source_target_pairs={{0,48},{16,0},{32,16},{48,32},{64,112},{80,64},{96,80},{112,96},{1... | collective-permute-start | bytes 245768 | tf_op jit(solution)/shard_map/ppermute | solution.py:64
  36.2 6.2 %collective-permute-start.11 = (f32[32,640]{1,0:T(8,128)S(1)}, f32[32,640]{1,0:T(8,128)S(1)}, u32[]{:S(2)}, u32[]{:S(2)}) collective-permute-start(f32[32,640]{1,0:T(8,128)S(1)} %get-tuple-element.16), channel_id=1, source_target_pairs={{0,48},{16,0},{32,16},{48,32},{64,112},{80,64},{96,80},{112,96},{1... | collective-permute-start | bytes 245768 | tf_op jit(solution)/shard_map/ppermute | solution.py:64
  38.2 5.7 %collective-permute-start.8 = (f32[32,640]{1,0:T(8,128)S(1)}, f32[32,640]{1,0:T(8,128)S(1)}, u32[]{:S(2)}, u32[]{:S(2)}) collective-permute-start(f32[32,640]{1,0:T(8,128)S(1)} %get-tuple-element.17), channel_id=1, source_target_pairs={{0,16},{16,32},{32,48},{48,0},{64,80},{80,96},{96,112},{112,64},{1... | collective-permute-start | bytes 245768 | tf_op jit(solution)/shard_map/ppermute | solution.py:63
  38.7 7.3 %collective-permute-start.16 = (f32[32,640]{1,0:T(8,128)S(1)}, f32[32,640]{1,0:T(8,128)S(1)}, u32[]{:S(2)}, u32[]{:S(2)}) collective-permute-start(f32[32,640]{1,0:T(8,128)S(1)} %get-tuple-element.11), channel_id=1, source_target_pairs={{0,16},{16,32},{32,48},{48,0},{64,80},{80,96},{96,112},{112,64},{1... | collective-permute-start | bytes 245768 | tf_op jit(solution)/shard_map/ppermute | solution.py:63
  40.8 5.2 %collective-permute-start.19 = (f32[32,640]{1,0:T(8,128)S(1)}, f32[32,640]{1,0:T(8,128)S(1)}, u32[]{:S(2)}, u32[]{:S(2)}) collective-permute-start(f32[32,640]{1,0:T(8,128)S(1)} %get-tuple-element.10), channel_id=1, source_target_pairs={{0,48},{16,0},{32,16},{48,32},{64,112},{80,64},{96,80},{112,96},{1... | collective-permute-start | bytes 245768 | tf_op jit(solution)/shard_map/ppermute | solution.py:64
  43.9 5.4 %collective-permute-start.12 = (f32[32,640]{1,0:T(8,128)S(1)}, f32[32,640]{1,0:T(8,128)S(1)}, u32[]{:S(2)}, u32[]{:S(2)}) collective-permute-start(f32[32,640]{1,0:T(8,128)S(1)} %get-tuple-element.14), channel_id=1, source_target_pairs={{0,48},{16,0},{32,16},{48,32},{64,112},{80,64},{96,80},{112,96},{1... | collective-permute-start | bytes 245768 | tf_op jit(solution)/shard_map/ppermute | solution.py:64
  44.5 5.7 %collective-permute-start.9 = (f32[32,640]{1,0:T(8,128)S(1)}, f32[32,640]{1,0:T(8,128)S(1)}, u32[]{:S(2)}, u32[]{:S(2)}) collective-permute-start(f32[32,640]{1,0:T(8,128)S(1)} %get-tuple-element.15), channel_id=1, source_target_pairs={{0,16},{16,32},{32,48},{48,0},{64,80},{80,96},{96,112},{112,64},{1... | collective-permute-start | bytes 245768 | tf_op jit(solution)/shard_map/ppermute | solution.py:63
  46.0 7.8 %collective-permute-start.17 = (f32[32,640]{1,0:T(8,128)S(1)}, f32[32,640]{1,0:T(8,128)S(1)}, u32[]{:S(2)}, u32[]{:S(2)}) collective-permute-start(f32[32,640]{1,0:T(8,128)S(1)} %get-tuple-element.9), channel_id=1, source_target_pairs={{0,16},{16,32},{32,48},{48,0},{64,80},{80,96},{96,112},{112,64},{1... | collective-permute-start | bytes 245768 | tf_op jit(solution)/shard_map/ppermute | solution.py:63
  47.1 6.8 %collective-permute-start.20 = (f32[32,640]{1,0:T(8,128)S(1)}, f32[32,640]{1,0:T(8,128)S(1)}, u32[]{:S(2)}, u32[]{:S(2)}) collective-permute-start(f32[32,640]{1,0:T(8,128)S(1)} %get-tuple-element.8), channel_id=1, source_target_pairs={{0,48},{16,0},{32,16},{48,32},{64,112},{80,64},{96,80},{112,96},{1... | collective-permute-start | bytes 245768 | tf_op jit(solution)/shard_map/ppermute | solution.py:64
  50.2 6.1 %collective-permute-start.13 = (f32[32,640]{1,0:T(8,128)S(1)}, f32[32,640]{1,0:T(8,128)S(1)}, u32[]{:S(2)}, u32[]{:S(2)}) collective-permute-start(f32[32,640]{1,0:T(8,128)S(1)} %broadcast_select_fusion.1), channel_id=1, source_target_pairs={{0,64},{16,80},{32,96},{48,112},{64,0},{80,16},{96,32},{112,48},{1... | collective-permute-start | bytes 245768 | tf_op jit(solution)/shard_map/ppermute | solution.py:67
  53.9 6.0 %collective-permute-start.21 = (f32[32,640]{1,0:T(8,128)S(1)}, f32[32,640]{1,0:T(8,128)S(1)}, u32[]{:S(2)}, u32[]{:S(2)}) collective-permute-start(f32[32,640]{1,0:T(8,128)S(1)} %broadcast_select_fusion), channel_id=1, source_target_pairs={{0,64},{16,80},{32,96},{48,112},{64,0},{80,16},{96,32},{112,48},{1... | collective-permute-start | bytes 245768 | tf_op jit(solution)/shard_map/ppermute | solution.py:67
  (1 other events, 18.0 us)

commit v14 on v13

--- a/solution.py
+++ b/solution.py
@@ -57,13 +57,23 @@
                 k = ((r % nx - y) % ny) * 2 + ((r // nx) ^ zl)
                 return lax.dynamic_index_in_dim(res, k, 0, keepdims=False)
 
-            sa = half_block((x - 1) % nx)
-            sb = half_block(nx + (x + 1) % nx)
-            for s in range(1, nx):
-                sa = lax.ppermute(sa, "occ", x_shift(1)) + half_block((x - s - 1) % nx)
-                sb = lax.ppermute(sb, "occ", x_shift(-1)) + half_block(nx + (x + s + 1) % nx)
-            keep = jnp.where(zh == 0, sa, sb)
-            send = jnp.where(zh == 0, sb, sa)
+            def a_blk(t):
+                return half_block(t % nx)
+
+            def b_blk(t):
+                return half_block(nx + t % nx)
+
+            p1 = lax.ppermute(a_blk(x + 2), "occ", x_shift(-1))
+            q1 = lax.ppermute(b_blk(x + 2), "occ", x_shift(1))
+            to_m = jnp.concatenate([a_blk(x + nx - 1) + p1, b_blk(x + nx - 1)], axis=0)
+            to_p = jnp.concatenate([a_blk(x + 1), b_blk(x + 1) + q1], axis=0)
+            total = (
+                lax.ppermute(to_m, "occ", x_shift(-1))
+                + lax.ppermute(to_p, "occ", x_shift(1))
+                + jnp.concatenate([a_blk(x), b_blk(x)], axis=0)
+            )
+            keep = jnp.where(zh == 0, total[:rows], total[rows:])
+            send = jnp.where(zh == 0, total[rows:], total[:rows])
             return keep + lax.ppermute(send, "occ", zhi_swap)
 
         sum_l = ring(res_l)

time: 61.8 us -> 60.7 us (0.982)
  waiting for transfers between devices: 13.3 us -> 21.1 us
  local copies, waits for them, and re-layouts: 6.51 us -> 1.82 us
  starting transfers between devices: 33.1 us -> 28.7 us
    unnamed x13 -> x11, local copies, waits for them, and re-layouts: 5.79 us -> 1.05 us
    ppermute x12 -> x8, starting transfers between devices: 17.4 us -> 12.8 us  [the longest x2 6.57 us: ring(): lax.ppermute(to_m, 'occ', x_shift(-1))]
    ppermute x12 -> x8, waiting for transfers between devices: 2.6 us -> 7.17 us  [the longest x2 4.11 us: ring(): q1 = lax.ppermute(b_blk(x + 2), 'occ', x_shift(1))]
    ppermute x1, waiting for transfers between devices: 3.86 us -> 5.17 us  [body(): z3 = lax.ppermute(yp2, 'vir', z_swap)]
    ppermute x1, waiting for transfers between devices: 1.94 us -> 3.25 us  [body(): yp2 = lax.ppermute(yp1, 'vir', y_shift(-1))]
    select_n x1, other arithmetic: 1.05 us -> 0.03 us  [body(): first = jnp.where(c == 0, sum_l, sum_o)]
    add x4 -> x3, other arithmetic: 0.08 us -> 1.02 us  [the longest x1 0.96 us: ring(): to_p = jnp.concatenate([a_blk(x + 1), b_blk(x + 1) + q1], axis=0)]
    ppermute x1, waiting for transfers between devices: 0.47 us -> 1.24 us  [body(): yp1 = lax.ppermute(own, 'vir', y_shift(-1))]
  transfers between devices with their start and end apart: 22 -> 18, of which waited for: 8 -> 9; matrix products, arithmetic and copies ran while one was open for 21% -> 13% of each run, Pallas kernels for 0% -> 0%
where the time goes in v14:
time: 60.7 us; the launch traced here: 60.2 us
  starting transfers between devices  28.7 us (47%)
  waiting for transfers between devices  21.1 us (35%)
  matrix products  6.16 us (10%)
  local copies, waits for them, and re-layouts  1.82 us (3%)
  other arithmetic  1.81 us (3%)
    ppermute x2, starting transfers between devices, ring(): lax.ppermute(to_m, 'occ', x_shift(-1))  6.57 us
    dot_general x2, matrix products, matmul(): return jnp.dot(a, b, preferred_element_type=jnp.float32, precision=HIGH)  6.16 us
    ppermute x2, starting transfers between devices, ring(): p1 = lax.ppermute(a_blk(x + 2), 'occ', x_shift(-1))  6.06 us
    ppermute x2, starting transfers between devices, ring(): return keep + lax.ppermute(send, 'occ', zhi_swap)  5.4 us
    ppermute x1, waiting for transfers between devices, body(): z3 = lax.ppermute(yp2, 'vir', z_swap)  5.17 us
    ppermute x2, waiting for transfers between devices, ring(): return keep + lax.ppermute(send, 'occ', zhi_swap)  4.29 us
    ppermute x2, waiting for transfers between devices, ring(): q1 = lax.ppermute(b_blk(x + 2), 'occ', x_shift(1))  4.11 us
    ppermute x1, waiting for transfers between devices, body(): yp2 = lax.ppermute(yp1, 'vir', y_shift(-1))  3.25 us
  transfers between devices with their start and end apart: 18, of which 9 were waited for; matrix products, arithmetic and copies ran while one was open for 13% of the time, Pallas kernels for 0%

profile of v14, /device:TPU:24, one launch (start us, length us, event | category | flops | bytes accessed | tf_op | source)
XLA Modules:
  0.0 60.2 jit_solution(18292790083832595926)
XLA Ops:
  0.0 0.7 %collective-permute-start.1 = (f32[32,1280]{1,0:T(8,128)}, f32[32,1280]{1,0:T(8,128)S(1)}, u32[]{:S(2)}, u32[]{:S(2)}) collective-permute-start(f32[32,1280]{1,0:T(8,128)} %param.2), channel_id=1, source_target_pairs={{0,6},{1,7},{2,0},{3,1},{4,2},{5,3},{6,4},{7,5},{8,14},{9,15},{10,... | collective-permute-start | bytes 491528 | tf_op jit(solution)/shard_map/ppermute | solution.py:43
  0.7 1.9 %collective-permute-start = (f32[32,1280]{1,0:T(8,128)}, f32[32,1280]{1,0:T(8,128)S(1)}, u32[]{:S(2)}, u32[]{:S(2)}) collective-permute-start(f32[32,1280]{1,0:T(8,128)} %param.2), channel_id=1, source_target_pairs={{0,8},{1,9},{2,10},{3,11},{4,12},{5,13},{6,14},{7,15},{8,0},{9,1},... | collective-permute-start | bytes 491528 | tf_op jit(solution)/shard_map/ppermute | solution.py:41
  2.7 2.5 %collective-permute-start.5 = (f32[32,1280]{1,0:T(8,128)}, f32[32,1280]{1,0:T(8,128)S(1)}, u32[]{:S(2)}, u32[]{:S(2)}) collective-permute-start(f32[32,1280]{1,0:T(8,128)} %param.2), channel_id=1, source_target_pairs={{0,2},{1,3},{2,4},{3,5},{4,6},{5,7},{6,0},{7,1},{8,10},{9,11},{10,... | collective-permute-start | bytes 491528 | tf_op jit(solution)/shard_map/ppermute | solution.py:42
  5.2 1.0 %constant_dynamic-update-slice_fusion.7 = f32[256,1280]{1,0:T(8,128)S(1)} fusion(f32[32,1280]{1,0:T(8,128)} %param.2), kind=kLoop, calls=%fused_computation.42 | loop fusion | bytes 327680
  6.1 1.2 %collective-permute-done.1 = f32[32,1280]{1,0:T(8,128)S(1)} collective-permute-done((f32[32,1280]{1,0:T(8,128)}, f32[32,1280]{1,0:T(8,128)S(1)}, u32[]{:S(2)}, u32[]{:S(2)}) %collective-permute-start.1) | collective-permute-done | bytes 163872 | tf_op jit(solution)/shard_map/ppermute | solution.py:43
  7.4 1.9 %collective-permute-start.2 = (f32[32,1280]{1,0:T(8,128)S(1)}, f32[32,1280]{1,0:T(8,128)S(1)}, u32[]{:S(2)}, u32[]{:S(2)}) collective-permute-start(f32[32,1280]{1,0:T(8,128)S(1)} %collective-permute-done.1), channel_id=1, source_target_pairs={{0,8},{1,9},{2,10},{3,11},{4,12},{5,13},{6,14},{7,15},{8,0},{9,1},... | collective-permute-start | bytes 491528 | tf_op jit(solution)/shard_map/ppermute | solution.py:44
  9.3 3.2 %collective-permute-start.6 = (f32[32,1280]{1,0:T(8,128)S(1)}, f32[32,1280]{1,0:T(8,128)S(1)}, u32[]{:S(2)}, u32[]{:S(2)}) collective-permute-start(f32[32,1280]{1,0:T(8,128)S(1)} %collective-permute-done), channel_id=1, source_target_pairs={{0,2},{1,3},{2,4},{3,5},{4,6},{5,7},{6,0},{7,1},{8,10},{9,11},{10,... | collective-permute-start | bytes 491528 | tf_op jit(solution)/shard_map/ppermute | solution.py:46
  12.6 3.3 %collective-permute-done.3 = f32[32,1280]{1,0:T(8,128)S(1)} collective-permute-done((f32[32,1280]{1,0:T(8,128)S(1)}, f32[32,1280]{1,0:T(8,128)S(1)}, u32[]{:S(2)}, u32[]{:S(2)}) %collective-permute-start.3) | collective-permute-done | bytes 163872 | tf_op jit(solution)/shard_map/ppermute | solution.py:45
  16.0 5.2 %collective-permute-done.4 = f32[32,1280]{1,0:T(8,128)S(1)} collective-permute-done((f32[32,1280]{1,0:T(8,128)S(1)}, f32[32,1280]{1,0:T(8,128)S(1)}, u32[]{:S(2)}, u32[]{:S(2)}) %collective-permute-start.4) | collective-permute-done | bytes 163872 | tf_op jit(solution)/shard_map/ppermute | solution.py:47
  21.7 4.1 %fusion.2 = f32[256,640]{1,0:T(8,128)S(1)} fusion(f32[256,1280]{1,0:T(8,128)S(1)} %constant_dynamic-update-slice_fusion, f32[1280,640]{1,0:T(8,128)} %param.3), kind=kOutput, calls=%fused_computation.2 | convolution fusion | flops 1259110400 | bytes 5242880 | tf_op jit(solution)/shard_map/dot_general | solution.py:32
  25.8 0.7 %dynamic-slice_bitcast_fusion.9 = (f32[32,640]{1,0:T(8,128)}, f32[32,640]{1,0:T(8,128)S(1)}, f32[32,640]{1,0:T(8,128)S(1)}, f32[32,640]{1,0:T(8,128)}, f32[32,640]{1,0:T(8,128)S(1)}, /*index=5*/f32[32,640]{1,0:T(8,128)}) fusion(f32[8,32,640]{2,1,0:T(8,128)S(1)} %bitcast.36, s32[]{:T(128)S(6)} %select_n.282, s32[]{:T(128)S(6)} %select_n.299, ...), kind=kLoop, calls=%fused_computation.28 | loop fusion | bytes 983064 | tf_op jit(solution)/shard_map/jit(dynamic_index_in_dim)/squeeze | solution.py:58
  26.5 2.8 %collective-permute-start.7 = (f32[32,640]{1,0:T(8,128)}, f32[32,640]{1,0:T(8,128)}, u32[]{:S(2)}, u32[]{:S(2)}) collective-permute-start(f32[32,640]{1,0:T(8,128)} %get-tuple-element.21), channel_id=1, source_target_pairs={{0,48},{16,0},{32,16},{48,32},{64,112},{80,64},{96,80},{112,96},{1... | collective-permute-start | bytes 245768 | tf_op jit(solution)/shard_map/ppermute | solution.py:66
  29.2 2.1 %fusion = f32[256,640]{1,0:T(8,128)S(1)} fusion(f32[256,1280]{1,0:T(8,128)S(1)} %collective-permute-done.12, f32[1280,640]{1,0:T(8,128)S(1)} %copy-done), kind=kOutput, calls=%fused_computation | convolution fusion | flops 1259110400 | bytes 5242880 | tf_op jit(solution)/shard_map/dot_general | solution.py:32
  31.4 3.3 %collective-permute-start.13 = (f32[32,640]{1,0:T(8,128)S(1)}, f32[32,640]{1,0:T(8,128)S(1)}, u32[]{:S(2)}, u32[]{:S(2)}) collective-permute-start(f32[32,640]{1,0:T(8,128)S(1)} %get-tuple-element.13), channel_id=1, source_target_pairs={{0,48},{16,0},{32,16},{48,32},{64,112},{80,64},{96,80},{112,96},{1... | collective-permute-start | bytes 245768 | tf_op jit(solution)/shard_map/ppermute | solution.py:66
  35.2 1.5 %collective-permute-done.13 = f32[32,640]{1,0:T(8,128)S(1)} collective-permute-done((f32[32,640]{1,0:T(8,128)S(1)}, f32[32,640]{1,0:T(8,128)S(1)}, u32[]{:S(2)}, u32[]{:S(2)}) %collective-permute-start.13) | collective-permute-done | bytes 81952 | tf_op jit(solution)/shard_map/ppermute | solution.py:66
  36.7 3.6 %collective-permute-done.15 = f32[32,640]{1,0:T(8,128)S(1)} collective-permute-done((f32[32,640]{1,0:T(8,128)S(1)}, f32[32,640]{1,0:T(8,128)S(1)}, u32[]{:S(2)}, u32[]{:S(2)}) %collective-permute-start.15) | collective-permute-done | bytes 81952 | tf_op jit(solution)/shard_map/ppermute | solution.py:67
  40.3 1.0 %bitcast_add_fusion = (f32[32,640]{1,0:T(8,128)S(1)}, f32[32,640]{1,0:T(8,128)S(1)}, f32[32,640]{1,0:T(8,128)S(1)}, f32[32,640]{1,0:T(8,128)S(1)}) fusion(f32[32,640]{1,0:T(8,128)S(1)} %collective-permute-done.15, f32[8,32,640]{2,1,0:T(8,128)S(1)} %bitcast.39, s32[]{:T(128)S(6)} %select_n.286, f32[32,640]{1,0:T(8,128)S(1)} %collective-permute-done.13, ...), kind=kLoop, calls=%fused_computation.13 | loop fusion | flops 81920 | bytes 983048 | tf_op jit(solution)/shard_map/add | solution.py:69
  41.4 3.3 %collective-permute-start.14 = (f32[64,640]{1,0:T(8,128)S(1)}, f32[64,640]{1,0:T(8,128)S(1)}, u32[]{:S(2)}, u32[]{:S(2)}) collective-permute-start(f32[64,640]{1,0:T(8,128)S(1)} %pad_maximum_fusion.2), channel_id=1, source_target_pairs={{0,48},{16,0},{32,16},{48,32},{64,112},{80,64},{96,80},{112,96},{1... | collective-permute-start | bytes 491528 | tf_op jit(solution)/shard_map/ppermute | solution.py:71
  44.8 3.3 %collective-permute-start.8 = (f32[64,640]{1,0:T(8,128)S(1)}, f32[64,640]{1,0:T(8,128)S(1)}, u32[]{:S(2)}, u32[]{:S(2)}) collective-permute-start(f32[64,640]{1,0:T(8,128)S(1)} %pad_maximum_fusion), channel_id=1, source_target_pairs={{0,48},{16,0},{32,16},{48,32},{64,112},{80,64},{96,80},{112,96},{1... | collective-permute-start | bytes 491528 | tf_op jit(solution)/shard_map/ppermute | solution.py:71
  48.1 1.5 %collective-permute-done.16 = f32[64,640]{1,0:T(8,128)S(1)} collective-permute-done((f32[64,640]{1,0:T(8,128)S(1)}, f32[64,640]{1,0:T(8,128)S(1)}, u32[]{:S(2)}, u32[]{:S(2)}) %collective-permute-start.16) | collective-permute-done | bytes 163872 | tf_op jit(solution)/shard_map/ppermute | solution.py:72
  49.7 3.7 %collective-permute-start.17 = (f32[32,640]{1,0:T(8,128)S(1)}, f32[32,640]{1,0:T(8,128)S(1)}, u32[]{:S(2)}, u32[]{:S(2)}) collective-permute-start(f32[32,640]{1,0:T(8,128)S(1)} %slice_select_fusion), channel_id=1, source_target_pairs={{0,64},{16,80},{32,96},{48,112},{64,0},{80,16},{96,32},{112,48},{1... | collective-permute-start | bytes 245768 | tf_op jit(solution)/shard_map/ppermute | solution.py:77
  53.4 1.7 %collective-permute-start.11 = (f32[32,640]{1,0:T(8,128)S(1)}, f32[32,640]{1,0:T(8,128)S(1)}, u32[]{:S(2)}, u32[]{:S(2)}) collective-permute-start(f32[32,640]{1,0:T(8,128)S(1)} %slice_select_fusion.1), channel_id=1, source_target_pairs={{0,64},{16,80},{32,96},{48,112},{64,0},{80,16},{96,32},{112,48},{1... | collective-permute-start | bytes 245768 | tf_op jit(solution)/shard_map/ppermute | solution.py:77
  55.1 1.0 %collective-permute-done.17 = f32[32,640]{1,0:T(8,128)S(1)} collective-permute-done((f32[32,640]{1,0:T(8,128)S(1)}, f32[32,640]{1,0:T(8,128)S(1)}, u32[]{:S(2)}, u32[]{:S(2)}) %collective-permute-start.17) | collective-permute-done | bytes 81952 | tf_op jit(solution)/shard_map/ppermute | solution.py:77
  56.1 3.3 %collective-permute-done.11 = f32[32,640]{1,0:T(8,128)S(1)} collective-permute-done((f32[32,640]{1,0:T(8,128)S(1)}, f32[32,640]{1,0:T(8,128)S(1)}, u32[]{:S(2)}, u32[]{:S(2)}) %collective-permute-start.11) | collective-permute-done | bytes 81952 | tf_op jit(solution)/shard_map/ppermute | solution.py:77
  (40 shorter events, 1.9 us)
Async XLA Ops:
  0.0 7.4 %collective-permute-start.1 = (f32[32,1280]{1,0:T(8,128)}, f32[32,1280]{1,0:T(8,128)S(1)}, u32[]{:S(2)}, u32[]{:S(2)}) collective-permute-start(f32[32,1280]{1,0:T(8,128)} %param.2), channel_id=1, source_target_pairs={{0,6},{1,7},{2,0},{3,1},{4,2},{5,3},{6,4},{7,5},{8,14},{9,15},{10,... | collective-permute-start | bytes 491528 | tf_op jit(solution)/shard_map/ppermute | solution.py:43
  0.7 8.5 %collective-permute-start = (f32[32,1280]{1,0:T(8,128)}, f32[32,1280]{1,0:T(8,128)S(1)}, u32[]{:S(2)}, u32[]{:S(2)}) collective-permute-start(f32[32,1280]{1,0:T(8,128)} %param.2), channel_id=1, source_target_pairs={{0,8},{1,9},{2,10},{3,11},{4,12},{5,13},{6,14},{7,15},{8,0},{9,1},... | collective-permute-start | bytes 491528 | tf_op jit(solution)/shard_map/ppermute | solution.py:41
  2.7 18.5 %collective-permute-start.5 = (f32[32,1280]{1,0:T(8,128)}, f32[32,1280]{1,0:T(8,128)S(1)}, u32[]{:S(2)}, u32[]{:S(2)}) collective-permute-start(f32[32,1280]{1,0:T(8,128)} %param.2), channel_id=1, source_target_pairs={{0,2},{1,3},{2,4},{3,5},{4,6},{5,7},{6,0},{7,1},{8,10},{9,11},{10,... | collective-permute-start | bytes 491528 | tf_op jit(solution)/shard_map/ppermute | solution.py:42
  7.4 8.6 %collective-permute-start.2 = (f32[32,1280]{1,0:T(8,128)S(1)}, f32[32,1280]{1,0:T(8,128)S(1)}, u32[]{:S(2)}, u32[]{:S(2)}) collective-permute-start(f32[32,1280]{1,0:T(8,128)S(1)} %collective-permute-done.1), channel_id=1, source_target_pairs={{0,8},{1,9},{2,10},{3,11},{4,12},{5,13},{6,14},{7,15},{8,0},{9,1},... | collective-permute-start | bytes 491528 | tf_op jit(solution)/shard_map/ppermute | solution.py:44
  9.3 6.5 %collective-permute-start.3 = (f32[32,1280]{1,0:T(8,128)S(1)}, f32[32,1280]{1,0:T(8,128)S(1)}, u32[]{:S(2)}, u32[]{:S(2)}) collective-permute-start(f32[32,1280]{1,0:T(8,128)S(1)} %collective-permute-done.1), channel_id=1, source_target_pairs={{0,6},{1,7},{2,0},{3,1},{4,2},{5,3},{6,4},{7,5},{8,14},{9,15},{10,... | collective-permute-start | bytes 491528 | tf_op jit(solution)/shard_map/ppermute | solution.py:45
  9.3 11.9 %collective-permute-start.6 = (f32[32,1280]{1,0:T(8,128)S(1)}, f32[32,1280]{1,0:T(8,128)S(1)}, u32[]{:S(2)}, u32[]{:S(2)}) collective-permute-start(f32[32,1280]{1,0:T(8,128)S(1)} %collective-permute-done), channel_id=1, source_target_pairs={{0,2},{1,3},{2,4},{3,5},{4,6},{5,7},{6,0},{7,1},{8,10},{9,11},{10,... | collective-permute-start | bytes 491528 | tf_op jit(solution)/shard_map/ppermute | solution.py:46
  15.8 5.3 %collective-permute-start.4 = (f32[32,1280]{1,0:T(8,128)S(1)}, f32[32,1280]{1,0:T(8,128)S(1)}, u32[]{:S(2)}, u32[]{:S(2)}) collective-permute-start(f32[32,1280]{1,0:T(8,128)S(1)} %collective-permute-done.3), channel_id=1, source_target_pairs={{0,8},{1,9},{2,10},{3,11},{4,12},{5,13},{6,14},{7,15},{8,0},{9,1},... | collective-permute-start | bytes 491528 | tf_op jit(solution)/shard_map/ppermute | solution.py:47
  21.2 8.0 %collective-permute-start.12 = (f32[256,1280]{1,0:T(8,128)S(1)}, f32[256,1280]{1,0:T(8,128)S(1)}, u32[]{:S(2)}, u32[]{:S(2)}) collective-permute-start(f32[256,1280]{1,0:T(8,128)S(1)} %constant_dynamic-update-slice_fusion), channel_id=1, source_target_pairs={{0,1},{1,0},{2,3},{3,2},{4,5},{5,4},{6,7},{7,6},{8,9},{9,8},{10,11... | collective-permute-start | bytes 3932168 | tf_op jit(solution)/shard_map/ppermute | solution.py:51
  21.6 7.6 %copy-start = (f32[1280,640]{1,0:T(8,128)S(1)}, f32[1280,640]{1,0:T(8,128)}, u32[]{:S(2)}) copy-start(f32[1280,640]{1,0:T(8,128)} %param.3) | copy-start | bytes 9830404
  26.5 8.2 %collective-permute-start.7 = (f32[32,640]{1,0:T(8,128)}, f32[32,640]{1,0:T(8,128)}, u32[]{:S(2)}, u32[]{:S(2)}) collective-permute-start(f32[32,640]{1,0:T(8,128)} %get-tuple-element.21), channel_id=1, source_target_pairs={{0,48},{16,0},{32,16},{48,32},{64,112},{80,64},{96,80},{112,96},{1... | collective-permute-start | bytes 245768 | tf_op jit(solution)/shard_map/ppermute | solution.py:66
  29.2 6.0 %collective-permute-start.9 = (f32[32,640]{1,0:T(8,128)}, f32[32,640]{1,0:T(8,128)}, u32[]{:S(2)}, u32[]{:S(2)}) collective-permute-start(f32[32,640]{1,0:T(8,128)} %get-tuple-element.19), channel_id=1, source_target_pairs={{0,16},{16,32},{32,48},{48,0},{64,80},{80,96},{96,112},{112,64},{1... | collective-permute-start | bytes 245768 | tf_op jit(solution)/shard_map/ppermute | solution.py:67
  31.3 13.4 %copy-start.1 = (f32[32,640]{1,0:T(8,128)S(1)}, f32[32,640]{1,0:T(8,128)}, u32[]{:S(2)}) copy-start(f32[32,640]{1,0:T(8,128)} %get-tuple-element.16) | copy-start | bytes 245764
  31.4 5.4 %collective-permute-start.13 = (f32[32,640]{1,0:T(8,128)S(1)}, f32[32,640]{1,0:T(8,128)S(1)}, u32[]{:S(2)}, u32[]{:S(2)}) collective-permute-start(f32[32,640]{1,0:T(8,128)S(1)} %get-tuple-element.13), channel_id=1, source_target_pairs={{0,48},{16,0},{32,16},{48,32},{64,112},{80,64},{96,80},{112,96},{1... | collective-permute-start | bytes 245768 | tf_op jit(solution)/shard_map/ppermute | solution.py:66
  34.7 5.7 %collective-permute-start.15 = (f32[32,640]{1,0:T(8,128)S(1)}, f32[32,640]{1,0:T(8,128)S(1)}, u32[]{:S(2)}, u32[]{:S(2)}) collective-permute-start(f32[32,640]{1,0:T(8,128)S(1)} %get-tuple-element.11), channel_id=1, source_target_pairs={{0,16},{16,32},{32,48},{48,0},{64,80},{80,96},{96,112},{112,64},{1... | collective-permute-start | bytes 245768 | tf_op jit(solution)/shard_map/ppermute | solution.py:67
  41.3 8.3 %collective-permute-start.16 = (f32[64,640]{1,0:T(8,128)S(1)}, f32[64,640]{1,0:T(8,128)S(1)}, u32[]{:S(2)}, u32[]{:S(2)}) collective-permute-start(f32[64,640]{1,0:T(8,128)S(1)} %pad_maximum_fusion.3), channel_id=1, source_target_pairs={{0,16},{16,32},{32,48},{48,0},{64,80},{80,96},{96,112},{112,64},{1... | collective-permute-start | bytes 491528 | tf_op jit(solution)/shard_map/ppermute | solution.py:72
  41.4 8.2 %collective-permute-start.14 = (f32[64,640]{1,0:T(8,128)S(1)}, f32[64,640]{1,0:T(8,128)S(1)}, u32[]{:S(2)}, u32[]{:S(2)}) collective-permute-start(f32[64,640]{1,0:T(8,128)S(1)} %pad_maximum_fusion.2), channel_id=1, source_target_pairs={{0,48},{16,0},{32,16},{48,32},{64,112},{80,64},{96,80},{112,96},{1... | collective-permute-start | bytes 491528 | tf_op jit(solution)/shard_map/ppermute | solution.py:71
  44.7 8.6 %collective-permute-start.10 = (f32[64,640]{1,0:T(8,128)S(1)}, f32[64,640]{1,0:T(8,128)S(1)}, u32[]{:S(2)}, u32[]{:S(2)}) collective-permute-start(f32[64,640]{1,0:T(8,128)S(1)} %pad_maximum_fusion.1), channel_id=1, source_target_pairs={{0,16},{16,32},{32,48},{48,0},{64,80},{80,96},{96,112},{112,64},{1... | collective-permute-start | bytes 491528 | tf_op jit(solution)/shard_map/ppermute | solution.py:72
  44.8 8.5 %collective-permute-start.8 = (f32[64,640]{1,0:T(8,128)S(1)}, f32[64,640]{1,0:T(8,128)S(1)}, u32[]{:S(2)}, u32[]{:S(2)}) collective-permute-start(f32[64,640]{1,0:T(8,128)S(1)} %pad_maximum_fusion), channel_id=1, source_target_pairs={{0,48},{16,0},{32,16},{48,32},{64,112},{80,64},{96,80},{112,96},{1... | collective-permute-start | bytes 491528 | tf_op jit(solution)/shard_map/ppermute | solution.py:71
  49.7 6.5 %collective-permute-start.17 = (f32[32,640]{1,0:T(8,128)S(1)}, f32[32,640]{1,0:T(8,128)S(1)}, u32[]{:S(2)}, u32[]{:S(2)}) collective-permute-start(f32[32,640]{1,0:T(8,128)S(1)} %slice_select_fusion), channel_id=1, source_target_pairs={{0,64},{16,80},{32,96},{48,112},{64,0},{80,16},{96,32},{112,48},{1... | collective-permute-start | bytes 245768 | tf_op jit(solution)/shard_map/ppermute | solution.py:77
  53.4 6.0 %collective-permute-start.11 = (f32[32,640]{1,0:T(8,128)S(1)}, f32[32,640]{1,0:T(8,128)S(1)}, u32[]{:S(2)}, u32[]{:S(2)}) collective-permute-start(f32[32,640]{1,0:T(8,128)S(1)} %slice_select_fusion.1), channel_id=1, source_target_pairs={{0,64},{16,80},{32,96},{48,112},{64,0},{80,16},{96,32},{112,48},{1... | collective-permute-start | bytes 245768 | tf_op jit(solution)/shard_map/ppermute | solution.py:77

commit v15 on v14

--- a/solution.py
+++ b/solution.py
@@ -76,8 +76,9 @@
             send = jnp.where(zh == 0, total[rows:], total[:rows])
             return keep + lax.ppermute(send, "occ", zhi_swap)
 
+        res_o = matmul(other, half).reshape(8, rows, -1)
+        res_l, res_o = lax.optimization_barrier((res_l, res_o))
         sum_l = ring(res_l)
-        res_o = matmul(other, half).reshape(8, rows, -1)
         sum_o = ring(res_o)
         first = jnp.where(c == 0, sum_l, sum_o)
         second = jnp.where(c == 0, sum_o, sum_l)

time: 60.7 us -> 58.7 us (0.967)
  waiting for transfers between devices: 21.1 us -> 14.2 us
  local copies, waits for them, and re-layouts: 1.82 us -> 6.52 us
  other arithmetic: 1.81 us -> 0.89 us
    unnamed x11 -> x9, local copies, waits for them, and re-layouts: 1.05 us -> 5.77 us
    ppermute x2, waiting for transfers between devices: 1.54 us -> 0.01 us  [ring(): p1 = lax.ppermute(a_blk(x + 2), 'occ', x_shift(-1))]
    ppermute x1, waiting for transfers between devices: 5.17 us -> 3.85 us  [body(): z3 = lax.ppermute(yp2, 'vir', z_swap)]
    ppermute x1, waiting for transfers between devices: 3.25 us -> 1.96 us  [body(): yp2 = lax.ppermute(yp1, 'vir', y_shift(-1))]
    ppermute x2, waiting for transfers between devices: 4.11 us -> 3.1 us  [ring(): q1 = lax.ppermute(b_blk(x + 2), 'occ', x_shift(1))]
    add x1 -> x2, other arithmetic: 0.96 us -> 0.04 us  [ring(): to_p = jnp.concatenate([a_blk(x + 1), b_blk(x + 1) + q1], axis=0)]
    ppermute x2, starting transfers between devices: 0.01 us -> 0.83 us  [ring(): q1 = lax.ppermute(b_blk(x + 2), 'occ', x_shift(1))]
    ppermute x1, waiting for transfers between devices: 1.24 us -> 0.48 us  [body(): yp1 = lax.ppermute(own, 'vir', y_shift(-1))]
  transfers between devices with their start and end apart: 18 -> 18, of which waited for: 9 -> 7; matrix products, arithmetic and copies ran while one was open for 13% -> 16% of each run, Pallas kernels for 0% -> 0%
where the time goes in v15:
time: 58.7 us; the launch traced here: 57.7 us
  starting transfers between devices  29.3 us (50%)
  waiting for transfers between devices  14.2 us (24%)
  matrix products  6.7 us (11%)
  local copies, waits for them, and re-layouts  6.52 us (11%)
  other arithmetic  0.89 us (2%)
    dot_general x2, matrix products, matmul(): return jnp.dot(a, b, preferred_element_type=jnp.float32, precision=HIGH)  6.7 us
    ppermute x2, starting transfers between devices, ring(): lax.ppermute(to_m, 'occ', x_shift(-1))  6.57 us
    ppermute x2, starting transfers between devices, ring(): return keep + lax.ppermute(send, 'occ', zhi_swap)  5.9 us
    unnamed x9, local copies, waits for them, and re-layouts  5.77 us
    ppermute x2, starting transfers between devices, ring(): p1 = lax.ppermute(a_blk(x + 2), 'occ', x_shift(-1))  5.39 us
    ppermute x1, waiting for transfers between devices, body(): z3 = lax.ppermute(yp2, 'vir', z_swap)  3.85 us
    ppermute x2, waiting for transfers between devices, ring(): return keep + lax.ppermute(send, 'occ', zhi_swap)  3.78 us
    ppermute x1, starting transfers between devices, body(): ym1z = lax.ppermute(z1, 'vir', y_shift(1))  3.23 us
  transfers between devices with their start and end apart: 18, of which 7 were waited for; matrix products, arithmetic and copies ran while one was open for 16% of the time, Pallas kernels for 0%

profile of v15, /device:TPU:24, one launch (start us, length us, event | category | flops | bytes accessed | tf_op | source)
XLA Modules:
  0.0 57.7 jit_solution(9395012424764301213)
XLA Ops:
  0.0 0.7 %collective-permute-start.1 = (f32[32,1280]{1,0:T(8,128)}, f32[32,1280]{1,0:T(8,128)S(1)}, u32[]{:S(2)}, u32[]{:S(2)}) collective-permute-start(f32[32,1280]{1,0:T(8,128)} %param.2), channel_id=1, source_target_pairs={{0,6},{1,7},{2,0},{3,1},{4,2},{5,3},{6,4},{7,5},{8,14},{9,15},{10,... | collective-permute-start | bytes 491528 | tf_op jit(solution)/shard_map/ppermute | solution.py:43
  0.7 1.9 %collective-permute-start = (f32[32,1280]{1,0:T(8,128)}, f32[32,1280]{1,0:T(8,128)S(1)}, u32[]{:S(2)}, u32[]{:S(2)}) collective-permute-start(f32[32,1280]{1,0:T(8,128)} %param.2), channel_id=1, source_target_pairs={{0,8},{1,9},{2,10},{3,11},{4,12},{5,13},{6,14},{7,15},{8,0},{9,1},... | collective-permute-start | bytes 491528 | tf_op jit(solution)/shard_map/ppermute | solution.py:41
  2.7 2.5 %collective-permute-start.5 = (f32[32,1280]{1,0:T(8,128)}, f32[32,1280]{1,0:T(8,128)S(1)}, u32[]{:S(2)}, u32[]{:S(2)}) collective-permute-start(f32[32,1280]{1,0:T(8,128)} %param.2), channel_id=1, source_target_pairs={{0,2},{1,3},{2,4},{3,5},{4,6},{5,7},{6,0},{7,1},{8,10},{9,11},{10,... | collective-permute-start | bytes 491528 | tf_op jit(solution)/shard_map/ppermute | solution.py:42
  5.2 1.7 %constant_dynamic-update-slice_fusion.7 = f32[256,1280]{1,0:T(8,128)} fusion(f32[32,1280]{1,0:T(8,128)} %param.2), kind=kLoop, calls=%fused_computation.42 | loop fusion | bytes 327680
  7.4 1.9 %collective-permute-start.2 = (f32[32,1280]{1,0:T(8,128)S(1)}, f32[32,1280]{1,0:T(8,128)S(1)}, u32[]{:S(2)}, u32[]{:S(2)}) collective-permute-start(f32[32,1280]{1,0:T(8,128)S(1)} %collective-permute-done.1), channel_id=1, source_target_pairs={{0,8},{1,9},{2,10},{3,11},{4,12},{5,13},{6,14},{7,15},{8,0},{9,1},... | collective-permute-start | bytes 491528 | tf_op jit(solution)/shard_map/ppermute | solution.py:44
  9.3 3.2 %collective-permute-start.6 = (f32[32,1280]{1,0:T(8,128)S(1)}, f32[32,1280]{1,0:T(8,128)S(1)}, u32[]{:S(2)}, u32[]{:S(2)}) collective-permute-start(f32[32,1280]{1,0:T(8,128)S(1)} %collective-permute-done), channel_id=1, source_target_pairs={{0,2},{1,3},{2,4},{3,5},{4,6},{5,7},{6,0},{7,1},{8,10},{9,11},{10,... | collective-permute-start | bytes 491528 | tf_op jit(solution)/shard_map/ppermute | solution.py:46
  13.9 2.0 %collective-permute-done.3 = f32[32,1280]{1,0:T(8,128)S(1)} collective-permute-done((f32[32,1280]{1,0:T(8,128)S(1)}, f32[32,1280]{1,0:T(8,128)S(1)}, u32[]{:S(2)}, u32[]{:S(2)}) %collective-permute-start.3) | collective-permute-done | bytes 163872 | tf_op jit(solution)/shard_map/ppermute | solution.py:45
  15.9 0.7 %constant_dynamic-update-slice_fusion.4 = f32[256,1280]{1,0:T(8,128)} fusion(f32[256,1280]{1,0:T(8,128)} %constant_dynamic-update-slice_fusion.5, f32[32,1280]{1,0:T(8,128)S(1)} %collective-permute-done.2), kind=kLoop, calls=%fused_computation.39 | loop fusion | bytes 327680
  17.3 3.8 %collective-permute-done.4 = f32[32,1280]{1,0:T(8,128)S(1)} collective-permute-done((f32[32,1280]{1,0:T(8,128)S(1)}, f32[32,1280]{1,0:T(8,128)S(1)}, u32[]{:S(2)}, u32[]{:S(2)}) %collective-permute-start.4) | collective-permute-done | bytes 163872 | tf_op jit(solution)/shard_map/ppermute | solution.py:47
  21.8 0.7 %constant_dynamic-update-slice_fusion.1 = f32[256,1280]{1,0:T(8,128)} fusion(f32[256,1280]{1,0:T(8,128)} %constant_dynamic-update-slice_fusion.2, f32[32,1280]{1,0:T(8,128)S(1)} %collective-permute-done.5), kind=kLoop, calls=%fused_computation.36 | loop fusion | bytes 327680
  23.2 3.4 %fusion.2 = f32[256,640]{1,0:T(8,128)S(1)} fusion(f32[256,1280]{1,0:T(8,128)} %constant_dynamic-update-slice_fusion, f32[1280,640]{1,0:T(8,128)S(1)} %copy-done), kind=kOutput, calls=%fused_computation.2 | convolution fusion | flops 1259110400 | bytes 5242880 | tf_op jit(solution)/shard_map/dot_general | solution.py:32
  26.5 3.4 %fusion = f32[256,640]{1,0:T(8,128)S(1)} fusion(f32[256,1280]{1,0:T(8,128)} %collective-permute-done.7, f32[1280,640]{1,0:T(8,128)S(1)} %copy-done), kind=kOutput, calls=%fused_computation | convolution fusion | flops 1259110400 | bytes 5242880 | tf_op jit(solution)/shard_map/dot_general | solution.py:32
  29.9 2.8 %collective-permute-start.13 = (f32[32,640]{1,0:T(8,128)S(1)}, f32[32,640]{1,0:T(8,128)S(1)}, u32[]{:S(2)}, u32[]{:S(2)}) collective-permute-start(f32[32,640]{1,0:T(8,128)S(1)} %get-tuple-element.17), channel_id=1, source_target_pairs={{0,48},{16,0},{32,16},{48,32},{64,112},{80,64},{96,80},{112,96},{1... | collective-permute-start | bytes 245768 | tf_op jit(solution)/shard_map/ppermute | solution.py:66
  32.8 0.8 %collective-permute-start.10 = (f32[32,640]{1,0:T(8,128)S(1)}, f32[32,640]{1,0:T(8,128)S(1)}, u32[]{:S(2)}, u32[]{:S(2)}) collective-permute-start(f32[32,640]{1,0:T(8,128)S(1)} %get-tuple-element.23), channel_id=1, source_target_pairs={{0,16},{16,32},{32,48},{48,0},{64,80},{80,96},{96,112},{112,64},{1... | collective-permute-start | bytes 245768 | tf_op jit(solution)/shard_map/ppermute | solution.py:67
  33.6 2.6 %collective-permute-start.8 = (f32[32,640]{1,0:T(8,128)S(1)}, f32[32,640]{1,0:T(8,128)S(1)}, u32[]{:S(2)}, u32[]{:S(2)}) collective-permute-start(f32[32,640]{1,0:T(8,128)S(1)} %get-tuple-element.25), channel_id=1, source_target_pairs={{0,48},{16,0},{32,16},{48,32},{64,112},{80,64},{96,80},{112,96},{1... | collective-permute-start | bytes 245768 | tf_op jit(solution)/shard_map/ppermute | solution.py:66
  36.2 3.1 %collective-permute-done.15 = f32[32,640]{1,0:T(8,128)S(1)} collective-permute-done((f32[32,640]{1,0:T(8,128)S(1)}, f32[32,640]{1,0:T(8,128)S(1)}, u32[]{:S(2)}, u32[]{:S(2)}) %collective-permute-start.15) | collective-permute-done | bytes 81952 | tf_op jit(solution)/shard_map/ppermute | solution.py:67
  39.4 3.3 %collective-permute-start.14 = (f32[64,640]{1,0:T(8,128)S(1)}, f32[64,640]{1,0:T(8,128)S(1)}, u32[]{:S(2)}, u32[]{:S(2)}) collective-permute-start(f32[64,640]{1,0:T(8,128)S(1)} %pad_maximum_fusion.2), channel_id=1, source_target_pairs={{0,48},{16,0},{32,16},{48,32},{64,112},{80,64},{96,80},{112,96},{1... | collective-permute-start | bytes 491528 | tf_op jit(solution)/shard_map/ppermute | solution.py:71
  42.9 3.3 %collective-permute-start.9 = (f32[64,640]{1,0:T(8,128)S(1)}, f32[64,640]{1,0:T(8,128)S(1)}, u32[]{:S(2)}, u32[]{:S(2)}) collective-permute-start(f32[64,640]{1,0:T(8,128)S(1)} %pad_maximum_fusion), channel_id=1, source_target_pairs={{0,48},{16,0},{32,16},{48,32},{64,112},{80,64},{96,80},{112,96},{1... | collective-permute-start | bytes 491528 | tf_op jit(solution)/shard_map/ppermute | solution.py:71
  46.2 1.0 %collective-permute-done.16 = f32[64,640]{1,0:T(8,128)S(1)} collective-permute-done((f32[64,640]{1,0:T(8,128)S(1)}, f32[64,640]{1,0:T(8,128)S(1)}, u32[]{:S(2)}, u32[]{:S(2)}) %collective-permute-start.16) | collective-permute-done | bytes 163872 | tf_op jit(solution)/shard_map/ppermute | solution.py:72
  47.2 3.7 %collective-permute-start.17 = (f32[32,640]{1,0:T(8,128)S(1)}, f32[32,640]{1,0:T(8,128)S(1)}, u32[]{:S(2)}, u32[]{:S(2)}) collective-permute-start(f32[32,640]{1,0:T(8,128)S(1)} %slice_select_fusion), channel_id=1, source_target_pairs={{0,64},{16,80},{32,96},{48,112},{64,0},{80,16},{96,32},{112,48},{1... | collective-permute-start | bytes 245768 | tf_op jit(solution)/shard_map/ppermute | solution.py:77
  50.9 2.2 %collective-permute-start.12 = (f32[32,640]{1,0:T(8,128)S(1)}, f32[32,640]{1,0:T(8,128)S(1)}, u32[]{:S(2)}, u32[]{:S(2)}) collective-permute-start(f32[32,640]{1,0:T(8,128)S(1)} %slice_select_fusion.1), channel_id=1, source_target_pairs={{0,64},{16,80},{32,96},{48,112},{64,0},{80,16},{96,32},{112,48},{1... | collective-permute-start | bytes 245768 | tf_op jit(solution)/shard_map/ppermute | solution.py:77
  53.2 1.0 %collective-permute-done.17 = f32[32,640]{1,0:T(8,128)S(1)} collective-permute-done((f32[32,640]{1,0:T(8,128)S(1)}, f32[32,640]{1,0:T(8,128)S(1)}, u32[]{:S(2)}, u32[]{:S(2)}) %collective-permute-start.17) | collective-permute-done | bytes 81952 | tf_op jit(solution)/shard_map/ppermute | solution.py:77
  54.1 2.8 %collective-permute-done.12 = f32[32,640]{1,0:T(8,128)S(1)} collective-permute-done((f32[32,640]{1,0:T(8,128)S(1)}, f32[32,640]{1,0:T(8,128)S(1)}, u32[]{:S(2)}, u32[]{:S(2)}) %collective-permute-start.12) | collective-permute-done | bytes 81952 | tf_op jit(solution)/shard_map/ppermute | solution.py:77
  57.0 0.7 %pad_maximum_fusion.4 = f32[64,640]{1,0:T(8,128)} fusion(f32[32,640]{1,0:T(8,128)S(1)} %broadcast_select_fusion, f32[32,640]{1,0:T(8,128)S(1)} %get-tuple-element.9), kind=kLoop, calls=%fused_computation.12 | loop fusion | flops 40960 | bytes 327680 | tf_op jit(solution)/shard_map/concatenate | solution.py:85
  (39 shorter events, 4.4 us)
Async XLA Ops:
  0.0 7.4 %collective-permute-start.1 = (f32[32,1280]{1,0:T(8,128)}, f32[32,1280]{1,0:T(8,128)S(1)}, u32[]{:S(2)}, u32[]{:S(2)}) collective-permute-start(f32[32,1280]{1,0:T(8,128)} %param.2), channel_id=1, source_target_pairs={{0,6},{1,7},{2,0},{3,1},{4,2},{5,3},{6,4},{7,5},{8,14},{9,15},{10,... | collective-permute-start | bytes 491528 | tf_op jit(solution)/shard_map/ppermute | solution.py:43
  0.7 8.5 %collective-permute-start = (f32[32,1280]{1,0:T(8,128)}, f32[32,1280]{1,0:T(8,128)S(1)}, u32[]{:S(2)}, u32[]{:S(2)}) collective-permute-start(f32[32,1280]{1,0:T(8,128)} %param.2), channel_id=1, source_target_pairs={{0,8},{1,9},{2,10},{3,11},{4,12},{5,13},{6,14},{7,15},{8,0},{9,1},... | collective-permute-start | bytes 491528 | tf_op jit(solution)/shard_map/ppermute | solution.py:41
  2.7 19.1 %collective-permute-start.5 = (f32[32,1280]{1,0:T(8,128)}, f32[32,1280]{1,0:T(8,128)S(1)}, u32[]{:S(2)}, u32[]{:S(2)}) collective-permute-start(f32[32,1280]{1,0:T(8,128)} %param.2), channel_id=1, source_target_pairs={{0,2},{1,3},{2,4},{3,5},{4,6},{5,7},{6,0},{7,1},{8,10},{9,11},{10,... | collective-permute-start | bytes 491528 | tf_op jit(solution)/shard_map/ppermute | solution.py:42
  5.2 18.0 %copy-start = (f32[1280,640]{1,0:T(8,128)S(1)}, f32[1280,640]{1,0:T(8,128)}, u32[]{:S(2)}) copy-start(f32[1280,640]{1,0:T(8,128)} %param.3) | copy-start | bytes 9830404
  7.4 8.6 %collective-permute-start.2 = (f32[32,1280]{1,0:T(8,128)S(1)}, f32[32,1280]{1,0:T(8,128)S(1)}, u32[]{:S(2)}, u32[]{:S(2)}) collective-permute-start(f32[32,1280]{1,0:T(8,128)S(1)} %collective-permute-done.1), channel_id=1, source_target_pairs={{0,8},{1,9},{2,10},{3,11},{4,12},{5,13},{6,14},{7,15},{8,0},{9,1},... | collective-permute-start | bytes 491528 | tf_op jit(solution)/shard_map/ppermute | solution.py:44
  9.3 6.5 %collective-permute-start.3 = (f32[32,1280]{1,0:T(8,128)S(1)}, f32[32,1280]{1,0:T(8,128)S(1)}, u32[]{:S(2)}, u32[]{:S(2)}) collective-permute-start(f32[32,1280]{1,0:T(8,128)S(1)} %collective-permute-done.1), channel_id=1, source_target_pairs={{0,6},{1,7},{2,0},{3,1},{4,2},{5,3},{6,4},{7,5},{8,14},{9,15},{10,... | collective-permute-start | bytes 491528 | tf_op jit(solution)/shard_map/ppermute | solution.py:45
  9.3 13.2 %collective-permute-start.6 = (f32[32,1280]{1,0:T(8,128)S(1)}, f32[32,1280]{1,0:T(8,128)S(1)}, u32[]{:S(2)}, u32[]{:S(2)}) collective-permute-start(f32[32,1280]{1,0:T(8,128)S(1)} %collective-permute-done), channel_id=1, source_target_pairs={{0,2},{1,3},{2,4},{3,5},{4,6},{5,7},{6,0},{7,1},{8,10},{9,11},{10,... | collective-permute-start | bytes 491528 | tf_op jit(solution)/shard_map/ppermute | solution.py:46
  15.8 5.3 %collective-permute-start.4 = (f32[32,1280]{1,0:T(8,128)S(1)}, f32[32,1280]{1,0:T(8,128)S(1)}, u32[]{:S(2)}, u32[]{:S(2)}) collective-permute-start(f32[32,1280]{1,0:T(8,128)S(1)} %collective-permute-done.3), channel_id=1, source_target_pairs={{0,8},{1,9},{2,10},{3,11},{4,12},{5,13},{6,14},{7,15},{8,0},{9,1},... | collective-permute-start | bytes 491528 | tf_op jit(solution)/shard_map/ppermute | solution.py:47
  23.2 3.4 %collective-permute-start.7 = (f32[256,1280]{1,0:T(8,128)}, f32[256,1280]{1,0:T(8,128)}, u32[]{:S(2)}, u32[]{:S(2)}) collective-permute-start(f32[256,1280]{1,0:T(8,128)} %constant_dynamic-update-slice_fusion), channel_id=1, source_target_pairs={{0,1},{1,0},{2,3},{3,2},{4,5},{5,4},{6,7},{7,6},{8,9},{9,8},{10,11... | collective-permute-start | bytes 3932168 | tf_op jit(solution)/shard_map/ppermute | solution.py:51
  29.9 6.3 %collective-permute-start.13 = (f32[32,640]{1,0:T(8,128)S(1)}, f32[32,640]{1,0:T(8,128)S(1)}, u32[]{:S(2)}, u32[]{:S(2)}) collective-permute-start(f32[32,640]{1,0:T(8,128)S(1)} %get-tuple-element.17), channel_id=1, source_target_pairs={{0,48},{16,0},{32,16},{48,32},{64,112},{80,64},{96,80},{112,96},{1... | collective-permute-start | bytes 245768 | tf_op jit(solution)/shard_map/ppermute | solution.py:66
  32.8 6.5 %collective-permute-start.15 = (f32[32,640]{1,0:T(8,128)S(1)}, f32[32,640]{1,0:T(8,128)S(1)}, u32[]{:S(2)}, u32[]{:S(2)}) collective-permute-start(f32[32,640]{1,0:T(8,128)S(1)} %get-tuple-element.15), channel_id=1, source_target_pairs={{0,16},{16,32},{32,48},{48,0},{64,80},{80,96},{96,112},{112,64},{1... | collective-permute-start | bytes 245768 | tf_op jit(solution)/shard_map/ppermute | solution.py:67
  32.8 9.9 %collective-permute-start.10 = (f32[32,640]{1,0:T(8,128)S(1)}, f32[32,640]{1,0:T(8,128)S(1)}, u32[]{:S(2)}, u32[]{:S(2)}) collective-permute-start(f32[32,640]{1,0:T(8,128)S(1)} %get-tuple-element.23), channel_id=1, source_target_pairs={{0,16},{16,32},{32,48},{48,0},{64,80},{80,96},{96,112},{112,64},{1... | collective-permute-start | bytes 245768 | tf_op jit(solution)/shard_map/ppermute | solution.py:67
  33.6 9.1 %collective-permute-start.8 = (f32[32,640]{1,0:T(8,128)S(1)}, f32[32,640]{1,0:T(8,128)S(1)}, u32[]{:S(2)}, u32[]{:S(2)}) collective-permute-start(f32[32,640]{1,0:T(8,128)S(1)} %get-tuple-element.25), channel_id=1, source_target_pairs={{0,48},{16,0},{32,16},{48,32},{64,112},{80,64},{96,80},{112,96},{1... | collective-permute-start | bytes 245768 | tf_op jit(solution)/shard_map/ppermute | solution.py:66
  39.3 7.8 %collective-permute-start.16 = (f32[64,640]{1,0:T(8,128)S(1)}, f32[64,640]{1,0:T(8,128)S(1)}, u32[]{:S(2)}, u32[]{:S(2)}) collective-permute-start(f32[64,640]{1,0:T(8,128)S(1)} %pad_maximum_fusion.3), channel_id=1, source_target_pairs={{0,16},{16,32},{32,48},{48,0},{64,80},{80,96},{96,112},{112,64},{1... | collective-permute-start | bytes 491528 | tf_op jit(solution)/shard_map/ppermute | solution.py:72
  39.4 7.7 %collective-permute-start.14 = (f32[64,640]{1,0:T(8,128)S(1)}, f32[64,640]{1,0:T(8,128)S(1)}, u32[]{:S(2)}, u32[]{:S(2)}) collective-permute-start(f32[64,640]{1,0:T(8,128)S(1)} %pad_maximum_fusion.2), channel_id=1, source_target_pairs={{0,48},{16,0},{32,16},{48,32},{64,112},{80,64},{96,80},{112,96},{1... | collective-permute-start | bytes 491528 | tf_op jit(solution)/shard_map/ppermute | solution.py:71
  42.8 8.1 %collective-permute-start.11 = (f32[64,640]{1,0:T(8,128)S(1)}, f32[64,640]{1,0:T(8,128)S(1)}, u32[]{:S(2)}, u32[]{:S(2)}) collective-permute-start(f32[64,640]{1,0:T(8,128)S(1)} %pad_maximum_fusion.1), channel_id=1, source_target_pairs={{0,16},{16,32},{32,48},{48,0},{64,80},{80,96},{96,112},{112,64},{1... | collective-permute-start | bytes 491528 | tf_op jit(solution)/shard_map/ppermute | solution.py:72
  42.9 8.0 %collective-permute-start.9 = (f32[64,640]{1,0:T(8,128)S(1)}, f32[64,640]{1,0:T(8,128)S(1)}, u32[]{:S(2)}, u32[]{:S(2)}) collective-permute-start(f32[64,640]{1,0:T(8,128)S(1)} %pad_maximum_fusion), channel_id=1, source_target_pairs={{0,48},{16,0},{32,16},{48,32},{64,112},{80,64},{96,80},{112,96},{1... | collective-permute-start | bytes 491528 | tf_op jit(solution)/shard_map/ppermute | solution.py:71
  47.2 6.9 %collective-permute-start.17 = (f32[32,640]{1,0:T(8,128)S(1)}, f32[32,640]{1,0:T(8,128)S(1)}, u32[]{:S(2)}, u32[]{:S(2)}) collective-permute-start(f32[32,640]{1,0:T(8,128)S(1)} %slice_select_fusion), channel_id=1, source_target_pairs={{0,64},{16,80},{32,96},{48,112},{64,0},{80,16},{96,32},{112,48},{1... | collective-permute-start | bytes 245768 | tf_op jit(solution)/shard_map/ppermute | solution.py:77
  50.9 6.0 %collective-permute-start.12 = (f32[32,640]{1,0:T(8,128)S(1)}, f32[32,640]{1,0:T(8,128)S(1)}, u32[]{:S(2)}, u32[]{:S(2)}) collective-permute-start(f32[32,640]{1,0:T(8,128)S(1)} %slice_select_fusion.1), channel_id=1, source_target_pairs={{0,64},{16,80},{32,96},{48,112},{64,0},{80,16},{96,32},{112,48},{1... | collective-permute-start | bytes 245768 | tf_op jit(solution)/shard_map/ppermute | solution.py:77

commit v16 on v15

--- a/solution.py
+++ b/solution.py
@@ -52,10 +52,15 @@
         mo = lax.axis_index("occ")
         x, zh = mo % nx, mo // nx
 
-        def ring(res):
+        def reduce_both(res_l, res_o):
             def half_block(r):
                 k = ((r % nx - y) % ny) * 2 + ((r // nx) ^ zl)
-                return lax.dynamic_index_in_dim(res, k, 0, keepdims=False)
+                return jnp.stack(
+                    [
+                        lax.dynamic_index_in_dim(res_l, k, 0, keepdims=False),
+                        lax.dynamic_index_in_dim(res_o, k, 0, keepdims=False),
+                    ]
+                )
 
             def a_blk(t):
                 return half_block(t % nx)
@@ -65,23 +70,22 @@
 
             p1 = lax.ppermute(a_blk(x + 2), "occ", x_shift(-1))
             q1 = lax.ppermute(b_blk(x + 2), "occ", x_shift(1))
-            to_m = jnp.concatenate([a_blk(x + nx - 1) + p1, b_blk(x + nx - 1)], axis=0)
-            to_p = jnp.concatenate([a_blk(x + 1), b_blk(x + 1) + q1], axis=0)
+            to_m = jnp.concatenate([a_blk(x + nx - 1) + p1, b_blk(x + nx - 1)], axis=1)
+            to_p = jnp.concatenate([a_blk(x + 1), b_blk(x + 1) + q1], axis=1)
             total = (
                 lax.ppermute(to_m, "occ", x_shift(-1))
                 + lax.ppermute(to_p, "occ", x_shift(1))
-                + jnp.concatenate([a_blk(x), b_blk(x)], axis=0)
+                + jnp.concatenate([a_blk(x), b_blk(x)], axis=1)
             )
-            keep = jnp.where(zh == 0, total[:rows], total[rows:])
-            send = jnp.where(zh == 0, total[rows:], total[:rows])
+            keep = jnp.where(zh == 0, total[:, :rows], total[:, rows:])
+            send = jnp.where(zh == 0, total[:, rows:], total[:, :rows])
             return keep + lax.ppermute(send, "occ", zhi_swap)
 
         res_o = matmul(other, half).reshape(8, rows, -1)
         res_l, res_o = lax.optimization_barrier((res_l, res_o))
-        sum_l = ring(res_l)
-        sum_o = ring(res_o)
-        first = jnp.where(c == 0, sum_l, sum_o)
-        second = jnp.where(c == 0, sum_o, sum_l)
+        sums = reduce_both(res_l, res_o)
+        first = jnp.where(c == 0, sums[0], sums[1])
+        second = jnp.where(c == 0, sums[1], sums[0])
         return jnp.concatenate([first, second], axis=0)
 
     return body

time: 58.7 us -> 56.8 us (0.968)
  starting transfers between devices: 29.3 us -> 20.8 us
  waiting for transfers between devices: 14.2 us -> 21.2 us
    ppermute x10 -> x5, starting transfers between devices: 18.8 us -> 10.4 us  [the longest x1 3.66 us: reduce_both(): return keep + lax.ppermute(send, 'occ', zhi_swap)]
    ppermute x10 -> x5, waiting for transfers between devices: 7.87 us -> 14.9 us  [the longest x1 7.11 us: reduce_both(): lax.ppermute(to_p, 'occ', x_shift(1))]
  transfers between devices with their start and end apart: 18 -> 13, of which waited for: 7 -> 6; matrix products, arithmetic and copies ran while one was open for 16% -> 16% of each run, Pallas kernels for 0% -> 0%
where the time goes in v16:
time: 56.8 us; the launch traced here: 56.3 us
  waiting for transfers between devices  21.2 us (37%)
  starting transfers between devices  20.8 us (37%)
  matrix products  6.7 us (12%)
  local copies, waits for them, and re-layouts  6.6 us (12%)
  other arithmetic  0.91 us (2%)
    ppermute x1, waiting for transfers between devices, reduce_both(): lax.ppermute(to_p, 'occ', x_shift(1))  7.11 us
    dot_general x2, matrix products, matmul(): return jnp.dot(a, b, preferred_element_type=jnp.float32, precision=HIGH)  6.7 us
    unnamed x9, local copies, waits for them, and re-layouts  5.76 us
    ppermute x1, waiting for transfers between devices, reduce_both(): q1 = lax.ppermute(b_blk(x + 2), 'occ', x_shift(1))  4.5 us
    ppermute x1, waiting for transfers between devices, body(): z3 = lax.ppermute(yp2, 'vir', z_swap)  3.86 us
    ppermute x1, starting transfers between devices, reduce_both(): return keep + lax.ppermute(send, 'occ', zhi_swap)  3.66 us
    ppermute x1, waiting for transfers between devices, reduce_both(): return keep + lax.ppermute(send, 'occ', zhi_swap)  3.3 us
    ppermute x1, starting transfers between devices, body(): ym1z = lax.ppermute(z1, 'vir', y_shift(1))  3.23 us
  transfers between devices with their start and end apart: 13, of which 6 were waited for; matrix products, arithmetic and copies ran while one was open for 16% of the time, Pallas kernels for 0%

profile of v16, /device:TPU:24, one launch (start us, length us, event | category | flops | bytes accessed | tf_op | source)
XLA Modules:
  0.0 56.3 jit_solution(13552324309426781127)
XLA Ops:
  0.0 0.7 %collective-permute-start.1 = (f32[32,1280]{1,0:T(8,128)}, f32[32,1280]{1,0:T(8,128)S(1)}, u32[]{:S(2)}, u32[]{:S(2)}) collective-permute-start(f32[32,1280]{1,0:T(8,128)} %param.2), channel_id=1, source_target_pairs={{0,6},{1,7},{2,0},{3,1},{4,2},{5,3},{6,4},{7,5},{8,14},{9,15},{10,... | collective-permute-start | bytes 491528 | tf_op jit(solution)/shard_map/ppermute | solution.py:43
  0.7 1.9 %collective-permute-start = (f32[32,1280]{1,0:T(8,128)}, f32[32,1280]{1,0:T(8,128)S(1)}, u32[]{:S(2)}, u32[]{:S(2)}) collective-permute-start(f32[32,1280]{1,0:T(8,128)} %param.2), channel_id=1, source_target_pairs={{0,8},{1,9},{2,10},{3,11},{4,12},{5,13},{6,14},{7,15},{8,0},{9,1},... | collective-permute-start | bytes 491528 | tf_op jit(solution)/shard_map/ppermute | solution.py:41
  2.7 2.5 %collective-permute-start.5 = (f32[32,1280]{1,0:T(8,128)}, f32[32,1280]{1,0:T(8,128)S(1)}, u32[]{:S(2)}, u32[]{:S(2)}) collective-permute-start(f32[32,1280]{1,0:T(8,128)} %param.2), channel_id=1, source_target_pairs={{0,2},{1,3},{2,4},{3,5},{4,6},{5,7},{6,0},{7,1},{8,10},{9,11},{10,... | collective-permute-start | bytes 491528 | tf_op jit(solution)/shard_map/ppermute | solution.py:42
  5.2 1.7 %constant_dynamic-update-slice_fusion.7 = f32[256,1280]{1,0:T(8,128)} fusion(f32[32,1280]{1,0:T(8,128)} %param.2), kind=kLoop, calls=%fused_computation.25 | loop fusion | bytes 327680
  7.4 1.9 %collective-permute-start.2 = (f32[32,1280]{1,0:T(8,128)S(1)}, f32[32,1280]{1,0:T(8,128)S(1)}, u32[]{:S(2)}, u32[]{:S(2)}) collective-permute-start(f32[32,1280]{1,0:T(8,128)S(1)} %collective-permute-done.1), channel_id=1, source_target_pairs={{0,8},{1,9},{2,10},{3,11},{4,12},{5,13},{6,14},{7,15},{8,0},{9,1},... | collective-permute-start | bytes 491528 | tf_op jit(solution)/shard_map/ppermute | solution.py:44
  9.3 3.2 %collective-permute-start.6 = (f32[32,1280]{1,0:T(8,128)S(1)}, f32[32,1280]{1,0:T(8,128)S(1)}, u32[]{:S(2)}, u32[]{:S(2)}) collective-permute-start(f32[32,1280]{1,0:T(8,128)S(1)} %collective-permute-done), channel_id=1, source_target_pairs={{0,2},{1,3},{2,4},{3,5},{4,6},{5,7},{6,0},{7,1},{8,10},{9,11},{10,... | collective-permute-start | bytes 491528 | tf_op jit(solution)/shard_map/ppermute | solution.py:46
  12.5 0.7 %constant_dynamic-update-slice_fusion.6 = f32[256,1280]{1,0:T(8,128)} fusion(f32[256,1280]{1,0:T(8,128)} %constant_dynamic-update-slice_fusion.7, f32[32,1280]{1,0:T(8,128)S(1)} %collective-permute-done), kind=kLoop, calls=%fused_computation.24 | loop fusion | bytes 327680
  13.2 0.7 %constant_dynamic-update-slice_fusion.5 = f32[256,1280]{1,0:T(8,128)} fusion(f32[256,1280]{1,0:T(8,128)} %constant_dynamic-update-slice_fusion.6, f32[32,1280]{1,0:T(8,128)S(1)} %collective-permute-done.1), kind=kLoop, calls=%fused_computation.23 | loop fusion | bytes 327680
  13.9 2.0 %collective-permute-done.3 = f32[32,1280]{1,0:T(8,128)S(1)} collective-permute-done((f32[32,1280]{1,0:T(8,128)S(1)}, f32[32,1280]{1,0:T(8,128)S(1)}, u32[]{:S(2)}, u32[]{:S(2)}) %collective-permute-start.3) | collective-permute-done | bytes 163872 | tf_op jit(solution)/shard_map/ppermute | solution.py:45
  15.9 0.7 %constant_dynamic-update-slice_fusion.4 = f32[256,1280]{1,0:T(8,128)} fusion(f32[256,1280]{1,0:T(8,128)} %constant_dynamic-update-slice_fusion.5, f32[32,1280]{1,0:T(8,128)S(1)} %collective-permute-done.2), kind=kLoop, calls=%fused_computation.22 | loop fusion | bytes 327680
  16.6 0.7 %constant_dynamic-update-slice_fusion.3 = f32[256,1280]{1,0:T(8,128)} fusion(f32[256,1280]{1,0:T(8,128)} %constant_dynamic-update-slice_fusion.4, f32[32,1280]{1,0:T(8,128)S(1)} %collective-permute-done.3), kind=kLoop, calls=%fused_computation.21 | loop fusion | bytes 327680
  17.3 3.9 %collective-permute-done.4 = f32[32,1280]{1,0:T(8,128)S(1)} collective-permute-done((f32[32,1280]{1,0:T(8,128)S(1)}, f32[32,1280]{1,0:T(8,128)S(1)}, u32[]{:S(2)}, u32[]{:S(2)}) %collective-permute-start.4) | collective-permute-done | bytes 163872 | tf_op jit(solution)/shard_map/ppermute | solution.py:47
  21.1 0.7 %constant_dynamic-update-slice_fusion.2 = f32[256,1280]{1,0:T(8,128)} fusion(f32[256,1280]{1,0:T(8,128)} %constant_dynamic-update-slice_fusion.3, f32[32,1280]{1,0:T(8,128)S(1)} %collective-permute-done.4), kind=kLoop, calls=%fused_computation.20 | loop fusion | bytes 327680
  22.5 0.7 %constant_dynamic-update-slice_fusion = f32[256,1280]{1,0:T(8,128)} fusion(f32[256,1280]{1,0:T(8,128)} %constant_dynamic-update-slice_fusion.1, f32[32,1280]{1,0:T(8,128)S(1)} %collective-permute-done.6), kind=kLoop, calls=%fused_computation.18 | loop fusion | bytes 327680 | tf_op jit(solution)/shard_map/concatenate | solution.py:48
  23.2 3.3 %fusion.2 = f32[256,640]{1,0:T(8,128)S(1)} fusion(f32[256,1280]{1,0:T(8,128)} %constant_dynamic-update-slice_fusion, f32[1280,640]{1,0:T(8,128)S(1)} %copy-done), kind=kOutput, calls=%fused_computation.2 | convolution fusion | flops 1259110400 | bytes 5242880 | tf_op jit(solution)/shard_map/dot_general | solution.py:32
  26.5 3.4 %fusion = f32[256,640]{1,0:T(8,128)S(1)} fusion(f32[256,1280]{1,0:T(8,128)} %collective-permute-done.7, f32[1280,640]{1,0:T(8,128)S(1)} %copy-done), kind=kOutput, calls=%fused_computation | convolution fusion | flops 1259110400 | bytes 5242880 | tf_op jit(solution)/shard_map/dot_general | solution.py:32
  30.1 1.6 %collective-permute-start.10 = (f32[2,32,640]{2,1,0:T(8,128)S(1)}, f32[2,32,640]{2,1,0:T(8,128)S(1)}, u32[]{:S(2)}, u32[]{:S(2)}) collective-permute-start(f32[2,32,640]{2,1,0:T(8,128)S(1)} %pad_maximum_fusion.2), channel_id=1, source_target_pairs={{0,16},{16,32},{32,48},{48,0},{64,80},{80,96},{96,112},{112,64},{1... | collective-permute-start | bytes 491528 | tf_op jit(solution)/shard_map/ppermute | solution.py:72
  31.7 1.8 %collective-permute-start.8 = (f32[2,32,640]{2,1,0:T(8,128)S(1)}, f32[2,32,640]{2,1,0:T(8,128)S(1)}, u32[]{:S(2)}, u32[]{:S(2)}) collective-permute-start(f32[2,32,640]{2,1,0:T(8,128)S(1)} %pad_maximum_fusion.1), channel_id=1, source_target_pairs={{0,48},{16,0},{32,16},{48,32},{64,112},{80,64},{96,80},{112,96},{1... | collective-permute-start | bytes 491528 | tf_op jit(solution)/shard_map/ppermute | solution.py:71
  33.5 4.5 %collective-permute-done.10 = f32[2,32,640]{2,1,0:T(8,128)S(1)} collective-permute-done((f32[2,32,640]{2,1,0:T(8,128)S(1)}, f32[2,32,640]{2,1,0:T(8,128)S(1)}, u32[]{:S(2)}, u32[]{:S(2)}) %collective-permute-start.10) | collective-permute-done | bytes 163872 | tf_op jit(solution)/shard_map/ppermute | solution.py:72
  38.4 3.0 %collective-permute-start.9 = (f32[2,64,640]{2,1,0:T(8,128)S(1)}, f32[2,64,640]{2,1,0:T(8,128)S(1)}, u32[]{:S(2)}, u32[]{:S(2)}) collective-permute-start(f32[2,64,640]{2,1,0:T(8,128)S(1)} %maximum_maximum_fusion), channel_id=1, source_target_pairs={{0,48},{16,0},{32,16},{48,32},{64,112},{80,64},{96,80},{112,96},{1... | collective-permute-start | bytes 983048 | tf_op jit(solution)/shard_map/ppermute | solution.py:76
  41.5 7.1 %collective-permute-done.11 = f32[2,64,640]{2,1,0:T(8,128)S(1)} collective-permute-done((f32[2,64,640]{2,1,0:T(8,128)S(1)}, f32[2,64,640]{2,1,0:T(8,128)S(1)}, u32[]{:S(2)}, u32[]{:S(2)}) %collective-permute-start.11) | collective-permute-done | bytes 327712 | tf_op jit(solution)/shard_map/ppermute | solution.py:77
  48.7 3.7 %collective-permute-start.12 = (f32[2,32,640]{2,1,0:T(8,128)S(1)}, f32[2,32,640]{2,1,0:T(8,128)S(1)}, u32[]{:S(2)}, u32[]{:S(2)}) collective-permute-start(f32[2,32,640]{2,1,0:T(8,128)S(1)} %slice_select_fusion), channel_id=1, source_target_pairs={{0,64},{16,80},{32,96},{48,112},{64,0},{80,16},{96,32},{112,48},{1... | collective-permute-start | bytes 491528 | tf_op jit(solution)/shard_map/ppermute | solution.py:82
  52.3 3.3 %collective-permute-done.12 = f32[2,32,640]{2,1,0:T(8,128)S(1)} collective-permute-done((f32[2,32,640]{2,1,0:T(8,128)S(1)}, f32[2,32,640]{2,1,0:T(8,128)S(1)}, u32[]{:S(2)}, u32[]{:S(2)}) %collective-permute-start.12) | collective-permute-done | bytes 163872 | tf_op jit(solution)/shard_map/ppermute | solution.py:82
  55.7 0.7 %pad_maximum_fusion.3 = f32[64,640]{1,0:T(8,128)} fusion(f32[32,640]{1,0:T(8,128)S(1)} %get-tuple-element.26, f32[32,640]{1,0:T(8,128)S(1)} %get-tuple-element.25), kind=kLoop, calls=%fused_computation.13 | loop fusion | flops 40960 | bytes 327680 | tf_op jit(solution)/shard_map/concatenate | solution.py:89
  (26 shorter events, 2.0 us)
Async XLA Ops:
  0.0 7.4 %collective-permute-start.1 = (f32[32,1280]{1,0:T(8,128)}, f32[32,1280]{1,0:T(8,128)S(1)}, u32[]{:S(2)}, u32[]{:S(2)}) collective-permute-start(f32[32,1280]{1,0:T(8,128)} %param.2), channel_id=1, source_target_pairs={{0,6},{1,7},{2,0},{3,1},{4,2},{5,3},{6,4},{7,5},{8,14},{9,15},{10,... | collective-permute-start | bytes 491528 | tf_op jit(solution)/shard_map/ppermute | solution.py:43
  0.7 8.5 %collective-permute-start = (f32[32,1280]{1,0:T(8,128)}, f32[32,1280]{1,0:T(8,128)S(1)}, u32[]{:S(2)}, u32[]{:S(2)}) collective-permute-start(f32[32,1280]{1,0:T(8,128)} %param.2), channel_id=1, source_target_pairs={{0,8},{1,9},{2,10},{3,11},{4,12},{5,13},{6,14},{7,15},{8,0},{9,1},... | collective-permute-start | bytes 491528 | tf_op jit(solution)/shard_map/ppermute | solution.py:41
  2.7 19.1 %collective-permute-start.5 = (f32[32,1280]{1,0:T(8,128)}, f32[32,1280]{1,0:T(8,128)S(1)}, u32[]{:S(2)}, u32[]{:S(2)}) collective-permute-start(f32[32,1280]{1,0:T(8,128)} %param.2), channel_id=1, source_target_pairs={{0,2},{1,3},{2,4},{3,5},{4,6},{5,7},{6,0},{7,1},{8,10},{9,11},{10,... | collective-permute-start | bytes 491528 | tf_op jit(solution)/shard_map/ppermute | solution.py:42
  5.2 18.0 %copy-start = (f32[1280,640]{1,0:T(8,128)S(1)}, f32[1280,640]{1,0:T(8,128)}, u32[]{:S(2)}) copy-start(f32[1280,640]{1,0:T(8,128)} %param.3) | copy-start | bytes 9830404
  7.4 8.6 %collective-permute-start.2 = (f32[32,1280]{1,0:T(8,128)S(1)}, f32[32,1280]{1,0:T(8,128)S(1)}, u32[]{:S(2)}, u32[]{:S(2)}) collective-permute-start(f32[32,1280]{1,0:T(8,128)S(1)} %collective-permute-done.1), channel_id=1, source_target_pairs={{0,8},{1,9},{2,10},{3,11},{4,12},{5,13},{6,14},{7,15},{8,0},{9,1},... | collective-permute-start | bytes 491528 | tf_op jit(solution)/shard_map/ppermute | solution.py:44
  9.3 6.5 %collective-permute-start.3 = (f32[32,1280]{1,0:T(8,128)S(1)}, f32[32,1280]{1,0:T(8,128)S(1)}, u32[]{:S(2)}, u32[]{:S(2)}) collective-permute-start(f32[32,1280]{1,0:T(8,128)S(1)} %collective-permute-done.1), channel_id=1, source_target_pairs={{0,6},{1,7},{2,0},{3,1},{4,2},{5,3},{6,4},{7,5},{8,14},{9,15},{10,... | collective-permute-start | bytes 491528 | tf_op jit(solution)/shard_map/ppermute | solution.py:45
  9.3 13.2 %collective-permute-start.6 = (f32[32,1280]{1,0:T(8,128)S(1)}, f32[32,1280]{1,0:T(8,128)S(1)}, u32[]{:S(2)}, u32[]{:S(2)}) collective-permute-start(f32[32,1280]{1,0:T(8,128)S(1)} %collective-permute-done), channel_id=1, source_target_pairs={{0,2},{1,3},{2,4},{3,5},{4,6},{5,7},{6,0},{7,1},{8,10},{9,11},{10,... | collective-permute-start | bytes 491528 | tf_op jit(solution)/shard_map/ppermute | solution.py:46
  15.8 5.3 %collective-permute-start.4 = (f32[32,1280]{1,0:T(8,128)S(1)}, f32[32,1280]{1,0:T(8,128)S(1)}, u32[]{:S(2)}, u32[]{:S(2)}) collective-permute-start(f32[32,1280]{1,0:T(8,128)S(1)} %collective-permute-done.3), channel_id=1, source_target_pairs={{0,8},{1,9},{2,10},{3,11},{4,12},{5,13},{6,14},{7,15},{8,0},{9,1},... | collective-permute-start | bytes 491528 | tf_op jit(solution)/shard_map/ppermute | solution.py:47
  23.2 3.4 %collective-permute-start.7 = (f32[256,1280]{1,0:T(8,128)}, f32[256,1280]{1,0:T(8,128)}, u32[]{:S(2)}, u32[]{:S(2)}) collective-permute-start(f32[256,1280]{1,0:T(8,128)} %constant_dynamic-update-slice_fusion), channel_id=1, source_target_pairs={{0,1},{1,0},{2,3},{3,2},{4,5},{5,4},{6,7},{7,6},{8,9},{9,8},{10,11... | collective-permute-start | bytes 3932168 | tf_op jit(solution)/shard_map/ppermute | solution.py:51
  30.1 7.9 %collective-permute-start.10 = (f32[2,32,640]{2,1,0:T(8,128)S(1)}, f32[2,32,640]{2,1,0:T(8,128)S(1)}, u32[]{:S(2)}, u32[]{:S(2)}) collective-permute-start(f32[2,32,640]{2,1,0:T(8,128)S(1)} %pad_maximum_fusion.2), channel_id=1, source_target_pairs={{0,16},{16,32},{32,48},{48,0},{64,80},{80,96},{96,112},{112,64},{1... | collective-permute-start | bytes 491528 | tf_op jit(solution)/shard_map/ppermute | solution.py:72
  31.7 6.7 %collective-permute-start.8 = (f32[2,32,640]{2,1,0:T(8,128)S(1)}, f32[2,32,640]{2,1,0:T(8,128)S(1)}, u32[]{:S(2)}, u32[]{:S(2)}) collective-permute-start(f32[2,32,640]{2,1,0:T(8,128)S(1)} %pad_maximum_fusion.1), channel_id=1, source_target_pairs={{0,48},{16,0},{32,16},{48,32},{64,112},{80,64},{96,80},{112,96},{1... | collective-permute-start | bytes 491528 | tf_op jit(solution)/shard_map/ppermute | solution.py:71
  38.0 10.5 %collective-permute-start.11 = (f32[2,64,640]{2,1,0:T(8,128)S(1)}, f32[2,64,640]{2,1,0:T(8,128)S(1)}, u32[]{:S(2)}, u32[]{:S(2)}) collective-permute-start(f32[2,64,640]{2,1,0:T(8,128)S(1)} %pad_maximum_fusion), channel_id=1, source_target_pairs={{0,16},{16,32},{32,48},{48,0},{64,80},{80,96},{96,112},{112,64},{1... | collective-permute-start | bytes 983048 | tf_op jit(solution)/shard_map/ppermute | solution.py:77
  38.4 10.1 %collective-permute-start.9 = (f32[2,64,640]{2,1,0:T(8,128)S(1)}, f32[2,64,640]{2,1,0:T(8,128)S(1)}, u32[]{:S(2)}, u32[]{:S(2)}) collective-permute-start(f32[2,64,640]{2,1,0:T(8,128)S(1)} %maximum_maximum_fusion), channel_id=1, source_target_pairs={{0,48},{16,0},{32,16},{48,32},{64,112},{80,64},{96,80},{112,96},{1... | collective-permute-start | bytes 983048 | tf_op jit(solution)/shard_map/ppermute | solution.py:76
  48.7 7.0 %collective-permute-start.12 = (f32[2,32,640]{2,1,0:T(8,128)S(1)}, f32[2,32,640]{2,1,0:T(8,128)S(1)}, u32[]{:S(2)}, u32[]{:S(2)}) collective-permute-start(f32[2,32,640]{2,1,0:T(8,128)S(1)} %slice_select_fusion), channel_id=1, source_target_pairs={{0,64},{16,80},{32,96},{48,112},{64,0},{80,16},{96,32},{112,48},{1... | collective-permute-start | bytes 491528 | tf_op jit(solution)/shard_map/ppermute | solution.py:82

commit v17 on v16

--- a/solution.py
+++ b/solution.py
@@ -70,16 +70,21 @@
 
             p1 = lax.ppermute(a_blk(x + 2), "occ", x_shift(-1))
             q1 = lax.ppermute(b_blk(x + 2), "occ", x_shift(1))
-            to_m = jnp.concatenate([a_blk(x + nx - 1) + p1, b_blk(x + nx - 1)], axis=1)
-            to_p = jnp.concatenate([a_blk(x + 1), b_blk(x + 1) + q1], axis=1)
-            total = (
-                lax.ppermute(to_m, "occ", x_shift(-1))
-                + lax.ppermute(to_p, "occ", x_shift(1))
-                + jnp.concatenate([a_blk(x), b_blk(x)], axis=1)
+            to_m_a, to_m_b = a_blk(x + nx - 1) + p1, b_blk(x + nx - 1)
+            to_p_a, to_p_b = a_blk(x + 1), b_blk(x + 1) + q1
+            low = zh == 0
+            got_send = (
+                lax.ppermute(jnp.where(low, to_m_b, to_m_a), "occ", x_shift(-1))
+                + lax.ppermute(jnp.where(low, to_p_b, to_p_a), "occ", x_shift(1))
+                + jnp.where(low, b_blk(x), a_blk(x))
             )
-            keep = jnp.where(zh == 0, total[:, :rows], total[:, rows:])
-            send = jnp.where(zh == 0, total[:, rows:], total[:, :rows])
-            return keep + lax.ppermute(send, "occ", zhi_swap)
+            from_zhi = lax.ppermute(got_send, "occ", zhi_swap)
+            got_keep = (
+                lax.ppermute(jnp.where(low, to_m_a, to_m_b), "occ", x_shift(-1))
+                + lax.ppermute(jnp.where(low, to_p_a, to_p_b), "occ", x_shift(1))
+                + jnp.where(low, a_blk(x), b_blk(x))
+            )
+            return got_keep + from_zhi
 
         res_o = matmul(other, half).reshape(8, rows, -1)
         res_l, res_o = lax.optimization_barrier((res_l, res_o))

time: 56.8 us -> 54.1 us (0.952)
  waiting for transfers between devices: 21.2 us -> 15.2 us
  starting transfers between devices: 20.8 us -> 24.1 us
    ppermute x3 -> x5, waiting for transfers between devices: 10.4 us -> 4.41 us  [the longest x1 3.29 us: reduce_both(): from_zhi = lax.ppermute(got_send, 'occ', zhi_swap)]
    ppermute x3 -> x5, starting transfers between devices: 7.04 us -> 10.3 us  [the longest x1 3.66 us: reduce_both(): from_zhi = lax.ppermute(got_send, 'occ', zhi_swap)]
  transfers between devices with their start and end apart: 13 -> 15, of which waited for: 6 -> 6; matrix products, arithmetic and copies ran while one was open for 16% -> 17% of each run, Pallas kernels for 0% -> 0%
where the time goes in v17:
time: 54.1 us; the launch traced here: 53.5 us
  starting transfers between devices  24.1 us (45%)
  waiting for transfers between devices  15.2 us (28%)
  matrix products  6.7 us (12%)
  local copies, waits for them, and re-layouts  6.62 us (12%)
  other arithmetic  0.85 us (2%)
    dot_general x2, matrix products, matmul(): return jnp.dot(a, b, preferred_element_type=jnp.float32, precision=HIGH)  6.7 us
    unnamed x9, local copies, waits for them, and re-layouts  5.78 us
    ppermute x1, waiting for transfers between devices, reduce_both(): q1 = lax.ppermute(b_blk(x + 2), 'occ', x_shift(1))  4.5 us
    ppermute x1, waiting for transfers between devices, body(): z3 = lax.ppermute(yp2, 'vir', z_swap)  3.85 us
    ppermute x1, starting transfers between devices, reduce_both(): from_zhi = lax.ppermute(got_send, 'occ', zhi_swap)  3.66 us
    ppermute x1, waiting for transfers between devices, reduce_both(): from_zhi = lax.ppermute(got_send, 'occ', zhi_swap)  3.29 us
    ppermute x1, starting transfers between devices, body(): ym1z = lax.ppermute(z1, 'vir', y_shift(1))  3.23 us
    ppermute x1, starting transfers between devices, reduce_both(): lax.ppermute(jnp.where(low, to_m_a, to_m_b), 'occ', x_shift(-1))  3.23 us
  transfers between devices with their start and end apart: 15, of which 6 were waited for; matrix products, arithmetic and copies ran while one was open for 17% of the time, Pallas kernels for 0%

profile of v17, /device:TPU:24, one launch (start us, length us, event | category | flops | bytes accessed | tf_op | source)
XLA Modules:
  0.0 53.5 jit_solution(11530026364459456433)
XLA Ops:
  0.0 0.7 %collective-permute-start.1 = (f32[32,1280]{1,0:T(8,128)}, f32[32,1280]{1,0:T(8,128)S(1)}, u32[]{:S(2)}, u32[]{:S(2)}) collective-permute-start(f32[32,1280]{1,0:T(8,128)} %param.2), channel_id=1, source_target_pairs={{0,6},{1,7},{2,0},{3,1},{4,2},{5,3},{6,4},{7,5},{8,14},{9,15},{10,... | collective-permute-start | bytes 491528 | tf_op jit(solution)/shard_map/ppermute | solution.py:43
  0.7 1.9 %collective-permute-start = (f32[32,1280]{1,0:T(8,128)}, f32[32,1280]{1,0:T(8,128)S(1)}, u32[]{:S(2)}, u32[]{:S(2)}) collective-permute-start(f32[32,1280]{1,0:T(8,128)} %param.2), channel_id=1, source_target_pairs={{0,8},{1,9},{2,10},{3,11},{4,12},{5,13},{6,14},{7,15},{8,0},{9,1},... | collective-permute-start | bytes 491528 | tf_op jit(solution)/shard_map/ppermute | solution.py:41
  2.7 2.5 %collective-permute-start.5 = (f32[32,1280]{1,0:T(8,128)}, f32[32,1280]{1,0:T(8,128)S(1)}, u32[]{:S(2)}, u32[]{:S(2)}) collective-permute-start(f32[32,1280]{1,0:T(8,128)} %param.2), channel_id=1, source_target_pairs={{0,2},{1,3},{2,4},{3,5},{4,6},{5,7},{6,0},{7,1},{8,10},{9,11},{10,... | collective-permute-start | bytes 491528 | tf_op jit(solution)/shard_map/ppermute | solution.py:42
  5.2 1.7 %constant_dynamic-update-slice_fusion.7 = f32[256,1280]{1,0:T(8,128)} fusion(f32[32,1280]{1,0:T(8,128)} %param.2), kind=kLoop, calls=%fused_computation.30 | loop fusion | bytes 327680
  7.4 1.9 %collective-permute-start.2 = (f32[32,1280]{1,0:T(8,128)S(1)}, f32[32,1280]{1,0:T(8,128)S(1)}, u32[]{:S(2)}, u32[]{:S(2)}) collective-permute-start(f32[32,1280]{1,0:T(8,128)S(1)} %collective-permute-done.1), channel_id=1, source_target_pairs={{0,8},{1,9},{2,10},{3,11},{4,12},{5,13},{6,14},{7,15},{8,0},{9,1},... | collective-permute-start | bytes 491528 | tf_op jit(solution)/shard_map/ppermute | solution.py:44
  9.3 3.2 %collective-permute-start.6 = (f32[32,1280]{1,0:T(8,128)S(1)}, f32[32,1280]{1,0:T(8,128)S(1)}, u32[]{:S(2)}, u32[]{:S(2)}) collective-permute-start(f32[32,1280]{1,0:T(8,128)S(1)} %collective-permute-done), channel_id=1, source_target_pairs={{0,2},{1,3},{2,4},{3,5},{4,6},{5,7},{6,0},{7,1},{8,10},{9,11},{10,... | collective-permute-start | bytes 491528 | tf_op jit(solution)/shard_map/ppermute | solution.py:46
  12.5 0.7 %constant_dynamic-update-slice_fusion.6 = f32[256,1280]{1,0:T(8,128)} fusion(f32[256,1280]{1,0:T(8,128)} %constant_dynamic-update-slice_fusion.7, f32[32,1280]{1,0:T(8,128)S(1)} %collective-permute-done), kind=kLoop, calls=%fused_computation.29 | loop fusion | bytes 327680
  13.9 1.9 %collective-permute-done.3 = f32[32,1280]{1,0:T(8,128)S(1)} collective-permute-done((f32[32,1280]{1,0:T(8,128)S(1)}, f32[32,1280]{1,0:T(8,128)S(1)}, u32[]{:S(2)}, u32[]{:S(2)}) %collective-permute-start.3) | collective-permute-done | bytes 163872 | tf_op jit(solution)/shard_map/ppermute | solution.py:45
  15.9 0.7 %constant_dynamic-update-slice_fusion.4 = f32[256,1280]{1,0:T(8,128)} fusion(f32[256,1280]{1,0:T(8,128)} %constant_dynamic-update-slice_fusion.5, f32[32,1280]{1,0:T(8,128)S(1)} %collective-permute-done.2), kind=kLoop, calls=%fused_computation.27 | loop fusion | bytes 327680
  16.6 0.7 %constant_dynamic-update-slice_fusion.3 = f32[256,1280]{1,0:T(8,128)} fusion(f32[256,1280]{1,0:T(8,128)} %constant_dynamic-update-slice_fusion.4, f32[32,1280]{1,0:T(8,128)S(1)} %collective-permute-done.3), kind=kLoop, calls=%fused_computation.26 | loop fusion | bytes 327680
  17.3 3.8 %collective-permute-done.4 = f32[32,1280]{1,0:T(8,128)S(1)} collective-permute-done((f32[32,1280]{1,0:T(8,128)S(1)}, f32[32,1280]{1,0:T(8,128)S(1)}, u32[]{:S(2)}, u32[]{:S(2)}) %collective-permute-start.4) | collective-permute-done | bytes 163872 | tf_op jit(solution)/shard_map/ppermute | solution.py:47
  21.8 0.7 %constant_dynamic-update-slice_fusion.1 = f32[256,1280]{1,0:T(8,128)} fusion(f32[256,1280]{1,0:T(8,128)} %constant_dynamic-update-slice_fusion.2, f32[32,1280]{1,0:T(8,128)S(1)} %collective-permute-done.5), kind=kLoop, calls=%fused_computation.24 | loop fusion | bytes 327680
  22.5 0.7 %constant_dynamic-update-slice_fusion = f32[256,1280]{1,0:T(8,128)} fusion(f32[256,1280]{1,0:T(8,128)} %constant_dynamic-update-slice_fusion.1, f32[32,1280]{1,0:T(8,128)S(1)} %collective-permute-done.6), kind=kLoop, calls=%fused_computation.23 | loop fusion | bytes 327680 | tf_op jit(solution)/shard_map/concatenate | solution.py:48
  23.2 3.4 %fusion.2 = f32[256,640]{1,0:T(8,128)S(1)} fusion(f32[256,1280]{1,0:T(8,128)} %constant_dynamic-update-slice_fusion, f32[1280,640]{1,0:T(8,128)S(1)} %copy-done), kind=kOutput, calls=%fused_computation.2 | convolution fusion | flops 1259110400 | bytes 5242880 | tf_op jit(solution)/shard_map/dot_general | solution.py:32
  26.5 3.3 %fusion = f32[256,640]{1,0:T(8,128)S(1)} fusion(f32[256,1280]{1,0:T(8,128)} %collective-permute-done.7, f32[1280,640]{1,0:T(8,128)S(1)} %copy-done), kind=kOutput, calls=%fused_computation | convolution fusion | flops 1259110400 | bytes 5242880 | tf_op jit(solution)/shard_map/dot_general | solution.py:32
  30.1 1.6 %collective-permute-start.10 = (f32[2,32,640]{2,1,0:T(8,128)S(1)}, f32[2,32,640]{2,1,0:T(8,128)S(1)}, u32[]{:S(2)}, u32[]{:S(2)}) collective-permute-start(f32[2,32,640]{2,1,0:T(8,128)S(1)} %pad_maximum_fusion.3), channel_id=1, source_target_pairs={{0,16},{16,32},{32,48},{48,0},{64,80},{80,96},{96,112},{112,64},{1... | collective-permute-start | bytes 491528 | tf_op jit(solution)/shard_map/ppermute | solution.py:72
  31.7 1.8 %collective-permute-start.8 = (f32[2,32,640]{2,1,0:T(8,128)S(1)}, f32[2,32,640]{2,1,0:T(8,128)S(1)}, u32[]{:S(2)}, u32[]{:S(2)}) collective-permute-start(f32[2,32,640]{2,1,0:T(8,128)S(1)} %pad_maximum_fusion), channel_id=1, source_target_pairs={{0,48},{16,0},{32,16},{48,32},{64,112},{80,64},{96,80},{112,96},{1... | collective-permute-start | bytes 491528 | tf_op jit(solution)/shard_map/ppermute | solution.py:71
  33.5 4.5 %collective-permute-done.10 = f32[2,32,640]{2,1,0:T(8,128)S(1)} collective-permute-done((f32[2,32,640]{2,1,0:T(8,128)S(1)}, f32[2,32,640]{2,1,0:T(8,128)S(1)}, u32[]{:S(2)}, u32[]{:S(2)}) %collective-permute-start.10) | collective-permute-done | bytes 163872 | tf_op jit(solution)/shard_map/ppermute | solution.py:72
  38.4 3.0 %collective-permute-start.12 = (f32[2,32,640]{2,1,0:T(8,128)S(1)}, f32[2,32,640]{2,1,0:T(8,128)S(1)}, u32[]{:S(2)}, u32[]{:S(2)}) collective-permute-start(f32[2,32,640]{2,1,0:T(8,128)S(1)} %get-tuple-element.28), channel_id=1, source_target_pairs={{0,48},{16,0},{32,16},{48,32},{64,112},{80,64},{96,80},{112,96},{1... | collective-permute-start | bytes 491528 | tf_op jit(solution)/shard_map/ppermute | solution.py:77
  41.4 3.2 %collective-permute-start.9 = (f32[2,32,640]{2,1,0:T(8,128)S(1)}, f32[2,32,640]{2,1,0:T(8,128)S(1)}, u32[]{:S(2)}, u32[]{:S(2)}) collective-permute-start(f32[2,32,640]{2,1,0:T(8,128)S(1)} %get-tuple-element.27), channel_id=1, source_target_pairs={{0,48},{16,0},{32,16},{48,32},{64,112},{80,64},{96,80},{112,96},{1... | collective-permute-start | bytes 491528 | tf_op jit(solution)/shard_map/ppermute | solution.py:83
  44.7 1.1 %collective-permute-done.13 = f32[2,32,640]{2,1,0:T(8,128)S(1)} collective-permute-done((f32[2,32,640]{2,1,0:T(8,128)S(1)}, f32[2,32,640]{2,1,0:T(8,128)S(1)}, u32[]{:S(2)}, u32[]{:S(2)}) %collective-permute-start.13) | collective-permute-done | bytes 163872 | tf_op jit(solution)/shard_map/ppermute | solution.py:78
  45.8 3.7 %collective-permute-start.14 = (f32[2,32,640]{2,1,0:T(8,128)S(1)}, f32[2,32,640]{2,1,0:T(8,128)S(1)}, u32[]{:S(2)}, u32[]{:S(2)}) collective-permute-start(f32[2,32,640]{2,1,0:T(8,128)S(1)} %select_add_fusion), channel_id=1, source_target_pairs={{0,64},{16,80},{32,96},{48,112},{64,0},{80,16},{96,32},{112,48},{1... | collective-permute-start | bytes 491528 | tf_op jit(solution)/shard_map/ppermute | solution.py:81
  49.5 3.3 %collective-permute-done.14 = f32[2,32,640]{2,1,0:T(8,128)S(1)} collective-permute-done((f32[2,32,640]{2,1,0:T(8,128)S(1)}, f32[2,32,640]{2,1,0:T(8,128)S(1)}, u32[]{:S(2)}, u32[]{:S(2)}) %collective-permute-start.14) | collective-permute-done | bytes 163872 | tf_op jit(solution)/shard_map/ppermute | solution.py:81
  52.8 0.7 %pad_maximum_fusion.6 = f32[64,640]{1,0:T(8,128)} fusion(f32[32,640]{1,0:T(8,128)S(1)} %get-tuple-element.30, f32[32,640]{1,0:T(8,128)S(1)} %get-tuple-element.29), kind=kLoop, calls=%fused_computation.14 | loop fusion | flops 40960 | bytes 327680 | tf_op jit(solution)/shard_map/concatenate | solution.py:94
  (27 shorter events, 2.6 us)
Async XLA Ops:
  0.0 7.4 %collective-permute-start.1 = (f32[32,1280]{1,0:T(8,128)}, f32[32,1280]{1,0:T(8,128)S(1)}, u32[]{:S(2)}, u32[]{:S(2)}) collective-permute-start(f32[32,1280]{1,0:T(8,128)} %param.2), channel_id=1, source_target_pairs={{0,6},{1,7},{2,0},{3,1},{4,2},{5,3},{6,4},{7,5},{8,14},{9,15},{10,... | collective-permute-start | bytes 491528 | tf_op jit(solution)/shard_map/ppermute | solution.py:43
  0.7 8.5 %collective-permute-start = (f32[32,1280]{1,0:T(8,128)}, f32[32,1280]{1,0:T(8,128)S(1)}, u32[]{:S(2)}, u32[]{:S(2)}) collective-permute-start(f32[32,1280]{1,0:T(8,128)} %param.2), channel_id=1, source_target_pairs={{0,8},{1,9},{2,10},{3,11},{4,12},{5,13},{6,14},{7,15},{8,0},{9,1},... | collective-permute-start | bytes 491528 | tf_op jit(solution)/shard_map/ppermute | solution.py:41
  2.7 19.1 %collective-permute-start.5 = (f32[32,1280]{1,0:T(8,128)}, f32[32,1280]{1,0:T(8,128)S(1)}, u32[]{:S(2)}, u32[]{:S(2)}) collective-permute-start(f32[32,1280]{1,0:T(8,128)} %param.2), channel_id=1, source_target_pairs={{0,2},{1,3},{2,4},{3,5},{4,6},{5,7},{6,0},{7,1},{8,10},{9,11},{10,... | collective-permute-start | bytes 491528 | tf_op jit(solution)/shard_map/ppermute | solution.py:42
  5.2 18.0 %copy-start = (f32[1280,640]{1,0:T(8,128)S(1)}, f32[1280,640]{1,0:T(8,128)}, u32[]{:S(2)}) copy-start(f32[1280,640]{1,0:T(8,128)} %param.3) | copy-start | bytes 9830404
  7.4 8.6 %collective-permute-start.2 = (f32[32,1280]{1,0:T(8,128)S(1)}, f32[32,1280]{1,0:T(8,128)S(1)}, u32[]{:S(2)}, u32[]{:S(2)}) collective-permute-start(f32[32,1280]{1,0:T(8,128)S(1)} %collective-permute-done.1), channel_id=1, source_target_pairs={{0,8},{1,9},{2,10},{3,11},{4,12},{5,13},{6,14},{7,15},{8,0},{9,1},... | collective-permute-start | bytes 491528 | tf_op jit(solution)/shard_map/ppermute | solution.py:44
  9.3 6.5 %collective-permute-start.3 = (f32[32,1280]{1,0:T(8,128)S(1)}, f32[32,1280]{1,0:T(8,128)S(1)}, u32[]{:S(2)}, u32[]{:S(2)}) collective-permute-start(f32[32,1280]{1,0:T(8,128)S(1)} %collective-permute-done.1), channel_id=1, source_target_pairs={{0,6},{1,7},{2,0},{3,1},{4,2},{5,3},{6,4},{7,5},{8,14},{9,15},{10,... | collective-permute-start | bytes 491528 | tf_op jit(solution)/shard_map/ppermute | solution.py:45
  9.3 13.2 %collective-permute-start.6 = (f32[32,1280]{1,0:T(8,128)S(1)}, f32[32,1280]{1,0:T(8,128)S(1)}, u32[]{:S(2)}, u32[]{:S(2)}) collective-permute-start(f32[32,1280]{1,0:T(8,128)S(1)} %collective-permute-done), channel_id=1, source_target_pairs={{0,2},{1,3},{2,4},{3,5},{4,6},{5,7},{6,0},{7,1},{8,10},{9,11},{10,... | collective-permute-start | bytes 491528 | tf_op jit(solution)/shard_map/ppermute | solution.py:46
  15.8 5.3 %collective-permute-start.4 = (f32[32,1280]{1,0:T(8,128)S(1)}, f32[32,1280]{1,0:T(8,128)S(1)}, u32[]{:S(2)}, u32[]{:S(2)}) collective-permute-start(f32[32,1280]{1,0:T(8,128)S(1)} %collective-permute-done.3), channel_id=1, source_target_pairs={{0,8},{1,9},{2,10},{3,11},{4,12},{5,13},{6,14},{7,15},{8,0},{9,1},... | collective-permute-start | bytes 491528 | tf_op jit(solution)/shard_map/ppermute | solution.py:47
  23.2 3.4 %collective-permute-start.7 = (f32[256,1280]{1,0:T(8,128)}, f32[256,1280]{1,0:T(8,128)}, u32[]{:S(2)}, u32[]{:S(2)}) collective-permute-start(f32[256,1280]{1,0:T(8,128)} %constant_dynamic-update-slice_fusion), channel_id=1, source_target_pairs={{0,1},{1,0},{2,3},{3,2},{4,5},{5,4},{6,7},{7,6},{8,9},{9,8},{10,11... | collective-permute-start | bytes 3932168 | tf_op jit(solution)/shard_map/ppermute | solution.py:51
  30.1 7.9 %collective-permute-start.10 = (f32[2,32,640]{2,1,0:T(8,128)S(1)}, f32[2,32,640]{2,1,0:T(8,128)S(1)}, u32[]{:S(2)}, u32[]{:S(2)}) collective-permute-start(f32[2,32,640]{2,1,0:T(8,128)S(1)} %pad_maximum_fusion.3), channel_id=1, source_target_pairs={{0,16},{16,32},{32,48},{48,0},{64,80},{80,96},{96,112},{112,64},{1... | collective-permute-start | bytes 491528 | tf_op jit(solution)/shard_map/ppermute | solution.py:72
  31.7 6.7 %collective-permute-start.8 = (f32[2,32,640]{2,1,0:T(8,128)S(1)}, f32[2,32,640]{2,1,0:T(8,128)S(1)}, u32[]{:S(2)}, u32[]{:S(2)}) collective-permute-start(f32[2,32,640]{2,1,0:T(8,128)S(1)} %pad_maximum_fusion), channel_id=1, source_target_pairs={{0,48},{16,0},{32,16},{48,32},{64,112},{80,64},{96,80},{112,96},{1... | collective-permute-start | bytes 491528 | tf_op jit(solution)/shard_map/ppermute | solution.py:71
  38.0 7.8 %collective-permute-start.13 = (f32[2,32,640]{2,1,0:T(8,128)S(1)}, f32[2,32,640]{2,1,0:T(8,128)S(1)}, u32[]{:S(2)}, u32[]{:S(2)}) collective-permute-start(f32[2,32,640]{2,1,0:T(8,128)S(1)} %get-tuple-element.26), channel_id=1, source_target_pairs={{0,16},{16,32},{32,48},{48,0},{64,80},{80,96},{96,112},{112,64},{1... | collective-permute-start | bytes 491528 | tf_op jit(solution)/shard_map/ppermute | solution.py:78
  38.4 7.4 %collective-permute-start.12 = (f32[2,32,640]{2,1,0:T(8,128)S(1)}, f32[2,32,640]{2,1,0:T(8,128)S(1)}, u32[]{:S(2)}, u32[]{:S(2)}) collective-permute-start(f32[2,32,640]{2,1,0:T(8,128)S(1)} %get-tuple-element.28), channel_id=1, source_target_pairs={{0,48},{16,0},{32,16},{48,32},{64,112},{80,64},{96,80},{112,96},{1... | collective-permute-start | bytes 491528 | tf_op jit(solution)/shard_map/ppermute | solution.py:77
  41.4 8.1 %collective-permute-start.11 = (f32[2,32,640]{2,1,0:T(8,128)S(1)}, f32[2,32,640]{2,1,0:T(8,128)S(1)}, u32[]{:S(2)}, u32[]{:S(2)}) collective-permute-start(f32[2,32,640]{2,1,0:T(8,128)S(1)} %get-tuple-element.25), channel_id=1, source_target_pairs={{0,16},{16,32},{32,48},{48,0},{64,80},{80,96},{96,112},{112,64},{1... | collective-permute-start | bytes 491528 | tf_op jit(solution)/shard_map/ppermute | solution.py:84
  41.4 8.1 %collective-permute-start.9 = (f32[2,32,640]{2,1,0:T(8,128)S(1)}, f32[2,32,640]{2,1,0:T(8,128)S(1)}, u32[]{:S(2)}, u32[]{:S(2)}) collective-permute-start(f32[2,32,640]{2,1,0:T(8,128)S(1)} %get-tuple-element.27), channel_id=1, source_target_pairs={{0,48},{16,0},{32,16},{48,32},{64,112},{80,64},{96,80},{112,96},{1... | collective-permute-start | bytes 491528 | tf_op jit(solution)/shard_map/ppermute | solution.py:83
  45.8 7.0 %collective-permute-start.14 = (f32[2,32,640]{2,1,0:T(8,128)S(1)}, f32[2,32,640]{2,1,0:T(8,128)S(1)}, u32[]{:S(2)}, u32[]{:S(2)}) collective-permute-start(f32[2,32,640]{2,1,0:T(8,128)S(1)} %select_add_fusion), channel_id=1, source_target_pairs={{0,64},{16,80},{32,96},{48,112},{64,0},{80,16},{96,32},{112,48},{1... | collective-permute-start | bytes 491528 | tf_op jit(solution)/shard_map/ppermute | solution.py:81

commit v18 on v17

--- a/solution.py
+++ b/solution.py
@@ -52,7 +52,7 @@
         mo = lax.axis_index("occ")
         x, zh = mo % nx, mo // nx
 
-        def reduce_both(res_l, res_o):
+        def reduce_both(res_l, res_o, far_o):
             def half_block(r):
                 k = ((r % nx - y) % ny) * 2 + ((r // nx) ^ zl)
                 return jnp.stack(
@@ -68,8 +68,10 @@
             def b_blk(t):
                 return half_block(nx + t % nx)
 
-            p1 = lax.ppermute(a_blk(x + 2), "occ", x_shift(-1))
-            q1 = lax.ppermute(b_blk(x + 2), "occ", x_shift(1))
+            far_l = lax.dynamic_index_in_dim(res_l, slot((x + 2) % nx), 0, keepdims=False)
+            far_lb = lax.dynamic_index_in_dim(res_l, slot(nx + (x + 2) % nx), 0, keepdims=False)
+            p1 = lax.ppermute(jnp.stack([far_l, far_o[:rows]]), "occ", x_shift(-1))
+            q1 = lax.ppermute(jnp.stack([far_lb, far_o[rows:]]), "occ", x_shift(1))
             to_m_a, to_m_b = a_blk(x + nx - 1) + p1, b_blk(x + nx - 1)
             to_p_a, to_p_b = a_blk(x + 1), b_blk(x + 1) + q1
             low = zh == 0
@@ -86,9 +88,21 @@
             )
             return got_keep + from_zhi
 
+        def slot(r):
+            return ((r % nx - y) % ny) * 2 + ((r // nx) ^ zl)
+
+        blocks = other.reshape(8, rows, -1)
+        far = jnp.concatenate(
+            [
+                lax.dynamic_index_in_dim(blocks, slot((x + 2) % nx), 0, keepdims=False),
+                lax.dynamic_index_in_dim(blocks, slot(nx + (x + 2) % nx), 0, keepdims=False),
+            ],
+            axis=0,
+        )
+        far_o = matmul(far, half)
+        res_l, far_o = lax.optimization_barrier((res_l, far_o))
         res_o = matmul(other, half).reshape(8, rows, -1)
-        res_l, res_o = lax.optimization_barrier((res_l, res_o))
-        sums = reduce_both(res_l, res_o)
+        sums = reduce_both(res_l, res_o, far_o)
         first = jnp.where(c == 0, sums[0], sums[1])
         second = jnp.where(c == 0, sums[1], sums[0])
         return jnp.concatenate([first, second], axis=0)

time: 54.1 us -> 53 us (0.980)
  waiting for transfers between devices: 15.2 us -> 11.8 us
  matrix products: 6.7 us -> 7.96 us
  local copies, waits for them, and re-layouts: 6.62 us -> 7.63 us
    ppermute x2, waiting for transfers between devices: 4.5 us -> 1.09 us  [the longest x1 1.09 us: reduce_both(): q1 = lax.ppermute(jnp.stack([far_lb, far_o[rows:]]), 'occ', x_shift(1))]
    dot_general x2 -> x3, matrix products: 6.7 us -> 7.96 us  [matmul(): return jnp.dot(a, b, preferred_element_type=jnp.float32, precision=HIGH)]
    squeeze x0 -> x1, local copies, waits for them, and re-layouts: none -> 1.02 us  [body(): lax.dynamic_index_in_dim(blocks, slot((x + 2) % nx), 0, keepdims=False)]
  transfers between devices with their start and end apart: 15 -> 15, of which waited for: 6 -> 6; matrix products, arithmetic and copies ran while one was open for 17% -> 24% of each run, Pallas kernels for 0% -> 0%
where the time goes in v18:
time: 53 us; the launch traced here: 52.4 us
  starting transfers between devices  24.1 us (45%)
  waiting for transfers between devices  11.8 us (22%)
  matrix products  7.96 us (15%)
  local copies, waits for them, and re-layouts  7.63 us (14%)
  other arithmetic  0.87 us (2%)
    dot_general x3, matrix products, matmul(): return jnp.dot(a, b, preferred_element_type=jnp.float32, precision=HIGH)  7.96 us
    unnamed x9, local copies, waits for them, and re-layouts  5.81 us
    ppermute x1, waiting for transfers between devices, body(): z3 = lax.ppermute(yp2, 'vir', z_swap)  3.85 us
    ppermute x1, starting transfers between devices, reduce_both(): from_zhi = lax.ppermute(got_send, 'occ', zhi_swap)  3.66 us
    ppermute x1, waiting for transfers between devices, reduce_both(): from_zhi = lax.ppermute(got_send, 'occ', zhi_swap)  3.29 us
    ppermute x1, starting transfers between devices, body(): ym1z = lax.ppermute(z1, 'vir', y_shift(1))  3.23 us
    ppermute x1, starting transfers between devices, reduce_both(): lax.ppermute(jnp.where(low, to_m_a, to_m_b), 'occ', x_shift(-1))  3.23 us
    ppermute x1, starting transfers between devices, reduce_both(): lax.ppermute(jnp.where(low, to_m_b, to_m_a), 'occ', x_shift(-1))  3.02 us
  transfers between devices with their start and end apart: 15, of which 6 were waited for; matrix products, arithmetic and copies ran while one was open for 24% of the time, Pallas kernels for 0%

profile of v18, /device:TPU:24, one launch (start us, length us, event | category | flops | bytes accessed | tf_op | source)
XLA Modules:
  0.0 52.4 jit_solution(9510588494508478341)
XLA Ops:
  0.0 0.7 %collective-permute-start.1 = (f32[32,1280]{1,0:T(8,128)}, f32[32,1280]{1,0:T(8,128)S(1)}, u32[]{:S(2)}, u32[]{:S(2)}) collective-permute-start(f32[32,1280]{1,0:T(8,128)} %param.2), channel_id=1, source_target_pairs={{0,6},{1,7},{2,0},{3,1},{4,2},{5,3},{6,4},{7,5},{8,14},{9,15},{10,... | collective-permute-start | bytes 491528 | tf_op jit(solution)/shard_map/ppermute | solution.py:43
  0.7 1.9 %collective-permute-start = (f32[32,1280]{1,0:T(8,128)}, f32[32,1280]{1,0:T(8,128)S(1)}, u32[]{:S(2)}, u32[]{:S(2)}) collective-permute-start(f32[32,1280]{1,0:T(8,128)} %param.2), channel_id=1, source_target_pairs={{0,8},{1,9},{2,10},{3,11},{4,12},{5,13},{6,14},{7,15},{8,0},{9,1},... | collective-permute-start | bytes 491528 | tf_op jit(solution)/shard_map/ppermute | solution.py:41
  2.7 2.5 %collective-permute-start.5 = (f32[32,1280]{1,0:T(8,128)}, f32[32,1280]{1,0:T(8,128)S(1)}, u32[]{:S(2)}, u32[]{:S(2)}) collective-permute-start(f32[32,1280]{1,0:T(8,128)} %param.2), channel_id=1, source_target_pairs={{0,2},{1,3},{2,4},{3,5},{4,6},{5,7},{6,0},{7,1},{8,10},{9,11},{10,... | collective-permute-start | bytes 491528 | tf_op jit(solution)/shard_map/ppermute | solution.py:42
  5.2 1.7 %constant_dynamic-update-slice_fusion.7 = f32[256,1280]{1,0:T(8,128)} fusion(f32[32,1280]{1,0:T(8,128)} %param.2), kind=kLoop, calls=%fused_computation.40 | loop fusion | bytes 327680
  7.4 1.9 %collective-permute-start.2 = (f32[32,1280]{1,0:T(8,128)S(1)}, f32[32,1280]{1,0:T(8,128)S(1)}, u32[]{:S(2)}, u32[]{:S(2)}) collective-permute-start(f32[32,1280]{1,0:T(8,128)S(1)} %collective-permute-done.1), channel_id=1, source_target_pairs={{0,8},{1,9},{2,10},{3,11},{4,12},{5,13},{6,14},{7,15},{8,0},{9,1},... | collective-permute-start | bytes 491528 | tf_op jit(solution)/shard_map/ppermute | solution.py:44
  9.3 3.2 %collective-permute-start.6 = (f32[32,1280]{1,0:T(8,128)S(1)}, f32[32,1280]{1,0:T(8,128)S(1)}, u32[]{:S(2)}, u32[]{:S(2)}) collective-permute-start(f32[32,1280]{1,0:T(8,128)S(1)} %collective-permute-done), channel_id=1, source_target_pairs={{0,2},{1,3},{2,4},{3,5},{4,6},{5,7},{6,0},{7,1},{8,10},{9,11},{10,... | collective-permute-start | bytes 491528 | tf_op jit(solution)/shard_map/ppermute | solution.py:46
  13.9 1.9 %collective-permute-done.3 = f32[32,1280]{1,0:T(8,128)S(1)} collective-permute-done((f32[32,1280]{1,0:T(8,128)S(1)}, f32[32,1280]{1,0:T(8,128)S(1)}, u32[]{:S(2)}, u32[]{:S(2)}) %collective-permute-start.3) | collective-permute-done | bytes 163872 | tf_op jit(solution)/shard_map/ppermute | solution.py:45
  15.9 0.7 %constant_dynamic-update-slice_fusion.4 = f32[256,1280]{1,0:T(8,128)} fusion(f32[256,1280]{1,0:T(8,128)} %constant_dynamic-update-slice_fusion.5, f32[32,1280]{1,0:T(8,128)S(1)} %collective-permute-done.2), kind=kLoop, calls=%fused_computation.37 | loop fusion | bytes 327680
  16.6 0.7 %constant_dynamic-update-slice_fusion.3 = f32[256,1280]{1,0:T(8,128)} fusion(f32[256,1280]{1,0:T(8,128)} %constant_dynamic-update-slice_fusion.4, f32[32,1280]{1,0:T(8,128)S(1)} %collective-permute-done.3), kind=kLoop, calls=%fused_computation.36 | loop fusion | bytes 327680
  17.3 3.8 %collective-permute-done.4 = f32[32,1280]{1,0:T(8,128)S(1)} collective-permute-done((f32[32,1280]{1,0:T(8,128)S(1)}, f32[32,1280]{1,0:T(8,128)S(1)}, u32[]{:S(2)}, u32[]{:S(2)}) %collective-permute-start.4) | collective-permute-done | bytes 163872 | tf_op jit(solution)/shard_map/ppermute | solution.py:47
  21.8 0.7 %constant_dynamic-update-slice_fusion.1 = f32[256,1280]{1,0:T(8,128)} fusion(f32[256,1280]{1,0:T(8,128)} %constant_dynamic-update-slice_fusion.2, f32[32,1280]{1,0:T(8,128)S(1)} %collective-permute-done.5), kind=kLoop, calls=%fused_computation.34 | loop fusion | bytes 327680
  23.2 3.4 %fusion.4 = f32[256,640]{1,0:T(8,128)S(1)} fusion(f32[256,1280]{1,0:T(8,128)} %constant_dynamic-update-slice_fusion, f32[1280,640]{1,0:T(8,128)S(1)} %copy-done), kind=kOutput, calls=%fused_computation.4 | convolution fusion | flops 1259110400 | bytes 5242880 | tf_op jit(solution)/shard_map/dot_general | solution.py:32
  26.6 1.0 %dynamic-slice_bitcast_fusion.1 = (f32[32,1280]{1,0:T(8,128)S(1)}, f32[32,1280]{1,0:T(8,128)S(1)}) fusion(f32[8,32,1280]{2,1,0:T(8,128)} %bitcast.1, s32[]{:T(128)S(6)} %select_n.261, s32[]{:T(128)S(6)} %select_n.265), kind=kLoop, calls=%fused_computation.24 | loop fusion | bytes 655368 | tf_op jit(solution)/shard_map/jit(dynamic_index_in_dim)/squeeze | solution.py:97
  27.6 1.3 %fusion.2 = f32[64,640]{1,0:T(8,128)S(1)} fusion(f32[1280,640]{1,0:T(8,128)S(1)} %copy-done, f32[32,1280]{1,0:T(8,128)S(1)} %get-tuple-element.10, f32[32,1280]{1,0:T(8,128)S(1)} %get-tuple-element.9), kind=kOutput, calls=%fused_computation.2 | convolution fusion | flops 315473920 | bytes 3768320 | tf_op jit(solution)/shard_map/dot_general | solution.py:32
  29.0 1.6 %collective-permute-start.10 = (f32[2,32,640]{2,1,0:T(8,128)S(1)}, f32[2,32,640]{2,1,0:T(8,128)S(1)}, u32[]{:S(2)}, u32[]{:S(2)}) collective-permute-start(f32[2,32,640]{2,1,0:T(8,128)S(1)} %pad_maximum_fusion.3), channel_id=1, source_target_pairs={{0,16},{16,32},{32,48},{48,0},{64,80},{80,96},{96,112},{112,64},{1... | collective-permute-start | bytes 491528 | tf_op jit(solution)/shard_map/ppermute | solution.py:74
  30.5 1.8 %collective-permute-start.8 = (f32[2,32,640]{2,1,0:T(8,128)S(1)}, f32[2,32,640]{2,1,0:T(8,128)S(1)}, u32[]{:S(2)}, u32[]{:S(2)}) collective-permute-start(f32[2,32,640]{2,1,0:T(8,128)S(1)} %pad_maximum_fusion), channel_id=1, source_target_pairs={{0,48},{16,0},{32,16},{48,32},{64,112},{80,64},{96,80},{112,96},{1... | collective-permute-start | bytes 491528 | tf_op jit(solution)/shard_map/ppermute | solution.py:73
  32.4 3.3 %fusion = f32[256,640]{1,0:T(8,128)S(1)} fusion(f32[256,1280]{1,0:T(8,128)} %collective-permute-done.7, f32[1280,640]{1,0:T(8,128)S(1)} %copy-done), kind=kOutput, calls=%fused_computation | convolution fusion | flops 1259110400 | bytes 5242880 | tf_op jit(solution)/shard_map/dot_general | solution.py:32
  35.8 1.1 %collective-permute-done.10 = f32[2,32,640]{2,1,0:T(8,128)S(1)} collective-permute-done((f32[2,32,640]{2,1,0:T(8,128)S(1)}, f32[2,32,640]{2,1,0:T(8,128)S(1)}, u32[]{:S(2)}, u32[]{:S(2)}) %collective-permute-start.10) | collective-permute-done | bytes 163872 | tf_op jit(solution)/shard_map/ppermute | solution.py:74
  37.3 3.0 %collective-permute-start.12 = (f32[2,32,640]{2,1,0:T(8,128)S(1)}, f32[2,32,640]{2,1,0:T(8,128)S(1)}, u32[]{:S(2)}, u32[]{:S(2)}) collective-permute-start(f32[2,32,640]{2,1,0:T(8,128)S(1)} %get-tuple-element.28), channel_id=1, source_target_pairs={{0,48},{16,0},{32,16},{48,32},{64,112},{80,64},{96,80},{112,96},{1... | collective-permute-start | bytes 491528 | tf_op jit(solution)/shard_map/ppermute | solution.py:79
  40.3 3.2 %collective-permute-start.9 = (f32[2,32,640]{2,1,0:T(8,128)S(1)}, f32[2,32,640]{2,1,0:T(8,128)S(1)}, u32[]{:S(2)}, u32[]{:S(2)}) collective-permute-start(f32[2,32,640]{2,1,0:T(8,128)S(1)} %get-tuple-element.27), channel_id=1, source_target_pairs={{0,48},{16,0},{32,16},{48,32},{64,112},{80,64},{96,80},{112,96},{1... | collective-permute-start | bytes 491528 | tf_op jit(solution)/shard_map/ppermute | solution.py:85
  43.5 1.1 %collective-permute-done.13 = f32[2,32,640]{2,1,0:T(8,128)S(1)} collective-permute-done((f32[2,32,640]{2,1,0:T(8,128)S(1)}, f32[2,32,640]{2,1,0:T(8,128)S(1)}, u32[]{:S(2)}, u32[]{:S(2)}) %collective-permute-start.13) | collective-permute-done | bytes 163872 | tf_op jit(solution)/shard_map/ppermute | solution.py:80
  44.7 3.7 %collective-permute-start.14 = (f32[2,32,640]{2,1,0:T(8,128)S(1)}, f32[2,32,640]{2,1,0:T(8,128)S(1)}, u32[]{:S(2)}, u32[]{:S(2)}) collective-permute-start(f32[2,32,640]{2,1,0:T(8,128)S(1)} %select_add_fusion), channel_id=1, source_target_pairs={{0,64},{16,80},{32,96},{48,112},{64,0},{80,16},{96,32},{112,48},{1... | collective-permute-start | bytes 491528 | tf_op jit(solution)/shard_map/ppermute | solution.py:83
  48.4 3.3 %collective-permute-done.14 = f32[2,32,640]{2,1,0:T(8,128)S(1)} collective-permute-done((f32[2,32,640]{2,1,0:T(8,128)S(1)}, f32[2,32,640]{2,1,0:T(8,128)S(1)}, u32[]{:S(2)}, u32[]{:S(2)}) %collective-permute-start.14) | collective-permute-done | bytes 163872 | tf_op jit(solution)/shard_map/ppermute | solution.py:83
  51.7 0.7 %pad_maximum_fusion.6 = f32[64,640]{1,0:T(8,128)} fusion(f32[32,640]{1,0:T(8,128)S(1)} %get-tuple-element.30, f32[32,640]{1,0:T(8,128)S(1)} %get-tuple-element.29), kind=kLoop, calls=%fused_computation.20 | loop fusion | flops 40960 | bytes 327680 | tf_op jit(solution)/shard_map/concatenate | solution.py:108
  (31 shorter events, 4.0 us)
Async XLA Ops:
  0.0 7.4 %collective-permute-start.1 = (f32[32,1280]{1,0:T(8,128)}, f32[32,1280]{1,0:T(8,128)S(1)}, u32[]{:S(2)}, u32[]{:S(2)}) collective-permute-start(f32[32,1280]{1,0:T(8,128)} %param.2), channel_id=1, source_target_pairs={{0,6},{1,7},{2,0},{3,1},{4,2},{5,3},{6,4},{7,5},{8,14},{9,15},{10,... | collective-permute-start | bytes 491528 | tf_op jit(solution)/shard_map/ppermute | solution.py:43
  0.7 8.5 %collective-permute-start = (f32[32,1280]{1,0:T(8,128)}, f32[32,1280]{1,0:T(8,128)S(1)}, u32[]{:S(2)}, u32[]{:S(2)}) collective-permute-start(f32[32,1280]{1,0:T(8,128)} %param.2), channel_id=1, source_target_pairs={{0,8},{1,9},{2,10},{3,11},{4,12},{5,13},{6,14},{7,15},{8,0},{9,1},... | collective-permute-start | bytes 491528 | tf_op jit(solution)/shard_map/ppermute | solution.py:41
  2.7 19.1 %collective-permute-start.5 = (f32[32,1280]{1,0:T(8,128)}, f32[32,1280]{1,0:T(8,128)S(1)}, u32[]{:S(2)}, u32[]{:S(2)}) collective-permute-start(f32[32,1280]{1,0:T(8,128)} %param.2), channel_id=1, source_target_pairs={{0,2},{1,3},{2,4},{3,5},{4,6},{5,7},{6,0},{7,1},{8,10},{9,11},{10,... | collective-permute-start | bytes 491528 | tf_op jit(solution)/shard_map/ppermute | solution.py:42
  5.2 18.0 %copy-start = (f32[1280,640]{1,0:T(8,128)S(1)}, f32[1280,640]{1,0:T(8,128)}, u32[]{:S(2)}) copy-start(f32[1280,640]{1,0:T(8,128)} %param.3) | copy-start | bytes 9830404
  7.4 8.6 %collective-permute-start.2 = (f32[32,1280]{1,0:T(8,128)S(1)}, f32[32,1280]{1,0:T(8,128)S(1)}, u32[]{:S(2)}, u32[]{:S(2)}) collective-permute-start(f32[32,1280]{1,0:T(8,128)S(1)} %collective-permute-done.1), channel_id=1, source_target_pairs={{0,8},{1,9},{2,10},{3,11},{4,12},{5,13},{6,14},{7,15},{8,0},{9,1},... | collective-permute-start | bytes 491528 | tf_op jit(solution)/shard_map/ppermute | solution.py:44
  9.3 6.5 %collective-permute-start.3 = (f32[32,1280]{1,0:T(8,128)S(1)}, f32[32,1280]{1,0:T(8,128)S(1)}, u32[]{:S(2)}, u32[]{:S(2)}) collective-permute-start(f32[32,1280]{1,0:T(8,128)S(1)} %collective-permute-done.1), channel_id=1, source_target_pairs={{0,6},{1,7},{2,0},{3,1},{4,2},{5,3},{6,4},{7,5},{8,14},{9,15},{10,... | collective-permute-start | bytes 491528 | tf_op jit(solution)/shard_map/ppermute | solution.py:45
  9.3 13.2 %collective-permute-start.6 = (f32[32,1280]{1,0:T(8,128)S(1)}, f32[32,1280]{1,0:T(8,128)S(1)}, u32[]{:S(2)}, u32[]{:S(2)}) collective-permute-start(f32[32,1280]{1,0:T(8,128)S(1)} %collective-permute-done), channel_id=1, source_target_pairs={{0,2},{1,3},{2,4},{3,5},{4,6},{5,7},{6,0},{7,1},{8,10},{9,11},{10,... | collective-permute-start | bytes 491528 | tf_op jit(solution)/shard_map/ppermute | solution.py:46
  15.8 5.3 %collective-permute-start.4 = (f32[32,1280]{1,0:T(8,128)S(1)}, f32[32,1280]{1,0:T(8,128)S(1)}, u32[]{:S(2)}, u32[]{:S(2)}) collective-permute-start(f32[32,1280]{1,0:T(8,128)S(1)} %collective-permute-done.3), channel_id=1, source_target_pairs={{0,8},{1,9},{2,10},{3,11},{4,12},{5,13},{6,14},{7,15},{8,0},{9,1},... | collective-permute-start | bytes 491528 | tf_op jit(solution)/shard_map/ppermute | solution.py:47
  23.2 3.4 %collective-permute-start.7 = (f32[256,1280]{1,0:T(8,128)}, f32[256,1280]{1,0:T(8,128)}, u32[]{:S(2)}, u32[]{:S(2)}) collective-permute-start(f32[256,1280]{1,0:T(8,128)} %constant_dynamic-update-slice_fusion), channel_id=1, source_target_pairs={{0,1},{1,0},{2,3},{3,2},{4,5},{5,4},{6,7},{7,6},{8,9},{9,8},{10,11... | collective-permute-start | bytes 3932168 | tf_op jit(solution)/shard_map/ppermute | solution.py:51
  29.0 7.9 %collective-permute-start.10 = (f32[2,32,640]{2,1,0:T(8,128)S(1)}, f32[2,32,640]{2,1,0:T(8,128)S(1)}, u32[]{:S(2)}, u32[]{:S(2)}) collective-permute-start(f32[2,32,640]{2,1,0:T(8,128)S(1)} %pad_maximum_fusion.3), channel_id=1, source_target_pairs={{0,16},{16,32},{32,48},{48,0},{64,80},{80,96},{96,112},{112,64},{1... | collective-permute-start | bytes 491528 | tf_op jit(solution)/shard_map/ppermute | solution.py:74
  30.5 6.7 %collective-permute-start.8 = (f32[2,32,640]{2,1,0:T(8,128)S(1)}, f32[2,32,640]{2,1,0:T(8,128)S(1)}, u32[]{:S(2)}, u32[]{:S(2)}) collective-permute-start(f32[2,32,640]{2,1,0:T(8,128)S(1)} %pad_maximum_fusion), channel_id=1, source_target_pairs={{0,48},{16,0},{32,16},{48,32},{64,112},{80,64},{96,80},{112,96},{1... | collective-permute-start | bytes 491528 | tf_op jit(solution)/shard_map/ppermute | solution.py:73
  36.9 7.8 %collective-permute-start.13 = (f32[2,32,640]{2,1,0:T(8,128)S(1)}, f32[2,32,640]{2,1,0:T(8,128)S(1)}, u32[]{:S(2)}, u32[]{:S(2)}) collective-permute-start(f32[2,32,640]{2,1,0:T(8,128)S(1)} %get-tuple-element.26), channel_id=1, source_target_pairs={{0,16},{16,32},{32,48},{48,0},{64,80},{80,96},{96,112},{112,64},{1... | collective-permute-start | bytes 491528 | tf_op jit(solution)/shard_map/ppermute | solution.py:80
  37.3 7.4 %collective-permute-start.12 = (f32[2,32,640]{2,1,0:T(8,128)S(1)}, f32[2,32,640]{2,1,0:T(8,128)S(1)}, u32[]{:S(2)}, u32[]{:S(2)}) collective-permute-start(f32[2,32,640]{2,1,0:T(8,128)S(1)} %get-tuple-element.28), channel_id=1, source_target_pairs={{0,48},{16,0},{32,16},{48,32},{64,112},{80,64},{96,80},{112,96},{1... | collective-permute-start | bytes 491528 | tf_op jit(solution)/shard_map/ppermute | solution.py:79
  40.3 8.1 %collective-permute-start.11 = (f32[2,32,640]{2,1,0:T(8,128)S(1)}, f32[2,32,640]{2,1,0:T(8,128)S(1)}, u32[]{:S(2)}, u32[]{:S(2)}) collective-permute-start(f32[2,32,640]{2,1,0:T(8,128)S(1)} %get-tuple-element.25), channel_id=1, source_target_pairs={{0,16},{16,32},{32,48},{48,0},{64,80},{80,96},{96,112},{112,64},{1... | collective-permute-start | bytes 491528 | tf_op jit(solution)/shard_map/ppermute | solution.py:86
  40.3 8.1 %collective-permute-start.9 = (f32[2,32,640]{2,1,0:T(8,128)S(1)}, f32[2,32,640]{2,1,0:T(8,128)S(1)}, u32[]{:S(2)}, u32[]{:S(2)}) collective-permute-start(f32[2,32,640]{2,1,0:T(8,128)S(1)} %get-tuple-element.27), channel_id=1, source_target_pairs={{0,48},{16,0},{32,16},{48,32},{64,112},{80,64},{96,80},{112,96},{1... | collective-permute-start | bytes 491528 | tf_op jit(solution)/shard_map/ppermute | solution.py:85
  44.7 7.0 %collective-permute-start.14 = (f32[2,32,640]{2,1,0:T(8,128)S(1)}, f32[2,32,640]{2,1,0:T(8,128)S(1)}, u32[]{:S(2)}, u32[]{:S(2)}) collective-permute-start(f32[2,32,640]{2,1,0:T(8,128)S(1)} %select_add_fusion), channel_id=1, source_target_pairs={{0,64},{16,80},{32,96},{48,112},{64,0},{80,16},{96,32},{112,48},{1... | collective-permute-start | bytes 491528 | tf_op jit(solution)/shard_map/ppermute | solution.py:83

commit v19 on v18

--- a/solution.py
+++ b/solution.py
@@ -91,7 +91,7 @@
         def slot(r):
             return ((r % nx - y) % ny) * 2 + ((r // nx) ^ zl)
 
-        blocks = other.reshape(8, rows, -1)
+        blocks = local.reshape(8, rows, -1)
         far = jnp.concatenate(
             [
                 lax.dynamic_index_in_dim(blocks, slot((x + 2) % nx), 0, keepdims=False),
@@ -99,7 +99,7 @@
             ],
             axis=0,
         )
-        far_o = matmul(far, half)
+        far_o = matmul(lax.ppermute(far, "vir", core_swap), half)
         res_l, far_o = lax.optimization_barrier((res_l, far_o))
         res_o = matmul(other, half).reshape(8, rows, -1)
         sums = reduce_both(res_l, res_o, far_o)

time: 53 us -> 52.2 us (0.985)
  waiting for transfers between devices: 11.8 us -> 19.6 us
  local copies, waits for them, and re-layouts: 7.63 us -> 1.21 us
  matrix products: 7.96 us -> 5.37 us
  starting transfers between devices: 24.1 us -> 24.8 us
    unnamed x9, local copies, waits for them, and re-layouts: 5.81 us -> 1.04 us
    ppermute x1, waiting for transfers between devices: 1.11 us -> 4.05 us  [reduce_both(): lax.ppermute(jnp.where(low, to_p_b, to_p_a), 'occ', x_shift(1))]
    dot_general x3, matrix products: 7.96 us -> 5.37 us  [matmul(): return jnp.dot(a, b, preferred_element_type=jnp.float32, precision=HIGH)]
    ppermute x1, waiting for transfers between devices: 0.47 us -> 2.88 us  [body(): yp1 = lax.ppermute(own, 'vir', y_shift(-1))]
    ppermute x1, starting transfers between devices: 1.92 us -> 0.28 us  [body(): z2 = lax.ppermute(yp1, 'vir', z_swap)]
    ppermute x1, starting transfers between devices: 0.11 us -> 1.74 us  [body(): z3 = lax.ppermute(yp2, 'vir', z_swap)]
    ppermute x1, waiting for transfers between devices: 0.01 us -> 1.53 us  [reduce_both(): p1 = lax.ppermute(jnp.stack([far_l, far_o[:rows]]), 'occ', x_shift(-1))]
    ppermute x1, starting transfers between devices: 1.56 us -> 0.07 us  [reduce_both(): q1 = lax.ppermute(jnp.stack([far_lb, far_o[rows:]]), 'occ', x_shift(1))]
  transfers between devices with their start and end apart: 15 -> 16, of which waited for: 6 -> 8; matrix products, arithmetic and copies ran while one was open for 24% -> 13% of each run, Pallas kernels for 0% -> 0%
where the time goes in v19:
time: 52.2 us; the launch traced here: 52.1 us
  starting transfers between devices  24.8 us (48%)
  waiting for transfers between devices  19.6 us (38%)
  matrix products  5.37 us (10%)
  local copies, waits for them, and re-layouts  1.21 us (2%)
  other arithmetic  0.89 us (2%)
    dot_general x3, matrix products, matmul(): return jnp.dot(a, b, preferred_element_type=jnp.float32, precision=HIGH)  5.37 us
    ppermute x1, waiting for transfers between devices, reduce_both(): lax.ppermute(jnp.where(low, to_p_b, to_p_a), 'occ', x_shift(1))  4.05 us
    ppermute x1, starting transfers between devices, reduce_both(): from_zhi = lax.ppermute(got_send, 'occ', zhi_swap)  3.78 us
    ppermute x1, starting transfers between devices, reduce_both(): lax.ppermute(jnp.where(low, to_m_b, to_m_a), 'occ', x_shift(-1))  3.76 us
    ppermute x1, waiting for transfers between devices, body(): z3 = lax.ppermute(yp2, 'vir', z_swap)  3.53 us
    ppermute x1, waiting for transfers between devices, reduce_both(): from_zhi = lax.ppermute(got_send, 'occ', zhi_swap)  3.29 us
    ppermute x1, waiting for transfers between devices, body(): yp2 = lax.ppermute(yp1, 'vir', y_shift(-1))  3.24 us
    ppermute x1, starting transfers between devices, body(): ym1z = lax.ppermute(z1, 'vir', y_shift(1))  3.23 us
  transfers between devices with their start and end apart: 16, of which 8 were waited for; matrix products, arithmetic and copies ran while one was open for 13% of the time, Pallas kernels for 0%

profile of v19, /device:TPU:24, one launch (start us, length us, event | category | flops | bytes accessed | tf_op | source)
XLA Modules:
  0.0 52.1 jit_solution(9738469392041261875)
XLA Ops:
  0.0 1.9 %collective-permute-start = (f32[32,1280]{1,0:T(8,128)}, f32[32,1280]{1,0:T(8,128)S(1)}, u32[]{:S(2)}, u32[]{:S(2)}) collective-permute-start(f32[32,1280]{1,0:T(8,128)} %param.2), channel_id=1, source_target_pairs={{0,8},{1,9},{2,10},{3,11},{4,12},{5,13},{6,14},{7,15},{8,0},{9,1},... | collective-permute-start | bytes 491528 | tf_op jit(solution)/shard_map/ppermute | solution.py:41
  1.9 0.7 %collective-permute-start.1 = (f32[32,1280]{1,0:T(8,128)}, f32[32,1280]{1,0:T(8,128)S(1)}, u32[]{:S(2)}, u32[]{:S(2)}) collective-permute-start(f32[32,1280]{1,0:T(8,128)} %param.2), channel_id=1, source_target_pairs={{0,6},{1,7},{2,0},{3,1},{4,2},{5,3},{6,4},{7,5},{8,14},{9,15},{10,... | collective-permute-start | bytes 491528 | tf_op jit(solution)/shard_map/ppermute | solution.py:43
  2.7 2.5 %collective-permute-start.5 = (f32[32,1280]{1,0:T(8,128)}, f32[32,1280]{1,0:T(8,128)S(1)}, u32[]{:S(2)}, u32[]{:S(2)}) collective-permute-start(f32[32,1280]{1,0:T(8,128)} %param.2), channel_id=1, source_target_pairs={{0,2},{1,3},{2,4},{3,5},{4,6},{5,7},{6,0},{7,1},{8,10},{9,11},{10,... | collective-permute-start | bytes 491528 | tf_op jit(solution)/shard_map/ppermute | solution.py:42
  5.2 1.0 %constant_dynamic-update-slice_fusion.7 = f32[256,1280]{1,0:T(8,128)S(1)} fusion(f32[32,1280]{1,0:T(8,128)} %param.2), kind=kLoop, calls=%fused_computation.38 | loop fusion | bytes 327680
  6.1 2.9 %collective-permute-done.1 = f32[32,1280]{1,0:T(8,128)S(1)} collective-permute-done((f32[32,1280]{1,0:T(8,128)}, f32[32,1280]{1,0:T(8,128)S(1)}, u32[]{:S(2)}, u32[]{:S(2)}) %collective-permute-start.1) | collective-permute-done | bytes 163872 | tf_op jit(solution)/shard_map/ppermute | solution.py:43
  9.0 0.3 collective-permute-start.2
  9.3 3.2 %collective-permute-start.6 = (f32[32,1280]{1,0:T(8,128)S(1)}, f32[32,1280]{1,0:T(8,128)S(1)}, u32[]{:S(2)}, u32[]{:S(2)}) collective-permute-start(f32[32,1280]{1,0:T(8,128)S(1)} %collective-permute-done), channel_id=1, source_target_pairs={{0,2},{1,3},{2,4},{3,5},{4,6},{5,7},{6,0},{7,1},{8,10},{9,11},{10,... | collective-permute-start | bytes 491528 | tf_op jit(solution)/shard_map/ppermute | solution.py:46
  12.6 3.2 %collective-permute-done.3 = f32[32,1280]{1,0:T(8,128)S(1)} collective-permute-done((f32[32,1280]{1,0:T(8,128)S(1)}, f32[32,1280]{1,0:T(8,128)S(1)}, u32[]{:S(2)}, u32[]{:S(2)}) %collective-permute-start.3) | collective-permute-done | bytes 163872 | tf_op jit(solution)/shard_map/ppermute | solution.py:45
  15.8 1.7 %collective-permute-start.4 = (f32[32,1280]{1,0:T(8,128)S(1)}, f32[32,1280]{1,0:T(8,128)S(1)}, u32[]{:S(2)}, u32[]{:S(2)}) collective-permute-start(f32[32,1280]{1,0:T(8,128)S(1)} %collective-permute-done.3), channel_id=1, source_target_pairs={{0,8},{1,9},{2,10},{3,11},{4,12},{5,13},{6,14},{7,15},{8,0},{9,1},... | collective-permute-start | bytes 491528 | tf_op jit(solution)/shard_map/ppermute | solution.py:47
  17.6 3.5 %collective-permute-done.4 = f32[32,1280]{1,0:T(8,128)S(1)} collective-permute-done((f32[32,1280]{1,0:T(8,128)S(1)}, f32[32,1280]{1,0:T(8,128)S(1)}, u32[]{:S(2)}, u32[]{:S(2)}) %collective-permute-start.4) | collective-permute-done | bytes 163872 | tf_op jit(solution)/shard_map/ppermute | solution.py:47
  21.4 0.6 %collective-permute-start.7 = (f32[64,1280]{1,0:T(8,128)S(1)}, f32[64,1280]{1,0:T(8,128)S(1)}, u32[]{:S(2)}, u32[]{:S(2)}) collective-permute-start(f32[64,1280]{1,0:T(8,128)S(1)} %pad_maximum_fusion), channel_id=1, source_target_pairs={{0,1},{1,0},{2,3},{3,2},{4,5},{5,4},{6,7},{7,6},{8,9},{9,8},{10,11... | collective-permute-start | bytes 983048 | tf_op jit(solution)/shard_map/ppermute | solution.py:102
  21.9 2.1 %fusion.4 = f32[256,640]{1,0:T(8,128)S(1)} fusion(f32[256,1280]{1,0:T(8,128)S(1)} %constant_dynamic-update-slice_fusion, f32[1280,640]{1,0:T(8,128)S(1)} %copy-done), kind=kOutput, calls=%fused_computation.4 | convolution fusion | flops 1259110400 | bytes 5242880 | tf_op jit(solution)/shard_map/dot_general | solution.py:32
  24.0 0.8 %collective-permute-done.7 = f32[64,1280]{1,0:T(8,128)S(1)} collective-permute-done((f32[64,1280]{1,0:T(8,128)S(1)}, f32[64,1280]{1,0:T(8,128)S(1)}, u32[]{:S(2)}, u32[]{:S(2)}) %collective-permute-start.7) | collective-permute-done | bytes 327712 | tf_op jit(solution)/shard_map/ppermute | solution.py:102
  24.8 1.3 %fusion.2 = f32[64,640]{1,0:T(8,128)S(1)} fusion(f32[64,1280]{1,0:T(8,128)S(1)} %collective-permute-done.7, f32[1280,640]{1,0:T(8,128)S(1)} %copy-done), kind=kOutput, calls=%fused_computation.2 | convolution fusion | flops 315392000 | bytes 3768320 | tf_op jit(solution)/shard_map/dot_general | solution.py:32
  26.2 2.8 %collective-permute-start.9 = (f32[2,32,640]{2,1,0:T(8,128)S(1)}, f32[2,32,640]{2,1,0:T(8,128)S(1)}, u32[]{:S(2)}, u32[]{:S(2)}) collective-permute-start(f32[2,32,640]{2,1,0:T(8,128)S(1)} %pad_maximum_fusion.1), channel_id=1, source_target_pairs={{0,48},{16,0},{32,16},{48,32},{64,112},{80,64},{96,80},{112,96},{1... | collective-permute-start | bytes 491528 | tf_op jit(solution)/shard_map/ppermute | solution.py:73
  29.1 2.1 %fusion = f32[256,640]{1,0:T(8,128)S(1)} fusion(f32[256,1280]{1,0:T(8,128)S(1)} %collective-permute-done.8, f32[1280,640]{1,0:T(8,128)S(1)} %copy-done), kind=kOutput, calls=%fused_computation | convolution fusion | flops 1259110400 | bytes 5242880 | tf_op jit(solution)/shard_map/dot_general | solution.py:32
  31.2 1.5 %collective-permute-done.9 = f32[2,32,640]{2,1,0:T(8,128)S(1)} collective-permute-done((f32[2,32,640]{2,1,0:T(8,128)S(1)}, f32[2,32,640]{2,1,0:T(8,128)S(1)}, u32[]{:S(2)}, u32[]{:S(2)}) %collective-permute-start.9) | collective-permute-done | bytes 163872 | tf_op jit(solution)/shard_map/ppermute | solution.py:73
  32.8 3.8 %collective-permute-start.13 = (f32[2,32,640]{2,1,0:T(8,128)S(1)}, f32[2,32,640]{2,1,0:T(8,128)S(1)}, u32[]{:S(2)}, u32[]{:S(2)}) collective-permute-start(f32[2,32,640]{2,1,0:T(8,128)S(1)} %get-tuple-element.28), channel_id=1, source_target_pairs={{0,48},{16,0},{32,16},{48,32},{64,112},{80,64},{96,80},{112,96},{1... | collective-permute-start | bytes 491528 | tf_op jit(solution)/shard_map/ppermute | solution.py:79
  36.7 3.2 %collective-permute-start.10 = (f32[2,32,640]{2,1,0:T(8,128)S(1)}, f32[2,32,640]{2,1,0:T(8,128)S(1)}, u32[]{:S(2)}, u32[]{:S(2)}) collective-permute-start(f32[2,32,640]{2,1,0:T(8,128)S(1)} %get-tuple-element.27), channel_id=1, source_target_pairs={{0,48},{16,0},{32,16},{48,32},{64,112},{80,64},{96,80},{112,96},{1... | collective-permute-start | bytes 491528 | tf_op jit(solution)/shard_map/ppermute | solution.py:85
  39.9 0.3 collective-permute-done.13
  40.2 4.1 %collective-permute-done.14 = f32[2,32,640]{2,1,0:T(8,128)S(1)} collective-permute-done((f32[2,32,640]{2,1,0:T(8,128)S(1)}, f32[2,32,640]{2,1,0:T(8,128)S(1)}, u32[]{:S(2)}, u32[]{:S(2)}) %collective-permute-start.14) | collective-permute-done | bytes 163872 | tf_op jit(solution)/shard_map/ppermute | solution.py:80
  44.3 3.8 %collective-permute-start.15 = (f32[2,32,640]{2,1,0:T(8,128)S(1)}, f32[2,32,640]{2,1,0:T(8,128)S(1)}, u32[]{:S(2)}, u32[]{:S(2)}) collective-permute-start(f32[2,32,640]{2,1,0:T(8,128)S(1)} %select_add_fusion), channel_id=1, source_target_pairs={{0,64},{16,80},{32,96},{48,112},{64,0},{80,16},{96,32},{112,48},{1... | collective-permute-start | bytes 491528 | tf_op jit(solution)/shard_map/ppermute | solution.py:83
  48.1 3.3 %collective-permute-done.15 = f32[2,32,640]{2,1,0:T(8,128)S(1)} collective-permute-done((f32[2,32,640]{2,1,0:T(8,128)S(1)}, f32[2,32,640]{2,1,0:T(8,128)S(1)}, u32[]{:S(2)}, u32[]{:S(2)}) %collective-permute-start.15) | collective-permute-done | bytes 163872 | tf_op jit(solution)/shard_map/ppermute | solution.py:83
  51.4 0.7 %pad_maximum_fusion.7 = f32[64,640]{1,0:T(8,128)} fusion(f32[32,640]{1,0:T(8,128)S(1)} %get-tuple-element.30, f32[32,640]{1,0:T(8,128)S(1)} %get-tuple-element.29), kind=kLoop, calls=%fused_computation.18 | loop fusion | flops 40960 | bytes 327680 | tf_op jit(solution)/shard_map/concatenate | solution.py:108
  (34 shorter events, 0.7 us)
Async XLA Ops:
  0.0 9.3 %collective-permute-start = (f32[32,1280]{1,0:T(8,128)}, f32[32,1280]{1,0:T(8,128)S(1)}, u32[]{:S(2)}, u32[]{:S(2)}) collective-permute-start(f32[32,1280]{1,0:T(8,128)} %param.2), channel_id=1, source_target_pairs={{0,8},{1,9},{2,10},{3,11},{4,12},{5,13},{6,14},{7,15},{8,0},{9,1},... | collective-permute-start | bytes 491528 | tf_op jit(solution)/shard_map/ppermute | solution.py:41
  1.9 7.1 %collective-permute-start.1 = (f32[32,1280]{1,0:T(8,128)}, f32[32,1280]{1,0:T(8,128)S(1)}, u32[]{:S(2)}, u32[]{:S(2)}) collective-permute-start(f32[32,1280]{1,0:T(8,128)} %param.2), channel_id=1, source_target_pairs={{0,6},{1,7},{2,0},{3,1},{4,2},{5,3},{6,4},{7,5},{8,14},{9,15},{10,... | collective-permute-start | bytes 491528 | tf_op jit(solution)/shard_map/ppermute | solution.py:43
  2.7 18.5 %collective-permute-start.5 = (f32[32,1280]{1,0:T(8,128)}, f32[32,1280]{1,0:T(8,128)S(1)}, u32[]{:S(2)}, u32[]{:S(2)}) collective-permute-start(f32[32,1280]{1,0:T(8,128)} %param.2), channel_id=1, source_target_pairs={{0,2},{1,3},{2,4},{3,5},{4,6},{5,7},{6,0},{7,1},{8,10},{9,11},{10,... | collective-permute-start | bytes 491528 | tf_op jit(solution)/shard_map/ppermute | solution.py:42
  9.0 8.6 %collective-permute-start.2 = (f32[32,1280]{1,0:T(8,128)S(1)}, f32[32,1280]{1,0:T(8,128)S(1)}, u32[]{:S(2)}, u32[]{:S(2)}) collective-permute-start(f32[32,1280]{1,0:T(8,128)S(1)} %collective-permute-done.1), channel_id=1, source_target_pairs={{0,8},{1,9},{2,10},{3,11},{4,12},{5,13},{6,14},{7,15},{8,0},{9,1},... | collective-permute-start | bytes 491528 | tf_op jit(solution)/shard_map/ppermute | solution.py:44
  9.3 6.5 %collective-permute-start.3 = (f32[32,1280]{1,0:T(8,128)S(1)}, f32[32,1280]{1,0:T(8,128)S(1)}, u32[]{:S(2)}, u32[]{:S(2)}) collective-permute-start(f32[32,1280]{1,0:T(8,128)S(1)} %collective-permute-done.1), channel_id=1, source_target_pairs={{0,6},{1,7},{2,0},{3,1},{4,2},{5,3},{6,4},{7,5},{8,14},{9,15},{10,... | collective-permute-start | bytes 491528 | tf_op jit(solution)/shard_map/ppermute | solution.py:45
  9.3 11.9 %collective-permute-start.6 = (f32[32,1280]{1,0:T(8,128)S(1)}, f32[32,1280]{1,0:T(8,128)S(1)}, u32[]{:S(2)}, u32[]{:S(2)}) collective-permute-start(f32[32,1280]{1,0:T(8,128)S(1)} %collective-permute-done), channel_id=1, source_target_pairs={{0,2},{1,3},{2,4},{3,5},{4,6},{5,7},{6,0},{7,1},{8,10},{9,11},{10,... | collective-permute-start | bytes 491528 | tf_op jit(solution)/shard_map/ppermute | solution.py:46
  12.5 9.4 %copy-start = (f32[1280,640]{1,0:T(8,128)S(1)}, f32[1280,640]{1,0:T(8,128)}, u32[]{:S(2)}) copy-start(f32[1280,640]{1,0:T(8,128)} %param.3) | copy-start | bytes 9830404
  15.8 5.3 %collective-permute-start.4 = (f32[32,1280]{1,0:T(8,128)S(1)}, f32[32,1280]{1,0:T(8,128)S(1)}, u32[]{:S(2)}, u32[]{:S(2)}) collective-permute-start(f32[32,1280]{1,0:T(8,128)S(1)} %collective-permute-done.3), channel_id=1, source_target_pairs={{0,8},{1,9},{2,10},{3,11},{4,12},{5,13},{6,14},{7,15},{8,0},{9,1},... | collective-permute-start | bytes 491528 | tf_op jit(solution)/shard_map/ppermute | solution.py:47
  21.2 7.9 %collective-permute-start.8 = (f32[256,1280]{1,0:T(8,128)S(1)}, f32[256,1280]{1,0:T(8,128)S(1)}, u32[]{:S(2)}, u32[]{:S(2)}) collective-permute-start(f32[256,1280]{1,0:T(8,128)S(1)} %constant_dynamic-update-slice_fusion), channel_id=1, source_target_pairs={{0,1},{1,0},{2,3},{3,2},{4,5},{5,4},{6,7},{7,6},{8,9},{9,8},{10,11... | collective-permute-start | bytes 3932168 | tf_op jit(solution)/shard_map/ppermute | solution.py:51
  21.4 3.4 %collective-permute-start.7 = (f32[64,1280]{1,0:T(8,128)S(1)}, f32[64,1280]{1,0:T(8,128)S(1)}, u32[]{:S(2)}, u32[]{:S(2)}) collective-permute-start(f32[64,1280]{1,0:T(8,128)S(1)} %pad_maximum_fusion), channel_id=1, source_target_pairs={{0,1},{1,0},{2,3},{3,2},{4,5},{5,4},{6,7},{7,6},{8,9},{9,8},{10,11... | collective-permute-start | bytes 983048 | tf_op jit(solution)/shard_map/ppermute | solution.py:102
  26.2 6.6 %collective-permute-start.9 = (f32[2,32,640]{2,1,0:T(8,128)S(1)}, f32[2,32,640]{2,1,0:T(8,128)S(1)}, u32[]{:S(2)}, u32[]{:S(2)}) collective-permute-start(f32[2,32,640]{2,1,0:T(8,128)S(1)} %pad_maximum_fusion.1), channel_id=1, source_target_pairs={{0,48},{16,0},{32,16},{48,32},{64,112},{80,64},{96,80},{112,96},{1... | collective-permute-start | bytes 491528 | tf_op jit(solution)/shard_map/ppermute | solution.py:73
  29.0 7.5 %collective-permute-start.11 = (f32[2,32,640]{2,1,0:T(8,128)S(1)}, f32[2,32,640]{2,1,0:T(8,128)S(1)}, u32[]{:S(2)}, u32[]{:S(2)}) collective-permute-start(f32[2,32,640]{2,1,0:T(8,128)S(1)} %pad_maximum_fusion.4), channel_id=1, source_target_pairs={{0,16},{16,32},{32,48},{48,0},{64,80},{80,96},{96,112},{112,64},{1... | collective-permute-start | bytes 491528 | tf_op jit(solution)/shard_map/ppermute | solution.py:74
  32.8 7.4 %collective-permute-start.13 = (f32[2,32,640]{2,1,0:T(8,128)S(1)}, f32[2,32,640]{2,1,0:T(8,128)S(1)}, u32[]{:S(2)}, u32[]{:S(2)}) collective-permute-start(f32[2,32,640]{2,1,0:T(8,128)S(1)} %get-tuple-element.28), channel_id=1, source_target_pairs={{0,48},{16,0},{32,16},{48,32},{64,112},{80,64},{96,80},{112,96},{1... | collective-permute-start | bytes 491528 | tf_op jit(solution)/shard_map/ppermute | solution.py:79
  36.6 7.6 %collective-permute-start.14 = (f32[2,32,640]{2,1,0:T(8,128)S(1)}, f32[2,32,640]{2,1,0:T(8,128)S(1)}, u32[]{:S(2)}, u32[]{:S(2)}) collective-permute-start(f32[2,32,640]{2,1,0:T(8,128)S(1)} %get-tuple-element.26), channel_id=1, source_target_pairs={{0,16},{16,32},{32,48},{48,0},{64,80},{80,96},{96,112},{112,64},{1... | collective-permute-start | bytes 491528 | tf_op jit(solution)/shard_map/ppermute | solution.py:80
  36.7 11.4 %collective-permute-start.10 = (f32[2,32,640]{2,1,0:T(8,128)S(1)}, f32[2,32,640]{2,1,0:T(8,128)S(1)}, u32[]{:S(2)}, u32[]{:S(2)}) collective-permute-start(f32[2,32,640]{2,1,0:T(8,128)S(1)} %get-tuple-element.27), channel_id=1, source_target_pairs={{0,48},{16,0},{32,16},{48,32},{64,112},{80,64},{96,80},{112,96},{1... | collective-permute-start | bytes 491528 | tf_op jit(solution)/shard_map/ppermute | solution.py:85
  39.9 8.2 %collective-permute-start.12 = (f32[2,32,640]{2,1,0:T(8,128)S(1)}, f32[2,32,640]{2,1,0:T(8,128)S(1)}, u32[]{:S(2)}, u32[]{:S(2)}) collective-permute-start(f32[2,32,640]{2,1,0:T(8,128)S(1)} %get-tuple-element.25), channel_id=1, source_target_pairs={{0,16},{16,32},{32,48},{48,0},{64,80},{80,96},{96,112},{112,64},{1... | collective-permute-start | bytes 491528 | tf_op jit(solution)/shard_map/ppermute | solution.py:86
  44.3 7.1 %collective-permute-start.15 = (f32[2,32,640]{2,1,0:T(8,128)S(1)}, f32[2,32,640]{2,1,0:T(8,128)S(1)}, u32[]{:S(2)}, u32[]{:S(2)}) collective-permute-start(f32[2,32,640]{2,1,0:T(8,128)S(1)} %select_add_fusion), channel_id=1, source_target_pairs={{0,64},{16,80},{32,96},{48,112},{64,0},{80,16},{96,32},{112,48},{1... | collective-permute-start | bytes 491528 | tf_op jit(solution)/shard_map/ppermute | solution.py:83

commit v20 on v19

--- a/solution.py
+++ b/solution.py
@@ -52,7 +52,7 @@
         mo = lax.axis_index("occ")
         x, zh = mo % nx, mo // nx
 
-        def reduce_both(res_l, res_o, far_o):
+        def reduce_both(res_l, res_o, far_l, far_o):
             def half_block(r):
                 k = ((r % nx - y) % ny) * 2 + ((r // nx) ^ zl)
                 return jnp.stack(
@@ -68,10 +68,8 @@
             def b_blk(t):
                 return half_block(nx + t % nx)
 
-            far_l = lax.dynamic_index_in_dim(res_l, slot((x + 2) % nx), 0, keepdims=False)
-            far_lb = lax.dynamic_index_in_dim(res_l, slot(nx + (x + 2) % nx), 0, keepdims=False)
-            p1 = lax.ppermute(jnp.stack([far_l, far_o[:rows]]), "occ", x_shift(-1))
-            q1 = lax.ppermute(jnp.stack([far_lb, far_o[rows:]]), "occ", x_shift(1))
+            p1 = lax.ppermute(jnp.stack([far_l[:rows], far_o[:rows]]), "occ", x_shift(-1))
+            q1 = lax.ppermute(jnp.stack([far_l[rows:], far_o[rows:]]), "occ", x_shift(1))
             to_m_a, to_m_b = a_blk(x + nx - 1) + p1, b_blk(x + nx - 1)
             to_p_a, to_p_b = a_blk(x + 1), b_blk(x + 1) + q1
             low = zh == 0
@@ -100,9 +98,10 @@
             axis=0,
         )
         far_o = matmul(lax.ppermute(far, "vir", core_swap), half)
-        res_l, far_o = lax.optimization_barrier((res_l, far_o))
+        far_l = matmul(far, half)
+        far_l, far_o = lax.optimization_barrier((far_l, far_o))
         res_o = matmul(other, half).reshape(8, rows, -1)
-        sums = reduce_both(res_l, res_o, far_o)
+        sums = reduce_both(res_l, res_o, far_l, far_o)
         first = jnp.where(c == 0, sums[0], sums[1])
         second = jnp.where(c == 0, sums[1], sums[0])
         return jnp.concatenate([first, second], axis=0)

time: 52.2 us -> 50.3 us (0.964)
  the two profiles are of different devices: /device:TPU:24 before, /device:TPU:30 now
where the time goes in v20:
time: 50.3 us; the launch traced here: 50.1 us
  starting transfers between devices  22 us (44%)
  waiting for transfers between devices  19.3 us (38%)
  matrix products  6.63 us (13%)
  local copies, waits for them, and re-layouts  1.2 us (2%)
  other arithmetic  0.89 us (2%)
    dot_general x4, matrix products, matmul(): return jnp.dot(a, b, preferred_element_type=jnp.float32, precision=HIGH)  6.63 us
    ppermute x1, waiting for transfers between devices, body(): z3 = lax.ppermute(yp2, 'vir', z_swap)  5.17 us
    ppermute x1, starting transfers between devices, reduce_both(): from_zhi = lax.ppermute(got_send, 'occ', zhi_swap)  3.66 us
    ppermute x1, waiting for transfers between devices, reduce_both(): from_zhi = lax.ppermute(got_send, 'occ', zhi_swap)  3.29 us
    ppermute x1, waiting for transfers between devices, body(): yp2 = lax.ppermute(yp1, 'vir', y_shift(-1))  3.24 us
    ppermute x1, starting transfers between devices, body(): ym1z = lax.ppermute(z1, 'vir', y_shift(1))  3.23 us
    ppermute x1, starting transfers between devices, reduce_both(): lax.ppermute(jnp.where(low, to_p_a, to_p_b), 'occ', x_shift(1))  2.9 us
    ppermute x1, starting transfers between devices, body(): ym1 = lax.ppermute(own, 'vir', y_shift(1))  2.49 us
  transfers between devices with their start and end apart: 16, of which 7 were waited for; matrix products, arithmetic and copies ran while one was open for 16% of the time, Pallas kernels for 0%

profile of v20, /device:TPU:30, one launch (start us, length us, event | category | flops | bytes accessed | tf_op | source)
XLA Modules:
  0.0 50.1 jit_solution(16051155371163483790)
XLA Ops:
  0.0 0.7 %collective-permute-start.1 = (f32[32,1280]{1,0:T(8,128)}, f32[32,1280]{1,0:T(8,128)S(1)}, u32[]{:S(2)}, u32[]{:S(2)}) collective-permute-start(f32[32,1280]{1,0:T(8,128)} %param.2), channel_id=1, source_target_pairs={{0,6},{1,7},{2,0},{3,1},{4,2},{5,3},{6,4},{7,5},{8,14},{9,15},{10,... | collective-permute-start | bytes 491528 | tf_op jit(solution)/shard_map/ppermute | solution.py:43
  0.7 1.9 %collective-permute-start = (f32[32,1280]{1,0:T(8,128)}, f32[32,1280]{1,0:T(8,128)S(1)}, u32[]{:S(2)}, u32[]{:S(2)}) collective-permute-start(f32[32,1280]{1,0:T(8,128)} %param.2), channel_id=1, source_target_pairs={{0,8},{1,9},{2,10},{3,11},{4,12},{5,13},{6,14},{7,15},{8,0},{9,1},... | collective-permute-start | bytes 491528 | tf_op jit(solution)/shard_map/ppermute | solution.py:41
  2.7 2.5 %collective-permute-start.5 = (f32[32,1280]{1,0:T(8,128)}, f32[32,1280]{1,0:T(8,128)S(1)}, u32[]{:S(2)}, u32[]{:S(2)}) collective-permute-start(f32[32,1280]{1,0:T(8,128)} %param.2), channel_id=1, source_target_pairs={{0,2},{1,3},{2,4},{3,5},{4,6},{5,7},{6,0},{7,1},{8,10},{9,11},{10,... | collective-permute-start | bytes 491528 | tf_op jit(solution)/shard_map/ppermute | solution.py:42
  5.2 1.0 %constant_dynamic-update-slice_fusion.7 = f32[256,1280]{1,0:T(8,128)S(1)} fusion(f32[32,1280]{1,0:T(8,128)} %param.2), kind=kLoop, calls=%fused_computation.43 | loop fusion | bytes 327680
  6.1 1.2 %collective-permute-done.1 = f32[32,1280]{1,0:T(8,128)S(1)} collective-permute-done((f32[32,1280]{1,0:T(8,128)}, f32[32,1280]{1,0:T(8,128)S(1)}, u32[]{:S(2)}, u32[]{:S(2)}) %collective-permute-start.1) | collective-permute-done | bytes 163872 | tf_op jit(solution)/shard_map/ppermute | solution.py:43
  7.4 1.9 %collective-permute-start.2 = (f32[32,1280]{1,0:T(8,128)S(1)}, f32[32,1280]{1,0:T(8,128)S(1)}, u32[]{:S(2)}, u32[]{:S(2)}) collective-permute-start(f32[32,1280]{1,0:T(8,128)S(1)} %collective-permute-done.1), channel_id=1, source_target_pairs={{0,8},{1,9},{2,10},{3,11},{4,12},{5,13},{6,14},{7,15},{8,0},{9,1},... | collective-permute-start | bytes 491528 | tf_op jit(solution)/shard_map/ppermute | solution.py:44
  9.3 3.2 %collective-permute-start.6 = (f32[32,1280]{1,0:T(8,128)S(1)}, f32[32,1280]{1,0:T(8,128)S(1)}, u32[]{:S(2)}, u32[]{:S(2)}) collective-permute-start(f32[32,1280]{1,0:T(8,128)S(1)} %collective-permute-done), channel_id=1, source_target_pairs={{0,2},{1,3},{2,4},{3,5},{4,6},{5,7},{6,0},{7,1},{8,10},{9,11},{10,... | collective-permute-start | bytes 491528 | tf_op jit(solution)/shard_map/ppermute | solution.py:46
  12.6 3.2 %collective-permute-done.3 = f32[32,1280]{1,0:T(8,128)S(1)} collective-permute-done((f32[32,1280]{1,0:T(8,128)S(1)}, f32[32,1280]{1,0:T(8,128)S(1)}, u32[]{:S(2)}, u32[]{:S(2)}) %collective-permute-start.3) | collective-permute-done | bytes 163872 | tf_op jit(solution)/shard_map/ppermute | solution.py:45
  16.0 5.2 %collective-permute-done.4 = f32[32,1280]{1,0:T(8,128)S(1)} collective-permute-done((f32[32,1280]{1,0:T(8,128)S(1)}, f32[32,1280]{1,0:T(8,128)S(1)}, u32[]{:S(2)}, u32[]{:S(2)}) %collective-permute-start.4) | collective-permute-done | bytes 163872 | tf_op jit(solution)/shard_map/ppermute | solution.py:47
  21.4 0.6 %collective-permute-start.8 = (f32[64,1280]{1,0:T(8,128)S(1)}, f32[64,1280]{1,0:T(8,128)S(1)}, u32[]{:S(2)}, u32[]{:S(2)}) collective-permute-start(f32[64,1280]{1,0:T(8,128)S(1)} %pad_maximum_fusion), channel_id=1, source_target_pairs={{0,1},{1,0},{2,3},{3,2},{4,5},{5,4},{6,7},{7,6},{8,9},{9,8},{10,11... | collective-permute-start | bytes 983048 | tf_op jit(solution)/shard_map/ppermute | solution.py:100
  21.9 2.1 %fusion.6 = f32[256,640]{1,0:T(8,128)S(1)} fusion(f32[256,1280]{1,0:T(8,128)S(1)} %constant_dynamic-update-slice_fusion, f32[1280,640]{1,0:T(8,128)S(1)} %copy-done), kind=kOutput, calls=%fused_computation.6 | convolution fusion | flops 1259110400 | bytes 5242880 | tf_op jit(solution)/shard_map/dot_general | solution.py:32
  24.0 1.3 %fusion.2 = f32[64,640]{1,0:T(8,128)S(1)} fusion(f32[1280,640]{1,0:T(8,128)S(1)} %copy-done, f32[32,1280]{1,0:T(8,128)S(1)} %get-tuple-element.10, f32[32,1280]{1,0:T(8,128)S(1)} %get-tuple-element.9), kind=kOutput, calls=%fused_computation.2 | convolution fusion | flops 315473920 | bytes 3768320 | tf_op jit(solution)/shard_map/dot_general | solution.py:32
  25.3 1.3 %fusion = f32[64,640]{1,0:T(8,128)S(1)} fusion(f32[64,1280]{1,0:T(8,128)S(1)} %collective-permute-done.8, f32[1280,640]{1,0:T(8,128)S(1)} %copy-done), kind=kOutput, calls=%fused_computation | convolution fusion | flops 315392000 | bytes 3768320 | tf_op jit(solution)/shard_map/dot_general | solution.py:32
  26.6 0.5 %collective-permute-start.11 = (f32[2,32,640]{2,1,0:T(8,128)S(1)}, f32[2,32,640]{2,1,0:T(8,128)S(1)}, u32[]{:S(2)}, u32[]{:S(2)}) collective-permute-start(f32[2,32,640]{2,1,0:T(8,128)S(1)} %pad_maximum_fusion.4), channel_id=1, source_target_pairs={{0,16},{16,32},{32,48},{48,0},{64,80},{80,96},{96,112},{112,64},{1... | collective-permute-start | bytes 491528 | tf_op jit(solution)/shard_map/ppermute | solution.py:72
  27.2 1.6 %collective-permute-start.9 = (f32[2,32,640]{2,1,0:T(8,128)S(1)}, f32[2,32,640]{2,1,0:T(8,128)S(1)}, u32[]{:S(2)}, u32[]{:S(2)}) collective-permute-start(f32[2,32,640]{2,1,0:T(8,128)S(1)} %pad_maximum_fusion.1), channel_id=1, source_target_pairs={{0,48},{16,0},{32,16},{48,32},{64,112},{80,64},{96,80},{112,96},{1... | collective-permute-start | bytes 491528 | tf_op jit(solution)/shard_map/ppermute | solution.py:71
  28.8 2.1 %fusion.4 = f32[256,640]{1,0:T(8,128)S(1)} fusion(f32[256,1280]{1,0:T(8,128)S(1)} %collective-permute-done.7, f32[1280,640]{1,0:T(8,128)S(1)} %copy-done), kind=kOutput, calls=%fused_computation.4 | convolution fusion | flops 1259110400 | bytes 5242880 | tf_op jit(solution)/shard_map/dot_general | solution.py:32
  30.9 1.9 %collective-permute-done.11 = f32[2,32,640]{2,1,0:T(8,128)S(1)} collective-permute-done((f32[2,32,640]{2,1,0:T(8,128)S(1)}, f32[2,32,640]{2,1,0:T(8,128)S(1)}, u32[]{:S(2)}, u32[]{:S(2)}) %collective-permute-start.11) | collective-permute-done | bytes 163872 | tf_op jit(solution)/shard_map/ppermute | solution.py:72
  32.8 1.8 %collective-permute-start.14 = (f32[2,32,640]{2,1,0:T(8,128)S(1)}, f32[2,32,640]{2,1,0:T(8,128)S(1)}, u32[]{:S(2)}, u32[]{:S(2)}) collective-permute-start(f32[2,32,640]{2,1,0:T(8,128)S(1)} %get-tuple-element.24), channel_id=1, source_target_pairs={{0,16},{16,32},{32,48},{48,0},{64,80},{80,96},{96,112},{112,64},{1... | collective-permute-start | bytes 491528 | tf_op jit(solution)/shard_map/ppermute | solution.py:78
  35.0 2.9 %collective-permute-start.12 = (f32[2,32,640]{2,1,0:T(8,128)S(1)}, f32[2,32,640]{2,1,0:T(8,128)S(1)}, u32[]{:S(2)}, u32[]{:S(2)}) collective-permute-start(f32[2,32,640]{2,1,0:T(8,128)S(1)} %get-tuple-element.23), channel_id=1, source_target_pairs={{0,16},{16,32},{32,48},{48,0},{64,80},{80,96},{96,112},{112,64},{1... | collective-permute-start | bytes 491528 | tf_op jit(solution)/shard_map/ppermute | solution.py:84
  37.9 2.0 %collective-permute-done.14 = f32[2,32,640]{2,1,0:T(8,128)S(1)} collective-permute-done((f32[2,32,640]{2,1,0:T(8,128)S(1)}, f32[2,32,640]{2,1,0:T(8,128)S(1)}, u32[]{:S(2)}, u32[]{:S(2)}) %collective-permute-start.14) | collective-permute-done | bytes 163872 | tf_op jit(solution)/shard_map/ppermute | solution.py:78
  39.9 2.4 %collective-permute-done.13 = f32[2,32,640]{2,1,0:T(8,128)S(1)} collective-permute-done((f32[2,32,640]{2,1,0:T(8,128)S(1)}, f32[2,32,640]{2,1,0:T(8,128)S(1)}, u32[]{:S(2)}, u32[]{:S(2)}) %collective-permute-start.13) | collective-permute-done | bytes 163872 | tf_op jit(solution)/shard_map/ppermute | solution.py:77
  42.4 3.7 %collective-permute-start.15 = (f32[2,32,640]{2,1,0:T(8,128)S(1)}, f32[2,32,640]{2,1,0:T(8,128)S(1)}, u32[]{:S(2)}, u32[]{:S(2)}) collective-permute-start(f32[2,32,640]{2,1,0:T(8,128)S(1)} %select_add_fusion), channel_id=1, source_target_pairs={{0,64},{16,80},{32,96},{48,112},{64,0},{80,16},{96,32},{112,48},{1... | collective-permute-start | bytes 491528 | tf_op jit(solution)/shard_map/ppermute | solution.py:81
  46.1 3.3 %collective-permute-done.15 = f32[2,32,640]{2,1,0:T(8,128)S(1)} collective-permute-done((f32[2,32,640]{2,1,0:T(8,128)S(1)}, f32[2,32,640]{2,1,0:T(8,128)S(1)}, u32[]{:S(2)}, u32[]{:S(2)}) %collective-permute-start.15) | collective-permute-done | bytes 163872 | tf_op jit(solution)/shard_map/ppermute | solution.py:81
  49.5 0.7 %pad_maximum_fusion.7 = f32[64,640]{1,0:T(8,128)} fusion(f32[32,640]{1,0:T(8,128)S(1)} %get-tuple-element.28, f32[32,640]{1,0:T(8,128)S(1)} %get-tuple-element.27), kind=kLoop, calls=%fused_computation.21 | loop fusion | flops 40960 | bytes 327680 | tf_op jit(solution)/shard_map/concatenate | solution.py:107
  (34 shorter events, 1.1 us)
Async XLA Ops:
  0.0 7.4 %collective-permute-start.1 = (f32[32,1280]{1,0:T(8,128)}, f32[32,1280]{1,0:T(8,128)S(1)}, u32[]{:S(2)}, u32[]{:S(2)}) collective-permute-start(f32[32,1280]{1,0:T(8,128)} %param.2), channel_id=1, source_target_pairs={{0,6},{1,7},{2,0},{3,1},{4,2},{5,3},{6,4},{7,5},{8,14},{9,15},{10,... | collective-permute-start | bytes 491528 | tf_op jit(solution)/shard_map/ppermute | solution.py:43
  0.7 8.5 %collective-permute-start = (f32[32,1280]{1,0:T(8,128)}, f32[32,1280]{1,0:T(8,128)S(1)}, u32[]{:S(2)}, u32[]{:S(2)}) collective-permute-start(f32[32,1280]{1,0:T(8,128)} %param.2), channel_id=1, source_target_pairs={{0,8},{1,9},{2,10},{3,11},{4,12},{5,13},{6,14},{7,15},{8,0},{9,1},... | collective-permute-start | bytes 491528 | tf_op jit(solution)/shard_map/ppermute | solution.py:41
  2.7 18.5 %collective-permute-start.5 = (f32[32,1280]{1,0:T(8,128)}, f32[32,1280]{1,0:T(8,128)S(1)}, u32[]{:S(2)}, u32[]{:S(2)}) collective-permute-start(f32[32,1280]{1,0:T(8,128)} %param.2), channel_id=1, source_target_pairs={{0,2},{1,3},{2,4},{3,5},{4,6},{5,7},{6,0},{7,1},{8,10},{9,11},{10,... | collective-permute-start | bytes 491528 | tf_op jit(solution)/shard_map/ppermute | solution.py:42
  7.4 8.6 %collective-permute-start.2 = (f32[32,1280]{1,0:T(8,128)S(1)}, f32[32,1280]{1,0:T(8,128)S(1)}, u32[]{:S(2)}, u32[]{:S(2)}) collective-permute-start(f32[32,1280]{1,0:T(8,128)S(1)} %collective-permute-done.1), channel_id=1, source_target_pairs={{0,8},{1,9},{2,10},{3,11},{4,12},{5,13},{6,14},{7,15},{8,0},{9,1},... | collective-permute-start | bytes 491528 | tf_op jit(solution)/shard_map/ppermute | solution.py:44
  9.3 6.5 %collective-permute-start.3 = (f32[32,1280]{1,0:T(8,128)S(1)}, f32[32,1280]{1,0:T(8,128)S(1)}, u32[]{:S(2)}, u32[]{:S(2)}) collective-permute-start(f32[32,1280]{1,0:T(8,128)S(1)} %collective-permute-done.1), channel_id=1, source_target_pairs={{0,6},{1,7},{2,0},{3,1},{4,2},{5,3},{6,4},{7,5},{8,14},{9,15},{10,... | collective-permute-start | bytes 491528 | tf_op jit(solution)/shard_map/ppermute | solution.py:45
  9.3 11.9 %collective-permute-start.6 = (f32[32,1280]{1,0:T(8,128)S(1)}, f32[32,1280]{1,0:T(8,128)S(1)}, u32[]{:S(2)}, u32[]{:S(2)}) collective-permute-start(f32[32,1280]{1,0:T(8,128)S(1)} %collective-permute-done), channel_id=1, source_target_pairs={{0,2},{1,3},{2,4},{3,5},{4,6},{5,7},{6,0},{7,1},{8,10},{9,11},{10,... | collective-permute-start | bytes 491528 | tf_op jit(solution)/shard_map/ppermute | solution.py:46
  12.5 9.4 %copy-start = (f32[1280,640]{1,0:T(8,128)S(1)}, f32[1280,640]{1,0:T(8,128)}, u32[]{:S(2)}) copy-start(f32[1280,640]{1,0:T(8,128)} %param.3) | copy-start | bytes 9830404
  15.8 5.3 %collective-permute-start.4 = (f32[32,1280]{1,0:T(8,128)S(1)}, f32[32,1280]{1,0:T(8,128)S(1)}, u32[]{:S(2)}, u32[]{:S(2)}) collective-permute-start(f32[32,1280]{1,0:T(8,128)S(1)} %collective-permute-done.3), channel_id=1, source_target_pairs={{0,8},{1,9},{2,10},{3,11},{4,12},{5,13},{6,14},{7,15},{8,0},{9,1},... | collective-permute-start | bytes 491528 | tf_op jit(solution)/shard_map/ppermute | solution.py:47
  21.2 7.6 %collective-permute-start.7 = (f32[256,1280]{1,0:T(8,128)S(1)}, f32[256,1280]{1,0:T(8,128)S(1)}, u32[]{:S(2)}, u32[]{:S(2)}) collective-permute-start(f32[256,1280]{1,0:T(8,128)S(1)} %constant_dynamic-update-slice_fusion), channel_id=1, source_target_pairs={{0,1},{1,0},{2,3},{3,2},{4,5},{5,4},{6,7},{7,6},{8,9},{9,8},{10,11... | collective-permute-start | bytes 3932168 | tf_op jit(solution)/shard_map/ppermute | solution.py:51
  21.4 3.9 %collective-permute-start.8 = (f32[64,1280]{1,0:T(8,128)S(1)}, f32[64,1280]{1,0:T(8,128)S(1)}, u32[]{:S(2)}, u32[]{:S(2)}) collective-permute-start(f32[64,1280]{1,0:T(8,128)S(1)} %pad_maximum_fusion), channel_id=1, source_target_pairs={{0,1},{1,0},{2,3},{3,2},{4,5},{5,4},{6,7},{7,6},{8,9},{9,8},{10,11... | collective-permute-start | bytes 983048 | tf_op jit(solution)/shard_map/ppermute | solution.py:100
  26.6 6.2 %collective-permute-start.11 = (f32[2,32,640]{2,1,0:T(8,128)S(1)}, f32[2,32,640]{2,1,0:T(8,128)S(1)}, u32[]{:S(2)}, u32[]{:S(2)}) collective-permute-start(f32[2,32,640]{2,1,0:T(8,128)S(1)} %pad_maximum_fusion.4), channel_id=1, source_target_pairs={{0,16},{16,32},{32,48},{48,0},{64,80},{80,96},{96,112},{112,64},{1... | collective-permute-start | bytes 491528 | tf_op jit(solution)/shard_map/ppermute | solution.py:72
  27.2 7.4 %collective-permute-start.9 = (f32[2,32,640]{2,1,0:T(8,128)S(1)}, f32[2,32,640]{2,1,0:T(8,128)S(1)}, u32[]{:S(2)}, u32[]{:S(2)}) collective-permute-start(f32[2,32,640]{2,1,0:T(8,128)S(1)} %pad_maximum_fusion.1), channel_id=1, source_target_pairs={{0,48},{16,0},{32,16},{48,32},{64,112},{80,64},{96,80},{112,96},{1... | collective-permute-start | bytes 491528 | tf_op jit(solution)/shard_map/ppermute | solution.py:71
  32.8 7.1 %collective-permute-start.14 = (f32[2,32,640]{2,1,0:T(8,128)S(1)}, f32[2,32,640]{2,1,0:T(8,128)S(1)}, u32[]{:S(2)}, u32[]{:S(2)}) collective-permute-start(f32[2,32,640]{2,1,0:T(8,128)S(1)} %get-tuple-element.24), channel_id=1, source_target_pairs={{0,16},{16,32},{32,48},{48,0},{64,80},{80,96},{96,112},{112,64},{1... | collective-permute-start | bytes 491528 | tf_op jit(solution)/shard_map/ppermute | solution.py:78
  34.6 7.8 %collective-permute-start.13 = (f32[2,32,640]{2,1,0:T(8,128)S(1)}, f32[2,32,640]{2,1,0:T(8,128)S(1)}, u32[]{:S(2)}, u32[]{:S(2)}) collective-permute-start(f32[2,32,640]{2,1,0:T(8,128)S(1)} %get-tuple-element.26), channel_id=1, source_target_pairs={{0,48},{16,0},{32,16},{48,32},{64,112},{80,64},{96,80},{112,96},{1... | collective-permute-start | bytes 491528 | tf_op jit(solution)/shard_map/ppermute | solution.py:77
  35.0 11.1 %collective-permute-start.12 = (f32[2,32,640]{2,1,0:T(8,128)S(1)}, f32[2,32,640]{2,1,0:T(8,128)S(1)}, u32[]{:S(2)}, u32[]{:S(2)}) collective-permute-start(f32[2,32,640]{2,1,0:T(8,128)S(1)} %get-tuple-element.23), channel_id=1, source_target_pairs={{0,16},{16,32},{32,48},{48,0},{64,80},{80,96},{96,112},{112,64},{1... | collective-permute-start | bytes 491528 | tf_op jit(solution)/shard_map/ppermute | solution.py:84
  37.9 8.2 %collective-permute-start.10 = (f32[2,32,640]{2,1,0:T(8,128)S(1)}, f32[2,32,640]{2,1,0:T(8,128)S(1)}, u32[]{:S(2)}, u32[]{:S(2)}) collective-permute-start(f32[2,32,640]{2,1,0:T(8,128)S(1)} %get-tuple-element.25), channel_id=1, source_target_pairs={{0,48},{16,0},{32,16},{48,32},{64,112},{80,64},{96,80},{112,96},{1... | collective-permute-start | bytes 491528 | tf_op jit(solution)/shard_map/ppermute | solution.py:83
  42.4 7.0 %collective-permute-start.15 = (f32[2,32,640]{2,1,0:T(8,128)S(1)}, f32[2,32,640]{2,1,0:T(8,128)S(1)}, u32[]{:S(2)}, u32[]{:S(2)}) collective-permute-start(f32[2,32,640]{2,1,0:T(8,128)S(1)} %select_add_fusion), channel_id=1, source_target_pairs={{0,64},{16,80},{32,96},{48,112},{64,0},{80,16},{96,32},{112,48},{1... | collective-permute-start | bytes 491528 | tf_op jit(solution)/shard_map/ppermute | solution.py:81
